TPU v7x, 32 devices: a whole 2x2x4 slice. The times are simulated.
32 devices in a mesh: lat: 4 (over y, x), lon: 8 (over z, core).
Axes of the slice: x: 2, y: 2, z: 4, core: 2. Of those that a mesh axis runs over, the one named last changes fastest.
Arguments:
- fields: float32 [5, 8, 64, 5760], P(None, None, 'lat', 'lon'), may hold values from -10 to 10
- lon_courant: float32 [8, 64, 5760], P(None, 'lat', 'lon'), may hold values from -0.45 to 0.45
- lat_courant: float32 [8, 64, 5760], P(None, 'lat', 'lon'), may hold values from -0.45 to 0.45
- filter_rows: int32 [32], replicated, may hold values from 0 to 63, as said below
- cutoff: int32 [32], replicated, may hold values from 90 to 1440
Outputs:
- advanced: float32 [5, 8, 64, 5760], P(None, None, 'lat', 'lon')
Inputs may be any that keep to these rules, and one draw needn't show every extreme that they name: `filter_rows`: sorted ascending and distinct: the first entries are the rows 0, 1, 2, ... and the rest the rows up to 63, the first group holding between 8 and 24 rows.
All inputs are finite; a program needn't handle non-finite values.
Results may differ from a plain program's by a relative error of at most 0.00005.
Values sent between devices are 32-bit elements; how exact they have to be, the bound alone decides.
No kernel may reach another device: no remote copies, remote signals or barrier semaphores. Data moves between devices by JAX's collectives and lax.ppermute only.
A program may use at most 64 MiB of HBM per device.

v0:
```python
from functools import partial
import math

import jax
import jax.numpy as jnp
from jax import lax
from jax.sharding import PartitionSpec as P

radix_len = 128


def with_halo(x, sides, width, wrap):
    for axis, dim in sides:
        size, length = (lax.axis_size(axis), x.shape[dim])
        up = [(i, (i + 1) % size) for i in range(size if wrap else size - 1)]
        down = [(j, i) for i, j in up]
        last = lax.slice_in_dim(x, length - width, length, axis=dim)
        leading = lax.slice_in_dim(x, 0, width, axis=dim)
        before = lax.ppermute(last, axis, up)
        after = lax.ppermute(leading, axis, down)
        x = jnp.concatenate([before, x, after], axis=dim)
    return x


def phase_table(row_total, col_total, modulus):
    product = (
        jnp.arange(row_total, dtype=jnp.int32)[:, None]
        * jnp.arange(col_total, dtype=jnp.int32)[None, :]
        % modulus
    )
    angle = product.astype(jnp.float32) * (2.0 * math.pi / modulus)
    return (jnp.cos(angle), jnp.sin(angle))


def filter_lines(lines, line_cut):
    line_total, circle = lines.shape
    outer = circle // radix_len
    mixer = partial(jnp.einsum, precision=lax.Precision.HIGHEST)
    outer_cos, outer_sin = phase_table(outer, outer, outer)
    inner_cos, inner_sin = phase_table(radix_len, radix_len, radix_len)
    twist_cos, twist_sin = phase_table(outer, radix_len, circle)
    values = lines.reshape(line_total, outer, radix_len)
    first_re = mixer("lan,aj->ljn", values, outer_cos)
    first_im = -mixer("lan,aj->ljn", values, outer_sin)
    turned_re = first_re * twist_cos + first_im * twist_sin
    turned_im = first_im * twist_cos - first_re * twist_sin
    spec_re = mixer("ljn,nk->ljk", turned_re, inner_cos) + mixer(
        "ljn,nk->ljk", turned_im, inner_sin
    )
    spec_im = mixer("ljn,nk->ljk", turned_im, inner_cos) - mixer(
        "ljn,nk->ljk", turned_re, inner_sin
    )
    wave = (
        jnp.arange(outer, dtype=jnp.int32)[:, None]
        + outer * jnp.arange(radix_len, dtype=jnp.int32)[None, :]
    )
    mode_value = jnp.minimum(wave, circle - wave).astype(jnp.float32)[None]
    cut_value = line_cut[:, None, None]
    damp = jnp.where(mode_value <= cut_value, 1.0, (cut_value / jnp.maximum(mode_value, 1.0)) ** 2)
    spec_re = spec_re * damp
    spec_im = spec_im * damp
    back_re = mixer("ljk,kn->ljn", spec_re, inner_cos) - mixer("ljk,kn->ljn", spec_im, inner_sin)
    back_im = mixer("ljk,kn->ljn", spec_im, inner_cos) + mixer("ljk,kn->ljn", spec_re, inner_sin)
    untwist_re = back_re * twist_cos - back_im * twist_sin
    untwist_im = back_im * twist_cos + back_re * twist_sin
    result = mixer("ljn,ja->lan", untwist_re, outer_cos) - mixer(
        "ljn,ja->lan", untwist_im, outer_sin
    )
    return (result / circle).reshape(line_total, circle)


def face_flux(courant, near_value, far_value):
    return 0.5 * courant * (near_value + far_value) - 0.5 * courant * courant * (
        far_value - near_value
    )


def body(fields, lon_courant, lat_courant, filter_rows, cutoff):
    field_count, level_count, rows_dev, columns = fields.shape
    stacked = field_count * level_count
    lon_devices = lax.axis_size("lon")
    lat_devices = lax.axis_size("lat")
    total_lon = columns * lon_devices
    flat_fields = fields.reshape(stacked, rows_dev, columns)
    east_west = with_halo(
        jnp.concatenate([flat_fields, lon_courant], axis=0), (("lon", 2),), 1, True
    )
    north_south = with_halo(
        jnp.concatenate([flat_fields, lat_courant], axis=0), (("lat", 1),), 1, False
    )
    wide_fields = east_west[:stacked].reshape(field_count, level_count, rows_dev, columns + 2)
    wide_courant = east_west[stacked:]
    column_flux = face_flux(wide_courant[..., :-1], wide_fields[..., :-1], wide_fields[..., 1:])
    tall_fields = north_south[:stacked].reshape(field_count, level_count, rows_dev + 2, columns)
    tall_courant = north_south[stacked:]
    row_flux = face_flux(tall_courant[:, :-1], tall_fields[:, :, :-1], tall_fields[:, :, 1:])
    tile_index = lax.axis_index("lat")
    lower_row = tile_index * rows_dev - 1 + jnp.arange(rows_dev + 1, dtype=jnp.int32)
    row_flux = jnp.where((lower_row == rows_dev * lat_devices - 1)[:, None], 0.0, row_flux)
    increment = -(column_flux[..., 1:] - column_flux[..., :-1]) - (
        row_flux[:, :, 1:] - row_flux[:, :, :-1]
    )
    flat_increment = increment.reshape(stacked, rows_dev, columns)
    half_rows = rows_dev // 2
    pair_shift = lat_devices // 2
    pair_perm = [(i, (i + pair_shift) % lat_devices) for i in range(lat_devices)]
    is_low = tile_index < pair_shift
    partner_index = (tile_index + pair_shift) % lat_devices

    def row_info(tile):
        row_global = tile * rows_dev + jnp.arange(rows_dev, dtype=jnp.int32)
        matched = filter_rows[None, :] == row_global[:, None]
        return jnp.any(matched, axis=1), jnp.sum(jnp.where(matched, cutoff[None, :], 0), axis=1)

    is_filtered, own_cut = row_info(tile_index)
    _, partner_cut = row_info(partner_index)
    row_cut = jnp.where(is_filtered, own_cut, partner_cut).astype(jnp.float32)
    low_half = flat_increment[:, :half_rows]
    high_half = flat_increment[:, half_rows:]
    kept = jnp.where(is_low, low_half, high_half)
    given = jnp.where(is_low, high_half, low_half)
    taken = lax.ppermute(given, "lat", pair_perm)
    kept_filtered = jnp.where(is_low, is_filtered[:half_rows], is_filtered[half_rows:])
    kept_cut = jnp.where(is_low, row_cut[:half_rows], row_cut[half_rows:])
    pair_lines = jnp.where(kept_filtered[None, :, None], kept, taken)
    line_count = stacked * half_rows // lon_devices
    full_lines = lax.all_to_all(
        pair_lines.reshape(stacked * half_rows, columns),
        "lon",
        split_axis=0,
        concat_axis=1,
        tiled=True,
    )
    line_index = lax.axis_index("lon") * line_count + jnp.arange(line_count, dtype=jnp.int32)
    smoothed = filter_lines(full_lines, kept_cut[line_index % half_rows])
    returned = lax.all_to_all(smoothed, "lon", split_axis=1, concat_axis=0, tiled=True).reshape(
        stacked, half_rows, columns
    )
    handed_back = lax.ppermute(returned, "lat", pair_perm)
    smooth_rows = jnp.where(
        is_low,
        jnp.concatenate([returned, handed_back], axis=1),
        jnp.concatenate([handed_back, returned], axis=1),
    )
    final_increment = jnp.where(is_filtered[None, :, None], smooth_rows, flat_increment)
    return (flat_fields + final_increment).reshape(fields.shape)


def solution(mesh):
    placed = (P(None, None, "lat", "lon"), P(None, "lat", "lon"), P(None, "lat", "lon"), P(), P())
    return jax.shard_map(
        body, mesh=mesh, in_specs=placed, out_specs=P(None, None, "lat", "lon"), check_vma=False
    )
```

profile of v0, /device:TPU:0, one launch (start us, length us, event | category | flops | bytes accessed | tf_op | source)
XLA Modules:
  0.0 156.4 jit_solution(2159467434216467830)
XLA Ops:
  0.0 2.8 %fusion.29 = (f32[48,1,720]{2,1,0:T(1,128)}, f32[48,1,720]{2,1,0:T(1,128)}) fusion(f32[8,16,720]{2,1,0:T(8,128)} %param.7, f32[40,16,720]{2,1,0:T(8,128)} %bitcast.72), kind=kLoop, calls=%fused_computation.62 | loop fusion | flops 69120 | bytes 2488320 | tf_op jit(solution)/shard_map/concatenate | solution.py:89
  2.8 4.8 %collective-permute-start.2 = (f32[48,1,720]{2,1,0:T(1,128)}, f32[48,1,720]{2,1,0:T(1,128)S(1)}, u32[]{:S(2)}, u32[]{:S(2)}) collective-permute-start(f32[48,1,720]{2,1,0:T(1,128)} %get-tuple-element.13), channel_id=1, source_target_pairs={{0,8},{8,16},{16,24},{1,9},{9,17},{17,25},{2,10},{10,18},{18,26},{... | collective-permute-start | bytes 414728 | tf_op jit(solution)/shard_map/ppermute | solution.py:19
  7.6 1.3 collective-permute-start.3
  8.9 0.9 fusion.26
  9.9 3.5 %collective-permute-start.1 = (f32[48,16,1]{2,1,0:T(8,128)S(1)}, f32[48,16,1]{2,1,0:T(8,128)}, u32[]{:S(2)}, u32[]{:S(2)}) collective-permute-start(f32[48,16,1]{2,1,0:T(8,128)S(1)} %get-tuple-element.12), channel_id=1, source_target_pairs={{1,0},{2,1},{3,2},{4,3},{5,4},{6,5},{7,6},{0,7},{9,8},{10,9},{11,1... | collective-permute-start | bytes 9224 | tf_op jit(solution)/shard_map/ppermute | solution.py:20
  13.4 7.9 %collective-permute-done = f32[48,16,1]{2,1,0:T(8,128)S(1)} collective-permute-done((f32[48,16,1]{2,1,0:T(8,128)}, f32[48,16,1]{2,1,0:T(8,128)S(1)}, u32[]{:S(2)}, u32[]{:S(2)}) %collective-permute-start) | collective-permute-done | bytes 3104 | tf_op jit(solution)/shard_map/ppermute | solution.py:19
  21.6 1.6 %pad_maximum_fusion.3 = f32[40,16,722]{2,1,0:T(8,128)S(1)} fusion(f32[48,16,1]{2,1,0:T(8,128)} %collective-permute-done.1, f32[48,16,1]{2,1,0:T(8,128)S(1)} %collective-permute-done, f32[8,16,720]{2,1,0:T(8,128)S(1)} %copy-done.3, f32[40,16,720]{2,1,0:T(8,128)S(1)} %bitcast.75), kind=kLoop, calls=%fused_computation.12 | loop fusion | flops 1386240 | bytes 4066304 | tf_op jit(solution)/shard_map/concatenate | solution.py:21
  26.4 3.6 %collective-permute-start.4 = (f32[40,8,720]{2,1,0:T(8,128)S(1)}, f32[40,8,720]{2,1,0:T(8,128)S(1)}, u32[]{:S(2)}, u32[]{:S(2)}) collective-permute-start(f32[40,8,720]{2,1,0:T(8,128)S(1)} %slice_select_fusion), channel_id=1, source_target_pairs={{0,16},{8,24},{16,0},{24,8},{1,17},{9,25},{17,1},{25,9},{2,18},{10... | collective-permute-start | bytes 2764808 | tf_op jit(solution)/shard_map/ppermute | solution.py:122
  30.3 21.5 %collective-permute-done.4 = f32[40,8,720]{2,1,0:T(8,128)S(1)} collective-permute-done((f32[40,8,720]{2,1,0:T(8,128)S(1)}, f32[40,8,720]{2,1,0:T(8,128)S(1)}, u32[]{:S(2)}, u32[]{:S(2)}) %collective-permute-start.4) | collective-permute-done | bytes 921632 | tf_op jit(solution)/shard_map/ppermute | solution.py:122
  51.8 1.1 select_select_fusion
  53.0 4.9 %all-to-all-start = ((f32[8,40,720]{2,1,0:T(8,128)}), f32[8,40,720]{2,1,0:T(8,128)S(1)}, u32[]{:S(2)}, u32[]{:S(2)}) async-start(f32[8,40,720]{2,1,0:T(8,128)} %bitcast.83), calls=%async_computation | async-start | bytes 1966080 | tf_op jit(solution)/shard_map/all_to_all | solution.py:127
  58.9 5.0 %bitcast_select_fusion = f32[40]{0:T(128)S(1)} fusion(f32[]{:T(128)} %bitcast.14, f32[]{:T(128)} %bitcast.15, f32[]{:T(128)} %bitcast.16, f32[]{:T(128)} %bitcast.17, f32[]{:T(128)} %bitcast.18, f32[]{:T(128)} %bitcast.20, f32[]{:T(128)} %bitcast.19, f32[]{:T(128)} %bitcast.13, s32[]{:T(128)S(6)} %mul.392), kind=kLoop, calls=%fused_computation.126 | loop fusion | flops 1160 | bytes 196 | tf_op jit(solution)/shard_map/gather | solution.py:135
  64.0 19.0 %all-to-all-done = f32[8,40,720]{2,1,0:T(8,128)S(1)} async-done(((f32[8,40,720]{2,1,0:T(8,128)}), f32[8,40,720]{2,1,0:T(8,128)S(1)}, u32[]{:S(2)}, u32[]{:S(2)}) %all-to-all-start) | async-done | bytes 921632 | tf_op jit(solution)/shard_map/all_to_all | solution.py:127
  83.1 1.2 copy.14
  84.3 1.8 %reshape.186 = f32[40,45,128]{2,1,0:T(8,128)S(1)} reshape(f32[40,8,720]{2,1,0:T(8,128)} %copy.14) | data formatting | bytes 1843200 | tf_op jit(solution)/shard_map/reshape | solution.py:42
  86.1 1.1 convolution_negate_fusion
  87.2 1.1 fusion.64
  88.3 1.2 fusion.13
  89.5 1.2 fusion.9
  90.7 1.2 fusion.7
  91.9 1.2 fusion.40
  93.1 1.2 fusion.6
  94.3 1.2 fusion.37
  95.5 1.2 convolution_subtract_fusion.1
  96.7 1.4 convolution_add_fusion
  98.1 1.1 fusion.18
  99.1 2.0 %fusion.5 = f32[40,45,128]{2,1,0:T(8,128)} fusion(f32[45,40,128]{2,0,1:T(8,128)S(1)} %fusion.18, f32[40,45,128]{2,1,0:T(8,128)S(1)} %convolution_subtract_fusion.1, f32[40,45,128]{2,1,0:T(8,128)S(1)} %convolution_add_fusion, f32[45,128]{1,0:T(8,128)S(1)} %get-tuple-element.23, f32[45,128]{1,0:T(8,128)S(1)} %get-tuple-element.24), kind=kOutput, calls=%fused_computation.21 | convolution fusion | flops 125586224 | bytes 3732480 | tf_op jit(solution)/shard_map/ljn,ja->lan/dot_general | solution.py:66
  101.2 2.0 %all_to_all.27 = f32[40,8,720]{2,1,0:T(8,128)S(1)} reshape(f32[40,45,128]{2,1,0:T(8,128)} %fusion.5) | data formatting | bytes 1843200 | tf_op jit(solution)/shard_map/all_to_all | solution.py:136
  103.5 27.7 %all_to_all.32 = f32[40,8,720]{2,0,1:T(8,128)S(1)} all-to-all(f32[40,8,720]{2,0,1:T(8,128)S(1)} %copy.15), channel_id=1, replica_groups=mesh['lat'=4,'lon'=8] {'lon'}, dimensions={1} | all-to-all | bytes 1843200 | tf_op jit(solution)/shard_map/all_to_all | solution.py:136
  131.2 1.7 %collective-permute-start.5 = (f32[40,8,720]{2,1,0:T(8,128)S(1)}, f32[40,8,720]{2,1,0:T(8,128)S(1)}, u32[]{:S(2)}, u32[]{:S(2)}) collective-permute-start(f32[40,8,720]{2,1,0:T(8,128)S(1)} %bitcast.84), channel_id=1, source_target_pairs={{0,16},{8,24},{16,0},{24,8},{1,17},{9,25},{17,1},{25,9},{2,18},{10... | collective-permute-start | bytes 2764808 | tf_op jit(solution)/shard_map/ppermute | solution.py:139
  133.0 21.5 %collective-permute-done.5 = f32[40,8,720]{2,1,0:T(8,128)S(1)} collective-permute-done((f32[40,8,720]{2,1,0:T(8,128)S(1)}, f32[40,8,720]{2,1,0:T(8,128)S(1)}, u32[]{:S(2)}, u32[]{:S(2)}) %collective-permute-start.5) | collective-permute-done | bytes 921632 | tf_op jit(solution)/shard_map/ppermute | solution.py:139
  154.5 1.9 %fusion.3 = f32[5,8,16,720]{3,2,1,0:T(8,128)} fusion(f32[5,8,16,720]{3,2,1,0:T(8,128)S(1)} %copy-done, f32[5,8,16,720]{3,2,1,0:T(8,128)S(1)} %copy-done.2, f32[5,8,8,720]{3,2,1,0:T(8,128)S(1)} %bitcast.86, f32[5,8,8,720]{3,2,1,0:T(8,128)S(1)} %bitcast.85, pred[16]{0:T(512)(128)(4,1)S(1)} %compare_reduce_fusion, pred[]{:T(512)S(6)} %lt.78), kind=kLoop, calls=%fused_computation.17 | loop fusion | flops 2304000 | bytes 7372817 | tf_op jit(solution)/shard_map/add | solution.py:146
  (41 shorter events, 5.0 us)
Async XLA Ops:
  0.0 8.9 %copy-start = (f32[5,8,16,720]{3,2,1,0:T(8,128)S(1)}, f32[5,8,16,720]{3,2,1,0:T(8,128)}, u32[]{:S(2)}) copy-start(f32[5,8,16,720]{3,2,1,0:T(8,128)} %param.5) | copy-start | bytes 5529604
  0.0 8.9 %copy-start.3 = (f32[8,16,720]{2,1,0:T(8,128)S(1)}, f32[8,16,720]{2,1,0:T(8,128)}, u32[]{:S(2)}) copy-start(f32[8,16,720]{2,1,0:T(8,128)} %param.6) | copy-start | bytes 1105924
  2.8 21.0 %collective-permute-start.2 = (f32[48,1,720]{2,1,0:T(1,128)}, f32[48,1,720]{2,1,0:T(1,128)S(1)}, u32[]{:S(2)}, u32[]{:S(2)}) collective-permute-start(f32[48,1,720]{2,1,0:T(1,128)} %get-tuple-element.13), channel_id=1, source_target_pairs={{0,8},{8,16},{16,24},{1,9},{9,17},{17,25},{2,10},{10,18},{18,26},{... | collective-permute-start | bytes 414728 | tf_op jit(solution)/shard_map/ppermute | solution.py:19
  7.6 16.7 %collective-permute-start.3 = (f32[48,1,720]{2,1,0:T(1,128)}, f32[48,1,720]{2,1,0:T(1,128)S(1)}, u32[]{:S(2)}, u32[]{:S(2)}) collective-permute-start(f32[48,1,720]{2,1,0:T(1,128)} %get-tuple-element.14), channel_id=1, source_target_pairs={{8,0},{16,8},{24,16},{9,1},{17,9},{25,17},{10,2},{18,10},{26,18},{... | collective-permute-start | bytes 414728 | tf_op jit(solution)/shard_map/ppermute | solution.py:20
  9.9 11.5 %collective-permute-start = (f32[48,16,1]{2,1,0:T(8,128)}, f32[48,16,1]{2,1,0:T(8,128)S(1)}, u32[]{:S(2)}, u32[]{:S(2)}) collective-permute-start(f32[48,16,1]{2,1,0:T(8,128)} %get-tuple-element.11), channel_id=1, source_target_pairs={{0,1},{1,2},{2,3},{3,4},{4,5},{5,6},{6,7},{7,0},{8,9},{9,10},{10,1... | collective-permute-start | bytes 9224 | tf_op jit(solution)/shard_map/ppermute | solution.py:19
  9.9 11.7 %collective-permute-start.1 = (f32[48,16,1]{2,1,0:T(8,128)S(1)}, f32[48,16,1]{2,1,0:T(8,128)}, u32[]{:S(2)}, u32[]{:S(2)}) collective-permute-start(f32[48,16,1]{2,1,0:T(8,128)S(1)} %get-tuple-element.12), channel_id=1, source_target_pairs={{1,0},{2,1},{3,2},{4,3},{5,4},{6,5},{7,6},{0,7},{9,8},{10,9},{11,1... | collective-permute-start | bytes 9224 | tf_op jit(solution)/shard_map/ppermute | solution.py:20
  23.2 1.0 copy-start.4
  26.2 26.7 %copy-start.1 = (f32[5,8,16,720]{3,2,1,0:T(8,128)}, f32[5,8,16,720]{3,2,1,0:T(8,128)S(1)}, u32[]{:S(2)}) copy-start(f32[5,8,16,720]{3,2,1,0:T(8,128)S(1)} %fusion) | copy-start | bytes 5529604
  26.3 3.8 %copy-start.5 = (s32[32]{0:T(128)S(1)}, s32[32]{0:T(128)}, u32[]{:S(2)}) copy-start(s32[32]{0:T(128)} %param.8) | copy-start | bytes 388
  26.4 25.4 %collective-permute-start.4 = (f32[40,8,720]{2,1,0:T(8,128)S(1)}, f32[40,8,720]{2,1,0:T(8,128)S(1)}, u32[]{:S(2)}, u32[]{:S(2)}) collective-permute-start(f32[40,8,720]{2,1,0:T(8,128)S(1)} %slice_select_fusion), channel_id=1, source_target_pairs={{0,16},{8,24},{16,0},{24,8},{1,17},{9,25},{17,1},{25,9},{2,18},{10... | collective-permute-start | bytes 2764808 | tf_op jit(solution)/shard_map/ppermute | solution.py:122
  53.0 4.9 %copy-start.6 = (s32[32]{0:T(128)S(1)}, s32[32]{0:T(128)}, u32[]{:S(2)}) copy-start(s32[32]{0:T(128)} %param.9) | copy-start | bytes 388
  53.0 30.1 %all-to-all-start = ((f32[8,40,720]{2,1,0:T(8,128)}), f32[8,40,720]{2,1,0:T(8,128)S(1)}, u32[]{:S(2)}, u32[]{:S(2)}) async-start(f32[8,40,720]{2,1,0:T(8,128)} %bitcast.83), calls=%async_computation | async-start | bytes 1966080 | tf_op jit(solution)/shard_map/all_to_all | solution.py:127
  103.2 51.3 %copy-start.2 = (f32[5,8,16,720]{3,2,1,0:T(8,128)S(1)}, f32[5,8,16,720]{3,2,1,0:T(8,128)}, u32[]{:S(2)}) copy-start(f32[5,8,16,720]{3,2,1,0:T(8,128)} %copy-done.1) | copy-start | bytes 5529604
  131.2 23.2 %collective-permute-start.5 = (f32[40,8,720]{2,1,0:T(8,128)S(1)}, f32[40,8,720]{2,1,0:T(8,128)S(1)}, u32[]{:S(2)}, u32[]{:S(2)}) collective-permute-start(f32[40,8,720]{2,1,0:T(8,128)S(1)} %bitcast.84), channel_id=1, source_target_pairs={{0,16},{8,24},{16,0},{24,8},{1,17},{9,25},{17,1},{25,9},{2,18},{10... | collective-permute-start | bytes 2764808 | tf_op jit(solution)/shard_map/ppermute | solution.py:139
where the time goes:
time: 157 us; the launch traced here: 156 us
  waiting for transfers between devices  70 us (45%)
  blocking collectives  27.7 us (18%)
  starting transfers between devices  20 us (13%)
  other arithmetic  17 us (11%)
  matrix products  15 us (10%)
  local copies, waits for them, and re-layouts  6.44 us (4%)
    all_to_all x1, blocking collectives, body(): lax.all_to_all(smoothed, 'lon', split_axis=1, concat_axis=0, tiled=True)  27.7 us
    ppermute x1, waiting for transfers between devices, body(): taken = lax.ppermute(given, 'lat', pair_perm)  21.5 us
    ppermute x1, waiting for transfers between devices, body(): handed_back = lax.ppermute(returned, 'lat', pair_perm)  21.5 us
    all_to_all x1, waiting for transfers between devices, body(): lax.all_to_all(pair_lines.reshape(stacked * half_rows, columns), 'lon', s...  19 us
    ppermute x2, waiting for transfers between devices, with_halo(): before = lax.ppermute(last, axis, up)  7.92 us
    gather x1, other arithmetic, body(): smoothed = filter_lines(full_lines, kept_cut[line_index % half_rows])  5.01 us
    all_to_all x1, starting transfers between devices, body(): lax.all_to_all(pair_lines.reshape(stacked * half_rows, columns), 'lon', s...  4.91 us
    ppermute x2, starting transfers between devices, with_halo(): before = lax.ppermute(last, axis, up)  4.84 us
  transfers between devices with their start and end apart: 7, of which 4 were waited for; matrix products, arithmetic and copies ran while one was open for 6% of the time, Pallas kernels for 0%

commit v1 on v0

--- a/solution.py
+++ b/solution.py
@@ -7,19 +7,6 @@
 from jax.sharding import PartitionSpec as P
 
 radix_len = 128
-
-
-def with_halo(x, sides, width, wrap):
-    for axis, dim in sides:
-        size, length = (lax.axis_size(axis), x.shape[dim])
-        up = [(i, (i + 1) % size) for i in range(size if wrap else size - 1)]
-        down = [(j, i) for i, j in up]
-        last = lax.slice_in_dim(x, length - width, length, axis=dim)
-        leading = lax.slice_in_dim(x, 0, width, axis=dim)
-        before = lax.ppermute(last, axis, up)
-        after = lax.ppermute(leading, axis, down)
-        x = jnp.concatenate([before, x, after], axis=dim)
-    return x
 
 
 def phase_table(row_total, col_total, modulus):
@@ -80,20 +67,29 @@
     stacked = field_count * level_count
     lon_devices = lax.axis_size("lon")
     lat_devices = lax.axis_size("lat")
-    total_lon = columns * lon_devices
     flat_fields = fields.reshape(stacked, rows_dev, columns)
-    east_west = with_halo(
-        jnp.concatenate([flat_fields, lon_courant], axis=0), (("lon", 2),), 1, True
+    eastward = [(i, (i + 1) % lon_devices) for i in range(lon_devices)]
+    westward = [((i + 1) % lon_devices, i) for i in range(lon_devices)]
+    northward = [(i, i + 1) for i in range(lat_devices - 1)]
+    southward = [(i + 1, i) for i in range(lat_devices - 1)]
+    from_west = lax.ppermute(
+        jnp.concatenate([flat_fields[..., -1], lon_courant[..., -1]], axis=0), "lon", eastward
     )
-    north_south = with_halo(
-        jnp.concatenate([flat_fields, lat_courant], axis=0), (("lat", 1),), 1, False
+    from_east = lax.ppermute(flat_fields[..., 0], "lon", westward)
+    from_below = lax.ppermute(
+        jnp.concatenate([flat_fields[:, -1], lat_courant[:, -1]], axis=0), "lat", northward
     )
-    wide_fields = east_west[:stacked].reshape(field_count, level_count, rows_dev, columns + 2)
-    wide_courant = east_west[stacked:]
-    column_flux = face_flux(wide_courant[..., :-1], wide_fields[..., :-1], wide_fields[..., 1:])
-    tall_fields = north_south[:stacked].reshape(field_count, level_count, rows_dev + 2, columns)
-    tall_courant = north_south[stacked:]
-    row_flux = face_flux(tall_courant[:, :-1], tall_fields[:, :, :-1], tall_fields[:, :, 1:])
+    from_above = lax.ppermute(flat_fields[:, 0], "lat", southward)
+    wide_fields = jnp.concatenate(
+        [from_west[:stacked, :, None], flat_fields, from_east[:, :, None]], axis=2
+    ).reshape(field_count, level_count, rows_dev, columns + 2)
+    wide_courant = jnp.concatenate([from_west[stacked:, :, None], lon_courant], axis=2)
+    column_flux = face_flux(wide_courant, wide_fields[..., :-1], wide_fields[..., 1:])
+    tall_fields = jnp.concatenate(
+        [from_below[:stacked, None], flat_fields, from_above[:, None]], axis=1
+    ).reshape(field_count, level_count, rows_dev + 2, columns)
+    tall_courant = jnp.concatenate([from_below[stacked:, None], lat_courant], axis=1)
+    row_flux = face_flux(tall_courant, tall_fields[:, :, :-1], tall_fields[:, :, 1:])
     tile_index = lax.axis_index("lat")
     lower_row = tile_index * rows_dev - 1 + jnp.arange(rows_dev + 1, dtype=jnp.int32)
     row_flux = jnp.where((lower_row == rows_dev * lat_devices - 1)[:, None], 0.0, row_flux)

time: 157 us -> 156 us (level)
  local copies, waits for them, and re-layouts: 6.44 us -> 17.8 us
  waiting for transfers between devices: 70 us -> 61.3 us
  other arithmetic: 17 us -> 14.7 us
    concatenate x4 -> x2, other arithmetic: 5.77 us -> 0.09 us  [the longest x1 0.08 us: body(): jnp.concatenate([flat_fields[..., -1], lon_courant[..., -1]], axis=0)]
    concatenate x0 -> x10, local copies, waits for them, and re-layouts: none -> 5.33 us  [the longest x4 4.43 us: body(): jnp.concatenate([from_below[:stacked, None], flat_fields, from_above[:, N...]
    ppermute x4, waiting for transfers between devices: 7.92 us -> 2.95 us  [the longest x1 2.94 us: body(): lax.ppermute(jnp.concatenate([flat_fields[..., -1], lon_courant[..., -1]]...]
    slice x0 -> x7, local copies, waits for them, and re-layouts: none -> 4.55 us  [the longest x1 1.82 us: body(): flat_fields[:, -1]]
    ppermute x1, waiting for transfers between devices: 21.5 us -> 18 us  [body(): taken = lax.ppermute(given, 'lat', pair_perm)]
    select_n x1, other arithmetic: 0.78 us -> 2.85 us  [body(): jnp.where((lower_row == rows_dev * lat_devices - 1)[:, None], 0.0, row_flux)]
  transfers between devices with their start and end apart: 7 -> 7, of which waited for: 4 -> 4; matrix products, arithmetic and copies ran while one was open for 6% -> 12% of each run, Pallas kernels for 0% -> 0%
where the time goes in v1:
time: 156 us
  waiting for transfers between devices  61.3 us (39%)
  blocking collectives  27.7 us (18%)
  starting transfers between devices  18.6 us (12%)
  local copies, waits for them, and re-layouts  17.8 us (11%)
  matrix products  15 us (10%)
  other arithmetic  14.7 us (9%)
    all_to_all x1, blocking collectives, body(): lax.all_to_all(smoothed, 'lon', split_axis=1, concat_axis=0, tiled=True)  27.7 us
    ppermute x1, waiting for transfers between devices, body(): handed_back = lax.ppermute(returned, 'lat', pair_perm)  21.5 us
    all_to_all x1, waiting for transfers between devices, body(): lax.all_to_all(pair_lines.reshape(stacked * half_rows, columns), 'lon', s...  18.9 us
    ppermute x1, waiting for transfers between devices, body(): taken = lax.ppermute(given, 'lat', pair_perm)  18 us
    ppermute x1, starting transfers between devices, body(): lax.ppermute(jnp.concatenate([flat_fields[:, -1], lat_courant[:, -1]], ax...  5.48 us
    gather x1, other arithmetic, body(): smoothed = filter_lines(full_lines, kept_cut[line_index % half_rows])  5.08 us
    all_to_all x1, starting transfers between devices, body(): lax.all_to_all(pair_lines.reshape(stacked * half_rows, columns), 'lon', s...  4.57 us
    concatenate x4, local copies, waits for them, and re-layouts, body(): jnp.concatenate([from_below[:stacked, None], flat_fields, from_above[:, N...  4.43 us
  transfers between devices with their start and end apart: 7, of which 4 were waited for; matrix products, arithmetic and copies ran while one was open for 12% of the time, Pallas kernels for 0%

profile of v1, /device:TPU:0, one launch (start us, length us, event | category | flops | bytes accessed | tf_op | source)
XLA Modules:
  0.0 155.5 jit_solution(2173642556439766701)
XLA Ops:
  0.0 1.8 %fusion.140 = (f32[40,1,720]{2,1,0:T(1,128)S(1)}, f32[40,1,720]{2,1,0:T(1,128)S(1)}) fusion(f32[40,16,720]{2,1,0:T(8,128)} %bitcast.93), kind=kLoop, calls=%fused_computation.184 | loop fusion | bytes 460800 | tf_op jit(solution)/shard_map/slice | solution.py:80
  1.8 1.3 collective-permute-start.3
  4.1 5.5 %collective-permute-start.2 = (f32[48,720]{1,0:T(8,128)S(1)}, f32[48,720]{1,0:T(8,128)S(1)}, u32[]{:S(2)}, u32[]{:S(2)}) collective-permute-start(f32[48,720]{1,0:T(8,128)S(1)} %pad_maximum_fusion.5), channel_id=1, source_target_pairs={{0,8},{8,16},{16,24},{1,9},{9,17},{17,25},{2,10},{10,18},{18,26},{... | collective-permute-start | bytes 414728 | tf_op jit(solution)/shard_map/ppermute | solution.py:79
  9.6 1.2 fusion.139
  11.1 3.0 %collective-permute-start.1 = (f32[40,16]{0,1:T(8,128)S(1)}, f32[40,16]{0,1:T(8,128)S(1)}, u32[]{:S(2)}, u32[]{:S(2)}) collective-permute-start(f32[40,16]{0,1:T(8,128)S(1)} %bitcast.110), channel_id=1, source_target_pairs={{1,0},{2,1},{3,2},{4,3},{5,4},{6,5},{7,6},{0,7},{9,8},{10,9},{11,1... | collective-permute-start | bytes 7688 | tf_op jit(solution)/shard_map/ppermute | solution.py:78
  14.7 1.5 constant_dynamic-update-slice_fusion
  16.6 2.9 %collective-permute-done = f32[48,16]{0,1:T(8,128)S(1)} collective-permute-done((f32[48,16]{0,1:T(8,128)S(1)}, f32[48,16]{0,1:T(8,128)S(1)}, u32[]{:S(2)}, u32[]{:S(2)}) %collective-permute-start) | collective-permute-done | bytes 3104 | tf_op jit(solution)/shard_map/ppermute | solution.py:75
  20.4 1.9 %multiply_subtract_fusion = f32[5,8,16,721]{3,2,1,0:T(8,128)} fusion(f32[5,8,16,1]{3,2,1,0:T(8,128)S(1)} %copy.111, f32[5,8,16,720]{3,2,1,0:T(8,128)S(1)} %copy-done, f32[5,8,16,1]{3,2,1,0:T(8,128)S(1)} %copy.108, f32[8,16,721]{2,1,0:T(8,128)S(1)} %get-tuple-element.12, f32[8,16,721]{2,1,0:T(8,128)S(1)} %get-tuple-element.11), kind=kLoop, calls=%fused_computation.11 | loop fusion | flops 3230080 | bytes 4432384 | tf_op jit(solution)/shard_map/sub | solution.py:60
  23.3 3.3 %dynamic-update-slice.1 = f32[5,8,17,720]{3,2,1,0:T(8,128)} dynamic-update-slice(f32[5,8,17,720]{3,2,1,0:T(8,128)} %constant_dynamic-update-slice_fusion, f32[5,8,1,720]{3,2,1,0:T(1,128)S(1)} %copy.115, s32[]{} %constant.116, s32[]{} %constant.116, s32[]{} %constant.117, s32[]{} %constant.116) | dynamic-update-slice | bytes 230404 | tf_op jit(solution)/shard_map/concatenate | solution.py:88
  26.9 2.9 %subtract_select_fusion = f32[5,8,17,720]{3,2,1,0:T(8,128)S(1)} fusion(f32[5,8,17,720]{3,2,1,0:T(8,128)} %dynamic-update-slice.1, f32[5,8,16,720]{3,2,1,0:T(8,128)S(1)} %copy-done, f32[5,8,1,720]{3,2,1,0:T(1,128)S(1)} %copy.114, f32[8,17,720]{2,1,0:T(8,128)S(1)} %get-tuple-element.14, f32[8,17,720]{2,1,0:T(8,128)S(1)} %get-tuple-element.13, ...), kind=kLoop, calls=%fused_computation.1 | loop fusion | flops 3427200 | bytes 6658577 | tf_op jit(solution)/shard_map/jit(_where)/select_n | solution.py:95
  30.6 2.2 %collective-permute-start.4 = (f32[40,8,720]{2,1,0:T(8,128)S(1)}, f32[40,8,720]{2,1,0:T(8,128)S(1)}, u32[]{:S(2)}, u32[]{:S(2)}) collective-permute-start(f32[40,8,720]{2,1,0:T(8,128)S(1)} %slice_select_fusion), channel_id=1, source_target_pairs={{0,16},{8,24},{16,0},{24,8},{1,17},{9,25},{17,1},{25,9},{2,18},{10... | collective-permute-start | bytes 2764808 | tf_op jit(solution)/shard_map/ppermute | solution.py:118
  33.1 18.0 %collective-permute-done.4 = f32[40,8,720]{2,1,0:T(8,128)S(1)} collective-permute-done((f32[40,8,720]{2,1,0:T(8,128)S(1)}, f32[40,8,720]{2,1,0:T(8,128)S(1)}, u32[]{:S(2)}, u32[]{:S(2)}) %collective-permute-start.4) | collective-permute-done | bytes 921632 | tf_op jit(solution)/shard_map/ppermute | solution.py:118
  51.0 1.1 select_select_fusion
  52.2 4.6 %all-to-all-start = ((f32[8,40,720]{2,1,0:T(8,128)}), f32[8,40,720]{2,1,0:T(8,128)S(1)}, u32[]{:S(2)}, u32[]{:S(2)}) async-start(f32[8,40,720]{2,1,0:T(8,128)} %bitcast.98), calls=%async_computation | async-start | bytes 1966080 | tf_op jit(solution)/shard_map/all_to_all | solution.py:123
  57.7 5.1 %bitcast_select_fusion = f32[40]{0:T(128)S(1)} fusion(f32[]{:T(128)} %bitcast.22, f32[]{:T(128)} %bitcast.23, f32[]{:T(128)} %bitcast.24, f32[]{:T(128)} %bitcast.25, f32[]{:T(128)} %bitcast.26, f32[]{:T(128)} %bitcast.28, f32[]{:T(128)} %bitcast.27, f32[]{:T(128)} %bitcast.21, s32[]{:T(128)S(6)} %mul.414), kind=kLoop, calls=%fused_computation.122 | loop fusion | flops 1160 | bytes 196 | tf_op jit(solution)/shard_map/gather | solution.py:131
  63.0 18.9 %all-to-all-done = f32[8,40,720]{2,1,0:T(8,128)S(1)} async-done(((f32[8,40,720]{2,1,0:T(8,128)}), f32[8,40,720]{2,1,0:T(8,128)S(1)}, u32[]{:S(2)}, u32[]{:S(2)}) %all-to-all-start) | async-done | bytes 921632 | tf_op jit(solution)/shard_map/all_to_all | solution.py:123
  81.9 1.3 copy.116
  83.2 1.8 %reshape.266 = f32[40,45,128]{2,1,0:T(8,128)S(1)} reshape(f32[40,8,720]{2,1,0:T(8,128)} %copy.116) | data formatting | bytes 1843200 | tf_op jit(solution)/shard_map/reshape | solution.py:29
  87.2 1.2 fusion.9
  88.4 1.2 fusion.13
  89.5 1.2 fusion.6
  90.8 1.2 fusion.37
  92.0 1.2 fusion.7
  93.2 1.2 fusion.40
  94.4 1.2 convolution_add_fusion
  95.5 1.4 convolution_subtract_fusion.1
  98.0 2.1 %fusion.5 = f32[40,45,128]{2,1,0:T(8,128)} fusion(f32[45,40,128]{2,0,1:T(8,128)S(1)} %fusion.18, f32[40,45,128]{2,1,0:T(8,128)S(1)} %convolution_subtract_fusion.1, f32[40,45,128]{2,1,0:T(8,128)S(1)} %convolution_add_fusion, f32[45,128]{1,0:T(8,128)S(1)} %get-tuple-element.23, f32[45,128]{1,0:T(8,128)S(1)} %get-tuple-element.24), kind=kOutput, calls=%fused_computation.14 | convolution fusion | flops 125586224 | bytes 3732480 | tf_op jit(solution)/shard_map/ljn,ja->lan/dot_general | solution.py:53
  100.1 2.0 %all_to_all.27 = f32[40,8,720]{2,1,0:T(8,128)S(1)} reshape(f32[40,45,128]{2,1,0:T(8,128)} %fusion.5) | data formatting | bytes 1843200 | tf_op jit(solution)/shard_map/all_to_all | solution.py:132
  102.4 27.7 %all_to_all.32 = f32[40,8,720]{2,0,1:T(8,128)S(1)} all-to-all(f32[40,8,720]{2,0,1:T(8,128)S(1)} %copy.117), channel_id=1, replica_groups=mesh['lat'=4,'lon'=8] {'lon'}, dimensions={1} | all-to-all | bytes 1843200 | tf_op jit(solution)/shard_map/all_to_all | solution.py:132
  130.1 2.0 %collective-permute-start.5 = (f32[40,8,720]{2,1,0:T(8,128)S(1)}, f32[40,8,720]{2,1,0:T(8,128)S(1)}, u32[]{:S(2)}, u32[]{:S(2)}) collective-permute-start(f32[40,8,720]{2,1,0:T(8,128)S(1)} %bitcast.99), channel_id=1, source_target_pairs={{0,16},{8,24},{16,0},{24,8},{1,17},{9,25},{17,1},{25,9},{2,18},{10... | collective-permute-start | bytes 2764808 | tf_op jit(solution)/shard_map/ppermute | solution.py:135
  132.1 21.5 %collective-permute-done.5 = f32[40,8,720]{2,1,0:T(8,128)S(1)} collective-permute-done((f32[40,8,720]{2,1,0:T(8,128)S(1)}, f32[40,8,720]{2,1,0:T(8,128)S(1)}, u32[]{:S(2)}, u32[]{:S(2)}) %collective-permute-start.5) | collective-permute-done | bytes 921632 | tf_op jit(solution)/shard_map/ppermute | solution.py:135
  153.6 1.9 %fusion.3 = f32[5,8,16,720]{3,2,1,0:T(8,128)} fusion(f32[5,8,16,720]{3,2,1,0:T(8,128)S(1)} %copy-done, f32[5,8,16,720]{3,2,1,0:T(8,128)S(1)} %copy-done.2, f32[5,8,8,720]{3,2,1,0:T(8,128)S(1)} %bitcast.101, f32[5,8,8,720]{3,2,1,0:T(8,128)S(1)} %bitcast.100, pred[16]{0:T(512)(128)(4,1)S(1)} %compare_reduce_fusion, pred[]{:T(512)S(6)} %lt.78), kind=kLoop, calls=%fused_computation.10 | loop fusion | flops 2304000 | bytes 7372817 | tf_op jit(solution)/shard_map/add | solution.py:142
  (62 shorter events, 10.0 us)
Async XLA Ops:
  0.0 14.7 %copy-start = (f32[5,8,16,720]{3,2,1,0:T(8,128)S(1)}, f32[5,8,16,720]{3,2,1,0:T(8,128)}, u32[]{:S(2)}) copy-start(f32[5,8,16,720]{3,2,1,0:T(8,128)} %param.5) | copy-start | bytes 5529604
  0.0 14.1 %copy-start.4 = (f32[8,16,720]{2,1,0:T(8,128)S(1)}, f32[8,16,720]{2,1,0:T(8,128)}, u32[]{:S(2)}) copy-start(f32[8,16,720]{2,1,0:T(8,128)} %param.6) | copy-start | bytes 1105924
  1.8 20.5 %collective-permute-start.3 = (f32[40,720]{1,0:T(8,128)S(1)}, f32[40,720]{1,0:T(8,128)}, u32[]{:S(2)}, u32[]{:S(2)}) collective-permute-start(f32[40,720]{1,0:T(8,128)S(1)} %bitcast.103), channel_id=1, source_target_pairs={{8,0},{16,8},{24,16},{9,1},{17,9},{25,17},{10,2},{18,10},{26,18},{... | collective-permute-start | bytes 345608 | tf_op jit(solution)/shard_map/ppermute | solution.py:82
  4.1 22.4 %collective-permute-start.2 = (f32[48,720]{1,0:T(8,128)S(1)}, f32[48,720]{1,0:T(8,128)S(1)}, u32[]{:S(2)}, u32[]{:S(2)}) collective-permute-start(f32[48,720]{1,0:T(8,128)S(1)} %pad_maximum_fusion.5), channel_id=1, source_target_pairs={{0,8},{8,16},{16,24},{1,9},{9,17},{17,25},{2,10},{10,18},{18,26},{... | collective-permute-start | bytes 414728 | tf_op jit(solution)/shard_map/ppermute | solution.py:79
  11.1 5.1 %collective-permute-start.1 = (f32[40,16]{0,1:T(8,128)S(1)}, f32[40,16]{0,1:T(8,128)S(1)}, u32[]{:S(2)}, u32[]{:S(2)}) collective-permute-start(f32[40,16]{0,1:T(8,128)S(1)} %bitcast.110), channel_id=1, source_target_pairs={{1,0},{2,1},{3,2},{4,3},{5,4},{6,5},{7,6},{0,7},{9,8},{10,9},{11,1... | collective-permute-start | bytes 7688 | tf_op jit(solution)/shard_map/ppermute | solution.py:78
  14.6 4.9 %collective-permute-start = (f32[48,16]{0,1:T(8,128)S(1)}, f32[48,16]{0,1:T(8,128)S(1)}, u32[]{:S(2)}, u32[]{:S(2)}) collective-permute-start(f32[48,16]{0,1:T(8,128)S(1)} %pad_maximum_fusion.6), channel_id=1, source_target_pairs={{0,1},{1,2},{2,3},{3,4},{4,5},{5,6},{6,7},{7,0},{8,9},{9,10},{10,1... | collective-permute-start | bytes 9224 | tf_op jit(solution)/shard_map/ppermute | solution.py:75
  20.4 6.4 %copy-start.5 = (f32[8,16,720]{2,1,0:T(8,128)S(1)}, f32[8,16,720]{2,1,0:T(8,128)}, u32[]{:S(2)}) copy-start(f32[8,16,720]{2,1,0:T(8,128)} %param.7) | copy-start | bytes 1105924
  26.9 2.9 %copy-start.3 = (f32[5,8,16,721]{3,2,1,0:T(8,128)S(1)}, f32[5,8,16,721]{3,2,1,0:T(8,128)}, u32[]{:S(2)}) copy-start(f32[5,8,16,721]{3,2,1,0:T(8,128)} %multiply_subtract_fusion) | copy-start | bytes 5537284
  30.4 21.7 %copy-start.1 = (f32[5,8,16,720]{3,2,1,0:T(8,128)}, f32[5,8,16,720]{3,2,1,0:T(8,128)S(1)}, u32[]{:S(2)}) copy-start(f32[5,8,16,720]{3,2,1,0:T(8,128)S(1)} %fusion) | copy-start | bytes 5529604
  30.4 2.4 %copy-start.6 = (s32[32]{0:T(128)S(1)}, s32[32]{0:T(128)}, u32[]{:S(2)}) copy-start(s32[32]{0:T(128)} %param.8) | copy-start | bytes 388
  30.6 20.4 %collective-permute-start.4 = (f32[40,8,720]{2,1,0:T(8,128)S(1)}, f32[40,8,720]{2,1,0:T(8,128)S(1)}, u32[]{:S(2)}, u32[]{:S(2)}) collective-permute-start(f32[40,8,720]{2,1,0:T(8,128)S(1)} %slice_select_fusion), channel_id=1, source_target_pairs={{0,16},{8,24},{16,0},{24,8},{1,17},{9,25},{17,1},{25,9},{2,18},{10... | collective-permute-start | bytes 2764808 | tf_op jit(solution)/shard_map/ppermute | solution.py:118
  52.2 4.6 %copy-start.7 = (s32[32]{0:T(128)S(1)}, s32[32]{0:T(128)}, u32[]{:S(2)}) copy-start(s32[32]{0:T(128)} %param.9) | copy-start | bytes 388
  52.2 29.8 %all-to-all-start = ((f32[8,40,720]{2,1,0:T(8,128)}), f32[8,40,720]{2,1,0:T(8,128)S(1)}, u32[]{:S(2)}, u32[]{:S(2)}) async-start(f32[8,40,720]{2,1,0:T(8,128)} %bitcast.98), calls=%async_computation | async-start | bytes 1966080 | tf_op jit(solution)/shard_map/all_to_all | solution.py:123
  102.1 51.6 %copy-start.2 = (f32[5,8,16,720]{3,2,1,0:T(8,128)S(1)}, f32[5,8,16,720]{3,2,1,0:T(8,128)}, u32[]{:S(2)}) copy-start(f32[5,8,16,720]{3,2,1,0:T(8,128)} %copy-done.1) | copy-start | bytes 5529604
  130.1 23.5 %collective-permute-start.5 = (f32[40,8,720]{2,1,0:T(8,128)S(1)}, f32[40,8,720]{2,1,0:T(8,128)S(1)}, u32[]{:S(2)}, u32[]{:S(2)}) collective-permute-start(f32[40,8,720]{2,1,0:T(8,128)S(1)} %bitcast.99), channel_id=1, source_target_pairs={{0,16},{8,24},{16,0},{24,8},{1,17},{9,25},{17,1},{25,9},{2,18},{10... | collective-permute-start | bytes 2764808 | tf_op jit(solution)/shard_map/ppermute | solution.py:135

commit v2 on v1

--- a/solution.py
+++ b/solution.py
@@ -115,24 +115,34 @@
     high_half = flat_increment[:, half_rows:]
     kept = jnp.where(is_low, low_half, high_half)
     given = jnp.where(is_low, high_half, low_half)
-    taken = lax.ppermute(given, "lat", pair_perm)
     kept_filtered = jnp.where(is_low, is_filtered[:half_rows], is_filtered[half_rows:])
     kept_cut = jnp.where(is_low, row_cut[:half_rows], row_cut[half_rows:])
-    pair_lines = jnp.where(kept_filtered[None, :, None], kept, taken)
-    line_count = stacked * half_rows // lon_devices
-    full_lines = lax.all_to_all(
-        pair_lines.reshape(stacked * half_rows, columns),
-        "lon",
-        split_axis=0,
-        concat_axis=1,
-        tiled=True,
-    )
-    line_index = lax.axis_index("lon") * line_count + jnp.arange(line_count, dtype=jnp.int32)
-    smoothed = filter_lines(full_lines, kept_cut[line_index % half_rows])
-    returned = lax.all_to_all(smoothed, "lon", split_axis=1, concat_axis=0, tiled=True).reshape(
-        stacked, half_rows, columns
-    )
-    handed_back = lax.ppermute(returned, "lat", pair_perm)
+    chunk_sizes = (stacked * 2 // 5, stacked - stacked * 2 // 5)
+    returned_parts, handed_parts = [], []
+    chunk_start = 0
+    for chunk_stack in chunk_sizes:
+        rows_of_part = slice(chunk_start, chunk_start + chunk_stack)
+        chunk_start += chunk_stack
+        line_count = chunk_stack * half_rows // lon_devices
+        line_index = lax.axis_index("lon") * line_count + jnp.arange(line_count, dtype=jnp.int32)
+        line_cut = kept_cut[line_index % half_rows]
+        taken = lax.ppermute(given[rows_of_part], "lat", pair_perm)
+        pair_lines = jnp.where(kept_filtered[None, :, None], kept[rows_of_part], taken)
+        full_lines = lax.all_to_all(
+            pair_lines.reshape(chunk_stack * half_rows, columns),
+            "lon",
+            split_axis=0,
+            concat_axis=1,
+            tiled=True,
+        )
+        smoothed = filter_lines(full_lines, line_cut)
+        returned = lax.all_to_all(
+            smoothed, "lon", split_axis=1, concat_axis=0, tiled=True
+        ).reshape(chunk_stack, half_rows, columns)
+        returned_parts.append(returned)
+        handed_parts.append(lax.ppermute(returned, "lat", pair_perm))
+    returned = jnp.concatenate(returned_parts, axis=0)
+    handed_back = jnp.concatenate(handed_parts, axis=0)
     smooth_rows = jnp.where(
         is_low,
         jnp.concatenate([returned, handed_back], axis=1),

time: 156 us -> 144 us (0.923)
  blocking collectives: 27.7 us -> 0 us
  starting transfers between devices: 18.6 us -> 30.3 us
  matrix products: 15 us -> 19.4 us
  local copies, waits for them, and re-layouts: 17.8 us -> 21.4 us
  other arithmetic: 14.7 us -> 11.6 us
    all_to_all x1 -> x0, blocking collectives: 27.7 us -> none  [body(): lax.all_to_all(smoothed, 'lon', split_axis=1, concat_axis=0, tiled=True)]
    ppermute x2 -> x4, waiting for transfers between devices: 39.4 us -> 21.9 us  [the longest x2 12.1 us: body(): taken = lax.ppermute(given[rows_of_part], 'lat', pair_perm)]
    all_to_all x1 -> x4, waiting for transfers between devices: 18.9 us -> 35.9 us  [the longest x2 22.1 us: body(): lax.all_to_all(smoothed, 'lon', split_axis=1, concat_axis=0, tiled=True)]
    all_to_all x1 -> x4, starting transfers between devices: 4.57 us -> 14.2 us  [the longest x2 7.17 us: body(): lax.all_to_all(pair_lines.reshape(chunk_stack * half_rows, columns), 'lon...]
    gather x1 -> x2, other arithmetic: 5.08 us -> 0.01 us  [body(): line_cut = kept_cut[line_index % half_rows]]
    ppermute x2 -> x4, starting transfers between devices: 4.24 us -> 6.34 us  [the longest x2 4.1 us: body(): handed_parts.append(lax.ppermute(returned, 'lat', pair_perm))]
    unnamed x20 -> x46, local copies, waits for them, and re-layouts: 1.59 us -> 3.51 us
    select_n x2 -> x5, other arithmetic: 1.26 us -> 3.05 us  [the longest x2 2.88 us: body(): jnp.where(kept_filtered[None, :, None], kept[rows_of_part], taken)]
  transfers between devices with their start and end apart: 7 -> 12, of which waited for: 4 -> 8; matrix products, arithmetic and copies ran while one was open for 12% -> 21% of each run, Pallas kernels for 0% -> 0%
where the time goes in v2:
time: 144 us
  waiting for transfers between devices  60.1 us (42%)
  starting transfers between devices  30.3 us (21%)
  local copies, waits for them, and re-layouts  21.4 us (15%)
  matrix products  19.4 us (13%)
  other arithmetic  11.6 us (8%)
    all_to_all x2, waiting for transfers between devices, body(): lax.all_to_all(smoothed, 'lon', split_axis=1, concat_axis=0, tiled=True)  22.1 us
    all_to_all x2, waiting for transfers between devices, body(): lax.all_to_all(pair_lines.reshape(chunk_stack * half_rows, columns), 'lon...  13.8 us
    ppermute x2, waiting for transfers between devices, body(): taken = lax.ppermute(given[rows_of_part], 'lat', pair_perm)  12.1 us
    ppermute x2, waiting for transfers between devices, body(): handed_parts.append(lax.ppermute(returned, 'lat', pair_perm))  9.78 us
    all_to_all x2, starting transfers between devices, body(): lax.all_to_all(pair_lines.reshape(chunk_stack * half_rows, columns), 'lon...  7.17 us
    all_to_all x2, starting transfers between devices, body(): lax.all_to_all(smoothed, 'lon', split_axis=1, concat_axis=0, tiled=True)  6.99 us
    ppermute x1, starting transfers between devices, body(): lax.ppermute(jnp.concatenate([flat_fields[:, -1], lat_courant[:, -1]], ax...  5.48 us
    concatenate x4, local copies, waits for them, and re-layouts, body(): jnp.concatenate([from_below[:stacked, None], flat_fields, from_above[:, N...  4.4 us
  transfers between devices with their start and end apart: 12, of which 8 were waited for; matrix products, arithmetic and copies ran while one was open for 21% of the time, Pallas kernels for 0%

profile of v2, /device:TPU:0, one launch (start us, length us, event | category | flops | bytes accessed | tf_op | source)
XLA Modules:
  0.0 143.5 jit_solution(11178613243373825932)
XLA Ops:
  0.0 1.8 %fusion.247 = (f32[40,1,720]{2,1,0:T(1,128)S(1)}, f32[40,1,720]{2,1,0:T(1,128)S(1)}) fusion(f32[40,16,720]{2,1,0:T(8,128)} %bitcast.129), kind=kLoop, calls=%fused_computation.289 | loop fusion | bytes 460800 | tf_op jit(solution)/shard_map/slice | solution.py:80
  1.8 1.3 collective-permute-start.3
  4.1 5.5 %collective-permute-start.2 = (f32[48,720]{1,0:T(8,128)S(1)}, f32[48,720]{1,0:T(8,128)S(1)}, u32[]{:S(2)}, u32[]{:S(2)}) collective-permute-start(f32[48,720]{1,0:T(8,128)S(1)} %pad_maximum_fusion.7), channel_id=1, source_target_pairs={{0,8},{8,16},{16,24},{1,9},{9,17},{17,25},{2,10},{10,18},{18,26},{... | collective-permute-start | bytes 414728 | tf_op jit(solution)/shard_map/ppermute | solution.py:79
  9.6 1.2 fusion.246
  11.1 3.0 %collective-permute-start.1 = (f32[40,16]{0,1:T(8,128)S(1)}, f32[40,16]{0,1:T(8,128)S(1)}, u32[]{:S(2)}, u32[]{:S(2)}) collective-permute-start(f32[40,16]{0,1:T(8,128)S(1)} %bitcast.149), channel_id=1, source_target_pairs={{1,0},{2,1},{3,2},{4,3},{5,4},{6,5},{7,6},{0,7},{9,8},{10,9},{11,1... | collective-permute-start | bytes 7688 | tf_op jit(solution)/shard_map/ppermute | solution.py:78
  14.7 1.6 %constant_dynamic-update-slice_fusion = f32[5,8,17,720]{3,2,1,0:T(8,128)} fusion(f32[5,8,16,720]{3,2,1,0:T(8,128)S(1)} %copy-done), kind=kLoop, calls=%fused_computation.186 | loop fusion | bytes 3809280
  17.2 2.3 %collective-permute-done = f32[48,16]{0,1:T(8,128)S(1)} collective-permute-done((f32[48,16]{0,1:T(8,128)S(1)}, f32[48,16]{0,1:T(8,128)S(1)}, u32[]{:S(2)}, u32[]{:S(2)}) %collective-permute-start) | collective-permute-done | bytes 3104 | tf_op jit(solution)/shard_map/ppermute | solution.py:75
  20.4 2.0 %multiply_subtract_fusion = f32[5,8,16,721]{3,2,1,0:T(8,128)} fusion(f32[5,8,16,1]{3,2,1,0:T(8,128)S(1)} %copy.106, f32[5,8,16,720]{3,2,1,0:T(8,128)S(1)} %copy-done, f32[5,8,16,1]{3,2,1,0:T(8,128)S(1)} %copy.103, f32[8,16,721]{2,1,0:T(8,128)S(1)} %get-tuple-element.14, f32[8,16,721]{2,1,0:T(8,128)S(1)} %get-tuple-element.13), kind=kLoop, calls=%fused_computation.13 | loop fusion | flops 3230080 | bytes 4432384 | tf_op jit(solution)/shard_map/sub | solution.py:60
  22.3 1.0 copy.110
  23.4 3.2 %dynamic-update-slice.1 = f32[5,8,17,720]{3,2,1,0:T(8,128)} dynamic-update-slice(f32[5,8,17,720]{3,2,1,0:T(8,128)} %constant_dynamic-update-slice_fusion, f32[5,8,1,720]{3,2,1,0:T(1,128)S(1)} %copy.110, s32[]{} %constant.131, s32[]{} %constant.131, s32[]{} %constant.132, s32[]{} %constant.131) | dynamic-update-slice | bytes 230404 | tf_op jit(solution)/shard_map/concatenate | solution.py:88
  26.9 2.9 %subtract_select_fusion = f32[5,8,17,720]{3,2,1,0:T(8,128)S(1)} fusion(f32[5,8,17,720]{3,2,1,0:T(8,128)} %dynamic-update-slice.1, f32[5,8,16,720]{3,2,1,0:T(8,128)S(1)} %copy-done, f32[5,8,1,720]{3,2,1,0:T(1,128)S(1)} %copy.109, f32[8,17,720]{2,1,0:T(8,128)S(1)} %get-tuple-element.16, f32[8,17,720]{2,1,0:T(8,128)S(1)} %get-tuple-element.15, ...), kind=kLoop, calls=%fused_computation.3 | loop fusion | flops 3427200 | bytes 6658577 | tf_op jit(solution)/shard_map/jit(_where)/select_n | solution.py:95
  30.6 1.1 copy-done.1
  31.7 2.2 %collective-permute-start.4 = (f32[16,8,720]{2,1,0:T(8,128)S(1)}, f32[16,8,720]{2,1,0:T(8,128)S(1)}, u32[]{:S(2)}, u32[]{:S(2)}) collective-permute-start(f32[16,8,720]{2,1,0:T(8,128)S(1)} %slice.123), channel_id=1, source_target_pairs={{0,16},{8,24},{16,0},{24,8},{1,17},{9,25},{17,1},{25,9},{2,18},{10... | collective-permute-start | bytes 1105928 | tf_op jit(solution)/shard_map/ppermute | solution.py:129
  34.9 9.1 %collective-permute-done.4 = f32[16,8,720]{2,1,0:T(8,128)S(1)} collective-permute-done((f32[16,8,720]{2,1,0:T(8,128)S(1)}, f32[16,8,720]{2,1,0:T(8,128)S(1)}, u32[]{:S(2)}, u32[]{:S(2)}) %collective-permute-start.4) | collective-permute-done | bytes 368672 | tf_op jit(solution)/shard_map/ppermute | solution.py:129
  44.8 3.5 %all-to-all-start = ((f32[8,16,720]{2,1,0:T(8,128)}), f32[8,16,720]{2,1,0:T(8,128)S(1)}, u32[]{:S(2)}, u32[]{:S(2)}) async-start(f32[8,16,720]{2,1,0:T(8,128)} %bitcast.138), calls=%async_computation | async-start | bytes 786432 | tf_op jit(solution)/shard_map/all_to_all | solution.py:131
  49.9 3.0 %collective-permute-done.5 = f32[24,8,720]{2,1,0:T(8,128)} collective-permute-done((f32[24,8,720]{2,1,0:T(8,128)}, f32[24,8,720]{2,1,0:T(8,128)}, u32[]{:S(2)}, u32[]{:S(2)}) %collective-permute-start.5) | collective-permute-done | bytes 552992 | tf_op jit(solution)/shard_map/ppermute | solution.py:129
  52.9 2.0 %slice_select_fusion.2 = f32[24,8,720]{2,1,0:T(8,128)} fusion(f32[24,8,720]{2,1,0:T(8,128)} %collective-permute-done.5, f32[40,8,720]{2,1,0:T(8,128)S(1)} %get-tuple-element.7, pred[8]{0:T(512)(128)(4,1)S(1)} %slice_select_fusion.4), kind=kLoop, calls=%fused_computation.40 | loop fusion | flops 138240 | bytes 1658888 | tf_op jit(solution)/shard_map/jit(_where)/select_n | solution.py:130
  55.0 5.8 %all-to-all-done = f32[8,16,720]{2,1,0:T(8,128)S(1)} async-done(((f32[8,16,720]{2,1,0:T(8,128)}), f32[8,16,720]{2,1,0:T(8,128)S(1)}, u32[]{:S(2)}, u32[]{:S(2)}) %all-to-all-start) | async-done | bytes 368672 | tf_op jit(solution)/shard_map/all_to_all | solution.py:131
  60.8 3.7 %all-to-all-start.2 = ((f32[8,24,720]{2,1,0:T(8,128)}), f32[8,24,720]{2,1,0:T(8,128)S(1)}, u32[]{:S(2)}, u32[]{:S(2)}) async-start(f32[8,24,720]{2,1,0:T(8,128)} %bitcast.24), calls=%async_computation.2 | async-start | bytes 1179648 | tf_op jit(solution)/shard_map/all_to_all | solution.py:131
  65.5 1.2 reshape.332
  73.1 7.9 %all-to-all-done.2 = f32[8,24,720]{2,1,0:T(8,128)S(1)} async-done(((f32[8,24,720]{2,1,0:T(8,128)}), f32[8,24,720]{2,1,0:T(8,128)S(1)}, u32[]{:S(2)}, u32[]{:S(2)}) %all-to-all-start.2) | async-done | bytes 552992 | tf_op jit(solution)/shard_map/all_to_all | solution.py:131
  86.7 1.1 fusion.7
  92.5 1.0 copy.114
  93.5 3.5 %all-to-all-start.3 = ((f32[24,8,720]{2,0,1:T(8,128)}), f32[24,8,720]{2,0,1:T(8,128)S(1)}, u32[]{:S(2)}, u32[]{:S(2)}) async-start(f32[24,8,720]{2,0,1:T(8,128)} %copy.114), calls=%async_computation.3 | async-start | bytes 1179648 | tf_op jit(solution)/shard_map/all_to_all | solution.py:139
  97.1 1.7 %fusion.72 = f32[16,45,128]{2,1,0:T(8,128)S(1)} fusion(f32[16,45,128]{2,1,0:T(8,128)} %copy-done.12), kind=kOutput, calls=%fused_computation.115 | convolution fusion | flops 141787136 | bytes 737280 | tf_op jit(solution)/shard_map/ljk,kn->ljn/dot_general | solution.py:49
  102.0 11.8 %all-to-all-done.3 = f32[24,8,720]{2,0,1:T(8,128)S(1)} async-done(((f32[24,8,720]{2,0,1:T(8,128)}), f32[24,8,720]{2,0,1:T(8,128)S(1)}, u32[]{:S(2)}, u32[]{:S(2)}) %all-to-all-start.3) | async-done | bytes 552992 | tf_op jit(solution)/shard_map/all_to_all | solution.py:139
  113.7 3.5 %all-to-all-start.1 = ((f32[16,8,720]{2,0,1:T(8,128)}), f32[16,8,720]{2,0,1:T(8,128)S(1)}, u32[]{:S(2)}, u32[]{:S(2)}) async-start(f32[16,8,720]{2,0,1:T(8,128)} %copy.112), calls=%async_computation.1 | async-start | bytes 786432 | tf_op jit(solution)/shard_map/all_to_all | solution.py:139
  117.2 2.1 %collective-permute-start.7 = (f32[24,8,720]{2,1,0:T(8,128)S(1)}, f32[24,8,720]{2,1,0:T(8,128)S(1)}, u32[]{:S(2)}, u32[]{:S(2)}) collective-permute-start(f32[24,8,720]{2,1,0:T(8,128)S(1)} %bitcast.135), channel_id=1, source_target_pairs={{0,16},{8,24},{16,0},{24,8},{1,17},{9,25},{17,1},{25,9},{2,18},{10... | collective-permute-start | bytes 1658888 | tf_op jit(solution)/shard_map/ppermute | solution.py:143
  119.3 10.4 %all-to-all-done.1 = f32[16,8,720]{2,0,1:T(8,128)S(1)} async-done(((f32[16,8,720]{2,0,1:T(8,128)}), f32[16,8,720]{2,0,1:T(8,128)S(1)}, u32[]{:S(2)}, u32[]{:S(2)}) %all-to-all-start.1) | async-done | bytes 368672 | tf_op jit(solution)/shard_map/all_to_all | solution.py:139
  129.7 2.0 %collective-permute-start.6 = (f32[16,8,720]{2,1,0:T(8,128)S(1)}, f32[16,8,720]{2,1,0:T(8,128)S(1)}, u32[]{:S(2)}, u32[]{:S(2)}) collective-permute-start(f32[16,8,720]{2,1,0:T(8,128)S(1)} %bitcast.139), channel_id=1, source_target_pairs={{0,16},{8,24},{16,0},{24,8},{1,17},{9,25},{17,1},{25,9},{2,18},{10... | collective-permute-start | bytes 1105928 | tf_op jit(solution)/shard_map/ppermute | solution.py:143
  131.8 9.8 %collective-permute-done.6 = f32[16,8,720]{2,1,0:T(8,128)S(1)} collective-permute-done((f32[16,8,720]{2,1,0:T(8,128)S(1)}, f32[16,8,720]{2,1,0:T(8,128)S(1)}, u32[]{:S(2)}, u32[]{:S(2)}) %collective-permute-start.6) | collective-permute-done | bytes 368672 | tf_op jit(solution)/shard_map/ppermute | solution.py:143
  141.6 1.9 %fusion.3 = f32[5,8,16,720]{3,2,1,0:T(8,128)} fusion(f32[5,8,16,720]{3,2,1,0:T(8,128)S(1)} %copy-done, f32[5,8,16,720]{3,2,1,0:T(8,128)S(1)} %copy-done.2, f32[5,8,8,720]{3,2,1,0:T(8,128)S(1)} %bitcast.133, f32[5,8,8,720]{3,2,1,0:T(8,128)S(1)} %bitcast.132, pred[16]{0:T(512)(128)(4,1)S(1)} %compare_reduce_fusion, pred[]{:T(512)S(6)} %lt.139), kind=kLoop, calls=%fused_computation.12 | loop fusion | flops 2304000 | bytes 7372817 | tf_op jit(solution)/shard_map/add | solution.py:152
  (121 shorter events, 28.6 us)
Async XLA Ops:
  0.0 14.7 %copy-start = (f32[5,8,16,720]{3,2,1,0:T(8,128)S(1)}, f32[5,8,16,720]{3,2,1,0:T(8,128)}, u32[]{:S(2)}) copy-start(f32[5,8,16,720]{3,2,1,0:T(8,128)} %param.5) | copy-start | bytes 5529604
  0.0 14.1 %copy-start.13 = (f32[8,16,720]{2,1,0:T(8,128)S(1)}, f32[8,16,720]{2,1,0:T(8,128)}, u32[]{:S(2)}) copy-start(f32[8,16,720]{2,1,0:T(8,128)} %param.6) | copy-start | bytes 1105924
  1.8 20.5 %collective-permute-start.3 = (f32[40,720]{1,0:T(8,128)S(1)}, f32[40,720]{1,0:T(8,128)}, u32[]{:S(2)}, u32[]{:S(2)}) collective-permute-start(f32[40,720]{1,0:T(8,128)S(1)} %bitcast.142), channel_id=1, source_target_pairs={{8,0},{16,8},{24,16},{9,1},{17,9},{25,17},{10,2},{18,10},{26,18},{... | collective-permute-start | bytes 345608 | tf_op jit(solution)/shard_map/ppermute | solution.py:82
  4.1 22.5 %collective-permute-start.2 = (f32[48,720]{1,0:T(8,128)S(1)}, f32[48,720]{1,0:T(8,128)S(1)}, u32[]{:S(2)}, u32[]{:S(2)}) collective-permute-start(f32[48,720]{1,0:T(8,128)S(1)} %pad_maximum_fusion.7), channel_id=1, source_target_pairs={{0,8},{8,16},{16,24},{1,9},{9,17},{17,25},{2,10},{10,18},{18,26},{... | collective-permute-start | bytes 414728 | tf_op jit(solution)/shard_map/ppermute | solution.py:79
  11.1 5.8 %collective-permute-start.1 = (f32[40,16]{0,1:T(8,128)S(1)}, f32[40,16]{0,1:T(8,128)S(1)}, u32[]{:S(2)}, u32[]{:S(2)}) collective-permute-start(f32[40,16]{0,1:T(8,128)S(1)} %bitcast.149), channel_id=1, source_target_pairs={{1,0},{2,1},{3,2},{4,3},{5,4},{6,5},{7,6},{0,7},{9,8},{10,9},{11,1... | collective-permute-start | bytes 7688 | tf_op jit(solution)/shard_map/ppermute | solution.py:78
  14.6 1.6 %copy-start.19 = (s32[32]{0:T(128)S(1)}, s32[32]{0:T(128)}, u32[]{:S(2)}) copy-start(s32[32]{0:T(128)} %param.8) | copy-start | bytes 388
  14.6 1.9 %copy-start.20 = (s32[32]{0:T(128)S(1)}, s32[32]{0:T(128)}, u32[]{:S(2)}) copy-start(s32[32]{0:T(128)} %param.9) | copy-start | bytes 388
  14.6 4.9 %collective-permute-start = (f32[48,16]{0,1:T(8,128)S(1)}, f32[48,16]{0,1:T(8,128)S(1)}, u32[]{:S(2)}, u32[]{:S(2)}) collective-permute-start(f32[48,16]{0,1:T(8,128)S(1)} %pad_maximum_fusion.8), channel_id=1, source_target_pairs={{0,1},{1,2},{2,3},{3,4},{4,5},{5,6},{6,7},{7,0},{8,9},{9,10},{10,1... | collective-permute-start | bytes 9224 | tf_op jit(solution)/shard_map/ppermute | solution.py:75
  20.4 6.4 %copy-start.14 = (f32[8,16,720]{2,1,0:T(8,128)S(1)}, f32[8,16,720]{2,1,0:T(8,128)}, u32[]{:S(2)}) copy-start(f32[8,16,720]{2,1,0:T(8,128)} %param.7) | copy-start | bytes 1105924
  26.9 2.9 %copy-start.3 = (f32[5,8,16,721]{3,2,1,0:T(8,128)S(1)}, f32[5,8,16,721]{3,2,1,0:T(8,128)}, u32[]{:S(2)}) copy-start(f32[5,8,16,721]{3,2,1,0:T(8,128)} %multiply_subtract_fusion) | copy-start | bytes 5537284
  30.4 1.3 copy-start.1
  31.7 12.3 %collective-permute-start.4 = (f32[16,8,720]{2,1,0:T(8,128)S(1)}, f32[16,8,720]{2,1,0:T(8,128)S(1)}, u32[]{:S(2)}, u32[]{:S(2)}) collective-permute-start(f32[16,8,720]{2,1,0:T(8,128)S(1)} %slice.123), channel_id=1, source_target_pairs={{0,16},{8,24},{16,0},{24,8},{1,17},{9,25},{17,1},{25,9},{2,18},{10... | collective-permute-start | bytes 1105928 | tf_op jit(solution)/shard_map/ppermute | solution.py:129
  34.0 36.8 %copy-start.15 = (f32[45,128]{1,0:T(8,128)}, f32[45,128]{1,0:T(8,128)S(1)}, u32[]{:S(2)}) copy-start(f32[45,128]{1,0:T(8,128)S(1)} %broadcast_maximum_fusion) | copy-start | bytes 69124
  34.9 18.0 %collective-permute-start.5 = (f32[24,8,720]{2,1,0:T(8,128)}, f32[24,8,720]{2,1,0:T(8,128)}, u32[]{:S(2)}, u32[]{:S(2)}) collective-permute-start(f32[24,8,720]{2,1,0:T(8,128)} %slice.125), channel_id=1, source_target_pairs={{0,16},{8,24},{16,0},{24,8},{1,17},{9,25},{17,1},{25,9},{2,18},{10... | collective-permute-start | bytes 1658888 | tf_op jit(solution)/shard_map/ppermute | solution.py:129
  44.8 15.9 %all-to-all-start = ((f32[8,16,720]{2,1,0:T(8,128)}), f32[8,16,720]{2,1,0:T(8,128)S(1)}, u32[]{:S(2)}, u32[]{:S(2)}) async-start(f32[8,16,720]{2,1,0:T(8,128)} %bitcast.138), calls=%async_computation | async-start | bytes 786432 | tf_op jit(solution)/shard_map/all_to_all | solution.py:131
  49.8 21.0 %copy-start.4 = (f32[45,128]{1,0:T(8,128)}, f32[45,128]{1,0:T(8,128)S(1)}, u32[]{:S(2)}) copy-start(f32[45,128]{1,0:T(8,128)S(1)} %get-tuple-element.17) | copy-start | bytes 69124
  49.8 21.0 %copy-start.7 = (f32[45,128]{1,0:T(8,128)}, f32[45,128]{1,0:T(8,128)S(1)}, u32[]{:S(2)}) copy-start(f32[45,128]{1,0:T(8,128)S(1)} %get-tuple-element.18) | copy-start | bytes 69124
  49.9 21.0 %copy-start.17 = (f32[45,128]{1,0:T(8,128)}, f32[45,128]{1,0:T(8,128)S(1)}, u32[]{:S(2)}) copy-start(f32[45,128]{1,0:T(8,128)S(1)} %fusion.100) | copy-start | bytes 69124
  60.8 20.2 %all-to-all-start.2 = ((f32[8,24,720]{2,1,0:T(8,128)}), f32[8,24,720]{2,1,0:T(8,128)S(1)}, u32[]{:S(2)}, u32[]{:S(2)}) async-start(f32[8,24,720]{2,1,0:T(8,128)} %bitcast.24), calls=%async_computation.2 | async-start | bytes 1179648 | tf_op jit(solution)/shard_map/all_to_all | solution.py:131
  69.4 2.2 %copy-start.10 = (f32[16,45,128]{2,1,0:T(8,128)}, f32[16,45,128]{2,1,0:T(8,128)S(1)}, u32[]{:S(2)}) copy-start(f32[16,45,128]{2,1,0:T(8,128)S(1)} %fusion.9) | copy-start | bytes 1105924
  81.6 1.5 %copy-start.5 = (f32[45,128]{1,0:T(8,128)S(1)}, f32[45,128]{1,0:T(8,128)}, u32[]{:S(2)}) copy-start(f32[45,128]{1,0:T(8,128)} %copy-done.4) | copy-start | bytes 69124
  81.6 1.5 %copy-start.8 = (f32[45,128]{1,0:T(8,128)S(1)}, f32[45,128]{1,0:T(8,128)}, u32[]{:S(2)}) copy-start(f32[45,128]{1,0:T(8,128)} %copy-done.7) | copy-start | bytes 69124
  83.1 1.8 %copy-start.16 = (f32[45,128]{1,0:T(8,128)S(1)}, f32[45,128]{1,0:T(8,128)}, u32[]{:S(2)}) copy-start(f32[45,128]{1,0:T(8,128)} %copy-done.15) | copy-start | bytes 69124
  83.1 1.8 %copy-start.18 = (f32[45,128]{1,0:T(8,128)S(1)}, f32[45,128]{1,0:T(8,128)}, u32[]{:S(2)}) copy-start(f32[45,128]{1,0:T(8,128)} %copy-done.17) | copy-start | bytes 69124
  92.5 6.3 %copy-start.11 = (f32[16,45,128]{2,1,0:T(8,128)S(1)}, f32[16,45,128]{2,1,0:T(8,128)}, u32[]{:S(2)}) copy-start(f32[16,45,128]{2,1,0:T(8,128)} %copy-done.10) | copy-start | bytes 1105924
  92.5 7.0 %copy-start.6 = (f32[45,128]{1,0:T(8,128)S(1)}, f32[45,128]{1,0:T(8,128)}, u32[]{:S(2)}) copy-start(f32[45,128]{1,0:T(8,128)} %copy-done.4) | copy-start | bytes 69124
  92.5 7.0 %copy-start.9 = (f32[45,128]{1,0:T(8,128)S(1)}, f32[45,128]{1,0:T(8,128)}, u32[]{:S(2)}) copy-start(f32[45,128]{1,0:T(8,128)} %copy-done.7) | copy-start | bytes 69124
  93.5 20.2 %all-to-all-start.3 = ((f32[24,8,720]{2,0,1:T(8,128)}), f32[24,8,720]{2,0,1:T(8,128)S(1)}, u32[]{:S(2)}, u32[]{:S(2)}) async-start(f32[24,8,720]{2,0,1:T(8,128)} %copy.114), calls=%async_computation.3 | async-start | bytes 1179648 | tf_op jit(solution)/shard_map/all_to_all | solution.py:139
  113.7 15.9 %all-to-all-start.1 = ((f32[16,8,720]{2,0,1:T(8,128)}), f32[16,8,720]{2,0,1:T(8,128)S(1)}, u32[]{:S(2)}, u32[]{:S(2)}) async-start(f32[16,8,720]{2,0,1:T(8,128)} %copy.112), calls=%async_computation.1 | async-start | bytes 786432 | tf_op jit(solution)/shard_map/all_to_all | solution.py:139
  117.2 24.3 %collective-permute-start.7 = (f32[24,8,720]{2,1,0:T(8,128)S(1)}, f32[24,8,720]{2,1,0:T(8,128)S(1)}, u32[]{:S(2)}, u32[]{:S(2)}) collective-permute-start(f32[24,8,720]{2,1,0:T(8,128)S(1)} %bitcast.135), channel_id=1, source_target_pairs={{0,16},{8,24},{16,0},{24,8},{1,17},{9,25},{17,1},{25,9},{2,18},{10... | collective-permute-start | bytes 1658888 | tf_op jit(solution)/shard_map/ppermute | solution.py:143
  129.7 11.9 %copy-start.2 = (f32[5,8,16,720]{3,2,1,0:T(8,128)S(1)}, f32[5,8,16,720]{3,2,1,0:T(8,128)}, u32[]{:S(2)}) copy-start(f32[5,8,16,720]{3,2,1,0:T(8,128)} %copy-done.1) | copy-start | bytes 5529604
  129.7 11.9 %collective-permute-start.6 = (f32[16,8,720]{2,1,0:T(8,128)S(1)}, f32[16,8,720]{2,1,0:T(8,128)S(1)}, u32[]{:S(2)}, u32[]{:S(2)}) collective-permute-start(f32[16,8,720]{2,1,0:T(8,128)S(1)} %bitcast.139), channel_id=1, source_target_pairs={{0,16},{8,24},{16,0},{24,8},{1,17},{9,25},{17,1},{25,9},{2,18},{10... | collective-permute-start | bytes 1105928 | tf_op jit(solution)/shard_map/ppermute | solution.py:143
  (1 other events, 0.7 us)

commit v3 on v2

--- a/solution.py
+++ b/solution.py
@@ -80,22 +80,24 @@
         jnp.concatenate([flat_fields[:, -1], lat_courant[:, -1]], axis=0), "lat", northward
     )
     from_above = lax.ppermute(flat_fields[:, 0], "lat", southward)
-    wide_fields = jnp.concatenate(
-        [from_west[:stacked, :, None], flat_fields, from_east[:, :, None]], axis=2
-    ).reshape(field_count, level_count, rows_dev, columns + 2)
-    wide_courant = jnp.concatenate([from_west[stacked:, :, None], lon_courant], axis=2)
-    column_flux = face_flux(wide_courant, wide_fields[..., :-1], wide_fields[..., 1:])
-    tall_fields = jnp.concatenate(
-        [from_below[:stacked, None], flat_fields, from_above[:, None]], axis=1
-    ).reshape(field_count, level_count, rows_dev + 2, columns)
-    tall_courant = jnp.concatenate([from_below[stacked:, None], lat_courant], axis=1)
-    row_flux = face_flux(tall_courant, tall_fields[:, :, :-1], tall_fields[:, :, 1:])
     tile_index = lax.axis_index("lat")
-    lower_row = tile_index * rows_dev - 1 + jnp.arange(rows_dev + 1, dtype=jnp.int32)
-    row_flux = jnp.where((lower_row == rows_dev * lat_devices - 1)[:, None], 0.0, row_flux)
-    increment = -(column_flux[..., 1:] - column_flux[..., :-1]) - (
-        row_flux[:, :, 1:] - row_flux[:, :, :-1]
-    )
+    column = jnp.arange(columns, dtype=jnp.int32)
+    row = jnp.arange(rows_dev, dtype=jnp.int32)[:, None]
+    west_fields = from_west[:stacked].reshape(field_count, level_count, rows_dev)
+    east_fields = from_east.reshape(field_count, level_count, rows_dev)
+    right = jnp.where(column == columns - 1, east_fields[..., None], jnp.roll(fields, -1, axis=3))
+    east_flux = face_flux(lon_courant, fields, right)
+    west_edge = face_flux(from_west[stacked:], west_fields, fields[..., 0])
+    west_flux = jnp.where(column == 0, west_edge[..., None], jnp.roll(east_flux, 1, axis=3))
+    below_fields = from_below[:stacked].reshape(field_count, level_count, columns)
+    above_fields = from_above.reshape(field_count, level_count, columns)
+    upper = jnp.where(row == rows_dev - 1, above_fields[:, :, None], jnp.roll(fields, -1, axis=2))
+    north_flux = face_flux(lat_courant, fields, upper)
+    top_face = (tile_index == lat_devices - 1) & (row == rows_dev - 1)
+    north_flux = jnp.where(top_face, 0.0, north_flux)
+    south_edge = face_flux(from_below[stacked:], below_fields, fields[:, :, 0])
+    south_flux = jnp.where(row == 0, south_edge[:, :, None], jnp.roll(north_flux, 1, axis=2))
+    increment = -(east_flux - west_flux) - (north_flux - south_flux)
     flat_increment = increment.reshape(stacked, rows_dev, columns)
     half_rows = rows_dev // 2
     pair_shift = lat_devices // 2

time: 144 us -> 149 us (1.035)
  other arithmetic: 11.6 us -> 18.7 us
  waiting for transfers between devices: 60.1 us -> 58.6 us
    concatenate x10 -> x0, local copies, waits for them, and re-layouts: 5.31 us -> none  [the longest x4 4.4 us: body(): jnp.concatenate([from_below[:stacked, None], flat_fields, from_above[:, N...]
    slice x1 -> x6, local copies, waits for them, and re-layouts: 0.08 us -> 4.37 us  [the longest x2 2.2 us: body(): jnp.roll(fields, -1, axis=2)]
    ppermute x1, waiting for transfers between devices: 2.3 us -> 0.01 us  [body(): lax.ppermute(jnp.concatenate([flat_fields[..., -1], lon_courant[..., -1]]...]
    mul x2 -> x4, other arithmetic: 0.28 us -> 2.32 us  [face_flux(): 0.5 * courant * (near_value + far_value)]
    eq x1 -> x3, other arithmetic: 0.01 us -> 1.71 us  [the longest x1 0.6 us: body(): row == 0]
    broadcast_in_dim x0 -> x2, other arithmetic: none -> 1.66 us  [the longest x1 0.93 us: body(): jnp.where(row == 0, south_edge[:, :, None], jnp.roll(north_flux, 1, axis=2))]
    unnamed x46 -> x49, local copies, waits for them, and re-layouts: 3.51 us -> 3.04 us
  transfers between devices with their start and end apart: 12 -> 12, of which waited for: 8 -> 7; matrix products, arithmetic and copies ran while one was open for 21% -> 24% of each run, Pallas kernels for 0% -> 0%
where the time goes in v3:
time: 149 us; the launch traced here: 148 us
  waiting for transfers between devices  58.6 us (39%)
  starting transfers between devices  30.3 us (20%)
  local copies, waits for them, and re-layouts  20.3 us (14%)
  matrix products  19.4 us (13%)
  other arithmetic  18.7 us (13%)
    all_to_all x2, waiting for transfers between devices, body(): lax.all_to_all(smoothed, 'lon', split_axis=1, concat_axis=0, tiled=True)  22.7 us
    ppermute x2, waiting for transfers between devices, body(): taken = lax.ppermute(given[rows_of_part], 'lat', pair_perm)  13.6 us
    all_to_all x2, waiting for transfers between devices, body(): lax.all_to_all(pair_lines.reshape(chunk_stack * half_rows, columns), 'lon...  12.4 us
    ppermute x2, waiting for transfers between devices, body(): handed_parts.append(lax.ppermute(returned, 'lat', pair_perm))  10 us
    all_to_all x2, starting transfers between devices, body(): lax.all_to_all(pair_lines.reshape(chunk_stack * half_rows, columns), 'lon...  7.76 us
    all_to_all x2, starting transfers between devices, body(): lax.all_to_all(smoothed, 'lon', split_axis=1, concat_axis=0, tiled=True)  6.99 us
    ppermute x1, starting transfers between devices, body(): lax.ppermute(jnp.concatenate([flat_fields[:, -1], lat_courant[:, -1]], ax...  6.14 us
    select_n x1, other arithmetic, body(): north_flux = jnp.where(top_face, 0.0, north_flux)  3.17 us
  transfers between devices with their start and end apart: 12, of which 7 were waited for; matrix products, arithmetic and copies ran while one was open for 24% of the time, Pallas kernels for 0%

profile of v3, /device:TPU:0, one launch (start us, length us, event | category | flops | bytes accessed | tf_op | source)
XLA Modules:
  0.0 148.1 jit_solution(3855542544395918991)
XLA Ops:
  0.0 1.7 %fusion.247 = (f32[40,1,720]{2,1,0:T(1,128)S(1)}, f32[40,1,720]{2,1,0:T(1,128)S(1)}) fusion(f32[40,16,720]{2,1,0:T(8,128)} %bitcast.135), kind=kLoop, calls=%fused_computation.296 | loop fusion | bytes 460800 | tf_op jit(solution)/shard_map/slice | solution.py:80
  2.4 1.3 collective-permute-start.2
  3.7 1.0 slice.109
  5.3 6.1 %collective-permute-start.3 = (f32[48,720]{1,0:T(8,128)}, f32[48,720]{1,0:T(8,128)}, u32[]{:S(2)}, u32[]{:S(2)}) collective-permute-start(f32[48,720]{1,0:T(8,128)} %pad_maximum_fusion.2), channel_id=1, source_target_pairs={{0,8},{8,16},{16,24},{1,9},{9,17},{17,25},{2,10},{10,18},{18,26},{... | collective-permute-start | bytes 414728 | tf_op jit(solution)/shard_map/ppermute | solution.py:79
  11.5 1.2 fusion.246
  13.5 3.0 %collective-permute-start = (f32[40,16]{0,1:T(8,128)}, f32[40,16]{0,1:T(8,128)S(1)}, u32[]{:S(2)}, u32[]{:S(2)}) collective-permute-start(f32[40,16]{0,1:T(8,128)} %bitcast.2), channel_id=1, source_target_pairs={{1,0},{2,1},{3,2},{4,3},{5,4},{6,5},{7,6},{0,7},{9,8},{10,9},{11,1... | collective-permute-start | bytes 7688 | tf_op jit(solution)/shard_map/ppermute | solution.py:78
  22.9 1.5 %slice.106 = f32[5,8,15,720]{3,2,1,0:T(8,128)} slice(f32[5,8,16,720]{3,2,1,0:T(8,128)S(1)} %copy-done), slice={[0:5], [0:8], [1:16], [0:720]} | slice | bytes 3456000 | tf_op jit(solution)/shard_map/jit(_roll_static)/slice | solution.py:94
  24.4 1.9 %slice.97 = f32[5,8,16,719]{3,2,1,0:T(8,128)} slice(f32[5,8,16,720]{3,2,1,0:T(8,128)S(1)} %copy-done), slice={[0:5], [0:8], [0:16], [1:720]} | slice | bytes 3681280 | tf_op jit(solution)/shard_map/jit(_roll_static)/slice | solution.py:88
  28.1 3.2 %subtract_select_fusion = (f32[5,8,16,720]{3,2,1,0:T(8,128)S(1)}, f32[5,8,16,720]{3,2,1,0:T(8,128)S(1)}) fusion(f32[5,8,16,720]{3,2,1,0:T(8,128)S(1)} %copy-done, f32[5,8,1,720]{3,2,1,0:T(1,128)} %slice.107, f32[5,8,15,720]{3,2,1,0:T(8,128)} %slice.106, f32[8,16,720]{2,1,0:T(8,128)} %get-tuple-element.16, f32[5,8,720]{2,1,0:T(8,128)} %bitcast.9, ...), kind=kLoop, calls=%fused_computation.13 | loop fusion | flops 6912000 | bytes 10809072 | tf_op jit(solution)/shard_map/jit(_where)/select_n | solution.py:97
  33.3 1.4 fusion.2
  34.9 1.1 copy-done.1
  36.0 1.6 %collective-permute-start.4 = (f32[16,8,720]{2,1,0:T(8,128)S(1)}, f32[16,8,720]{2,1,0:T(8,128)S(1)}, u32[]{:S(2)}, u32[]{:S(2)}) collective-permute-start(f32[16,8,720]{2,1,0:T(8,128)S(1)} %slice.141), channel_id=1, source_target_pairs={{0,16},{8,24},{16,0},{24,8},{1,17},{9,25},{17,1},{25,9},{2,18},{10... | collective-permute-start | bytes 1105928 | tf_op jit(solution)/shard_map/ppermute | solution.py:131
  39.1 9.1 %collective-permute-done.4 = f32[16,8,720]{2,1,0:T(8,128)S(1)} collective-permute-done((f32[16,8,720]{2,1,0:T(8,128)S(1)}, f32[16,8,720]{2,1,0:T(8,128)S(1)}, u32[]{:S(2)}, u32[]{:S(2)}) %collective-permute-start.4) | collective-permute-done | bytes 368672 | tf_op jit(solution)/shard_map/ppermute | solution.py:131
  49.0 4.0 %all-to-all-start = ((f32[8,16,720]{2,1,0:T(8,128)}), f32[8,16,720]{2,1,0:T(8,128)S(1)}, u32[]{:S(2)}, u32[]{:S(2)}) async-start(f32[8,16,720]{2,1,0:T(8,128)} %bitcast.146), calls=%async_computation | async-start | bytes 786432 | tf_op jit(solution)/shard_map/all_to_all | solution.py:133
  54.6 4.5 %collective-permute-done.5 = f32[24,8,720]{2,1,0:T(8,128)} collective-permute-done((f32[24,8,720]{2,1,0:T(8,128)}, f32[24,8,720]{2,1,0:T(8,128)}, u32[]{:S(2)}, u32[]{:S(2)}) %collective-permute-start.5) | collective-permute-done | bytes 552992 | tf_op jit(solution)/shard_map/ppermute | solution.py:131
  59.1 2.0 %slice_select_fusion.2 = f32[24,8,720]{2,1,0:T(8,128)} fusion(f32[24,8,720]{2,1,0:T(8,128)} %collective-permute-done.5, f32[40,8,720]{2,1,0:T(8,128)S(1)} %get-tuple-element.7, pred[8]{0:T(512)(128)(4,1)S(1)} %slice_select_fusion.4), kind=kLoop, calls=%fused_computation.41 | loop fusion | flops 138240 | bytes 1658888 | tf_op jit(solution)/shard_map/jit(_where)/select_n | solution.py:132
  61.1 4.5 %all-to-all-done = f32[8,16,720]{2,1,0:T(8,128)S(1)} async-done(((f32[8,16,720]{2,1,0:T(8,128)}), f32[8,16,720]{2,1,0:T(8,128)S(1)}, u32[]{:S(2)}, u32[]{:S(2)}) %all-to-all-start) | async-done | bytes 368672 | tf_op jit(solution)/shard_map/all_to_all | solution.py:133
  65.6 3.7 %all-to-all-start.2 = ((f32[8,24,720]{2,1,0:T(8,128)}), f32[8,24,720]{2,1,0:T(8,128)S(1)}, u32[]{:S(2)}, u32[]{:S(2)}) async-start(f32[8,24,720]{2,1,0:T(8,128)} %bitcast.25), calls=%async_computation.2 | async-start | bytes 1179648 | tf_op jit(solution)/shard_map/all_to_all | solution.py:133
  69.3 1.0 copy.132
  70.3 1.2 reshape.271
  77.9 7.9 %all-to-all-done.2 = f32[8,24,720]{2,1,0:T(8,128)S(1)} async-done(((f32[8,24,720]{2,1,0:T(8,128)}), f32[8,24,720]{2,1,0:T(8,128)S(1)}, u32[]{:S(2)}, u32[]{:S(2)}) %all-to-all-start.2) | async-done | bytes 552992 | tf_op jit(solution)/shard_map/all_to_all | solution.py:133
  91.5 1.1 fusion.9
  97.3 1.0 copy.135
  98.4 3.5 %all-to-all-start.3 = ((f32[24,8,720]{2,0,1:T(8,128)}), f32[24,8,720]{2,0,1:T(8,128)S(1)}, u32[]{:S(2)}, u32[]{:S(2)}) async-start(f32[24,8,720]{2,0,1:T(8,128)} %copy.135), calls=%async_computation.3 | async-start | bytes 1179648 | tf_op jit(solution)/shard_map/all_to_all | solution.py:141
  101.9 1.7 %fusion.72 = f32[16,45,128]{2,1,0:T(8,128)S(1)} fusion(f32[16,45,128]{2,1,0:T(8,128)} %copy-done.11), kind=kOutput, calls=%fused_computation.115 | convolution fusion | flops 141787136 | bytes 737280 | tf_op jit(solution)/shard_map/ljk,kn->ljn/dot_general | solution.py:49
  106.8 11.8 %all-to-all-done.3 = f32[24,8,720]{2,0,1:T(8,128)S(1)} async-done(((f32[24,8,720]{2,0,1:T(8,128)}), f32[24,8,720]{2,0,1:T(8,128)S(1)}, u32[]{:S(2)}, u32[]{:S(2)}) %all-to-all-start.3) | async-done | bytes 552992 | tf_op jit(solution)/shard_map/all_to_all | solution.py:141
  118.6 3.5 %all-to-all-start.1 = ((f32[16,8,720]{2,0,1:T(8,128)}), f32[16,8,720]{2,0,1:T(8,128)S(1)}, u32[]{:S(2)}, u32[]{:S(2)}) async-start(f32[16,8,720]{2,0,1:T(8,128)} %copy.133), calls=%async_computation.1 | async-start | bytes 786432 | tf_op jit(solution)/shard_map/all_to_all | solution.py:141
  122.1 1.6 %collective-permute-start.7 = (f32[24,8,720]{2,1,0:T(8,128)S(1)}, f32[24,8,720]{2,1,0:T(8,128)S(1)}, u32[]{:S(2)}, u32[]{:S(2)}) collective-permute-start(f32[24,8,720]{2,1,0:T(8,128)S(1)} %bitcast.143), channel_id=1, source_target_pairs={{0,16},{8,24},{16,0},{24,8},{1,17},{9,25},{17,1},{25,9},{2,18},{10... | collective-permute-start | bytes 1658888 | tf_op jit(solution)/shard_map/ppermute | solution.py:145
  123.6 10.9 %all-to-all-done.1 = f32[16,8,720]{2,0,1:T(8,128)S(1)} async-done(((f32[16,8,720]{2,0,1:T(8,128)}), f32[16,8,720]{2,0,1:T(8,128)S(1)}, u32[]{:S(2)}, u32[]{:S(2)}) %all-to-all-start.1) | async-done | bytes 368672 | tf_op jit(solution)/shard_map/all_to_all | solution.py:141
  134.5 1.5 %collective-permute-start.6 = (f32[16,8,720]{2,1,0:T(8,128)S(1)}, f32[16,8,720]{2,1,0:T(8,128)S(1)}, u32[]{:S(2)}, u32[]{:S(2)}) collective-permute-start(f32[16,8,720]{2,1,0:T(8,128)S(1)} %bitcast.147), channel_id=1, source_target_pairs={{0,16},{8,24},{16,0},{24,8},{1,17},{9,25},{17,1},{25,9},{2,18},{10... | collective-permute-start | bytes 1105928 | tf_op jit(solution)/shard_map/ppermute | solution.py:145
  136.1 10.0 %collective-permute-done.6 = f32[16,8,720]{2,1,0:T(8,128)S(1)} collective-permute-done((f32[16,8,720]{2,1,0:T(8,128)S(1)}, f32[16,8,720]{2,1,0:T(8,128)S(1)}, u32[]{:S(2)}, u32[]{:S(2)}) %collective-permute-start.6) | collective-permute-done | bytes 368672 | tf_op jit(solution)/shard_map/ppermute | solution.py:145
  146.2 1.9 %fusion.5 = f32[5,8,16,720]{3,2,1,0:T(8,128)} fusion(f32[5,8,16,720]{3,2,1,0:T(8,128)S(1)} %copy-done, f32[5,8,16,720]{3,2,1,0:T(8,128)S(1)} %copy-done.2, f32[5,8,8,720]{3,2,1,0:T(8,128)S(1)} %bitcast.141, f32[5,8,8,720]{3,2,1,0:T(8,128)S(1)} %bitcast.140, pred[16]{0:T(512)(128)(4,1)S(1)} %compare_reduce_fusion, pred[]{:T(512)S(6)} %lt.139), kind=kLoop, calls=%fused_computation.12 | loop fusion | flops 2304000 | bytes 7372817 | tf_op jit(solution)/shard_map/add | solution.py:154
  (125 shorter events, 35.9 us)
Async XLA Ops:
  0.0 16.5 %copy-start.13 = (f32[8,16,720]{2,1,0:T(8,128)S(1)}, f32[8,16,720]{2,1,0:T(8,128)}, u32[]{:S(2)}) copy-start(f32[8,16,720]{2,1,0:T(8,128)} %param.6) | copy-start | bytes 1105924
  2.4 25.7 %collective-permute-start.2 = (f32[40,720]{1,0:T(8,128)}, f32[40,720]{1,0:T(8,128)}, u32[]{:S(2)}, u32[]{:S(2)}) collective-permute-start(f32[40,720]{1,0:T(8,128)} %bitcast.131), channel_id=1, source_target_pairs={{8,0},{16,8},{24,16},{9,1},{17,9},{25,17},{10,2},{18,10},{26,18},{... | collective-permute-start | bytes 345608 | tf_op jit(solution)/shard_map/ppermute | solution.py:82
  4.7 14.8 %copy-start.14 = (f32[8,16,720]{2,1,0:T(8,128)S(1)}, f32[8,16,720]{2,1,0:T(8,128)}, u32[]{:S(2)}) copy-start(f32[8,16,720]{2,1,0:T(8,128)} %param.7) | copy-start | bytes 1105924
  5.3 26.2 %collective-permute-start.3 = (f32[48,720]{1,0:T(8,128)}, f32[48,720]{1,0:T(8,128)}, u32[]{:S(2)}, u32[]{:S(2)}) collective-permute-start(f32[48,720]{1,0:T(8,128)} %pad_maximum_fusion.2), channel_id=1, source_target_pairs={{0,8},{8,16},{16,24},{1,9},{9,17},{17,25},{2,10},{10,18},{18,26},{... | collective-permute-start | bytes 414728 | tf_op jit(solution)/shard_map/ppermute | solution.py:79
  12.7 9.4 %copy-start = (f32[5,8,16,720]{3,2,1,0:T(8,128)S(1)}, f32[5,8,16,720]{3,2,1,0:T(8,128)}, u32[]{:S(2)}) copy-start(f32[5,8,16,720]{3,2,1,0:T(8,128)} %param.5) | copy-start | bytes 5529604
  13.5 13.1 %collective-permute-start = (f32[40,16]{0,1:T(8,128)}, f32[40,16]{0,1:T(8,128)S(1)}, u32[]{:S(2)}, u32[]{:S(2)}) collective-permute-start(f32[40,16]{0,1:T(8,128)} %bitcast.2), channel_id=1, source_target_pairs={{1,0},{2,1},{3,2},{4,3},{5,4},{6,5},{7,6},{0,7},{9,8},{10,9},{11,1... | collective-permute-start | bytes 7688 | tf_op jit(solution)/shard_map/ppermute | solution.py:78
  17.6 9.0 %collective-permute-start.1 = (f32[48,16]{1,0:T(8,128)}, f32[48,16]{1,0:T(8,128)}, u32[]{:S(2)}, u32[]{:S(2)}) collective-permute-start(f32[48,16]{1,0:T(8,128)} %pad_maximum_fusion.3), channel_id=1, source_target_pairs={{0,1},{1,2},{2,3},{3,4},{4,5},{5,6},{6,7},{7,0},{8,9},{9,10},{10,1... | collective-permute-start | bytes 9224 | tf_op jit(solution)/shard_map/ppermute | solution.py:75
  24.4 3.7 %copy-start.20 = (pred[720]{0:T(1024)(128)(4,1)S(1)}, pred[720]{0:T(1024)(128)(4,1)}, u32[]{:S(2)}) copy-start(pred[720]{0:T(1024)(128)(4,1)} %iota_compare_fusion.1) | copy-start | bytes 2164
  28.1 4.2 %copy-start.12 = (f32[5,8,1,720]{3,2,1,0:T(1,128)S(1)}, f32[5,8,1,720]{3,2,1,0:T(1,128)}, u32[]{:S(2)}) copy-start(f32[5,8,1,720]{3,2,1,0:T(1,128)} %slice.107) | copy-start | bytes 345604
  28.1 5.2 %copy-start.19 = (pred[720]{0:T(1024)(128)(4,1)S(1)}, pred[720]{0:T(1024)(128)(4,1)}, u32[]{:S(2)}) copy-start(pred[720]{0:T(1024)(128)(4,1)} %iota_compare_fusion) | copy-start | bytes 2164
  28.1 5.2 %copy-start.21 = (pred[16]{0:T(512)(128)(4,1)S(1)}, pred[16]{0:T(512)(128)(4,1)}, u32[]{:S(2)}) copy-start(pred[16]{0:T(512)(128)(4,1)} %iota_compare_fusion.2) | copy-start | bytes 52
  36.0 12.1 %collective-permute-start.4 = (f32[16,8,720]{2,1,0:T(8,128)S(1)}, f32[16,8,720]{2,1,0:T(8,128)S(1)}, u32[]{:S(2)}, u32[]{:S(2)}) collective-permute-start(f32[16,8,720]{2,1,0:T(8,128)S(1)} %slice.141), channel_id=1, source_target_pairs={{0,16},{8,24},{16,0},{24,8},{1,17},{9,25},{17,1},{25,9},{2,18},{10... | collective-permute-start | bytes 1105928 | tf_op jit(solution)/shard_map/ppermute | solution.py:131
  37.7 38.0 %copy-start.15 = (f32[45,128]{1,0:T(8,128)}, f32[45,128]{1,0:T(8,128)S(1)}, u32[]{:S(2)}) copy-start(f32[45,128]{1,0:T(8,128)S(1)} %broadcast_maximum_fusion) | copy-start | bytes 69124
  38.6 20.5 %collective-permute-start.5 = (f32[24,8,720]{2,1,0:T(8,128)}, f32[24,8,720]{2,1,0:T(8,128)}, u32[]{:S(2)}, u32[]{:S(2)}) collective-permute-start(f32[24,8,720]{2,1,0:T(8,128)} %slice.143), channel_id=1, source_target_pairs={{0,16},{8,24},{16,0},{24,8},{1,17},{9,25},{17,1},{25,9},{2,18},{10... | collective-permute-start | bytes 1658888 | tf_op jit(solution)/shard_map/ppermute | solution.py:131
  49.0 16.6 %all-to-all-start = ((f32[8,16,720]{2,1,0:T(8,128)}), f32[8,16,720]{2,1,0:T(8,128)S(1)}, u32[]{:S(2)}, u32[]{:S(2)}) async-start(f32[8,16,720]{2,1,0:T(8,128)} %bitcast.146), calls=%async_computation | async-start | bytes 786432 | tf_op jit(solution)/shard_map/all_to_all | solution.py:133
  54.5 21.1 %copy-start.3 = (f32[45,128]{1,0:T(8,128)}, f32[45,128]{1,0:T(8,128)S(1)}, u32[]{:S(2)}) copy-start(f32[45,128]{1,0:T(8,128)S(1)} %get-tuple-element.25) | copy-start | bytes 69124
  54.6 21.1 %copy-start.6 = (f32[45,128]{1,0:T(8,128)}, f32[45,128]{1,0:T(8,128)S(1)}, u32[]{:S(2)}) copy-start(f32[45,128]{1,0:T(8,128)S(1)} %get-tuple-element.26) | copy-start | bytes 69124
  54.6 21.1 %copy-start.17 = (f32[45,128]{1,0:T(8,128)}, f32[45,128]{1,0:T(8,128)S(1)}, u32[]{:S(2)}) copy-start(f32[45,128]{1,0:T(8,128)S(1)} %fusion.100) | copy-start | bytes 69124
  65.6 20.2 %all-to-all-start.2 = ((f32[8,24,720]{2,1,0:T(8,128)}), f32[8,24,720]{2,1,0:T(8,128)S(1)}, u32[]{:S(2)}, u32[]{:S(2)}) async-start(f32[8,24,720]{2,1,0:T(8,128)} %bitcast.25), calls=%async_computation.2 | async-start | bytes 1179648 | tf_op jit(solution)/shard_map/all_to_all | solution.py:133
  74.2 2.2 %copy-start.9 = (f32[16,45,128]{2,1,0:T(8,128)}, f32[16,45,128]{2,1,0:T(8,128)S(1)}, u32[]{:S(2)}) copy-start(f32[16,45,128]{2,1,0:T(8,128)S(1)} %fusion.11) | copy-start | bytes 1105924
  86.4 1.5 %copy-start.4 = (f32[45,128]{1,0:T(8,128)S(1)}, f32[45,128]{1,0:T(8,128)}, u32[]{:S(2)}) copy-start(f32[45,128]{1,0:T(8,128)} %copy-done.3) | copy-start | bytes 69124
  86.4 1.5 %copy-start.7 = (f32[45,128]{1,0:T(8,128)S(1)}, f32[45,128]{1,0:T(8,128)}, u32[]{:S(2)}) copy-start(f32[45,128]{1,0:T(8,128)} %copy-done.6) | copy-start | bytes 69124
  88.0 1.8 %copy-start.16 = (f32[45,128]{1,0:T(8,128)S(1)}, f32[45,128]{1,0:T(8,128)}, u32[]{:S(2)}) copy-start(f32[45,128]{1,0:T(8,128)} %copy-done.15) | copy-start | bytes 69124
  88.0 1.8 %copy-start.18 = (f32[45,128]{1,0:T(8,128)S(1)}, f32[45,128]{1,0:T(8,128)}, u32[]{:S(2)}) copy-start(f32[45,128]{1,0:T(8,128)} %copy-done.17) | copy-start | bytes 69124
  97.3 6.3 %copy-start.10 = (f32[16,45,128]{2,1,0:T(8,128)S(1)}, f32[16,45,128]{2,1,0:T(8,128)}, u32[]{:S(2)}) copy-start(f32[16,45,128]{2,1,0:T(8,128)} %copy-done.9) | copy-start | bytes 1105924
  97.3 7.0 %copy-start.5 = (f32[45,128]{1,0:T(8,128)S(1)}, f32[45,128]{1,0:T(8,128)}, u32[]{:S(2)}) copy-start(f32[45,128]{1,0:T(8,128)} %copy-done.3) | copy-start | bytes 69124
  97.3 7.0 %copy-start.8 = (f32[45,128]{1,0:T(8,128)S(1)}, f32[45,128]{1,0:T(8,128)}, u32[]{:S(2)}) copy-start(f32[45,128]{1,0:T(8,128)} %copy-done.6) | copy-start | bytes 69124
  98.4 20.2 %all-to-all-start.3 = ((f32[24,8,720]{2,0,1:T(8,128)}), f32[24,8,720]{2,0,1:T(8,128)S(1)}, u32[]{:S(2)}, u32[]{:S(2)}) async-start(f32[24,8,720]{2,0,1:T(8,128)} %copy.135), calls=%async_computation.3 | async-start | bytes 1179648 | tf_op jit(solution)/shard_map/all_to_all | solution.py:141
  118.6 15.9 %all-to-all-start.1 = ((f32[16,8,720]{2,0,1:T(8,128)}), f32[16,8,720]{2,0,1:T(8,128)S(1)}, u32[]{:S(2)}, u32[]{:S(2)}) async-start(f32[16,8,720]{2,0,1:T(8,128)} %copy.133), calls=%async_computation.1 | async-start | bytes 786432 | tf_op jit(solution)/shard_map/all_to_all | solution.py:141
  122.1 24.1 %collective-permute-start.7 = (f32[24,8,720]{2,1,0:T(8,128)S(1)}, f32[24,8,720]{2,1,0:T(8,128)S(1)}, u32[]{:S(2)}, u32[]{:S(2)}) collective-permute-start(f32[24,8,720]{2,1,0:T(8,128)S(1)} %bitcast.143), channel_id=1, source_target_pairs={{0,16},{8,24},{16,0},{24,8},{1,17},{9,25},{17,1},{25,9},{2,18},{10... | collective-permute-start | bytes 1658888 | tf_op jit(solution)/shard_map/ppermute | solution.py:145
  134.5 11.7 %copy-start.2 = (f32[5,8,16,720]{3,2,1,0:T(8,128)S(1)}, f32[5,8,16,720]{3,2,1,0:T(8,128)}, u32[]{:S(2)}) copy-start(f32[5,8,16,720]{3,2,1,0:T(8,128)} %copy-done.1) | copy-start | bytes 5529604
  134.5 11.6 %collective-permute-start.6 = (f32[16,8,720]{2,1,0:T(8,128)S(1)}, f32[16,8,720]{2,1,0:T(8,128)S(1)}, u32[]{:S(2)}, u32[]{:S(2)}) collective-permute-start(f32[16,8,720]{2,1,0:T(8,128)S(1)} %bitcast.147), channel_id=1, source_target_pairs={{0,16},{8,24},{16,0},{24,8},{1,17},{9,25},{17,1},{25,9},{2,18},{10... | collective-permute-start | bytes 1105928 | tf_op jit(solution)/shard_map/ppermute | solution.py:145
  (2 other events, 2.0 us)

commit v4 on v2

--- a/solution.py
+++ b/solution.py
@@ -22,7 +22,7 @@
 def filter_lines(lines, line_cut):
     line_total, circle = lines.shape
     outer = circle // radix_len
-    mixer = partial(jnp.einsum, precision=lax.Precision.HIGHEST)
+    mixer = partial(jnp.einsum, precision=lax.Precision.HIGH)
     outer_cos, outer_sin = phase_table(outer, outer, outer)
     inner_cos, inner_sin = phase_table(radix_len, radix_len, radix_len)
     twist_cos, twist_sin = phase_table(outer, radix_len, circle)

time: 144 us -> 141 us (0.979)
  matrix products: 19.4 us -> 14.7 us
  waiting for transfers between devices: 60.1 us -> 62 us
  transfers between devices with their start and end apart: 12 -> 12, of which waited for: 8 -> 8; matrix products, arithmetic and copies ran while one was open for 21% -> 20% of each run, Pallas kernels for 0% -> 0%
where the time goes in v4:
time: 141 us
  waiting for transfers between devices  62 us (44%)
  starting transfers between devices  30.3 us (21%)
  local copies, waits for them, and re-layouts  21.4 us (15%)
  matrix products  14.7 us (10%)
  other arithmetic  11.6 us (8%)
    all_to_all x2, waiting for transfers between devices, body(): lax.all_to_all(smoothed, 'lon', split_axis=1, concat_axis=0, tiled=True)  22.8 us
    all_to_all x2, waiting for transfers between devices, body(): lax.all_to_all(pair_lines.reshape(chunk_stack * half_rows, columns), 'lon...  15 us
    ppermute x2, waiting for transfers between devices, body(): taken = lax.ppermute(given[rows_of_part], 'lat', pair_perm)  12.1 us
    ppermute x2, waiting for transfers between devices, body(): handed_parts.append(lax.ppermute(returned, 'lat', pair_perm))  9.78 us
    all_to_all x2, starting transfers between devices, body(): lax.all_to_all(pair_lines.reshape(chunk_stack * half_rows, columns), 'lon...  7.17 us
    all_to_all x2, starting transfers between devices, body(): lax.all_to_all(smoothed, 'lon', split_axis=1, concat_axis=0, tiled=True)  6.99 us
    ppermute x1, starting transfers between devices, body(): lax.ppermute(jnp.concatenate([flat_fields[:, -1], lat_courant[:, -1]], ax...  5.48 us
    concatenate x4, local copies, waits for them, and re-layouts, body(): jnp.concatenate([from_below[:stacked, None], flat_fields, from_above[:, N...  4.4 us
  transfers between devices with their start and end apart: 12, of which 8 were waited for; matrix products, arithmetic and copies ran while one was open for 20% of the time, Pallas kernels for 0%

profile of v4, /device:TPU:0, one launch (start us, length us, event | category | flops | bytes accessed | tf_op | source)
XLA Modules:
  0.0 140.7 jit_solution(3245262672680632288)
XLA Ops:
  0.0 1.8 %fusion.247 = (f32[40,1,720]{2,1,0:T(1,128)S(1)}, f32[40,1,720]{2,1,0:T(1,128)S(1)}) fusion(f32[40,16,720]{2,1,0:T(8,128)} %bitcast.129), kind=kLoop, calls=%fused_computation.289 | loop fusion | bytes 460800 | tf_op jit(solution)/shard_map/slice | solution.py:80
  1.8 1.3 collective-permute-start.3
  4.1 5.5 %collective-permute-start.2 = (f32[48,720]{1,0:T(8,128)S(1)}, f32[48,720]{1,0:T(8,128)S(1)}, u32[]{:S(2)}, u32[]{:S(2)}) collective-permute-start(f32[48,720]{1,0:T(8,128)S(1)} %pad_maximum_fusion.7), channel_id=1, source_target_pairs={{0,8},{8,16},{16,24},{1,9},{9,17},{17,25},{2,10},{10,18},{18,26},{... | collective-permute-start | bytes 414728 | tf_op jit(solution)/shard_map/ppermute | solution.py:79
  9.6 1.2 fusion.246
  11.1 3.0 %collective-permute-start.1 = (f32[40,16]{0,1:T(8,128)S(1)}, f32[40,16]{0,1:T(8,128)S(1)}, u32[]{:S(2)}, u32[]{:S(2)}) collective-permute-start(f32[40,16]{0,1:T(8,128)S(1)} %bitcast.149), channel_id=1, source_target_pairs={{1,0},{2,1},{3,2},{4,3},{5,4},{6,5},{7,6},{0,7},{9,8},{10,9},{11,1... | collective-permute-start | bytes 7688 | tf_op jit(solution)/shard_map/ppermute | solution.py:78
  14.7 1.6 %constant_dynamic-update-slice_fusion = f32[5,8,17,720]{3,2,1,0:T(8,128)} fusion(f32[5,8,16,720]{3,2,1,0:T(8,128)S(1)} %copy-done), kind=kLoop, calls=%fused_computation.186 | loop fusion | bytes 3809280
  17.2 2.3 %collective-permute-done = f32[48,16]{0,1:T(8,128)S(1)} collective-permute-done((f32[48,16]{0,1:T(8,128)S(1)}, f32[48,16]{0,1:T(8,128)S(1)}, u32[]{:S(2)}, u32[]{:S(2)}) %collective-permute-start) | collective-permute-done | bytes 3104 | tf_op jit(solution)/shard_map/ppermute | solution.py:75
  20.4 2.0 %multiply_subtract_fusion = f32[5,8,16,721]{3,2,1,0:T(8,128)} fusion(f32[5,8,16,1]{3,2,1,0:T(8,128)S(1)} %copy.106, f32[5,8,16,720]{3,2,1,0:T(8,128)S(1)} %copy-done, f32[5,8,16,1]{3,2,1,0:T(8,128)S(1)} %copy.103, f32[8,16,721]{2,1,0:T(8,128)S(1)} %get-tuple-element.14, f32[8,16,721]{2,1,0:T(8,128)S(1)} %get-tuple-element.13), kind=kLoop, calls=%fused_computation.13 | loop fusion | flops 3230080 | bytes 4432384 | tf_op jit(solution)/shard_map/sub | solution.py:60
  22.3 1.0 copy.110
  23.4 3.2 %dynamic-update-slice.1 = f32[5,8,17,720]{3,2,1,0:T(8,128)} dynamic-update-slice(f32[5,8,17,720]{3,2,1,0:T(8,128)} %constant_dynamic-update-slice_fusion, f32[5,8,1,720]{3,2,1,0:T(1,128)S(1)} %copy.110, s32[]{} %constant.131, s32[]{} %constant.131, s32[]{} %constant.132, s32[]{} %constant.131) | dynamic-update-slice | bytes 230404 | tf_op jit(solution)/shard_map/concatenate | solution.py:88
  26.9 2.9 %subtract_select_fusion = f32[5,8,17,720]{3,2,1,0:T(8,128)S(1)} fusion(f32[5,8,17,720]{3,2,1,0:T(8,128)} %dynamic-update-slice.1, f32[5,8,16,720]{3,2,1,0:T(8,128)S(1)} %copy-done, f32[5,8,1,720]{3,2,1,0:T(1,128)S(1)} %copy.109, f32[8,17,720]{2,1,0:T(8,128)S(1)} %get-tuple-element.16, f32[8,17,720]{2,1,0:T(8,128)S(1)} %get-tuple-element.15, ...), kind=kLoop, calls=%fused_computation.3 | loop fusion | flops 3427200 | bytes 6658577 | tf_op jit(solution)/shard_map/jit(_where)/select_n | solution.py:95
  30.6 1.1 copy-done.1
  31.7 2.2 %collective-permute-start.4 = (f32[16,8,720]{2,1,0:T(8,128)S(1)}, f32[16,8,720]{2,1,0:T(8,128)S(1)}, u32[]{:S(2)}, u32[]{:S(2)}) collective-permute-start(f32[16,8,720]{2,1,0:T(8,128)S(1)} %slice.123), channel_id=1, source_target_pairs={{0,16},{8,24},{16,0},{24,8},{1,17},{9,25},{17,1},{25,9},{2,18},{10... | collective-permute-start | bytes 1105928 | tf_op jit(solution)/shard_map/ppermute | solution.py:129
  34.9 9.1 %collective-permute-done.4 = f32[16,8,720]{2,1,0:T(8,128)S(1)} collective-permute-done((f32[16,8,720]{2,1,0:T(8,128)S(1)}, f32[16,8,720]{2,1,0:T(8,128)S(1)}, u32[]{:S(2)}, u32[]{:S(2)}) %collective-permute-start.4) | collective-permute-done | bytes 368672 | tf_op jit(solution)/shard_map/ppermute | solution.py:129
  44.8 3.5 %all-to-all-start = ((f32[8,16,720]{2,1,0:T(8,128)}), f32[8,16,720]{2,1,0:T(8,128)S(1)}, u32[]{:S(2)}, u32[]{:S(2)}) async-start(f32[8,16,720]{2,1,0:T(8,128)} %bitcast.138), calls=%async_computation | async-start | bytes 786432 | tf_op jit(solution)/shard_map/all_to_all | solution.py:131
  49.9 3.0 %collective-permute-done.5 = f32[24,8,720]{2,1,0:T(8,128)} collective-permute-done((f32[24,8,720]{2,1,0:T(8,128)}, f32[24,8,720]{2,1,0:T(8,128)}, u32[]{:S(2)}, u32[]{:S(2)}) %collective-permute-start.5) | collective-permute-done | bytes 552992 | tf_op jit(solution)/shard_map/ppermute | solution.py:129
  52.9 2.0 %slice_select_fusion.2 = f32[24,8,720]{2,1,0:T(8,128)} fusion(f32[24,8,720]{2,1,0:T(8,128)} %collective-permute-done.5, f32[40,8,720]{2,1,0:T(8,128)S(1)} %get-tuple-element.7, pred[8]{0:T(512)(128)(4,1)S(1)} %slice_select_fusion.4), kind=kLoop, calls=%fused_computation.40 | loop fusion | flops 138240 | bytes 1658888 | tf_op jit(solution)/shard_map/jit(_where)/select_n | solution.py:130
  55.0 5.8 %all-to-all-done = f32[8,16,720]{2,1,0:T(8,128)S(1)} async-done(((f32[8,16,720]{2,1,0:T(8,128)}), f32[8,16,720]{2,1,0:T(8,128)S(1)}, u32[]{:S(2)}, u32[]{:S(2)}) %all-to-all-start) | async-done | bytes 368672 | tf_op jit(solution)/shard_map/all_to_all | solution.py:131
  60.8 3.7 %all-to-all-start.2 = ((f32[8,24,720]{2,1,0:T(8,128)}), f32[8,24,720]{2,1,0:T(8,128)S(1)}, u32[]{:S(2)}, u32[]{:S(2)}) async-start(f32[8,24,720]{2,1,0:T(8,128)} %bitcast.24), calls=%async_computation.2 | async-start | bytes 1179648 | tf_op jit(solution)/shard_map/all_to_all | solution.py:131
  64.5 1.0 copy.111
  65.5 1.2 reshape.332
  71.8 9.2 %all-to-all-done.2 = f32[8,24,720]{2,1,0:T(8,128)S(1)} async-done(((f32[8,24,720]{2,1,0:T(8,128)}), f32[8,24,720]{2,1,0:T(8,128)S(1)}, u32[]{:S(2)}, u32[]{:S(2)}) %all-to-all-start.2) | async-done | bytes 552992 | tf_op jit(solution)/shard_map/all_to_all | solution.py:131
  89.7 1.0 copy.114
  90.7 3.5 %all-to-all-start.3 = ((f32[24,8,720]{2,0,1:T(8,128)}), f32[24,8,720]{2,0,1:T(8,128)S(1)}, u32[]{:S(2)}, u32[]{:S(2)}) async-start(f32[24,8,720]{2,0,1:T(8,128)} %copy.114), calls=%async_computation.3 | async-start | bytes 1179648 | tf_op jit(solution)/shard_map/all_to_all | solution.py:139
  94.3 1.6 %fusion.72 = f32[16,45,128]{2,1,0:T(8,128)S(1)} fusion(f32[16,45,128]{2,1,0:T(8,128)} %copy-done.12), kind=kOutput, calls=%fused_computation.115 | convolution fusion | flops 71008256 | bytes 737280 | tf_op jit(solution)/shard_map/ljk,kn->ljn/dot_general | solution.py:49
  98.6 12.4 %all-to-all-done.3 = f32[24,8,720]{2,0,1:T(8,128)S(1)} async-done(((f32[24,8,720]{2,0,1:T(8,128)}), f32[24,8,720]{2,0,1:T(8,128)S(1)}, u32[]{:S(2)}, u32[]{:S(2)}) %all-to-all-start.3) | async-done | bytes 552992 | tf_op jit(solution)/shard_map/all_to_all | solution.py:139
  110.9 3.5 %all-to-all-start.1 = ((f32[16,8,720]{2,0,1:T(8,128)}), f32[16,8,720]{2,0,1:T(8,128)S(1)}, u32[]{:S(2)}, u32[]{:S(2)}) async-start(f32[16,8,720]{2,0,1:T(8,128)} %copy.112), calls=%async_computation.1 | async-start | bytes 786432 | tf_op jit(solution)/shard_map/all_to_all | solution.py:139
  114.4 2.1 %collective-permute-start.7 = (f32[24,8,720]{2,1,0:T(8,128)S(1)}, f32[24,8,720]{2,1,0:T(8,128)S(1)}, u32[]{:S(2)}, u32[]{:S(2)}) collective-permute-start(f32[24,8,720]{2,1,0:T(8,128)S(1)} %bitcast.135), channel_id=1, source_target_pairs={{0,16},{8,24},{16,0},{24,8},{1,17},{9,25},{17,1},{25,9},{2,18},{10... | collective-permute-start | bytes 1658888 | tf_op jit(solution)/shard_map/ppermute | solution.py:143
  116.5 10.4 %all-to-all-done.1 = f32[16,8,720]{2,0,1:T(8,128)S(1)} async-done(((f32[16,8,720]{2,0,1:T(8,128)}), f32[16,8,720]{2,0,1:T(8,128)S(1)}, u32[]{:S(2)}, u32[]{:S(2)}) %all-to-all-start.1) | async-done | bytes 368672 | tf_op jit(solution)/shard_map/all_to_all | solution.py:139
  126.9 2.0 %collective-permute-start.6 = (f32[16,8,720]{2,1,0:T(8,128)S(1)}, f32[16,8,720]{2,1,0:T(8,128)S(1)}, u32[]{:S(2)}, u32[]{:S(2)}) collective-permute-start(f32[16,8,720]{2,1,0:T(8,128)S(1)} %bitcast.139), channel_id=1, source_target_pairs={{0,16},{8,24},{16,0},{24,8},{1,17},{9,25},{17,1},{25,9},{2,18},{10... | collective-permute-start | bytes 1105928 | tf_op jit(solution)/shard_map/ppermute | solution.py:143
  128.9 9.8 %collective-permute-done.6 = f32[16,8,720]{2,1,0:T(8,128)S(1)} collective-permute-done((f32[16,8,720]{2,1,0:T(8,128)S(1)}, f32[16,8,720]{2,1,0:T(8,128)S(1)}, u32[]{:S(2)}, u32[]{:S(2)}) %collective-permute-start.6) | collective-permute-done | bytes 368672 | tf_op jit(solution)/shard_map/ppermute | solution.py:143
  138.8 1.9 %fusion.3 = f32[5,8,16,720]{3,2,1,0:T(8,128)} fusion(f32[5,8,16,720]{3,2,1,0:T(8,128)S(1)} %copy-done, f32[5,8,16,720]{3,2,1,0:T(8,128)S(1)} %copy-done.2, f32[5,8,8,720]{3,2,1,0:T(8,128)S(1)} %bitcast.133, f32[5,8,8,720]{3,2,1,0:T(8,128)S(1)} %bitcast.132, pred[16]{0:T(512)(128)(4,1)S(1)} %compare_reduce_fusion, pred[]{:T(512)S(6)} %lt.139), kind=kLoop, calls=%fused_computation.12 | loop fusion | flops 2304000 | bytes 7372817 | tf_op jit(solution)/shard_map/add | solution.py:152
  (121 shorter events, 24.2 us)
Async XLA Ops:
  0.0 14.7 %copy-start = (f32[5,8,16,720]{3,2,1,0:T(8,128)S(1)}, f32[5,8,16,720]{3,2,1,0:T(8,128)}, u32[]{:S(2)}) copy-start(f32[5,8,16,720]{3,2,1,0:T(8,128)} %param.5) | copy-start | bytes 5529604
  0.0 14.1 %copy-start.13 = (f32[8,16,720]{2,1,0:T(8,128)S(1)}, f32[8,16,720]{2,1,0:T(8,128)}, u32[]{:S(2)}) copy-start(f32[8,16,720]{2,1,0:T(8,128)} %param.6) | copy-start | bytes 1105924
  1.8 20.5 %collective-permute-start.3 = (f32[40,720]{1,0:T(8,128)S(1)}, f32[40,720]{1,0:T(8,128)}, u32[]{:S(2)}, u32[]{:S(2)}) collective-permute-start(f32[40,720]{1,0:T(8,128)S(1)} %bitcast.142), channel_id=1, source_target_pairs={{8,0},{16,8},{24,16},{9,1},{17,9},{25,17},{10,2},{18,10},{26,18},{... | collective-permute-start | bytes 345608 | tf_op jit(solution)/shard_map/ppermute | solution.py:82
  4.1 22.5 %collective-permute-start.2 = (f32[48,720]{1,0:T(8,128)S(1)}, f32[48,720]{1,0:T(8,128)S(1)}, u32[]{:S(2)}, u32[]{:S(2)}) collective-permute-start(f32[48,720]{1,0:T(8,128)S(1)} %pad_maximum_fusion.7), channel_id=1, source_target_pairs={{0,8},{8,16},{16,24},{1,9},{9,17},{17,25},{2,10},{10,18},{18,26},{... | collective-permute-start | bytes 414728 | tf_op jit(solution)/shard_map/ppermute | solution.py:79
  11.1 5.8 %collective-permute-start.1 = (f32[40,16]{0,1:T(8,128)S(1)}, f32[40,16]{0,1:T(8,128)S(1)}, u32[]{:S(2)}, u32[]{:S(2)}) collective-permute-start(f32[40,16]{0,1:T(8,128)S(1)} %bitcast.149), channel_id=1, source_target_pairs={{1,0},{2,1},{3,2},{4,3},{5,4},{6,5},{7,6},{0,7},{9,8},{10,9},{11,1... | collective-permute-start | bytes 7688 | tf_op jit(solution)/shard_map/ppermute | solution.py:78
  14.6 1.6 %copy-start.19 = (s32[32]{0:T(128)S(1)}, s32[32]{0:T(128)}, u32[]{:S(2)}) copy-start(s32[32]{0:T(128)} %param.8) | copy-start | bytes 388
  14.6 1.9 %copy-start.20 = (s32[32]{0:T(128)S(1)}, s32[32]{0:T(128)}, u32[]{:S(2)}) copy-start(s32[32]{0:T(128)} %param.9) | copy-start | bytes 388
  14.6 4.9 %collective-permute-start = (f32[48,16]{0,1:T(8,128)S(1)}, f32[48,16]{0,1:T(8,128)S(1)}, u32[]{:S(2)}, u32[]{:S(2)}) collective-permute-start(f32[48,16]{0,1:T(8,128)S(1)} %pad_maximum_fusion.8), channel_id=1, source_target_pairs={{0,1},{1,2},{2,3},{3,4},{4,5},{5,6},{6,7},{7,0},{8,9},{9,10},{10,1... | collective-permute-start | bytes 9224 | tf_op jit(solution)/shard_map/ppermute | solution.py:75
  20.4 6.4 %copy-start.14 = (f32[8,16,720]{2,1,0:T(8,128)S(1)}, f32[8,16,720]{2,1,0:T(8,128)}, u32[]{:S(2)}) copy-start(f32[8,16,720]{2,1,0:T(8,128)} %param.7) | copy-start | bytes 1105924
  26.9 2.9 %copy-start.3 = (f32[5,8,16,721]{3,2,1,0:T(8,128)S(1)}, f32[5,8,16,721]{3,2,1,0:T(8,128)}, u32[]{:S(2)}) copy-start(f32[5,8,16,721]{3,2,1,0:T(8,128)} %multiply_subtract_fusion) | copy-start | bytes 5537284
  30.4 1.3 copy-start.1
  31.7 12.3 %collective-permute-start.4 = (f32[16,8,720]{2,1,0:T(8,128)S(1)}, f32[16,8,720]{2,1,0:T(8,128)S(1)}, u32[]{:S(2)}, u32[]{:S(2)}) collective-permute-start(f32[16,8,720]{2,1,0:T(8,128)S(1)} %slice.123), channel_id=1, source_target_pairs={{0,16},{8,24},{16,0},{24,8},{1,17},{9,25},{17,1},{25,9},{2,18},{10... | collective-permute-start | bytes 1105928 | tf_op jit(solution)/shard_map/ppermute | solution.py:129
  34.0 35.8 %copy-start.15 = (f32[45,128]{1,0:T(8,128)}, f32[45,128]{1,0:T(8,128)S(1)}, u32[]{:S(2)}) copy-start(f32[45,128]{1,0:T(8,128)S(1)} %broadcast_maximum_fusion) | copy-start | bytes 69124
  34.9 18.0 %collective-permute-start.5 = (f32[24,8,720]{2,1,0:T(8,128)}, f32[24,8,720]{2,1,0:T(8,128)}, u32[]{:S(2)}, u32[]{:S(2)}) collective-permute-start(f32[24,8,720]{2,1,0:T(8,128)} %slice.125), channel_id=1, source_target_pairs={{0,16},{8,24},{16,0},{24,8},{1,17},{9,25},{17,1},{25,9},{2,18},{10... | collective-permute-start | bytes 1658888 | tf_op jit(solution)/shard_map/ppermute | solution.py:129
  44.8 15.9 %all-to-all-start = ((f32[8,16,720]{2,1,0:T(8,128)}), f32[8,16,720]{2,1,0:T(8,128)S(1)}, u32[]{:S(2)}, u32[]{:S(2)}) async-start(f32[8,16,720]{2,1,0:T(8,128)} %bitcast.138), calls=%async_computation | async-start | bytes 786432 | tf_op jit(solution)/shard_map/all_to_all | solution.py:131
  49.8 20.1 %copy-start.4 = (f32[45,128]{1,0:T(8,128)}, f32[45,128]{1,0:T(8,128)S(1)}, u32[]{:S(2)}) copy-start(f32[45,128]{1,0:T(8,128)S(1)} %get-tuple-element.17) | copy-start | bytes 69124
  49.8 20.1 %copy-start.7 = (f32[45,128]{1,0:T(8,128)}, f32[45,128]{1,0:T(8,128)S(1)}, u32[]{:S(2)}) copy-start(f32[45,128]{1,0:T(8,128)S(1)} %get-tuple-element.18) | copy-start | bytes 69124
  49.9 20.0 %copy-start.17 = (f32[45,128]{1,0:T(8,128)}, f32[45,128]{1,0:T(8,128)S(1)}, u32[]{:S(2)}) copy-start(f32[45,128]{1,0:T(8,128)S(1)} %fusion.100) | copy-start | bytes 69124
  60.8 20.2 %all-to-all-start.2 = ((f32[8,24,720]{2,1,0:T(8,128)}), f32[8,24,720]{2,1,0:T(8,128)S(1)}, u32[]{:S(2)}, u32[]{:S(2)}) async-start(f32[8,24,720]{2,1,0:T(8,128)} %bitcast.24), calls=%async_computation.2 | async-start | bytes 1179648 | tf_op jit(solution)/shard_map/all_to_all | solution.py:131
  68.7 1.8 %copy-start.10 = (f32[16,45,128]{2,1,0:T(8,128)}, f32[16,45,128]{2,1,0:T(8,128)S(1)}, u32[]{:S(2)}) copy-start(f32[16,45,128]{2,1,0:T(8,128)S(1)} %fusion.9) | copy-start | bytes 1105924
  81.6 1.0 copy-start.5
  81.6 1.0 copy-start.8
  82.6 1.3 copy-start.16
  82.6 1.3 copy-start.18
  89.7 6.1 %copy-start.11 = (f32[16,45,128]{2,1,0:T(8,128)S(1)}, f32[16,45,128]{2,1,0:T(8,128)}, u32[]{:S(2)}) copy-start(f32[16,45,128]{2,1,0:T(8,128)} %copy-done.10) | copy-start | bytes 1105924
  89.7 6.7 %copy-start.6 = (f32[45,128]{1,0:T(8,128)S(1)}, f32[45,128]{1,0:T(8,128)}, u32[]{:S(2)}) copy-start(f32[45,128]{1,0:T(8,128)} %copy-done.4) | copy-start | bytes 69124
  89.7 6.7 %copy-start.9 = (f32[45,128]{1,0:T(8,128)S(1)}, f32[45,128]{1,0:T(8,128)}, u32[]{:S(2)}) copy-start(f32[45,128]{1,0:T(8,128)} %copy-done.7) | copy-start | bytes 69124
  90.7 20.2 %all-to-all-start.3 = ((f32[24,8,720]{2,0,1:T(8,128)}), f32[24,8,720]{2,0,1:T(8,128)S(1)}, u32[]{:S(2)}, u32[]{:S(2)}) async-start(f32[24,8,720]{2,0,1:T(8,128)} %copy.114), calls=%async_computation.3 | async-start | bytes 1179648 | tf_op jit(solution)/shard_map/all_to_all | solution.py:139
  110.9 15.9 %all-to-all-start.1 = ((f32[16,8,720]{2,0,1:T(8,128)}), f32[16,8,720]{2,0,1:T(8,128)S(1)}, u32[]{:S(2)}, u32[]{:S(2)}) async-start(f32[16,8,720]{2,0,1:T(8,128)} %copy.112), calls=%async_computation.1 | async-start | bytes 786432 | tf_op jit(solution)/shard_map/all_to_all | solution.py:139
  114.4 24.3 %collective-permute-start.7 = (f32[24,8,720]{2,1,0:T(8,128)S(1)}, f32[24,8,720]{2,1,0:T(8,128)S(1)}, u32[]{:S(2)}, u32[]{:S(2)}) collective-permute-start(f32[24,8,720]{2,1,0:T(8,128)S(1)} %bitcast.135), channel_id=1, source_target_pairs={{0,16},{8,24},{16,0},{24,8},{1,17},{9,25},{17,1},{25,9},{2,18},{10... | collective-permute-start | bytes 1658888 | tf_op jit(solution)/shard_map/ppermute | solution.py:143
  126.9 11.9 %copy-start.2 = (f32[5,8,16,720]{3,2,1,0:T(8,128)S(1)}, f32[5,8,16,720]{3,2,1,0:T(8,128)}, u32[]{:S(2)}) copy-start(f32[5,8,16,720]{3,2,1,0:T(8,128)} %copy-done.1) | copy-start | bytes 5529604
  126.9 11.8 %collective-permute-start.6 = (f32[16,8,720]{2,1,0:T(8,128)S(1)}, f32[16,8,720]{2,1,0:T(8,128)S(1)}, u32[]{:S(2)}, u32[]{:S(2)}) collective-permute-start(f32[16,8,720]{2,1,0:T(8,128)S(1)} %bitcast.139), channel_id=1, source_target_pairs={{0,16},{8,24},{16,0},{24,8},{1,17},{9,25},{17,1},{25,9},{2,18},{10... | collective-permute-start | bytes 1105928 | tf_op jit(solution)/shard_map/ppermute | solution.py:143
  (1 other events, 0.7 us)

commit v5 on v3

--- a/solution.py
+++ b/solution.py
@@ -22,7 +22,7 @@
 def filter_lines(lines, line_cut):
     line_total, circle = lines.shape
     outer = circle // radix_len
-    mixer = partial(jnp.einsum, precision=lax.Precision.HIGHEST)
+    mixer = partial(jnp.einsum, precision=lax.Precision.HIGH)
     outer_cos, outer_sin = phase_table(outer, outer, outer)
     inner_cos, inner_sin = phase_table(radix_len, radix_len, radix_len)
     twist_cos, twist_sin = phase_table(outer, radix_len, circle)
@@ -83,21 +83,39 @@
     tile_index = lax.axis_index("lat")
     column = jnp.arange(columns, dtype=jnp.int32)
     row = jnp.arange(rows_dev, dtype=jnp.int32)[:, None]
+    local_right = jnp.concatenate([fields[..., 1:], jnp.zeros_like(fields[..., :1])], axis=3)
+    local_east = face_flux(lon_courant, fields, local_right)
+    local_west = jnp.concatenate([jnp.zeros_like(local_east[..., :1]), local_east[..., :-1]], axis=3)
+    local_upper = jnp.concatenate([fields[:, :, 1:], jnp.zeros_like(fields[:, :, :1])], axis=2)
+    top_face = (tile_index == lat_devices - 1) & (row == rows_dev - 1)
+    local_north = jnp.where(top_face, 0.0, face_flux(lat_courant, fields, local_upper))
+    local_south = jnp.concatenate(
+        [jnp.zeros_like(local_north[:, :, :1]), local_north[:, :, :-1]], axis=2
+    )
+    local_increment = -(local_east - local_west) - (local_north - local_south)
     west_fields = from_west[:stacked].reshape(field_count, level_count, rows_dev)
     east_fields = from_east.reshape(field_count, level_count, rows_dev)
-    right = jnp.where(column == columns - 1, east_fields[..., None], jnp.roll(fields, -1, axis=3))
-    east_flux = face_flux(lon_courant, fields, right)
     west_edge = face_flux(from_west[stacked:], west_fields, fields[..., 0])
-    west_flux = jnp.where(column == 0, west_edge[..., None], jnp.roll(east_flux, 1, axis=3))
+    east_change = face_flux(
+        lon_courant[..., -1], fields[..., -1], east_fields
+    ) - face_flux(lon_courant[..., -1], fields[..., -1], 0.0)
     below_fields = from_below[:stacked].reshape(field_count, level_count, columns)
     above_fields = from_above.reshape(field_count, level_count, columns)
-    upper = jnp.where(row == rows_dev - 1, above_fields[:, :, None], jnp.roll(fields, -1, axis=2))
-    north_flux = face_flux(lat_courant, fields, upper)
-    top_face = (tile_index == lat_devices - 1) & (row == rows_dev - 1)
-    north_flux = jnp.where(top_face, 0.0, north_flux)
     south_edge = face_flux(from_below[stacked:], below_fields, fields[:, :, 0])
-    south_flux = jnp.where(row == 0, south_edge[:, :, None], jnp.roll(north_flux, 1, axis=2))
-    increment = -(east_flux - west_flux) - (north_flux - south_flux)
+    top_tile = tile_index == lat_devices - 1
+    north_change = jnp.where(
+        top_tile,
+        0.0,
+        face_flux(lat_courant[:, -1], fields[:, :, -1], above_fields)
+        - face_flux(lat_courant[:, -1], fields[:, :, -1], 0.0),
+    )
+    edge_change = (
+        jnp.where(column == 0, west_edge[..., None], 0.0)
+        - jnp.where(column == columns - 1, east_change[..., None], 0.0)
+        + jnp.where(row == 0, south_edge[:, :, None], 0.0)
+        - jnp.where(row == rows_dev - 1, north_change[:, :, None], 0.0)
+    )
+    increment = local_increment + edge_change
     flat_increment = increment.reshape(stacked, rows_dev, columns)
     half_rows = rows_dev // 2
     pair_shift = lat_devices // 2

time: 149 us -> 161 us (1.081)
  other arithmetic: 18.7 us -> 28 us
  local copies, waits for them, and re-layouts: 20.3 us -> 26.5 us
  matrix products: 19.4 us -> 14.7 us
    add x0 -> x1, other arithmetic: none -> 4.8 us  [body(): increment = local_increment + edge_change]
    unnamed x49 -> x58, local copies, waits for them, and re-layouts: 3.04 us -> 6.55 us
    sub x1, other arithmetic: 1.43 us -> 4.94 us  [face_flux(): 0.5 * courant * (near_value + far_value)]
    select_n x1 -> x0, other arithmetic: 3.17 us -> none  [body(): north_flux = jnp.where(top_face, 0.0, north_flux)]
    all_to_all x2, waiting for transfers between devices: 12.4 us -> 14.4 us  [body(): lax.all_to_all(pair_lines.reshape(chunk_stack * half_rows, columns), 'lon...]
    ppermute x2, waiting for transfers between devices: 13.6 us -> 11.8 us  [body(): taken = lax.ppermute(given[rows_of_part], 'lat', pair_perm)]
    slice x6 -> x4, local copies, waits for them, and re-layouts: 4.37 us -> 5.19 us  [the longest x1 1.85 us: body(): fields[..., 1:]]
  transfers between devices with their start and end apart: 12 -> 12, of which waited for: 7 -> 7; matrix products, arithmetic and copies ran while one was open for 24% -> 27% of each run, Pallas kernels for 0% -> 0%
where the time goes in v5:
time: 161 us; the launch traced here: 160 us
  waiting for transfers between devices  59.5 us (37%)
  starting transfers between devices  30.4 us (19%)
  other arithmetic  28 us (17%)
  local copies, waits for them, and re-layouts  26.5 us (16%)
  matrix products  14.7 us (9%)
    all_to_all x2, waiting for transfers between devices, body(): lax.all_to_all(smoothed, 'lon', split_axis=1, concat_axis=0, tiled=True)  23.2 us
    all_to_all x2, waiting for transfers between devices, body(): lax.all_to_all(pair_lines.reshape(chunk_stack * half_rows, columns), 'lon...  14.4 us
    ppermute x2, waiting for transfers between devices, body(): taken = lax.ppermute(given[rows_of_part], 'lat', pair_perm)  11.8 us
    ppermute x2, waiting for transfers between devices, body(): handed_parts.append(lax.ppermute(returned, 'lat', pair_perm))  10 us
    all_to_all x2, starting transfers between devices, body(): lax.all_to_all(pair_lines.reshape(chunk_stack * half_rows, columns), 'lon...  7.76 us
    all_to_all x2, starting transfers between devices, body(): lax.all_to_all(smoothed, 'lon', split_axis=1, concat_axis=0, tiled=True)  6.99 us
    unnamed x58, local copies, waits for them, and re-layouts  6.55 us
    ppermute x1, starting transfers between devices, body(): lax.ppermute(jnp.concatenate([flat_fields[:, -1], lat_courant[:, -1]], ax...  6.12 us
  transfers between devices with their start and end apart: 12, of which 7 were waited for; matrix products, arithmetic and copies ran while one was open for 27% of the time, Pallas kernels for 0%

profile of v5, /device:TPU:0, one launch (start us, length us, event | category | flops | bytes accessed | tf_op | source)
XLA Modules:
  0.0 159.7 jit_solution(10648818765474786950)
XLA Ops:
  0.0 1.8 %fusion.258 = (f32[40,1,720]{2,1,0:T(1,128)S(1)}, f32[40,1,720]{2,1,0:T(1,128)S(1)}) fusion(f32[40,16,720]{2,1,0:T(8,128)} %bitcast.175), kind=kLoop, calls=%fused_computation.310 | loop fusion | bytes 460800 | tf_op jit(solution)/shard_map/slice | solution.py:80
  2.5 1.3 collective-permute-start.3
  6.0 6.1 %collective-permute-start.2 = (f32[48,720]{1,0:T(8,128)}, f32[48,720]{1,0:T(8,128)}, u32[]{:S(2)}, u32[]{:S(2)}) collective-permute-start(f32[48,720]{1,0:T(8,128)} %pad_maximum_fusion.2), channel_id=1, source_target_pairs={{0,8},{8,16},{16,24},{1,9},{9,17},{17,25},{2,10},{10,18},{18,26},{... | collective-permute-start | bytes 414728 | tf_op jit(solution)/shard_map/ppermute | solution.py:79
  12.1 1.2 fusion.255
  14.1 3.0 %collective-permute-start.1 = (f32[40,16]{0,1:T(8,128)}, f32[40,16]{0,1:T(8,128)}, u32[]{:S(2)}, u32[]{:S(2)}) collective-permute-start(f32[40,16]{0,1:T(8,128)} %bitcast.7), channel_id=1, source_target_pairs={{1,0},{2,1},{3,2},{4,3},{5,4},{6,5},{7,6},{0,7},{9,8},{10,9},{11,1... | collective-permute-start | bytes 7688 | tf_op jit(solution)/shard_map/ppermute | solution.py:78
  18.3 1.8 %slice.92 = f32[5,8,16,719]{3,2,1,0:T(8,128)} slice(f32[5,8,16,720]{3,2,1,0:T(8,128)S(1)} %copy-done), slice={[0:5], [0:8], [0:16], [1:720]} | slice | bytes 3681280 | tf_op jit(solution)/shard_map/slice | solution.py:86
  20.3 1.5 slice.94
  29.3 4.9 %multiply_subtract_fusion = (f32[5,8,16,720]{3,2,1,0:T(8,128)}, f32[5,8,16,720]{3,2,1,0:T(8,128)}) fusion(f32[5,8,16,720]{3,2,1,0:T(8,128)S(1)} %copy-done, f32[5,8,16,719]{3,2,1,0:T(8,128)} %slice.92, f32[8,16,720]{2,1,0:T(8,128)S(1)} %get-tuple-element.20, f32[8,16,720]{2,1,0:T(8,128)S(1)} %get-tuple-element.19, f32[8,16,720]{2,1,0:T(8,128)S(1)} %get-tuple-element.22, ...), kind=kLoop, calls=%fused_computation.7 | loop fusion | flops 5068800 | bytes 10572816 | tf_op jit(solution)/shard_map/sub | solution.py:60
  34.2 1.2 copy.142
  35.5 1.3 copy.141
  39.0 1.0 fusion.52
  41.8 4.8 %subtract_add_fusion = f32[5,8,16,720]{3,2,1,0:T(8,128)S(1)} fusion(f32[5,8,16,720]{3,2,1,0:T(8,128)} %get-tuple-element.18, f32[5,8,15,720]{3,2,1,0:T(8,128)} %bitcast.178, f32[5,8,16,720]{3,2,1,0:T(8,128)} %get-tuple-element.17, f32[5,8,16,719]{3,2,1,0:T(8,128)} %bitcast.177, f32[5,8,720]{2,1,0:T(8,128)S(1)} %fusion.52, ...), kind=kLoop, calls=%fused_computation.5 | loop fusion | flops 5529600 | bytes 9335232 | tf_op jit(solution)/shard_map/add | solution.py:118
  46.7 1.1 copy-done.1
  47.9 1.6 collective-permute-start.4
  51.5 8.5 %collective-permute-done.4 = f32[16,8,720]{2,1,0:T(8,128)S(1)} collective-permute-done((f32[16,8,720]{2,1,0:T(8,128)S(1)}, f32[16,8,720]{2,1,0:T(8,128)S(1)}, u32[]{:S(2)}, u32[]{:S(2)}) %collective-permute-start.4) | collective-permute-done | bytes 368672 | tf_op jit(solution)/shard_map/ppermute | solution.py:149
  60.9 4.0 %all-to-all-start = ((f32[8,16,720]{2,1,0:T(8,128)}), f32[8,16,720]{2,1,0:T(8,128)S(1)}, u32[]{:S(2)}, u32[]{:S(2)}) async-start(f32[8,16,720]{2,1,0:T(8,128)} %bitcast.187), calls=%async_computation | async-start | bytes 786432 | tf_op jit(solution)/shard_map/all_to_all | solution.py:151
  67.6 3.3 %collective-permute-done.5 = f32[24,8,720]{2,1,0:T(8,128)} collective-permute-done((f32[24,8,720]{2,1,0:T(8,128)}, f32[24,8,720]{2,1,0:T(8,128)}, u32[]{:S(2)}, u32[]{:S(2)}) %collective-permute-start.5) | collective-permute-done | bytes 552992 | tf_op jit(solution)/shard_map/ppermute | solution.py:149
  70.9 2.0 %slice_select_fusion.2 = f32[24,8,720]{2,1,0:T(8,128)} fusion(f32[24,8,720]{2,1,0:T(8,128)} %collective-permute-done.5, f32[40,8,720]{2,1,0:T(8,128)S(1)} %get-tuple-element.7, pred[8]{0:T(512)(128)(4,1)S(1)} %copy-done.23), kind=kLoop, calls=%fused_computation.34 | loop fusion | flops 138240 | bytes 1658888 | tf_op jit(solution)/shard_map/jit(_where)/select_n | solution.py:150
  72.9 4.5 %all-to-all-done = f32[8,16,720]{2,1,0:T(8,128)S(1)} async-done(((f32[8,16,720]{2,1,0:T(8,128)}), f32[8,16,720]{2,1,0:T(8,128)S(1)}, u32[]{:S(2)}, u32[]{:S(2)}) %all-to-all-start) | async-done | bytes 368672 | tf_op jit(solution)/shard_map/all_to_all | solution.py:151
  78.2 3.7 %all-to-all-start.2 = ((f32[8,24,720]{2,1,0:T(8,128)}), f32[8,24,720]{2,1,0:T(8,128)S(1)}, u32[]{:S(2)}, u32[]{:S(2)}) async-start(f32[8,24,720]{2,1,0:T(8,128)} %bitcast.185), calls=%async_computation.2 | async-start | bytes 1179648 | tf_op jit(solution)/shard_map/all_to_all | solution.py:151
  81.9 1.2 copy.133
  88.5 9.9 %all-to-all-done.2 = f32[8,24,720]{2,1,0:T(8,128)S(1)} async-done(((f32[8,24,720]{2,1,0:T(8,128)}), f32[8,24,720]{2,1,0:T(8,128)S(1)}, u32[]{:S(2)}, u32[]{:S(2)}) %all-to-all-start.2) | async-done | bytes 552992 | tf_op jit(solution)/shard_map/all_to_all | solution.py:151
  99.4 1.4 reshape.305
  110.0 3.5 %all-to-all-start.3 = ((f32[24,8,720]{2,0,1:T(8,128)}), f32[24,8,720]{2,0,1:T(8,128)S(1)}, u32[]{:S(2)}, u32[]{:S(2)}) async-start(f32[24,8,720]{2,0,1:T(8,128)} %copy.136), calls=%async_computation.3 | async-start | bytes 1179648 | tf_op jit(solution)/shard_map/all_to_all | solution.py:159
  113.6 1.6 fusion.74
  117.9 12.4 %all-to-all-done.3 = f32[24,8,720]{2,0,1:T(8,128)S(1)} async-done(((f32[24,8,720]{2,0,1:T(8,128)}), f32[24,8,720]{2,0,1:T(8,128)S(1)}, u32[]{:S(2)}, u32[]{:S(2)}) %all-to-all-start.3) | async-done | bytes 552992 | tf_op jit(solution)/shard_map/all_to_all | solution.py:159
  130.2 3.5 %all-to-all-start.1 = ((f32[16,8,720]{2,0,1:T(8,128)}), f32[16,8,720]{2,0,1:T(8,128)S(1)}, u32[]{:S(2)}, u32[]{:S(2)}) async-start(f32[16,8,720]{2,0,1:T(8,128)} %copy.134), calls=%async_computation.1 | async-start | bytes 786432 | tf_op jit(solution)/shard_map/all_to_all | solution.py:159
  133.7 1.6 collective-permute-start.7
  135.3 10.9 %all-to-all-done.1 = f32[16,8,720]{2,0,1:T(8,128)S(1)} async-done(((f32[16,8,720]{2,0,1:T(8,128)}), f32[16,8,720]{2,0,1:T(8,128)S(1)}, u32[]{:S(2)}, u32[]{:S(2)}) %all-to-all-start.1) | async-done | bytes 368672 | tf_op jit(solution)/shard_map/all_to_all | solution.py:159
  146.2 1.5 collective-permute-start.6
  147.8 10.0 %collective-permute-done.6 = f32[16,8,720]{2,1,0:T(8,128)S(1)} collective-permute-done((f32[16,8,720]{2,1,0:T(8,128)S(1)}, f32[16,8,720]{2,1,0:T(8,128)S(1)}, u32[]{:S(2)}, u32[]{:S(2)}) %collective-permute-start.6) | collective-permute-done | bytes 368672 | tf_op jit(solution)/shard_map/ppermute | solution.py:163
  157.8 1.9 %fusion.1 = f32[5,8,16,720]{3,2,1,0:T(8,128)} fusion(f32[5,8,16,720]{3,2,1,0:T(8,128)S(1)} %copy-done, f32[5,8,16,720]{3,2,1,0:T(8,128)S(1)} %copy-done.2, f32[5,8,8,720]{3,2,1,0:T(8,128)S(1)} %bitcast.181, f32[5,8,8,720]{3,2,1,0:T(8,128)S(1)} %bitcast.180, pred[16]{0:T(512)(128)(4,1)S(1)} %compare_reduce_fusion, pred[]{:T(512)S(6)} %lt.139), kind=kLoop, calls=%fused_computation.4 | loop fusion | flops 2304000 | bytes 7372817 | tf_op jit(solution)/shard_map/add | solution.py:172
  (135 shorter events, 40.8 us)
Async XLA Ops:
  0.0 18.3 %copy-start = (f32[5,8,16,720]{3,2,1,0:T(8,128)S(1)}, f32[5,8,16,720]{3,2,1,0:T(8,128)}, u32[]{:S(2)}) copy-start(f32[5,8,16,720]{3,2,1,0:T(8,128)} %param.5) | copy-start | bytes 5529604
  0.0 17.1 %copy-start.15 = (f32[8,16,720]{2,1,0:T(8,128)S(1)}, f32[8,16,720]{2,1,0:T(8,128)}, u32[]{:S(2)}) copy-start(f32[8,16,720]{2,1,0:T(8,128)} %param.6) | copy-start | bytes 1105924
  2.5 36.5 %collective-permute-start.3 = (f32[40,720]{1,0:T(8,128)}, f32[40,720]{1,0:T(8,128)}, u32[]{:S(2)}, u32[]{:S(2)}) collective-permute-start(f32[40,720]{1,0:T(8,128)} %bitcast.170), channel_id=1, source_target_pairs={{8,0},{16,8},{24,16},{9,1},{17,9},{25,17},{10,2},{18,10},{26,18},{... | collective-permute-start | bytes 345608 | tf_op jit(solution)/shard_map/ppermute | solution.py:82
  6.0 34.0 %collective-permute-start.2 = (f32[48,720]{1,0:T(8,128)}, f32[48,720]{1,0:T(8,128)}, u32[]{:S(2)}, u32[]{:S(2)}) collective-permute-start(f32[48,720]{1,0:T(8,128)} %pad_maximum_fusion.2), channel_id=1, source_target_pairs={{0,8},{8,16},{16,24},{1,9},{9,17},{17,25},{2,10},{10,18},{18,26},{... | collective-permute-start | bytes 414728 | tf_op jit(solution)/shard_map/ppermute | solution.py:79
  14.1 22.6 %collective-permute-start.1 = (f32[40,16]{0,1:T(8,128)}, f32[40,16]{0,1:T(8,128)}, u32[]{:S(2)}, u32[]{:S(2)}) collective-permute-start(f32[40,16]{0,1:T(8,128)} %bitcast.7), channel_id=1, source_target_pairs={{1,0},{2,1},{3,2},{4,3},{5,4},{6,5},{7,6},{0,7},{9,8},{10,9},{11,1... | collective-permute-start | bytes 7688 | tf_op jit(solution)/shard_map/ppermute | solution.py:78
  18.3 1.9 %copy-start.16 = (f32[8,16,720]{2,1,0:T(8,128)S(1)}, f32[8,16,720]{2,1,0:T(8,128)}, u32[]{:S(2)}) copy-start(f32[8,16,720]{2,1,0:T(8,128)} %param.7) | copy-start | bytes 1105924
  18.3 19.3 %collective-permute-start = (f32[48,16]{1,0:T(8,128)}, f32[48,16]{1,0:T(8,128)}, u32[]{:S(2)}, u32[]{:S(2)}) collective-permute-start(f32[48,16]{1,0:T(8,128)} %pad_maximum_fusion.3), channel_id=1, source_target_pairs={{0,1},{1,2},{2,3},{3,4},{4,5},{5,6},{6,7},{7,0},{8,9},{9,10},{10,1... | collective-permute-start | bytes 9224 | tf_op jit(solution)/shard_map/ppermute | solution.py:75
  20.3 2.4 %copy-start.18 = (f32[8,1,720]{2,1,0:T(1,128)S(1)}, f32[8,1,720]{2,1,0:T(1,128)}, u32[]{:S(2)}) copy-start(f32[8,1,720]{2,1,0:T(1,128)} %copy-done.17) | copy-start | bytes 69124
  20.3 6.7 %copy-start.25 = (s32[32]{0:T(128)S(1)}, s32[32]{0:T(128)}, u32[]{:S(2)}) copy-start(s32[32]{0:T(128)} %param.8) | copy-start | bytes 388
  46.6 1.3 copy-start.1
  46.6 2.9 %copy-start.24 = (s32[128]{0:T(128)S(1)}, s32[128]{0:T(128)}, u32[]{:S(2)}) copy-start(s32[128]{0:T(128)} %iota_multiply_fusion) | copy-start | bytes 1540
  47.8 12.2 %copy-start.23 = (pred[8]{0:T(512)(128)(4,1)S(1)}, pred[8]{0:T(512)(128)(4,1)}, u32[]{:S(2)}) copy-start(pred[8]{0:T(512)(128)(4,1)} %slice_select_fusion.4) | copy-start | bytes 28
  47.9 12.1 %collective-permute-start.4 = (f32[16,8,720]{2,1,0:T(8,128)S(1)}, f32[16,8,720]{2,1,0:T(8,128)S(1)}, u32[]{:S(2)}, u32[]{:S(2)}) collective-permute-start(f32[16,8,720]{2,1,0:T(8,128)S(1)} %slice.135), channel_id=1, source_target_pairs={{0,16},{8,24},{16,0},{24,8},{1,17},{9,25},{17,1},{25,9},{2,18},{10... | collective-permute-start | bytes 1105928 | tf_op jit(solution)/shard_map/ppermute | solution.py:149
  51.0 19.9 %collective-permute-start.5 = (f32[24,8,720]{2,1,0:T(8,128)}, f32[24,8,720]{2,1,0:T(8,128)}, u32[]{:S(2)}, u32[]{:S(2)}) collective-permute-start(f32[24,8,720]{2,1,0:T(8,128)} %slice.137), channel_id=1, source_target_pairs={{0,16},{8,24},{16,0},{24,8},{1,17},{9,25},{17,1},{25,9},{2,18},{10... | collective-permute-start | bytes 1658888 | tf_op jit(solution)/shard_map/ppermute | solution.py:149
  60.9 16.6 %all-to-all-start = ((f32[8,16,720]{2,1,0:T(8,128)}), f32[8,16,720]{2,1,0:T(8,128)S(1)}, u32[]{:S(2)}, u32[]{:S(2)}) async-start(f32[8,16,720]{2,1,0:T(8,128)} %bitcast.187), calls=%async_computation | async-start | bytes 786432 | tf_op jit(solution)/shard_map/all_to_all | solution.py:151
  77.5 6.8 %copy-start.3 = (f32[45,128]{1,0:T(8,128)S(1)}, f32[45,128]{1,0:T(8,128)}, u32[]{:S(2)}) copy-start(f32[45,128]{1,0:T(8,128)} %get-tuple-element.35) | copy-start | bytes 69124
  77.5 6.8 %copy-start.7 = (f32[45,128]{1,0:T(8,128)S(1)}, f32[45,128]{1,0:T(8,128)}, u32[]{:S(2)}) copy-start(f32[45,128]{1,0:T(8,128)} %get-tuple-element.36) | copy-start | bytes 69124
  78.2 20.2 %all-to-all-start.2 = ((f32[8,24,720]{2,1,0:T(8,128)}), f32[8,24,720]{2,1,0:T(8,128)S(1)}, u32[]{:S(2)}, u32[]{:S(2)}) async-start(f32[8,24,720]{2,1,0:T(8,128)} %bitcast.185), calls=%async_computation.2 | async-start | bytes 1179648 | tf_op jit(solution)/shard_map/all_to_all | solution.py:151
  83.2 1.7 %copy-start.19 = (f32[45,128]{1,0:T(8,128)S(1)}, f32[45,128]{1,0:T(8,128)}, u32[]{:S(2)}) copy-start(f32[45,128]{1,0:T(8,128)} %broadcast_maximum_fusion) | copy-start | bytes 69124
  83.2 1.7 %copy-start.21 = (f32[45,128]{1,0:T(8,128)S(1)}, f32[45,128]{1,0:T(8,128)}, u32[]{:S(2)}) copy-start(f32[45,128]{1,0:T(8,128)} %fusion.102) | copy-start | bytes 69124
  99.4 2.5 %copy-start.4 = (f32[45,128]{1,0:T(8,128)S(1)}, f32[45,128]{1,0:T(8,128)}, u32[]{:S(2)}) copy-start(f32[45,128]{1,0:T(8,128)} %get-tuple-element.35) | copy-start | bytes 69124
  99.4 2.5 %copy-start.8 = (f32[45,128]{1,0:T(8,128)S(1)}, f32[45,128]{1,0:T(8,128)}, u32[]{:S(2)}) copy-start(f32[45,128]{1,0:T(8,128)} %get-tuple-element.36) | copy-start | bytes 69124
  101.9 1.3 copy-start.20
  101.9 1.3 copy-start.22
  109.0 6.1 %copy-start.13 = (f32[16,45,128]{2,1,0:T(8,128)S(1)}, f32[16,45,128]{2,1,0:T(8,128)}, u32[]{:S(2)}) copy-start(f32[16,45,128]{2,1,0:T(8,128)} %copy-done.12) | copy-start | bytes 1105924
  109.0 6.7 %copy-start.6 = (f32[45,128]{1,0:T(8,128)S(1)}, f32[45,128]{1,0:T(8,128)}, u32[]{:S(2)}) copy-start(f32[45,128]{1,0:T(8,128)} %get-tuple-element.35) | copy-start | bytes 69124
  109.0 6.7 %copy-start.10 = (f32[45,128]{1,0:T(8,128)S(1)}, f32[45,128]{1,0:T(8,128)}, u32[]{:S(2)}) copy-start(f32[45,128]{1,0:T(8,128)} %get-tuple-element.36) | copy-start | bytes 69124
  110.0 20.2 %all-to-all-start.3 = ((f32[24,8,720]{2,0,1:T(8,128)}), f32[24,8,720]{2,0,1:T(8,128)S(1)}, u32[]{:S(2)}, u32[]{:S(2)}) async-start(f32[24,8,720]{2,0,1:T(8,128)} %copy.136), calls=%async_computation.3 | async-start | bytes 1179648 | tf_op jit(solution)/shard_map/all_to_all | solution.py:159
  130.2 15.9 %all-to-all-start.1 = ((f32[16,8,720]{2,0,1:T(8,128)}), f32[16,8,720]{2,0,1:T(8,128)S(1)}, u32[]{:S(2)}, u32[]{:S(2)}) async-start(f32[16,8,720]{2,0,1:T(8,128)} %copy.134), calls=%async_computation.1 | async-start | bytes 786432 | tf_op jit(solution)/shard_map/all_to_all | solution.py:159
  133.7 24.1 %collective-permute-start.7 = (f32[24,8,720]{2,1,0:T(8,128)S(1)}, f32[24,8,720]{2,1,0:T(8,128)S(1)}, u32[]{:S(2)}, u32[]{:S(2)}) collective-permute-start(f32[24,8,720]{2,1,0:T(8,128)S(1)} %bitcast.183), channel_id=1, source_target_pairs={{0,16},{8,24},{16,0},{24,8},{1,17},{9,25},{17,1},{25,9},{2,18},{10... | collective-permute-start | bytes 1658888 | tf_op jit(solution)/shard_map/ppermute | solution.py:163
  146.2 11.7 %copy-start.2 = (f32[5,8,16,720]{3,2,1,0:T(8,128)S(1)}, f32[5,8,16,720]{3,2,1,0:T(8,128)}, u32[]{:S(2)}) copy-start(f32[5,8,16,720]{3,2,1,0:T(8,128)} %copy-done.1) | copy-start | bytes 5529604
  146.2 11.6 %collective-permute-start.6 = (f32[16,8,720]{2,1,0:T(8,128)S(1)}, f32[16,8,720]{2,1,0:T(8,128)S(1)}, u32[]{:S(2)}, u32[]{:S(2)}) collective-permute-start(f32[16,8,720]{2,1,0:T(8,128)S(1)} %bitcast.188), channel_id=1, source_target_pairs={{0,16},{8,24},{16,0},{24,8},{1,17},{9,25},{17,1},{25,9},{2,18},{10... | collective-permute-start | bytes 1105928 | tf_op jit(solution)/shard_map/ppermute | solution.py:163
  (6 other events, 5.6 us)

commit v6 on v4

--- a/solution.py
+++ b/solution.py
@@ -26,17 +26,30 @@
     outer_cos, outer_sin = phase_table(outer, outer, outer)
     inner_cos, inner_sin = phase_table(radix_len, radix_len, radix_len)
     twist_cos, twist_sin = phase_table(outer, radix_len, circle)
+    forward_outer = jnp.concatenate([outer_cos, -outer_sin], axis=1)
+    forward_inner = jnp.concatenate(
+        [
+            jnp.concatenate([inner_cos, -inner_sin], axis=1),
+            jnp.concatenate([inner_sin, inner_cos], axis=1),
+        ],
+        axis=0,
+    )
+    inverse_inner = jnp.concatenate(
+        [
+            jnp.concatenate([inner_cos, inner_sin], axis=1),
+            jnp.concatenate([-inner_sin, inner_cos], axis=1),
+        ],
+        axis=0,
+    )
+    inverse_outer = jnp.concatenate([outer_cos, -outer_sin], axis=0)
     values = lines.reshape(line_total, outer, radix_len)
-    first_re = mixer("lan,aj->ljn", values, outer_cos)
-    first_im = -mixer("lan,aj->ljn", values, outer_sin)
-    turned_re = first_re * twist_cos + first_im * twist_sin
-    turned_im = first_im * twist_cos - first_re * twist_sin
-    spec_re = mixer("ljn,nk->ljk", turned_re, inner_cos) + mixer(
-        "ljn,nk->ljk", turned_im, inner_sin
+    first = mixer("lan,ab->lbn", values, forward_outer)
+    first_re, first_im = first[:, :outer], first[:, outer:]
+    turned = jnp.concatenate(
+        [first_re * twist_cos + first_im * twist_sin, first_im * twist_cos - first_re * twist_sin],
+        axis=2,
     )
-    spec_im = mixer("ljn,nk->ljk", turned_im, inner_cos) - mixer(
-        "ljn,nk->ljk", turned_re, inner_sin
-    )
+    spectrum = mixer("ljn,nk->ljk", turned, forward_inner)
     wave = (
         jnp.arange(outer, dtype=jnp.int32)[:, None]
         + outer * jnp.arange(radix_len, dtype=jnp.int32)[None, :]
@@ -44,15 +57,14 @@
     mode_value = jnp.minimum(wave, circle - wave).astype(jnp.float32)[None]
     cut_value = line_cut[:, None, None]
     damp = jnp.where(mode_value <= cut_value, 1.0, (cut_value / jnp.maximum(mode_value, 1.0)) ** 2)
-    spec_re = spec_re * damp
-    spec_im = spec_im * damp
-    back_re = mixer("ljk,kn->ljn", spec_re, inner_cos) - mixer("ljk,kn->ljn", spec_im, inner_sin)
-    back_im = mixer("ljk,kn->ljn", spec_im, inner_cos) + mixer("ljk,kn->ljn", spec_re, inner_sin)
-    untwist_re = back_re * twist_cos - back_im * twist_sin
-    untwist_im = back_im * twist_cos + back_re * twist_sin
-    result = mixer("ljn,ja->lan", untwist_re, outer_cos) - mixer(
-        "ljn,ja->lan", untwist_im, outer_sin
+    spectrum = spectrum * jnp.concatenate([damp, damp], axis=2)
+    back = mixer("ljk,kn->ljn", spectrum, inverse_inner)
+    back_re, back_im = back[..., :radix_len], back[..., radix_len:]
+    untwisted = jnp.concatenate(
+        [back_re * twist_cos - back_im * twist_sin, back_im * twist_cos + back_re * twist_sin],
+        axis=1,
     )
+    result = mixer("lbn,ba->lan", untwisted, inverse_outer)
     return (result / circle).reshape(line_total, circle)
 
 

time: 141 us -> 147 us (1.043)
  other arithmetic: 11.6 us -> 22.5 us
  matrix products: 14.7 us -> 7.36 us
  local copies, waits for them, and re-layouts: 21.4 us -> 24.7 us
  waiting for transfers between devices: 62 us -> 59.8 us
    dot_general x24 -> x8, matrix products: 14.7 us -> 7.36 us  [the longest x2 3.17 us: filter_lines(): first = mixer('lan,ab->lbn', values, forward_outer)]
    all_to_all x4, local copies, waits for them, and re-layouts: 2.69 us -> 4.64 us  [body(): lax.all_to_all(smoothed, 'lon', split_axis=1, concat_axis=0, tiled=True)]
    select_n x0 -> x2, other arithmetic: none -> 1.87 us  [filter_lines(): jnp.where(mode_value <= cut_value, 1.0, (cut_value / jnp.maximum(mode_val...]
    add x0 -> x2, other arithmetic: none -> 1.79 us  [filter_lines(): first_re * twist_cos + first_im * twist_sin]
    unnamed x46 -> x42, local copies, waits for them, and re-layouts: 3.51 us -> 2.18 us
  transfers between devices with their start and end apart: 12 -> 12, of which waited for: 8 -> 8; matrix products, arithmetic and copies ran while one was open for 20% -> 22% of each run, Pallas kernels for 0% -> 0%
where the time goes in v6:
time: 147 us; the launch traced here: 146 us
  waiting for transfers between devices  59.8 us (41%)
  starting transfers between devices  30.9 us (21%)
  local copies, waits for them, and re-layouts  24.7 us (17%)
  other arithmetic  22.5 us (15%)
  matrix products  7.36 us (5%)
    all_to_all x2, waiting for transfers between devices, body(): lax.all_to_all(smoothed, 'lon', split_axis=1, concat_axis=0, tiled=True)  22.2 us
    all_to_all x2, waiting for transfers between devices, body(): lax.all_to_all(pair_lines.reshape(chunk_stack * half_rows, columns), 'lon...  15.1 us
    ppermute x2, waiting for transfers between devices, body(): taken = lax.ppermute(given[rows_of_part], 'lat', pair_perm)  11.7 us
    ppermute x2, waiting for transfers between devices, body(): handed_parts.append(lax.ppermute(returned, 'lat', pair_perm))  9.78 us
    all_to_all x2, starting transfers between devices, body(): lax.all_to_all(pair_lines.reshape(chunk_stack * half_rows, columns), 'lon...  7.82 us
    all_to_all x2, starting transfers between devices, body(): lax.all_to_all(smoothed, 'lon', split_axis=1, concat_axis=0, tiled=True)  6.99 us
    ppermute x1, starting transfers between devices, body(): lax.ppermute(jnp.concatenate([flat_fields[:, -1], lat_courant[:, -1]], ax...  5.48 us
    all_to_all x4, local copies, waits for them, and re-layouts, body(): lax.all_to_all(smoothed, 'lon', split_axis=1, concat_axis=0, tiled=True)  4.64 us
  transfers between devices with their start and end apart: 12, of which 8 were waited for; matrix products, arithmetic and copies ran while one was open for 22% of the time, Pallas kernels for 0%

profile of v6, /device:TPU:0, one launch (start us, length us, event | category | flops | bytes accessed | tf_op | source)
XLA Modules:
  0.0 145.7 jit_solution(14197794721795969585)
XLA Ops:
  0.0 1.8 %fusion.71 = (f32[40,1,720]{2,1,0:T(1,128)S(1)}, f32[40,1,720]{2,1,0:T(1,128)S(1)}) fusion(f32[40,16,720]{2,1,0:T(8,128)} %bitcast.70), kind=kLoop, calls=%fused_computation.146 | loop fusion | bytes 460800 | tf_op jit(solution)/shard_map/slice | solution.py:92
  1.8 1.3 collective-permute-start.3
  4.1 5.5 %collective-permute-start.2 = (f32[48,720]{1,0:T(8,128)S(1)}, f32[48,720]{1,0:T(8,128)S(1)}, u32[]{:S(2)}, u32[]{:S(2)}) collective-permute-start(f32[48,720]{1,0:T(8,128)S(1)} %pad_maximum_fusion.11), channel_id=1, source_target_pairs={{0,8},{8,16},{16,24},{1,9},{9,17},{17,25},{2,10},{10,18},{18,26},{... | collective-permute-start | bytes 414728 | tf_op jit(solution)/shard_map/ppermute | solution.py:91
  9.6 1.2 fusion.70
  11.1 3.0 %collective-permute-start.1 = (f32[40,16]{0,1:T(8,128)S(1)}, f32[40,16]{0,1:T(8,128)S(1)}, u32[]{:S(2)}, u32[]{:S(2)}) collective-permute-start(f32[40,16]{0,1:T(8,128)S(1)} %bitcast.90), channel_id=1, source_target_pairs={{1,0},{2,1},{3,2},{4,3},{5,4},{6,5},{7,6},{0,7},{9,8},{10,9},{11,1... | collective-permute-start | bytes 7688 | tf_op jit(solution)/shard_map/ppermute | solution.py:90
  14.7 1.5 %constant_dynamic-update-slice_fusion = f32[5,8,17,720]{3,2,1,0:T(8,128)} fusion(f32[5,8,16,720]{3,2,1,0:T(8,128)S(1)} %copy-done), kind=kLoop, calls=%fused_computation.123 | loop fusion | bytes 3809280
  20.4 1.9 %multiply_subtract_fusion = f32[5,8,16,721]{3,2,1,0:T(8,128)} fusion(f32[5,8,16,1]{3,2,1,0:T(8,128)S(1)} %copy.118, f32[5,8,16,720]{3,2,1,0:T(8,128)S(1)} %copy-done, f32[5,8,16,1]{3,2,1,0:T(8,128)S(1)} %copy.115, f32[8,16,721]{2,1,0:T(8,128)S(1)} %get-tuple-element.22, f32[8,16,721]{2,1,0:T(8,128)S(1)} %get-tuple-element.21), kind=kLoop, calls=%fused_computation.13 | loop fusion | flops 3230080 | bytes 4432384 | tf_op jit(solution)/shard_map/sub | solution.py:72
  23.3 3.3 %dynamic-update-slice.1 = f32[5,8,17,720]{3,2,1,0:T(8,128)} dynamic-update-slice(f32[5,8,17,720]{3,2,1,0:T(8,128)} %constant_dynamic-update-slice_fusion, f32[5,8,1,720]{3,2,1,0:T(1,128)S(1)} %copy.122, s32[]{} %constant.139, s32[]{} %constant.139, s32[]{} %constant.140, s32[]{} %constant.139) | dynamic-update-slice | bytes 230404 | tf_op jit(solution)/shard_map/concatenate | solution.py:100
  26.9 2.9 %subtract_select_fusion = f32[5,8,17,720]{3,2,1,0:T(8,128)S(1)} fusion(f32[5,8,17,720]{3,2,1,0:T(8,128)} %dynamic-update-slice.1, f32[5,8,16,720]{3,2,1,0:T(8,128)S(1)} %copy-done, f32[5,8,1,720]{3,2,1,0:T(1,128)S(1)} %copy.121, f32[8,17,720]{2,1,0:T(8,128)S(1)} %get-tuple-element.24, f32[8,17,720]{2,1,0:T(8,128)S(1)} %get-tuple-element.23, ...), kind=kLoop, calls=%fused_computation.3 | loop fusion | flops 3427200 | bytes 6658577 | tf_op jit(solution)/shard_map/jit(_where)/select_n | solution.py:107
  32.8 2.1 %collective-permute-start.4 = (f32[16,8,720]{2,1,0:T(8,128)}, f32[16,8,720]{2,1,0:T(8,128)}, u32[]{:S(2)}, u32[]{:S(2)}) collective-permute-start(f32[16,8,720]{2,1,0:T(8,128)} %slice.155), channel_id=1, source_target_pairs={{0,16},{8,24},{16,0},{24,8},{1,17},{9,25},{17,1},{25,9},{2,18},{10... | collective-permute-start | bytes 1105928 | tf_op jit(solution)/shard_map/ppermute | solution.py:141
  36.2 9.1 %collective-permute-done.4 = f32[16,8,720]{2,1,0:T(8,128)} collective-permute-done((f32[16,8,720]{2,1,0:T(8,128)}, f32[16,8,720]{2,1,0:T(8,128)}, u32[]{:S(2)}, u32[]{:S(2)}) %collective-permute-start.4) | collective-permute-done | bytes 368672 | tf_op jit(solution)/shard_map/ppermute | solution.py:141
  45.3 2.0 %slice_select_fusion.3 = f32[16,8,720]{2,1,0:T(8,128)} fusion(f32[16,8,720]{2,1,0:T(8,128)} %collective-permute-done.4, f32[40,8,720]{2,1,0:T(8,128)} %get-tuple-element.7, pred[8]{0:T(512)(128)(4,1)S(1)} %slice_select_fusion.4), kind=kLoop, calls=%fused_computation.50 | loop fusion | flops 92160 | bytes 1105928 | tf_op jit(solution)/shard_map/jit(_where)/select_n | solution.py:142
  47.3 4.1 %all-to-all-start = ((f32[8,16,720]{2,1,0:T(8,128)}), f32[8,16,720]{2,1,0:T(8,128)}, u32[]{:S(2)}, u32[]{:S(2)}) async-start(f32[8,16,720]{2,1,0:T(8,128)} %bitcast.79), calls=%async_computation | async-start | bytes 786432 | tf_op jit(solution)/shard_map/all_to_all | solution.py:143
  52.9 2.6 %collective-permute-done.5 = f32[24,8,720]{2,1,0:T(8,128)} collective-permute-done((f32[24,8,720]{2,1,0:T(8,128)}, f32[24,8,720]{2,1,0:T(8,128)}, u32[]{:S(2)}, u32[]{:S(2)}) %collective-permute-start.5) | collective-permute-done | bytes 552992 | tf_op jit(solution)/shard_map/ppermute | solution.py:141
  55.5 2.0 %slice_select_fusion.2 = f32[24,8,720]{2,1,0:T(8,128)} fusion(f32[24,8,720]{2,1,0:T(8,128)} %collective-permute-done.5, f32[40,8,720]{2,1,0:T(8,128)S(1)} %copy-done.4, pred[8]{0:T(512)(128)(4,1)S(1)} %slice_select_fusion.4), kind=kLoop, calls=%fused_computation.40 | loop fusion | flops 138240 | bytes 1658888 | tf_op jit(solution)/shard_map/jit(_where)/select_n | solution.py:142
  57.5 6.4 %all-to-all-done = f32[8,16,720]{2,1,0:T(8,128)} async-done(((f32[8,16,720]{2,1,0:T(8,128)}), f32[8,16,720]{2,1,0:T(8,128)}, u32[]{:S(2)}, u32[]{:S(2)}) %all-to-all-start) | async-done | bytes 368672 | tf_op jit(solution)/shard_map/all_to_all | solution.py:143
  63.9 3.7 %all-to-all-start.2 = ((f32[8,24,720]{2,1,0:T(8,128)}), f32[8,24,720]{2,1,0:T(8,128)S(1)}, u32[]{:S(2)}, u32[]{:S(2)}) async-start(f32[8,24,720]{2,1,0:T(8,128)} %bitcast.78), calls=%async_computation.2 | async-start | bytes 1179648 | tf_op jit(solution)/shard_map/all_to_all | solution.py:143
  73.9 1.6 %convolution_bitcast_fusion.1 = f32[16,90,128]{2,1,0:T(8,128)S(1)} fusion(f32[16,45,128]{2,1,0:T(8,128)} %reshape.332, f32[45,45]{1,0:T(8,128)} %get-tuple-element.25, f32[45,45]{1,0:T(8,128)} %get-tuple-element.26), kind=kOutput, calls=%fused_computation.17 | convolution fusion | flops 49770448 | bytes 1122120 | tf_op jit(solution)/shard_map/lan,ab->lbn/dot_general | solution.py:46
  75.5 8.7 %all-to-all-done.2 = f32[8,24,720]{2,1,0:T(8,128)S(1)} async-done(((f32[8,24,720]{2,1,0:T(8,128)}), f32[8,24,720]{2,1,0:T(8,128)S(1)}, u32[]{:S(2)}, u32[]{:S(2)}) %all-to-all-start.2) | async-done | bytes 552992 | tf_op jit(solution)/shard_map/all_to_all | solution.py:143
  85.2 1.4 reshape.334
  86.6 1.6 %convolution_bitcast_fusion = f32[24,90,128]{2,1,0:T(8,128)S(1)} fusion(f32[24,45,128]{2,1,0:T(8,128)S(1)} %reshape.334, f32[45,45]{1,0:T(8,128)} %get-tuple-element.25, f32[45,45]{1,0:T(8,128)} %get-tuple-element.26), kind=kOutput, calls=%fused_computation.15 | convolution fusion | flops 74653648 | bytes 1675080 | tf_op jit(solution)/shard_map/lan,ab->lbn/dot_general | solution.py:46
  91.1 1.3 all_to_all.57
  92.5 2.1 %copy.128 = f32[24,8,720]{2,0,1:T(8,128)} copy(f32[24,8,720]{2,1,0:T(8,128)} %all_to_all.57) | data formatting | bytes 1105920 | tf_op jit(solution)/shard_map/all_to_all | solution.py:151
  94.6 3.5 %all-to-all-start.3 = ((f32[24,8,720]{2,0,1:T(8,128)}), f32[24,8,720]{2,0,1:T(8,128)S(1)}, u32[]{:S(2)}, u32[]{:S(2)}) async-start(f32[24,8,720]{2,0,1:T(8,128)} %copy.128), calls=%async_computation.3 | async-start | bytes 1179648 | tf_op jit(solution)/shard_map/all_to_all | solution.py:151
  99.0 1.6 %convolution_multiply_fusion.1 = f32[16,45,256]{2,1,0:T(8,128)S(1)} fusion(f32[16,45,128]{2,1,0:T(8,128)S(1)} %get-tuple-element.20, f32[16,45,128]{2,1,0:T(8,128)S(1)} %get-tuple-element.19, f32[16,45,128]{2,1,0:T(8,128)} %fusion.21, f32[128,128]{1,0:T(8,128)S(1)} %get-tuple-element.32, f32[128,128]{1,0:T(8,128)S(1)} %get-tuple-element.31, ...), kind=kOutput, calls=%fused_computation.16 | convolution fusion | flops 283865088 | bytes 2039808 | tf_op jit(solution)/shard_map/ljn,nk->ljk/dot_general | solution.py:52
  103.0 11.8 %all-to-all-done.3 = f32[24,8,720]{2,0,1:T(8,128)S(1)} async-done(((f32[24,8,720]{2,0,1:T(8,128)}), f32[24,8,720]{2,0,1:T(8,128)S(1)}, u32[]{:S(2)}, u32[]{:S(2)}) %all-to-all-start.3) | async-done | bytes 552992 | tf_op jit(solution)/shard_map/all_to_all | solution.py:151
  114.8 3.5 %all-to-all-start.1 = ((f32[16,8,720]{2,0,1:T(8,128)}), f32[16,8,720]{2,0,1:T(8,128)S(1)}, u32[]{:S(2)}, u32[]{:S(2)}) async-start(f32[16,8,720]{2,0,1:T(8,128)} %copy.125), calls=%async_computation.1 | async-start | bytes 786432 | tf_op jit(solution)/shard_map/all_to_all | solution.py:151
  118.3 2.1 %collective-permute-start.7 = (f32[24,8,720]{2,1,0:T(8,128)S(1)}, f32[24,8,720]{2,1,0:T(8,128)}, u32[]{:S(2)}, u32[]{:S(2)}) collective-permute-start(f32[24,8,720]{2,1,0:T(8,128)S(1)} %bitcast.76), channel_id=1, source_target_pairs={{0,16},{8,24},{16,0},{24,8},{1,17},{9,25},{17,1},{25,9},{2,18},{10... | collective-permute-start | bytes 1658888 | tf_op jit(solution)/shard_map/ppermute | solution.py:155
  120.4 10.4 %all-to-all-done.1 = f32[16,8,720]{2,0,1:T(8,128)S(1)} async-done(((f32[16,8,720]{2,0,1:T(8,128)}), f32[16,8,720]{2,0,1:T(8,128)S(1)}, u32[]{:S(2)}, u32[]{:S(2)}) %all-to-all-start.1) | async-done | bytes 368672 | tf_op jit(solution)/shard_map/all_to_all | solution.py:151
  130.7 2.0 %collective-permute-start.6 = (f32[16,8,720]{2,1,0:T(8,128)S(1)}, f32[16,8,720]{2,1,0:T(8,128)S(1)}, u32[]{:S(2)}, u32[]{:S(2)}) collective-permute-start(f32[16,8,720]{2,1,0:T(8,128)S(1)} %bitcast.80), channel_id=1, source_target_pairs={{0,16},{8,24},{16,0},{24,8},{1,17},{9,25},{17,1},{25,9},{2,18},{10... | collective-permute-start | bytes 1105928 | tf_op jit(solution)/shard_map/ppermute | solution.py:155
  132.8 9.8 %collective-permute-done.6 = f32[16,8,720]{2,1,0:T(8,128)S(1)} collective-permute-done((f32[16,8,720]{2,1,0:T(8,128)S(1)}, f32[16,8,720]{2,1,0:T(8,128)S(1)}, u32[]{:S(2)}, u32[]{:S(2)}) %collective-permute-start.6) | collective-permute-done | bytes 368672 | tf_op jit(solution)/shard_map/ppermute | solution.py:155
  143.8 1.9 %fusion.3 = f32[5,8,16,720]{3,2,1,0:T(8,128)} fusion(f32[5,8,16,720]{3,2,1,0:T(8,128)S(1)} %copy-done, f32[5,8,16,720]{3,2,1,0:T(8,128)S(1)} %copy-done.2, f32[5,8,8,720]{3,2,1,0:T(8,128)S(1)} %bitcast.74, f32[5,8,8,720]{3,2,1,0:T(8,128)S(1)} %bitcast.73, pred[16]{0:T(512)(128)(4,1)S(1)} %compare_reduce_fusion, pred[]{:T(512)S(6)} %lt.115), kind=kLoop, calls=%fused_computation.12 | loop fusion | flops 2304000 | bytes 7372817 | tf_op jit(solution)/shard_map/add | solution.py:164
  (110 shorter events, 27.3 us)
Async XLA Ops:
  0.0 14.7 %copy-start = (f32[5,8,16,720]{3,2,1,0:T(8,128)S(1)}, f32[5,8,16,720]{3,2,1,0:T(8,128)}, u32[]{:S(2)}) copy-start(f32[5,8,16,720]{3,2,1,0:T(8,128)} %param.5) | copy-start | bytes 5529604
  0.0 14.1 %copy-start.14 = (f32[8,16,720]{2,1,0:T(8,128)S(1)}, f32[8,16,720]{2,1,0:T(8,128)}, u32[]{:S(2)}) copy-start(f32[8,16,720]{2,1,0:T(8,128)} %param.6) | copy-start | bytes 1105924
  1.8 20.5 %collective-permute-start.3 = (f32[40,720]{1,0:T(8,128)S(1)}, f32[40,720]{1,0:T(8,128)}, u32[]{:S(2)}, u32[]{:S(2)}) collective-permute-start(f32[40,720]{1,0:T(8,128)S(1)} %bitcast.83), channel_id=1, source_target_pairs={{8,0},{16,8},{24,16},{9,1},{17,9},{25,17},{10,2},{18,10},{26,18},{... | collective-permute-start | bytes 345608 | tf_op jit(solution)/shard_map/ppermute | solution.py:94
  4.1 22.5 %collective-permute-start.2 = (f32[48,720]{1,0:T(8,128)S(1)}, f32[48,720]{1,0:T(8,128)S(1)}, u32[]{:S(2)}, u32[]{:S(2)}) collective-permute-start(f32[48,720]{1,0:T(8,128)S(1)} %pad_maximum_fusion.11), channel_id=1, source_target_pairs={{0,8},{8,16},{16,24},{1,9},{9,17},{17,25},{2,10},{10,18},{18,26},{... | collective-permute-start | bytes 414728 | tf_op jit(solution)/shard_map/ppermute | solution.py:91
  11.1 7.2 %collective-permute-start.1 = (f32[40,16]{0,1:T(8,128)S(1)}, f32[40,16]{0,1:T(8,128)S(1)}, u32[]{:S(2)}, u32[]{:S(2)}) collective-permute-start(f32[40,16]{0,1:T(8,128)S(1)} %bitcast.90), channel_id=1, source_target_pairs={{1,0},{2,1},{3,2},{4,3},{5,4},{6,5},{7,6},{0,7},{9,8},{10,9},{11,1... | collective-permute-start | bytes 7688 | tf_op jit(solution)/shard_map/ppermute | solution.py:90
  14.6 3.1 %copy-start.17 = (s32[32]{0:T(128)S(1)}, s32[32]{0:T(128)}, u32[]{:S(2)}) copy-start(s32[32]{0:T(128)} %param.8) | copy-start | bytes 388
  14.6 3.4 %copy-start.18 = (s32[32]{0:T(128)S(1)}, s32[32]{0:T(128)}, u32[]{:S(2)}) copy-start(s32[32]{0:T(128)} %param.9) | copy-start | bytes 388
  14.6 4.9 %collective-permute-start = (f32[48,16]{0,1:T(8,128)S(1)}, f32[48,16]{0,1:T(8,128)S(1)}, u32[]{:S(2)}, u32[]{:S(2)}) collective-permute-start(f32[48,16]{0,1:T(8,128)S(1)} %pad_maximum_fusion.12), channel_id=1, source_target_pairs={{0,1},{1,2},{2,3},{3,4},{4,5},{5,6},{6,7},{7,0},{8,9},{9,10},{10,1... | collective-permute-start | bytes 9224 | tf_op jit(solution)/shard_map/ppermute | solution.py:87
  20.4 6.5 %copy-start.15 = (f32[8,16,720]{2,1,0:T(8,128)S(1)}, f32[8,16,720]{2,1,0:T(8,128)}, u32[]{:S(2)}) copy-start(f32[8,16,720]{2,1,0:T(8,128)} %param.7) | copy-start | bytes 1105924
  26.9 2.9 %copy-start.3 = (f32[5,8,16,721]{3,2,1,0:T(8,128)S(1)}, f32[5,8,16,721]{3,2,1,0:T(8,128)}, u32[]{:S(2)}) copy-start(f32[5,8,16,721]{3,2,1,0:T(8,128)} %multiply_subtract_fusion) | copy-start | bytes 5537284
  30.5 1.6 %copy-start.1 = (f32[5,8,16,720]{3,2,1,0:T(8,128)}, f32[5,8,16,720]{3,2,1,0:T(8,128)S(1)}, u32[]{:S(2)}) copy-start(f32[5,8,16,720]{3,2,1,0:T(8,128)S(1)} %fusion) | copy-start | bytes 5529604
  32.8 12.5 %collective-permute-start.4 = (f32[16,8,720]{2,1,0:T(8,128)}, f32[16,8,720]{2,1,0:T(8,128)}, u32[]{:S(2)}, u32[]{:S(2)}) collective-permute-start(f32[16,8,720]{2,1,0:T(8,128)} %slice.155), channel_id=1, source_target_pairs={{0,16},{8,24},{16,0},{24,8},{1,17},{9,25},{17,1},{25,9},{2,18},{10... | collective-permute-start | bytes 1105928 | tf_op jit(solution)/shard_map/ppermute | solution.py:141
  36.2 19.3 %copy-start.4 = (f32[40,8,720]{2,1,0:T(8,128)S(1)}, f32[40,8,720]{2,1,0:T(8,128)}, u32[]{:S(2)}) copy-start(f32[40,8,720]{2,1,0:T(8,128)} %get-tuple-element.7) | copy-start | bytes 2764804
  36.2 19.3 %collective-permute-start.5 = (f32[24,8,720]{2,1,0:T(8,128)}, f32[24,8,720]{2,1,0:T(8,128)}, u32[]{:S(2)}, u32[]{:S(2)}) collective-permute-start(f32[24,8,720]{2,1,0:T(8,128)} %slice.161), channel_id=1, source_target_pairs={{0,16},{8,24},{16,0},{24,8},{1,17},{9,25},{17,1},{25,9},{2,18},{10... | collective-permute-start | bytes 1658888 | tf_op jit(solution)/shard_map/ppermute | solution.py:141
  47.3 16.7 %all-to-all-start = ((f32[8,16,720]{2,1,0:T(8,128)}), f32[8,16,720]{2,1,0:T(8,128)}, u32[]{:S(2)}, u32[]{:S(2)}) async-start(f32[8,16,720]{2,1,0:T(8,128)} %bitcast.79), calls=%async_computation | async-start | bytes 786432 | tf_op jit(solution)/shard_map/all_to_all | solution.py:143
  57.5 12.2 %copy-start.16 = (f32[45,128]{1,0:T(8,128)S(1)}, f32[45,128]{1,0:T(8,128)}, u32[]{:S(2)}) copy-start(f32[45,128]{1,0:T(8,128)} %broadcast_maximum_fusion) | copy-start | bytes 69124
  63.9 20.2 %all-to-all-start.2 = ((f32[8,24,720]{2,1,0:T(8,128)}), f32[8,24,720]{2,1,0:T(8,128)S(1)}, u32[]{:S(2)}, u32[]{:S(2)}) async-start(f32[8,24,720]{2,1,0:T(8,128)} %bitcast.78), calls=%async_computation.2 | async-start | bytes 1179648 | tf_op jit(solution)/shard_map/all_to_all | solution.py:143
  86.6 2.5 %copy-start.5 = (f32[24,45,128]{2,1,0:T(8,128)S(1)}, f32[24,45,128]{2,1,0:T(8,128)}, u32[]{:S(2)}) copy-start(f32[24,45,128]{2,1,0:T(8,128)} %fusion.18) | copy-start | bytes 1658884
  89.8 0.7 copy-start.10
  89.8 0.7 copy-start.12
  89.8 0.9 copy-start.6
  89.8 0.9 copy-start.8
  94.6 20.2 %all-to-all-start.3 = ((f32[24,8,720]{2,0,1:T(8,128)}), f32[24,8,720]{2,0,1:T(8,128)S(1)}, u32[]{:S(2)}, u32[]{:S(2)}) async-start(f32[24,8,720]{2,0,1:T(8,128)} %copy.128), calls=%async_computation.3 | async-start | bytes 1179648 | tf_op jit(solution)/shard_map/all_to_all | solution.py:151
  99.0 2.1 %copy-start.11 = (f32[45,128]{1,0:T(8,128)S(1)}, f32[45,128]{1,0:T(8,128)}, u32[]{:S(2)}) copy-start(f32[45,128]{1,0:T(8,128)} %get-tuple-element.27) | copy-start | bytes 69124
  99.0 2.1 %copy-start.13 = (f32[45,128]{1,0:T(8,128)S(1)}, f32[45,128]{1,0:T(8,128)}, u32[]{:S(2)}) copy-start(f32[45,128]{1,0:T(8,128)} %get-tuple-element.28) | copy-start | bytes 69124
  100.6 0.7 copy-start.7
  100.6 0.7 copy-start.9
  114.8 15.9 %all-to-all-start.1 = ((f32[16,8,720]{2,0,1:T(8,128)}), f32[16,8,720]{2,0,1:T(8,128)S(1)}, u32[]{:S(2)}, u32[]{:S(2)}) async-start(f32[16,8,720]{2,0,1:T(8,128)} %copy.125), calls=%async_computation.1 | async-start | bytes 786432 | tf_op jit(solution)/shard_map/all_to_all | solution.py:151
  118.3 24.3 %collective-permute-start.7 = (f32[24,8,720]{2,1,0:T(8,128)S(1)}, f32[24,8,720]{2,1,0:T(8,128)}, u32[]{:S(2)}, u32[]{:S(2)}) collective-permute-start(f32[24,8,720]{2,1,0:T(8,128)S(1)} %bitcast.76), channel_id=1, source_target_pairs={{0,16},{8,24},{16,0},{24,8},{1,17},{9,25},{17,1},{25,9},{2,18},{10... | collective-permute-start | bytes 1658888 | tf_op jit(solution)/shard_map/ppermute | solution.py:155
  130.7 13.0 %copy-start.2 = (f32[5,8,16,720]{3,2,1,0:T(8,128)S(1)}, f32[5,8,16,720]{3,2,1,0:T(8,128)}, u32[]{:S(2)}) copy-start(f32[5,8,16,720]{3,2,1,0:T(8,128)} %copy-done.1) | copy-start | bytes 5529604
  130.7 11.9 %collective-permute-start.6 = (f32[16,8,720]{2,1,0:T(8,128)S(1)}, f32[16,8,720]{2,1,0:T(8,128)S(1)}, u32[]{:S(2)}, u32[]{:S(2)}) collective-permute-start(f32[16,8,720]{2,1,0:T(8,128)S(1)} %bitcast.80), channel_id=1, source_target_pairs={{0,16},{8,24},{16,0},{24,8},{1,17},{9,25},{17,1},{25,9},{2,18},{10... | collective-permute-start | bytes 1105928 | tf_op jit(solution)/shard_map/ppermute | solution.py:155

commit v7 on v4

--- a/solution.py
+++ b/solution.py
@@ -80,23 +80,28 @@
         jnp.concatenate([flat_fields[:, -1], lat_courant[:, -1]], axis=0), "lat", northward
     )
     from_above = lax.ppermute(flat_fields[:, 0], "lat", southward)
-    wide_fields = jnp.concatenate(
-        [from_west[:stacked, :, None], flat_fields, from_east[:, :, None]], axis=2
-    ).reshape(field_count, level_count, rows_dev, columns + 2)
-    wide_courant = jnp.concatenate([from_west[stacked:, :, None], lon_courant], axis=2)
-    column_flux = face_flux(wide_courant, wide_fields[..., :-1], wide_fields[..., 1:])
-    tall_fields = jnp.concatenate(
-        [from_below[:stacked, None], flat_fields, from_above[:, None]], axis=1
-    ).reshape(field_count, level_count, rows_dev + 2, columns)
-    tall_courant = jnp.concatenate([from_below[stacked:, None], lat_courant], axis=1)
-    row_flux = face_flux(tall_courant, tall_fields[:, :, :-1], tall_fields[:, :, 1:])
     tile_index = lax.axis_index("lat")
     lower_row = tile_index * rows_dev - 1 + jnp.arange(rows_dev + 1, dtype=jnp.int32)
-    row_flux = jnp.where((lower_row == rows_dev * lat_devices - 1)[:, None], 0.0, row_flux)
-    increment = -(column_flux[..., 1:] - column_flux[..., :-1]) - (
-        row_flux[:, :, 1:] - row_flux[:, :, :-1]
-    )
-    flat_increment = increment.reshape(stacked, rows_dev, columns)
+    top_face = (lower_row == rows_dev * lat_devices - 1)[:, None]
+    wide_courant = jnp.concatenate([from_west[stacked:, :, None], lon_courant], axis=2)
+    tall_courant = jnp.concatenate([from_below[stacked:, None], lat_courant], axis=1)
+
+    def increment_of(first, last):
+        span = slice(first * level_count, last * level_count)
+        wide_fields = jnp.concatenate(
+            [from_west[span][:, :, None], flat_fields[span], from_east[span][:, :, None]], axis=2
+        ).reshape(last - first, level_count, rows_dev, columns + 2)
+        column_flux = face_flux(wide_courant, wide_fields[..., :-1], wide_fields[..., 1:])
+        tall_fields = jnp.concatenate(
+            [from_below[span][:, None], flat_fields[span], from_above[span][:, None]], axis=1
+        ).reshape(last - first, level_count, rows_dev + 2, columns)
+        row_flux = face_flux(tall_courant, tall_fields[:, :, :-1], tall_fields[:, :, 1:])
+        row_flux = jnp.where(top_face, 0.0, row_flux)
+        increment = -(column_flux[..., 1:] - column_flux[..., :-1]) - (
+            row_flux[:, :, 1:] - row_flux[:, :, :-1]
+        )
+        return increment.reshape((last - first) * level_count, rows_dev, columns)
+
     half_rows = rows_dev // 2
     pair_shift = lat_devices // 2
     pair_perm = [(i, (i + pair_shift) % lat_devices) for i in range(lat_devices)]
@@ -111,23 +116,23 @@
     is_filtered, own_cut = row_info(tile_index)
     _, partner_cut = row_info(partner_index)
     row_cut = jnp.where(is_filtered, own_cut, partner_cut).astype(jnp.float32)
-    low_half = flat_increment[:, :half_rows]
-    high_half = flat_increment[:, half_rows:]
-    kept = jnp.where(is_low, low_half, high_half)
-    given = jnp.where(is_low, high_half, low_half)
     kept_filtered = jnp.where(is_low, is_filtered[:half_rows], is_filtered[half_rows:])
     kept_cut = jnp.where(is_low, row_cut[:half_rows], row_cut[half_rows:])
-    chunk_sizes = (stacked * 2 // 5, stacked - stacked * 2 // 5)
-    returned_parts, handed_parts = [], []
-    chunk_start = 0
-    for chunk_stack in chunk_sizes:
-        rows_of_part = slice(chunk_start, chunk_start + chunk_stack)
-        chunk_start += chunk_stack
+    first_fields = field_count * 2 // 5
+    field_spans = ((0, first_fields), (first_fields, field_count))
+    outputs = []
+    for first, last in field_spans:
+        chunk_stack = (last - first) * level_count
+        flat_increment = increment_of(first, last)
+        low_half = flat_increment[:, :half_rows]
+        high_half = flat_increment[:, half_rows:]
+        kept = jnp.where(is_low, low_half, high_half)
+        given = jnp.where(is_low, high_half, low_half)
         line_count = chunk_stack * half_rows // lon_devices
         line_index = lax.axis_index("lon") * line_count + jnp.arange(line_count, dtype=jnp.int32)
         line_cut = kept_cut[line_index % half_rows]
-        taken = lax.ppermute(given[rows_of_part], "lat", pair_perm)
-        pair_lines = jnp.where(kept_filtered[None, :, None], kept[rows_of_part], taken)
+        taken = lax.ppermute(given, "lat", pair_perm)
+        pair_lines = jnp.where(kept_filtered[None, :, None], kept, taken)
         full_lines = lax.all_to_all(
             pair_lines.reshape(chunk_stack * half_rows, columns),
             "lon",
@@ -139,17 +144,15 @@
         returned = lax.all_to_all(
             smoothed, "lon", split_axis=1, concat_axis=0, tiled=True
         ).reshape(chunk_stack, half_rows, columns)
-        returned_parts.append(returned)
-        handed_parts.append(lax.ppermute(returned, "lat", pair_perm))
-    returned = jnp.concatenate(returned_parts, axis=0)
-    handed_back = jnp.concatenate(handed_parts, axis=0)
-    smooth_rows = jnp.where(
-        is_low,
-        jnp.concatenate([returned, handed_back], axis=1),
-        jnp.concatenate([handed_back, returned], axis=1),
-    )
-    final_increment = jnp.where(is_filtered[None, :, None], smooth_rows, flat_increment)
-    return (flat_fields + final_increment).reshape(fields.shape)
+        handed_back = lax.ppermute(returned, "lat", pair_perm)
+        smooth_rows = jnp.where(
+            is_low,
+            jnp.concatenate([returned, handed_back], axis=1),
+            jnp.concatenate([handed_back, returned], axis=1),
+        )
+        final_increment = jnp.where(is_filtered[None, :, None], smooth_rows, flat_increment)
+        outputs.append(flat_fields[first * level_count : last * level_count] + final_increment)
+    return jnp.concatenate(outputs, axis=0).reshape(fields.shape)
 
 
 def solution(mesh):

time: 141 us -> 143 us (1.014)
  waiting for transfers between devices: 62 us -> 44.6 us
  local copies, waits for them, and re-layouts: 21.4 us -> 30.1 us
  other arithmetic: 11.6 us -> 16.7 us
  starting transfers between devices: 30.3 us -> 33.9 us
    all_to_all x2, waiting for transfers between devices: 22.8 us -> 14.8 us  [body(): lax.all_to_all(smoothed, 'lon', split_axis=1, concat_axis=0, tiled=True)]
    all_to_all x2, waiting for transfers between devices: 15 us -> 9.57 us  [body(): lax.all_to_all(pair_lines.reshape(chunk_stack * half_rows, columns), 'lon...]
    all_to_all x4, local copies, waits for them, and re-layouts: 2.69 us -> 6.65 us  [body(): lax.all_to_all(smoothed, 'lon', split_axis=1, concat_axis=0, tiled=True)]
    ppermute x1, waiting for transfers between devices: 2.3 us -> 0.01 us  [body(): lax.ppermute(jnp.concatenate([flat_fields[..., -1], lon_courant[..., -1]]...]
    unnamed x46 -> x41, local copies, waits for them, and re-layouts: 3.51 us -> 1.3 us
    slice x3 -> x8, local copies, waits for them, and re-layouts: 0.99 us -> 2.97 us  [the longest x2 2.53 us: body(): flat_fields[first * level_count:last * level_count] + final_increment]
    all_to_all x2, local copies, waits for them, and re-layouts: 1.17 us -> 3.07 us  [body(): lax.all_to_all(pair_lines.reshape(chunk_stack * half_rows, columns), 'lon...]
    reshape x2, local copies, waits for them, and re-layouts: 1.6 us -> 3.49 us  [filter_lines(): values = lines.reshape(line_total, outer, radix_len)]
  transfers between devices with their start and end apart: 12 -> 12, of which waited for: 8 -> 6; matrix products, arithmetic and copies ran while one was open for 20% -> 35% of each run, Pallas kernels for 0% -> 0%
where the time goes in v7:
time: 143 us; the launch traced here: 142 us
  waiting for transfers between devices  44.6 us (31%)
  starting transfers between devices  33.9 us (24%)
  local copies, waits for them, and re-layouts  30.1 us (21%)
  other arithmetic  16.7 us (12%)
  matrix products  16.1 us (11%)
    all_to_all x2, waiting for transfers between devices, body(): lax.all_to_all(smoothed, 'lon', split_axis=1, concat_axis=0, tiled=True)  14.8 us
    ppermute x2, waiting for transfers between devices, body(): handed_back = lax.ppermute(returned, 'lat', pair_perm)  11.8 us
    all_to_all x2, waiting for transfers between devices, body(): lax.all_to_all(pair_lines.reshape(chunk_stack * half_rows, columns), 'lon...  9.57 us
    all_to_all x2, starting transfers between devices, body(): lax.all_to_all(smoothed, 'lon', split_axis=1, concat_axis=0, tiled=True)  8.48 us
    ppermute x2, waiting for transfers between devices, body(): taken = lax.ppermute(given, 'lat', pair_perm)  8.44 us
    all_to_all x2, starting transfers between devices, body(): lax.all_to_all(pair_lines.reshape(chunk_stack * half_rows, columns), 'lon...  7.84 us
    all_to_all x4, local copies, waits for them, and re-layouts, body(): lax.all_to_all(smoothed, 'lon', split_axis=1, concat_axis=0, tiled=True)  6.65 us
    ppermute x1, starting transfers between devices, body(): lax.ppermute(jnp.concatenate([flat_fields[:, -1], lat_courant[:, -1]], ax...  5.5 us
  transfers between devices with their start and end apart: 12, of which 6 were waited for; matrix products, arithmetic and copies ran while one was open for 35% of the time, Pallas kernels for 0%

profile of v7, /device:TPU:0, one launch (start us, length us, event | category | flops | bytes accessed | tf_op | source)
XLA Modules:
  0.0 142.0 jit_solution(15480500095585646298)
XLA Ops:
  0.0 1.7 %fusion.251 = (f32[40,1,720]{2,1,0:T(1,128)S(1)}, f32[40,1,720]{2,1,0:T(1,128)S(1)}) fusion(f32[40,16,720]{2,1,0:T(8,128)} %bitcast.147), kind=kLoop, calls=%fused_computation.304 | loop fusion | bytes 460800 | tf_op jit(solution)/shard_map/slice | solution.py:80
  3.4 5.5 %collective-permute-start.2 = (f32[48,720]{1,0:T(8,128)}, f32[48,720]{1,0:T(8,128)}, u32[]{:S(2)}, u32[]{:S(2)}) collective-permute-start(f32[48,720]{1,0:T(8,128)} %pad_maximum_fusion.11), channel_id=1, source_target_pairs={{0,8},{8,16},{16,24},{1,9},{9,17},{17,25},{2,10},{10,18},{18,26},{... | collective-permute-start | bytes 414728 | tf_op jit(solution)/shard_map/ppermute | solution.py:79
  9.6 1.4 collective-permute-start.3
  13.0 3.6 %collective-permute-start.1 = (f32[40,16]{0,1:T(8,128)S(1)}, f32[40,16]{0,1:T(8,128)S(1)}, u32[]{:S(2)}, u32[]{:S(2)}) collective-permute-start(f32[40,16]{0,1:T(8,128)S(1)} %bitcast.164), channel_id=1, source_target_pairs={{1,0},{2,1},{3,2},{4,3},{5,4},{6,5},{7,6},{0,7},{9,8},{10,9},{11,1... | collective-permute-start | bytes 7688 | tf_op jit(solution)/shard_map/ppermute | solution.py:78
  20.0 1.4 slice.152
  29.3 3.0 %collective-permute-start.4 = (f32[16,8,720]{2,1,0:T(8,128)S(1)}, f32[16,8,720]{2,1,0:T(8,128)S(1)}, u32[]{:S(2)}, u32[]{:S(2)}) collective-permute-start(f32[16,8,720]{2,1,0:T(8,128)S(1)} %slice_select_fusion.1), channel_id=1, source_target_pairs={{0,16},{8,24},{16,0},{24,8},{1,17},{9,25},{17,1},{25,9},{2,18},{10... | collective-permute-start | bytes 1105928 | tf_op jit(solution)/shard_map/ppermute | solution.py:134
  35.2 7.1 %collective-permute-done.4 = f32[16,8,720]{2,1,0:T(8,128)S(1)} collective-permute-done((f32[16,8,720]{2,1,0:T(8,128)S(1)}, f32[16,8,720]{2,1,0:T(8,128)S(1)}, u32[]{:S(2)}, u32[]{:S(2)}) %collective-permute-start.4) | collective-permute-done | bytes 368672 | tf_op jit(solution)/shard_map/ppermute | solution.py:134
  43.2 3.5 %all-to-all-start = ((f32[8,16,720]{2,1,0:T(8,128)}), f32[8,16,720]{2,1,0:T(8,128)S(1)}, u32[]{:S(2)}, u32[]{:S(2)}) async-start(f32[8,16,720]{2,1,0:T(8,128)} %bitcast.151), calls=%async_computation | async-start | bytes 786432 | tf_op jit(solution)/shard_map/all_to_all | solution.py:136
  47.2 1.2 gather_fusion
  49.9 1.3 fusion.104
  51.2 1.3 collective-permute-done.6
  52.5 2.0 %select_select_fusion = f32[24,8,720]{2,1,0:T(8,128)} fusion(f32[24,8,720]{2,1,0:T(8,128)} %collective-permute-done.6, f32[24,16,720]{2,1,0:T(8,128)S(1)} %bitcast.144, pred[8]{0:T(512)(128)(4,1)} %copy-done.13, pred[]{:T(512)S(6)} %lt.139), kind=kLoop, calls=%fused_computation.67 | loop fusion | flops 276480 | bytes 2211849 | tf_op jit(solution)/shard_map/jit(_where)/select_n | solution.py:135
  54.5 4.6 %all-to-all-done = f32[8,16,720]{2,1,0:T(8,128)S(1)} async-done(((f32[8,16,720]{2,1,0:T(8,128)}), f32[8,16,720]{2,1,0:T(8,128)S(1)}, u32[]{:S(2)}, u32[]{:S(2)}) %all-to-all-start) | async-done | bytes 368672 | tf_op jit(solution)/shard_map/all_to_all | solution.py:136
  59.1 4.4 %all-to-all-start.2 = ((f32[8,24,720]{2,1,0:T(8,128)}), f32[8,24,720]{2,1,0:T(8,128)}, u32[]{:S(2)}, u32[]{:S(2)}) async-start(f32[8,24,720]{2,1,0:T(8,128)} %bitcast.149), calls=%async_computation.2 | async-start | bytes 1179648 | tf_op jit(solution)/shard_map/all_to_all | solution.py:136
  64.5 1.2 reshape.349
  72.9 1.3 all_to_all.51
  75.1 5.0 %all-to-all-done.2 = f32[8,24,720]{2,1,0:T(8,128)} async-done(((f32[8,24,720]{2,1,0:T(8,128)}), f32[8,24,720]{2,1,0:T(8,128)}, u32[]{:S(2)}, u32[]{:S(2)}) %all-to-all-start.2) | async-done | bytes 552992 | tf_op jit(solution)/shard_map/all_to_all | solution.py:136
  80.1 3.7 %all-to-all-start.1 = ((f32[16,8,720]{2,0,1:T(8,128)}), f32[16,8,720]{2,0,1:T(8,128)S(1)}, u32[]{:S(2)}, u32[]{:S(2)}) async-start(f32[16,8,720]{2,0,1:T(8,128)} %copy.139), calls=%async_computation.1 | async-start | bytes 786432 | tf_op jit(solution)/shard_map/all_to_all | solution.py:144
  83.7 2.1 %copy.146 = f32[24,8,720]{2,1,0:T(8,128)} copy(f32[24,8,720]{2,0,1:T(8,128)} %bitcast.33) | data formatting | bytes 1105920 | tf_op jit(solution)/shard_map/all_to_all | solution.py:136
  85.8 2.3 %reshape.352 = f32[24,45,128]{2,1,0:T(8,128)} reshape(f32[24,8,720]{2,1,0:T(8,128)} %copy.146) | data formatting | bytes 1105920 | tf_op jit(solution)/shard_map/reshape | solution.py:29
  88.1 1.6 %convolution_negate_fusion = f32[45,24,128]{2,0,1:T(8,128)S(1)} fusion(f32[24,45,128]{2,1,0:T(8,128)} %reshape.352), kind=kOutput, calls=%fused_computation.15 | convolution fusion | flops 37481264 | bytes 1105920 | tf_op jit(solution)/shard_map/lan,aj->ljn/dot_general | solution.py:31
  96.1 1.4 fusion.1
  97.5 2.4 %all_to_all.57 = f32[24,8,720]{2,1,0:T(8,128)} reshape(f32[24,45,128]{2,1,0:T(8,128)} %fusion.1) | data formatting | bytes 1105920 | tf_op jit(solution)/shard_map/all_to_all | solution.py:144
  99.9 2.1 %copy.147 = f32[24,8,720]{2,0,1:T(8,128)} copy(f32[24,8,720]{2,1,0:T(8,128)} %all_to_all.57) | data formatting | bytes 1105920 | tf_op jit(solution)/shard_map/all_to_all | solution.py:144
  101.9 4.8 %all-to-all-start.3 = ((f32[24,8,720]{2,0,1:T(8,128)}), f32[24,8,720]{2,0,1:T(8,128)}, u32[]{:S(2)}, u32[]{:S(2)}) async-start(f32[24,8,720]{2,0,1:T(8,128)} %copy.147), calls=%async_computation.3 | async-start | bytes 1179648 | tf_op jit(solution)/shard_map/all_to_all | solution.py:144
  106.7 2.0 %collective-permute-start.5 = (f32[16,8,720]{2,1,0:T(8,128)S(1)}, f32[16,8,720]{2,1,0:T(8,128)}, u32[]{:S(2)}, u32[]{:S(2)}) collective-permute-start(f32[16,8,720]{2,1,0:T(8,128)S(1)} %bitcast.152), channel_id=1, source_target_pairs={{0,16},{8,24},{16,0},{24,8},{1,17},{9,25},{17,1},{25,9},{2,18},{10... | collective-permute-start | bytes 1105928 | tf_op jit(solution)/shard_map/ppermute | solution.py:147
  108.8 14.8 %all-to-all-done.3 = f32[24,8,720]{2,0,1:T(8,128)} async-done(((f32[24,8,720]{2,0,1:T(8,128)}), f32[24,8,720]{2,0,1:T(8,128)}, u32[]{:S(2)}, u32[]{:S(2)}) %all-to-all-start.3) | async-done | bytes 552992 | tf_op jit(solution)/shard_map/all_to_all | solution.py:144
  123.6 2.0 %collective-permute-start.7 = (f32[24,8,720]{2,1,0:T(8,128)}, f32[24,8,720]{2,1,0:T(8,128)S(1)}, u32[]{:S(2)}, u32[]{:S(2)}) collective-permute-start(f32[24,8,720]{2,1,0:T(8,128)} %bitcast.39), channel_id=1, source_target_pairs={{0,16},{8,24},{16,0},{24,8},{1,17},{9,25},{17,1},{25,9},{2,18},{10... | collective-permute-start | bytes 1658888 | tf_op jit(solution)/shard_map/ppermute | solution.py:147
  125.6 1.6 %fusion.15 = f32[16,16,720]{2,1,0:T(8,128)S(1)} fusion(f32[16,8,720]{2,1,0:T(8,128)} %collective-permute-done.5, f32[16,8,720]{2,1,0:T(8,128)S(1)} %bitcast.153, f32[2,8,16,720]{3,2,1,0:T(8,128)S(1)} %slice.128, pred[16]{0:T(512)(128)(4,1)S(1)} %compare_reduce_fusion, pred[]{:T(512)S(6)} %lt.139, f32[2,8,16,720]{3,2,1,0:T(8,128)} %copy-done), kind=kLoop, calls=%fused_computation.47 | loop fusion | flops 921600 | bytes 2949137 | tf_op jit(solution)/shard_map/add | solution.py:154
  127.2 11.8 %collective-permute-done.7 = f32[24,8,720]{2,1,0:T(8,128)S(1)} collective-permute-done((f32[24,8,720]{2,1,0:T(8,128)}, f32[24,8,720]{2,1,0:T(8,128)S(1)}, u32[]{:S(2)}, u32[]{:S(2)}) %collective-permute-start.7) | collective-permute-done | bytes 552992 | tf_op jit(solution)/shard_map/ppermute | solution.py:147
  139.0 1.6 %fusion.11 = f32[24,16,720]{2,1,0:T(8,128)S(1)} fusion(f32[24,8,720]{2,1,0:T(8,128)S(1)} %collective-permute-done.7, f32[24,8,720]{2,1,0:T(8,128)} %bitcast.39, f32[3,8,16,720]{3,2,1,0:T(8,128)S(1)} %slice.152, pred[16]{0:T(512)(128)(4,1)S(1)} %compare_reduce_fusion, pred[]{:T(512)S(6)} %lt.139, f32[3,8,16,720]{3,2,1,0:T(8,128)S(1)} %fusion.8), kind=kLoop, calls=%fused_computation.36 | loop fusion | flops 1382400 | bytes 4423697 | tf_op jit(solution)/shard_map/add | solution.py:154
  140.6 1.4 pad_maximum_fusion
  (131 shorter events, 36.5 us)
Async XLA Ops:
  1.7 10.7 %copy-start.6 = (f32[8,16,720]{2,1,0:T(8,128)S(1)}, f32[8,16,720]{2,1,0:T(8,128)}, u32[]{:S(2)}) copy-start(f32[8,16,720]{2,1,0:T(8,128)} %param.6) | copy-start | bytes 1105924
  3.4 23.4 %collective-permute-start.2 = (f32[48,720]{1,0:T(8,128)}, f32[48,720]{1,0:T(8,128)}, u32[]{:S(2)}, u32[]{:S(2)}) collective-permute-start(f32[48,720]{1,0:T(8,128)} %pad_maximum_fusion.11), channel_id=1, source_target_pairs={{0,8},{8,16},{16,24},{1,9},{9,17},{17,25},{2,10},{10,18},{18,26},{... | collective-permute-start | bytes 414728 | tf_op jit(solution)/shard_map/ppermute | solution.py:79
  9.6 7.6 %copy-start.16 = (s32[32]{0:T(128)S(1)}, s32[32]{0:T(128)}, u32[]{:S(2)}) copy-start(s32[32]{0:T(128)} %param.8) | copy-start | bytes 388
  9.6 7.8 %copy-start.17 = (s32[32]{0:T(128)S(1)}, s32[32]{0:T(128)}, u32[]{:S(2)}) copy-start(s32[32]{0:T(128)} %param.9) | copy-start | bytes 388
  9.6 15.4 %collective-permute-start.3 = (f32[40,720]{1,0:T(8,128)}, f32[40,720]{1,0:T(8,128)}, u32[]{:S(2)}, u32[]{:S(2)}) collective-permute-start(f32[40,720]{1,0:T(8,128)} %bitcast.138), channel_id=1, source_target_pairs={{8,0},{16,8},{24,16},{9,1},{17,9},{25,17},{10,2},{18,10},{26,18},{... | collective-permute-start | bytes 345608 | tf_op jit(solution)/shard_map/ppermute | solution.py:82
  12.8 9.9 %collective-permute-start = (f32[48,16]{0,1:T(8,128)S(1)}, f32[48,16]{0,1:T(8,128)S(1)}, u32[]{:S(2)}, u32[]{:S(2)}) collective-permute-start(f32[48,16]{0,1:T(8,128)S(1)} %pad_maximum_fusion.12), channel_id=1, source_target_pairs={{0,1},{1,2},{2,3},{3,4},{4,5},{5,6},{6,7},{7,0},{8,9},{9,10},{10,1... | collective-permute-start | bytes 9224 | tf_op jit(solution)/shard_map/ppermute | solution.py:75
  13.0 8.4 %collective-permute-start.1 = (f32[40,16]{0,1:T(8,128)S(1)}, f32[40,16]{0,1:T(8,128)S(1)}, u32[]{:S(2)}, u32[]{:S(2)}) collective-permute-start(f32[40,16]{0,1:T(8,128)S(1)} %bitcast.164), channel_id=1, source_target_pairs={{1,0},{2,1},{3,2},{4,3},{5,4},{6,5},{7,6},{0,7},{9,8},{10,9},{11,1... | collective-permute-start | bytes 7688 | tf_op jit(solution)/shard_map/ppermute | solution.py:78
  16.5 4.8 %copy-start.14 = (s32[128]{0:T(128)}, s32[128]{0:T(128)S(1)}, u32[]{:S(2)}) copy-start(s32[128]{0:T(128)S(1)} %iota_multiply_fusion) | copy-start | bytes 1540
  17.4 24.9 %copy-start.13 = (pred[8]{0:T(512)(128)(4,1)}, pred[8]{0:T(512)(128)(4,1)S(1)}, u32[]{:S(2)}) copy-start(pred[8]{0:T(512)(128)(4,1)S(1)} %slice_select_fusion.2) | copy-start | bytes 28
  23.7 0.9 copy-start.7
  24.6 3.0 %copy-start.8 = (f32[8,16,720]{2,1,0:T(8,128)S(1)}, f32[8,16,720]{2,1,0:T(8,128)}, u32[]{:S(2)}) copy-start(f32[8,16,720]{2,1,0:T(8,128)} %param.7) | copy-start | bytes 1105924
  24.9 3.6 %copy-start.15 = (pred[17]{0:T(512)(128)(4,1)S(1)}, pred[17]{0:T(512)(128)(4,1)}, u32[]{:S(2)}) copy-start(pred[17]{0:T(512)(128)(4,1)} %add_compare_fusion) | copy-start | bytes 55
  29.2 13.1 %copy-start = (f32[2,8,16,720]{3,2,1,0:T(8,128)}, f32[2,8,16,720]{3,2,1,0:T(8,128)S(1)}, u32[]{:S(2)}) copy-start(f32[2,8,16,720]{3,2,1,0:T(8,128)S(1)} %fusion.12) | copy-start | bytes 2211844
  29.3 13.0 %collective-permute-start.4 = (f32[16,8,720]{2,1,0:T(8,128)S(1)}, f32[16,8,720]{2,1,0:T(8,128)S(1)}, u32[]{:S(2)}, u32[]{:S(2)}) collective-permute-start(f32[16,8,720]{2,1,0:T(8,128)S(1)} %slice_select_fusion.1), channel_id=1, source_target_pairs={{0,16},{8,24},{16,0},{24,8},{1,17},{9,25},{17,1},{25,9},{2,18},{10... | collective-permute-start | bytes 1105928 | tf_op jit(solution)/shard_map/ppermute | solution.py:134
  35.1 17.4 %collective-permute-start.6 = (f32[24,8,720]{2,1,0:T(8,128)}, f32[24,8,720]{2,1,0:T(8,128)}, u32[]{:S(2)}, u32[]{:S(2)}) collective-permute-start(f32[24,8,720]{2,1,0:T(8,128)} %slice_select_fusion), channel_id=1, source_target_pairs={{0,16},{8,24},{16,0},{24,8},{1,17},{9,25},{17,1},{25,9},{2,18},{10... | collective-permute-start | bytes 1658888 | tf_op jit(solution)/shard_map/ppermute | solution.py:134
  43.2 15.9 %all-to-all-start = ((f32[8,16,720]{2,1,0:T(8,128)}), f32[8,16,720]{2,1,0:T(8,128)S(1)}, u32[]{:S(2)}, u32[]{:S(2)}) async-start(f32[8,16,720]{2,1,0:T(8,128)} %bitcast.151), calls=%async_computation | async-start | bytes 786432 | tf_op jit(solution)/shard_map/all_to_all | solution.py:136
  59.1 21.0 %all-to-all-start.2 = ((f32[8,24,720]{2,1,0:T(8,128)}), f32[8,24,720]{2,1,0:T(8,128)}, u32[]{:S(2)}, u32[]{:S(2)}) async-start(f32[8,24,720]{2,1,0:T(8,128)} %bitcast.149), calls=%async_computation.2 | async-start | bytes 1179648 | tf_op jit(solution)/shard_map/all_to_all | solution.py:136
  65.7 0.9 copy-start.2
  65.7 0.9 copy-start.4
  66.6 1.2 copy-start.9
  66.6 1.2 copy-start.11
  66.6 1.2 copy-start.18
  80.1 21.9 %all-to-all-start.1 = ((f32[16,8,720]{2,0,1:T(8,128)}), f32[16,8,720]{2,0,1:T(8,128)S(1)}, u32[]{:S(2)}, u32[]{:S(2)}) async-start(f32[16,8,720]{2,0,1:T(8,128)} %copy.139), calls=%async_computation.1 | async-start | bytes 786432 | tf_op jit(solution)/shard_map/all_to_all | solution.py:144
  88.1 1.6 %copy-start.1 = (f32[24,45,128]{2,1,0:T(8,128)S(1)}, f32[24,45,128]{2,1,0:T(8,128)}, u32[]{:S(2)}) copy-start(f32[24,45,128]{2,1,0:T(8,128)} %reshape.352) | copy-start | bytes 1658884
  88.1 2.2 %copy-start.3 = (f32[45,128]{1,0:T(8,128)S(1)}, f32[45,128]{1,0:T(8,128)}, u32[]{:S(2)}) copy-start(f32[45,128]{1,0:T(8,128)} %get-tuple-element.15) | copy-start | bytes 69124
  88.1 2.2 %copy-start.5 = (f32[45,128]{1,0:T(8,128)S(1)}, f32[45,128]{1,0:T(8,128)}, u32[]{:S(2)}) copy-start(f32[45,128]{1,0:T(8,128)} %get-tuple-element.16) | copy-start | bytes 69124
  90.9 0.7 copy-start.10
  90.9 0.7 copy-start.12
  101.9 21.7 %all-to-all-start.3 = ((f32[24,8,720]{2,0,1:T(8,128)}), f32[24,8,720]{2,0,1:T(8,128)}, u32[]{:S(2)}, u32[]{:S(2)}) async-start(f32[24,8,720]{2,0,1:T(8,128)} %copy.147), calls=%async_computation.3 | async-start | bytes 1179648 | tf_op jit(solution)/shard_map/all_to_all | solution.py:144
  106.7 18.9 %collective-permute-start.5 = (f32[16,8,720]{2,1,0:T(8,128)S(1)}, f32[16,8,720]{2,1,0:T(8,128)}, u32[]{:S(2)}, u32[]{:S(2)}) collective-permute-start(f32[16,8,720]{2,1,0:T(8,128)S(1)} %bitcast.152), channel_id=1, source_target_pairs={{0,16},{8,24},{16,0},{24,8},{1,17},{9,25},{17,1},{25,9},{2,18},{10... | collective-permute-start | bytes 1105928 | tf_op jit(solution)/shard_map/ppermute | solution.py:147
  123.6 15.4 %collective-permute-start.7 = (f32[24,8,720]{2,1,0:T(8,128)}, f32[24,8,720]{2,1,0:T(8,128)S(1)}, u32[]{:S(2)}, u32[]{:S(2)}) collective-permute-start(f32[24,8,720]{2,1,0:T(8,128)} %bitcast.39), channel_id=1, source_target_pairs={{0,16},{8,24},{16,0},{24,8},{1,17},{9,25},{17,1},{25,9},{2,18},{10... | collective-permute-start | bytes 1658888 | tf_op jit(solution)/shard_map/ppermute | solution.py:147

commit v8 on v4

--- a/solution.py
+++ b/solution.py
@@ -117,7 +117,7 @@
     given = jnp.where(is_low, high_half, low_half)
     kept_filtered = jnp.where(is_low, is_filtered[:half_rows], is_filtered[half_rows:])
     kept_cut = jnp.where(is_low, row_cut[:half_rows], row_cut[half_rows:])
-    chunk_sizes = (stacked * 2 // 5, stacked - stacked * 2 // 5)
+    chunk_sizes = (stacked * 3 // 5, stacked - stacked * 3 // 5)
     returned_parts, handed_parts = [], []
     chunk_start = 0
     for chunk_stack in chunk_sizes:

time: 141 us -> 141 us (level)
  no operation moved by 1% of the time
where the time goes in v8:
time: 141 us
  waiting for transfers between devices  62 us (44%)
  starting transfers between devices  30.3 us (21%)
  local copies, waits for them, and re-layouts  21.4 us (15%)
  matrix products  14.7 us (10%)
  other arithmetic  11.6 us (8%)
    all_to_all x2, waiting for transfers between devices, body(): lax.all_to_all(smoothed, 'lon', split_axis=1, concat_axis=0, tiled=True)  22.8 us
    all_to_all x2, waiting for transfers between devices, body(): lax.all_to_all(pair_lines.reshape(chunk_stack * half_rows, columns), 'lon...  15 us
    ppermute x2, waiting for transfers between devices, body(): taken = lax.ppermute(given[rows_of_part], 'lat', pair_perm)  12.1 us
    ppermute x2, waiting for transfers between devices, body(): handed_parts.append(lax.ppermute(returned, 'lat', pair_perm))  9.78 us
    all_to_all x2, starting transfers between devices, body(): lax.all_to_all(pair_lines.reshape(chunk_stack * half_rows, columns), 'lon...  7.17 us
    all_to_all x2, starting transfers between devices, body(): lax.all_to_all(smoothed, 'lon', split_axis=1, concat_axis=0, tiled=True)  6.99 us
    ppermute x1, starting transfers between devices, body(): lax.ppermute(jnp.concatenate([flat_fields[:, -1], lat_courant[:, -1]], ax...  5.48 us
    concatenate x4, local copies, waits for them, and re-layouts, body(): jnp.concatenate([from_below[:stacked, None], flat_fields, from_above[:, N...  4.4 us
  transfers between devices with their start and end apart: 12, of which 8 were waited for; matrix products, arithmetic and copies ran while one was open for 20% of the time, Pallas kernels for 0%

profile of v8, /device:TPU:0, one launch (start us, length us, event | category | flops | bytes accessed | tf_op | source)
XLA Modules:
  0.0 140.7 jit_solution(17780402658534838869)
XLA Ops:
  0.0 1.8 %fusion.247 = (f32[40,1,720]{2,1,0:T(1,128)S(1)}, f32[40,1,720]{2,1,0:T(1,128)S(1)}) fusion(f32[40,16,720]{2,1,0:T(8,128)} %bitcast.129), kind=kLoop, calls=%fused_computation.289 | loop fusion | bytes 460800 | tf_op jit(solution)/shard_map/slice | solution.py:80
  1.8 1.3 collective-permute-start.3
  4.1 5.5 %collective-permute-start.2 = (f32[48,720]{1,0:T(8,128)S(1)}, f32[48,720]{1,0:T(8,128)S(1)}, u32[]{:S(2)}, u32[]{:S(2)}) collective-permute-start(f32[48,720]{1,0:T(8,128)S(1)} %pad_maximum_fusion.7), channel_id=1, source_target_pairs={{0,8},{8,16},{16,24},{1,9},{9,17},{17,25},{2,10},{10,18},{18,26},{... | collective-permute-start | bytes 414728 | tf_op jit(solution)/shard_map/ppermute | solution.py:79
  9.6 1.2 fusion.246
  11.1 3.0 %collective-permute-start.1 = (f32[40,16]{0,1:T(8,128)S(1)}, f32[40,16]{0,1:T(8,128)S(1)}, u32[]{:S(2)}, u32[]{:S(2)}) collective-permute-start(f32[40,16]{0,1:T(8,128)S(1)} %bitcast.149), channel_id=1, source_target_pairs={{1,0},{2,1},{3,2},{4,3},{5,4},{6,5},{7,6},{0,7},{9,8},{10,9},{11,1... | collective-permute-start | bytes 7688 | tf_op jit(solution)/shard_map/ppermute | solution.py:78
  14.7 1.6 %constant_dynamic-update-slice_fusion = f32[5,8,17,720]{3,2,1,0:T(8,128)} fusion(f32[5,8,16,720]{3,2,1,0:T(8,128)S(1)} %copy-done), kind=kLoop, calls=%fused_computation.186 | loop fusion | bytes 3809280
  17.2 2.3 %collective-permute-done = f32[48,16]{0,1:T(8,128)S(1)} collective-permute-done((f32[48,16]{0,1:T(8,128)S(1)}, f32[48,16]{0,1:T(8,128)S(1)}, u32[]{:S(2)}, u32[]{:S(2)}) %collective-permute-start) | collective-permute-done | bytes 3104 | tf_op jit(solution)/shard_map/ppermute | solution.py:75
  20.4 2.0 %multiply_subtract_fusion = f32[5,8,16,721]{3,2,1,0:T(8,128)} fusion(f32[5,8,16,1]{3,2,1,0:T(8,128)S(1)} %copy.106, f32[5,8,16,720]{3,2,1,0:T(8,128)S(1)} %copy-done, f32[5,8,16,1]{3,2,1,0:T(8,128)S(1)} %copy.103, f32[8,16,721]{2,1,0:T(8,128)S(1)} %get-tuple-element.14, f32[8,16,721]{2,1,0:T(8,128)S(1)} %get-tuple-element.13), kind=kLoop, calls=%fused_computation.13 | loop fusion | flops 3230080 | bytes 4432384 | tf_op jit(solution)/shard_map/sub | solution.py:60
  22.3 1.0 copy.110
  23.4 3.2 %dynamic-update-slice.1 = f32[5,8,17,720]{3,2,1,0:T(8,128)} dynamic-update-slice(f32[5,8,17,720]{3,2,1,0:T(8,128)} %constant_dynamic-update-slice_fusion, f32[5,8,1,720]{3,2,1,0:T(1,128)S(1)} %copy.110, s32[]{} %constant.131, s32[]{} %constant.131, s32[]{} %constant.132, s32[]{} %constant.131) | dynamic-update-slice | bytes 230404 | tf_op jit(solution)/shard_map/concatenate | solution.py:88
  26.9 2.9 %subtract_select_fusion = f32[5,8,17,720]{3,2,1,0:T(8,128)S(1)} fusion(f32[5,8,17,720]{3,2,1,0:T(8,128)} %dynamic-update-slice.1, f32[5,8,16,720]{3,2,1,0:T(8,128)S(1)} %copy-done, f32[5,8,1,720]{3,2,1,0:T(1,128)S(1)} %copy.109, f32[8,17,720]{2,1,0:T(8,128)S(1)} %get-tuple-element.16, f32[8,17,720]{2,1,0:T(8,128)S(1)} %get-tuple-element.15, ...), kind=kLoop, calls=%fused_computation.3 | loop fusion | flops 3427200 | bytes 6658577 | tf_op jit(solution)/shard_map/jit(_where)/select_n | solution.py:95
  30.6 1.1 copy-done.1
  31.7 2.2 %collective-permute-start.5 = (f32[16,8,720]{2,1,0:T(8,128)S(1)}, f32[16,8,720]{2,1,0:T(8,128)S(1)}, u32[]{:S(2)}, u32[]{:S(2)}) collective-permute-start(f32[16,8,720]{2,1,0:T(8,128)S(1)} %slice.125), channel_id=1, source_target_pairs={{0,16},{8,24},{16,0},{24,8},{1,17},{9,25},{17,1},{25,9},{2,18},{10... | collective-permute-start | bytes 1105928 | tf_op jit(solution)/shard_map/ppermute | solution.py:129
  34.9 9.1 %collective-permute-done.5 = f32[16,8,720]{2,1,0:T(8,128)S(1)} collective-permute-done((f32[16,8,720]{2,1,0:T(8,128)S(1)}, f32[16,8,720]{2,1,0:T(8,128)S(1)}, u32[]{:S(2)}, u32[]{:S(2)}) %collective-permute-start.5) | collective-permute-done | bytes 368672 | tf_op jit(solution)/shard_map/ppermute | solution.py:129
  44.8 3.5 %all-to-all-start.2 = ((f32[8,16,720]{2,1,0:T(8,128)}), f32[8,16,720]{2,1,0:T(8,128)S(1)}, u32[]{:S(2)}, u32[]{:S(2)}) async-start(f32[8,16,720]{2,1,0:T(8,128)} %bitcast.138), calls=%async_computation.2 | async-start | bytes 786432 | tf_op jit(solution)/shard_map/all_to_all | solution.py:131
  49.9 3.0 %collective-permute-done.4 = f32[24,8,720]{2,1,0:T(8,128)} collective-permute-done((f32[24,8,720]{2,1,0:T(8,128)}, f32[24,8,720]{2,1,0:T(8,128)}, u32[]{:S(2)}, u32[]{:S(2)}) %collective-permute-start.4) | collective-permute-done | bytes 552992 | tf_op jit(solution)/shard_map/ppermute | solution.py:129
  52.9 2.0 %slice_select_fusion.2 = f32[24,8,720]{2,1,0:T(8,128)} fusion(f32[24,8,720]{2,1,0:T(8,128)} %collective-permute-done.4, f32[40,8,720]{2,1,0:T(8,128)S(1)} %get-tuple-element.7, pred[8]{0:T(512)(128)(4,1)S(1)} %slice_select_fusion.4), kind=kLoop, calls=%fused_computation.40 | loop fusion | flops 138240 | bytes 1658888 | tf_op jit(solution)/shard_map/jit(_where)/select_n | solution.py:130
  55.0 5.8 %all-to-all-done.2 = f32[8,16,720]{2,1,0:T(8,128)S(1)} async-done(((f32[8,16,720]{2,1,0:T(8,128)}), f32[8,16,720]{2,1,0:T(8,128)S(1)}, u32[]{:S(2)}, u32[]{:S(2)}) %all-to-all-start.2) | async-done | bytes 368672 | tf_op jit(solution)/shard_map/all_to_all | solution.py:131
  60.8 3.7 %all-to-all-start = ((f32[8,24,720]{2,1,0:T(8,128)}), f32[8,24,720]{2,1,0:T(8,128)S(1)}, u32[]{:S(2)}, u32[]{:S(2)}) async-start(f32[8,24,720]{2,1,0:T(8,128)} %bitcast.13), calls=%async_computation | async-start | bytes 1179648 | tf_op jit(solution)/shard_map/all_to_all | solution.py:131
  64.5 1.0 copy.113
  65.5 1.2 reshape.334
  71.8 9.2 %all-to-all-done = f32[8,24,720]{2,1,0:T(8,128)S(1)} async-done(((f32[8,24,720]{2,1,0:T(8,128)}), f32[8,24,720]{2,1,0:T(8,128)S(1)}, u32[]{:S(2)}, u32[]{:S(2)}) %all-to-all-start) | async-done | bytes 552992 | tf_op jit(solution)/shard_map/all_to_all | solution.py:131
  89.7 1.0 copy.112
  90.7 3.5 %all-to-all-start.1 = ((f32[24,8,720]{2,0,1:T(8,128)}), f32[24,8,720]{2,0,1:T(8,128)S(1)}, u32[]{:S(2)}, u32[]{:S(2)}) async-start(f32[24,8,720]{2,0,1:T(8,128)} %copy.112), calls=%async_computation.1 | async-start | bytes 1179648 | tf_op jit(solution)/shard_map/all_to_all | solution.py:139
  94.3 1.6 %fusion.66 = f32[16,45,128]{2,1,0:T(8,128)S(1)} fusion(f32[16,45,128]{2,1,0:T(8,128)} %copy-done.12), kind=kOutput, calls=%fused_computation.109 | convolution fusion | flops 71008256 | bytes 737280 | tf_op jit(solution)/shard_map/ljk,kn->ljn/dot_general | solution.py:49
  98.6 12.4 %all-to-all-done.1 = f32[24,8,720]{2,0,1:T(8,128)S(1)} async-done(((f32[24,8,720]{2,0,1:T(8,128)}), f32[24,8,720]{2,0,1:T(8,128)S(1)}, u32[]{:S(2)}, u32[]{:S(2)}) %all-to-all-start.1) | async-done | bytes 552992 | tf_op jit(solution)/shard_map/all_to_all | solution.py:139
  110.9 3.5 %all-to-all-start.3 = ((f32[16,8,720]{2,0,1:T(8,128)}), f32[16,8,720]{2,0,1:T(8,128)S(1)}, u32[]{:S(2)}, u32[]{:S(2)}) async-start(f32[16,8,720]{2,0,1:T(8,128)} %copy.114), calls=%async_computation.3 | async-start | bytes 786432 | tf_op jit(solution)/shard_map/all_to_all | solution.py:139
  114.4 2.1 %collective-permute-start.6 = (f32[24,8,720]{2,1,0:T(8,128)S(1)}, f32[24,8,720]{2,1,0:T(8,128)S(1)}, u32[]{:S(2)}, u32[]{:S(2)}) collective-permute-start(f32[24,8,720]{2,1,0:T(8,128)S(1)} %bitcast.135), channel_id=1, source_target_pairs={{0,16},{8,24},{16,0},{24,8},{1,17},{9,25},{17,1},{25,9},{2,18},{10... | collective-permute-start | bytes 1658888 | tf_op jit(solution)/shard_map/ppermute | solution.py:143
  116.5 10.4 %all-to-all-done.3 = f32[16,8,720]{2,0,1:T(8,128)S(1)} async-done(((f32[16,8,720]{2,0,1:T(8,128)}), f32[16,8,720]{2,0,1:T(8,128)S(1)}, u32[]{:S(2)}, u32[]{:S(2)}) %all-to-all-start.3) | async-done | bytes 368672 | tf_op jit(solution)/shard_map/all_to_all | solution.py:139
  126.9 2.0 %collective-permute-start.7 = (f32[16,8,720]{2,1,0:T(8,128)S(1)}, f32[16,8,720]{2,1,0:T(8,128)S(1)}, u32[]{:S(2)}, u32[]{:S(2)}) collective-permute-start(f32[16,8,720]{2,1,0:T(8,128)S(1)} %bitcast.139), channel_id=1, source_target_pairs={{0,16},{8,24},{16,0},{24,8},{1,17},{9,25},{17,1},{25,9},{2,18},{10... | collective-permute-start | bytes 1105928 | tf_op jit(solution)/shard_map/ppermute | solution.py:143
  128.9 9.8 %collective-permute-done.7 = f32[16,8,720]{2,1,0:T(8,128)S(1)} collective-permute-done((f32[16,8,720]{2,1,0:T(8,128)S(1)}, f32[16,8,720]{2,1,0:T(8,128)S(1)}, u32[]{:S(2)}, u32[]{:S(2)}) %collective-permute-start.7) | collective-permute-done | bytes 368672 | tf_op jit(solution)/shard_map/ppermute | solution.py:143
  138.8 1.9 %fusion.3 = f32[5,8,16,720]{3,2,1,0:T(8,128)} fusion(f32[5,8,16,720]{3,2,1,0:T(8,128)S(1)} %copy-done, f32[5,8,16,720]{3,2,1,0:T(8,128)S(1)} %copy-done.2, f32[5,8,8,720]{3,2,1,0:T(8,128)S(1)} %bitcast.133, f32[5,8,8,720]{3,2,1,0:T(8,128)S(1)} %bitcast.132, pred[16]{0:T(512)(128)(4,1)S(1)} %compare_reduce_fusion, pred[]{:T(512)S(6)} %lt.139), kind=kLoop, calls=%fused_computation.12 | loop fusion | flops 2304000 | bytes 7372817 | tf_op jit(solution)/shard_map/add | solution.py:152
  (121 shorter events, 24.2 us)
Async XLA Ops:
  0.0 14.7 %copy-start = (f32[5,8,16,720]{3,2,1,0:T(8,128)S(1)}, f32[5,8,16,720]{3,2,1,0:T(8,128)}, u32[]{:S(2)}) copy-start(f32[5,8,16,720]{3,2,1,0:T(8,128)} %param.5) | copy-start | bytes 5529604
  0.0 14.1 %copy-start.13 = (f32[8,16,720]{2,1,0:T(8,128)S(1)}, f32[8,16,720]{2,1,0:T(8,128)}, u32[]{:S(2)}) copy-start(f32[8,16,720]{2,1,0:T(8,128)} %param.6) | copy-start | bytes 1105924
  1.8 20.5 %collective-permute-start.3 = (f32[40,720]{1,0:T(8,128)S(1)}, f32[40,720]{1,0:T(8,128)}, u32[]{:S(2)}, u32[]{:S(2)}) collective-permute-start(f32[40,720]{1,0:T(8,128)S(1)} %bitcast.142), channel_id=1, source_target_pairs={{8,0},{16,8},{24,16},{9,1},{17,9},{25,17},{10,2},{18,10},{26,18},{... | collective-permute-start | bytes 345608 | tf_op jit(solution)/shard_map/ppermute | solution.py:82
  4.1 22.5 %collective-permute-start.2 = (f32[48,720]{1,0:T(8,128)S(1)}, f32[48,720]{1,0:T(8,128)S(1)}, u32[]{:S(2)}, u32[]{:S(2)}) collective-permute-start(f32[48,720]{1,0:T(8,128)S(1)} %pad_maximum_fusion.7), channel_id=1, source_target_pairs={{0,8},{8,16},{16,24},{1,9},{9,17},{17,25},{2,10},{10,18},{18,26},{... | collective-permute-start | bytes 414728 | tf_op jit(solution)/shard_map/ppermute | solution.py:79
  11.1 5.8 %collective-permute-start.1 = (f32[40,16]{0,1:T(8,128)S(1)}, f32[40,16]{0,1:T(8,128)S(1)}, u32[]{:S(2)}, u32[]{:S(2)}) collective-permute-start(f32[40,16]{0,1:T(8,128)S(1)} %bitcast.149), channel_id=1, source_target_pairs={{1,0},{2,1},{3,2},{4,3},{5,4},{6,5},{7,6},{0,7},{9,8},{10,9},{11,1... | collective-permute-start | bytes 7688 | tf_op jit(solution)/shard_map/ppermute | solution.py:78
  14.6 1.6 %copy-start.19 = (s32[32]{0:T(128)S(1)}, s32[32]{0:T(128)}, u32[]{:S(2)}) copy-start(s32[32]{0:T(128)} %param.8) | copy-start | bytes 388
  14.6 1.9 %copy-start.20 = (s32[32]{0:T(128)S(1)}, s32[32]{0:T(128)}, u32[]{:S(2)}) copy-start(s32[32]{0:T(128)} %param.9) | copy-start | bytes 388
  14.6 4.9 %collective-permute-start = (f32[48,16]{0,1:T(8,128)S(1)}, f32[48,16]{0,1:T(8,128)S(1)}, u32[]{:S(2)}, u32[]{:S(2)}) collective-permute-start(f32[48,16]{0,1:T(8,128)S(1)} %pad_maximum_fusion.8), channel_id=1, source_target_pairs={{0,1},{1,2},{2,3},{3,4},{4,5},{5,6},{6,7},{7,0},{8,9},{9,10},{10,1... | collective-permute-start | bytes 9224 | tf_op jit(solution)/shard_map/ppermute | solution.py:75
  20.4 6.4 %copy-start.14 = (f32[8,16,720]{2,1,0:T(8,128)S(1)}, f32[8,16,720]{2,1,0:T(8,128)}, u32[]{:S(2)}) copy-start(f32[8,16,720]{2,1,0:T(8,128)} %param.7) | copy-start | bytes 1105924
  26.9 2.9 %copy-start.3 = (f32[5,8,16,721]{3,2,1,0:T(8,128)S(1)}, f32[5,8,16,721]{3,2,1,0:T(8,128)}, u32[]{:S(2)}) copy-start(f32[5,8,16,721]{3,2,1,0:T(8,128)} %multiply_subtract_fusion) | copy-start | bytes 5537284
  30.4 1.3 copy-start.1
  31.7 12.3 %collective-permute-start.5 = (f32[16,8,720]{2,1,0:T(8,128)S(1)}, f32[16,8,720]{2,1,0:T(8,128)S(1)}, u32[]{:S(2)}, u32[]{:S(2)}) collective-permute-start(f32[16,8,720]{2,1,0:T(8,128)S(1)} %slice.125), channel_id=1, source_target_pairs={{0,16},{8,24},{16,0},{24,8},{1,17},{9,25},{17,1},{25,9},{2,18},{10... | collective-permute-start | bytes 1105928 | tf_op jit(solution)/shard_map/ppermute | solution.py:129
  34.0 35.8 %copy-start.15 = (f32[45,128]{1,0:T(8,128)}, f32[45,128]{1,0:T(8,128)S(1)}, u32[]{:S(2)}) copy-start(f32[45,128]{1,0:T(8,128)S(1)} %broadcast_maximum_fusion) | copy-start | bytes 69124
  34.9 18.0 %collective-permute-start.4 = (f32[24,8,720]{2,1,0:T(8,128)}, f32[24,8,720]{2,1,0:T(8,128)}, u32[]{:S(2)}, u32[]{:S(2)}) collective-permute-start(f32[24,8,720]{2,1,0:T(8,128)} %slice.123), channel_id=1, source_target_pairs={{0,16},{8,24},{16,0},{24,8},{1,17},{9,25},{17,1},{25,9},{2,18},{10... | collective-permute-start | bytes 1658888 | tf_op jit(solution)/shard_map/ppermute | solution.py:129
  44.8 15.9 %all-to-all-start.2 = ((f32[8,16,720]{2,1,0:T(8,128)}), f32[8,16,720]{2,1,0:T(8,128)S(1)}, u32[]{:S(2)}, u32[]{:S(2)}) async-start(f32[8,16,720]{2,1,0:T(8,128)} %bitcast.138), calls=%async_computation.2 | async-start | bytes 786432 | tf_op jit(solution)/shard_map/all_to_all | solution.py:131
  49.8 20.1 %copy-start.4 = (f32[45,128]{1,0:T(8,128)}, f32[45,128]{1,0:T(8,128)S(1)}, u32[]{:S(2)}) copy-start(f32[45,128]{1,0:T(8,128)S(1)} %get-tuple-element.17) | copy-start | bytes 69124
  49.8 20.1 %copy-start.7 = (f32[45,128]{1,0:T(8,128)}, f32[45,128]{1,0:T(8,128)S(1)}, u32[]{:S(2)}) copy-start(f32[45,128]{1,0:T(8,128)S(1)} %get-tuple-element.18) | copy-start | bytes 69124
  49.9 20.0 %copy-start.17 = (f32[45,128]{1,0:T(8,128)}, f32[45,128]{1,0:T(8,128)S(1)}, u32[]{:S(2)}) copy-start(f32[45,128]{1,0:T(8,128)S(1)} %fusion.100) | copy-start | bytes 69124
  60.8 20.2 %all-to-all-start = ((f32[8,24,720]{2,1,0:T(8,128)}), f32[8,24,720]{2,1,0:T(8,128)S(1)}, u32[]{:S(2)}, u32[]{:S(2)}) async-start(f32[8,24,720]{2,1,0:T(8,128)} %bitcast.13), calls=%async_computation | async-start | bytes 1179648 | tf_op jit(solution)/shard_map/all_to_all | solution.py:131
  68.7 1.8 %copy-start.10 = (f32[16,45,128]{2,1,0:T(8,128)}, f32[16,45,128]{2,1,0:T(8,128)S(1)}, u32[]{:S(2)}) copy-start(f32[16,45,128]{2,1,0:T(8,128)S(1)} %fusion.9) | copy-start | bytes 1105924
  81.6 1.0 copy-start.5
  81.6 1.0 copy-start.8
  82.6 1.3 copy-start.16
  82.6 1.3 copy-start.18
  89.7 6.1 %copy-start.11 = (f32[16,45,128]{2,1,0:T(8,128)S(1)}, f32[16,45,128]{2,1,0:T(8,128)}, u32[]{:S(2)}) copy-start(f32[16,45,128]{2,1,0:T(8,128)} %copy-done.10) | copy-start | bytes 1105924
  89.7 6.7 %copy-start.6 = (f32[45,128]{1,0:T(8,128)S(1)}, f32[45,128]{1,0:T(8,128)}, u32[]{:S(2)}) copy-start(f32[45,128]{1,0:T(8,128)} %copy-done.4) | copy-start | bytes 69124
  89.7 6.7 %copy-start.9 = (f32[45,128]{1,0:T(8,128)S(1)}, f32[45,128]{1,0:T(8,128)}, u32[]{:S(2)}) copy-start(f32[45,128]{1,0:T(8,128)} %copy-done.7) | copy-start | bytes 69124
  90.7 20.2 %all-to-all-start.1 = ((f32[24,8,720]{2,0,1:T(8,128)}), f32[24,8,720]{2,0,1:T(8,128)S(1)}, u32[]{:S(2)}, u32[]{:S(2)}) async-start(f32[24,8,720]{2,0,1:T(8,128)} %copy.112), calls=%async_computation.1 | async-start | bytes 1179648 | tf_op jit(solution)/shard_map/all_to_all | solution.py:139
  110.9 15.9 %all-to-all-start.3 = ((f32[16,8,720]{2,0,1:T(8,128)}), f32[16,8,720]{2,0,1:T(8,128)S(1)}, u32[]{:S(2)}, u32[]{:S(2)}) async-start(f32[16,8,720]{2,0,1:T(8,128)} %copy.114), calls=%async_computation.3 | async-start | bytes 786432 | tf_op jit(solution)/shard_map/all_to_all | solution.py:139
  114.4 24.3 %collective-permute-start.6 = (f32[24,8,720]{2,1,0:T(8,128)S(1)}, f32[24,8,720]{2,1,0:T(8,128)S(1)}, u32[]{:S(2)}, u32[]{:S(2)}) collective-permute-start(f32[24,8,720]{2,1,0:T(8,128)S(1)} %bitcast.135), channel_id=1, source_target_pairs={{0,16},{8,24},{16,0},{24,8},{1,17},{9,25},{17,1},{25,9},{2,18},{10... | collective-permute-start | bytes 1658888 | tf_op jit(solution)/shard_map/ppermute | solution.py:143
  126.9 11.9 %copy-start.2 = (f32[5,8,16,720]{3,2,1,0:T(8,128)S(1)}, f32[5,8,16,720]{3,2,1,0:T(8,128)}, u32[]{:S(2)}) copy-start(f32[5,8,16,720]{3,2,1,0:T(8,128)} %copy-done.1) | copy-start | bytes 5529604
  126.9 11.8 %collective-permute-start.7 = (f32[16,8,720]{2,1,0:T(8,128)S(1)}, f32[16,8,720]{2,1,0:T(8,128)S(1)}, u32[]{:S(2)}, u32[]{:S(2)}) collective-permute-start(f32[16,8,720]{2,1,0:T(8,128)S(1)} %bitcast.139), channel_id=1, source_target_pairs={{0,16},{8,24},{16,0},{24,8},{1,17},{9,25},{17,1},{25,9},{2,18},{10... | collective-permute-start | bytes 1105928 | tf_op jit(solution)/shard_map/ppermute | solution.py:143
  (1 other events, 0.7 us)

commit v9 on v8

--- a/solution.py
+++ b/solution.py
@@ -117,7 +117,7 @@
     given = jnp.where(is_low, high_half, low_half)
     kept_filtered = jnp.where(is_low, is_filtered[:half_rows], is_filtered[half_rows:])
     kept_cut = jnp.where(is_low, row_cut[:half_rows], row_cut[half_rows:])
-    chunk_sizes = (stacked * 3 // 5, stacked - stacked * 3 // 5)
+    chunk_sizes = (stacked // 5, stacked // 2, stacked - stacked // 5 - stacked // 2)
     returned_parts, handed_parts = [], []
     chunk_start = 0
     for chunk_stack in chunk_sizes:

time: 141 us -> 166 us (1.18)
  starting transfers between devices: 30.3 us -> 41.4 us
  other arithmetic: 11.6 us -> 18.4 us
  matrix products: 14.7 us -> 18.4 us
  local copies, waits for them, and re-layouts: 21.4 us -> 24.4 us
    all_to_all x2 -> x3, starting transfers between devices: 7.17 us -> 11.9 us  [body(): lax.all_to_all(pair_lines.reshape(chunk_stack * half_rows, columns), 'lon...]
    ppermute x2 -> x3, waiting for transfers between devices: 9.78 us -> 14.1 us  [body(): handed_parts.append(lax.ppermute(returned, 'lat', pair_perm))]
    all_to_all x2 -> x3, starting transfers between devices: 6.99 us -> 11.2 us  [body(): lax.all_to_all(smoothed, 'lon', split_axis=1, concat_axis=0, tiled=True)]
    ppermute x2 -> x3, waiting for transfers between devices: 12.1 us -> 8.07 us  [body(): taken = lax.ppermute(given[rows_of_part], 'lat', pair_perm)]
    ppermute x1, waiting for transfers between devices: 2.3 us -> 0.01 us  [body(): lax.ppermute(jnp.concatenate([flat_fields[..., -1], lon_courant[..., -1]]...]
    ppermute x2 -> x3, starting transfers between devices: 2.24 us -> 4.3 us  [body(): taken = lax.ppermute(given[rows_of_part], 'lat', pair_perm)]
    all_to_all x2 -> x5, local copies, waits for them, and re-layouts: 1.17 us -> 2.97 us  [body(): lax.all_to_all(pair_lines.reshape(chunk_stack * half_rows, columns), 'lon...]
    unnamed x46 -> x36, local copies, waits for them, and re-layouts: 3.51 us -> 1.85 us
  transfers between devices with their start and end apart: 12 -> 16, of which waited for: 8 -> 9; matrix products, arithmetic and copies ran while one was open for 20% -> 30% of each run, Pallas kernels for 0% -> 0%
where the time goes in v9:
time: 166 us; the launch traced here: 164 us
  waiting for transfers between devices  61.2 us (37%)
  starting transfers between devices  41.4 us (25%)
  local copies, waits for them, and re-layouts  24.4 us (15%)
  other arithmetic  18.4 us (11%)
  matrix products  18.4 us (11%)
    all_to_all x3, waiting for transfers between devices, body(): lax.all_to_all(smoothed, 'lon', split_axis=1, concat_axis=0, tiled=True)  22.7 us
    all_to_all x3, waiting for transfers between devices, body(): lax.all_to_all(pair_lines.reshape(chunk_stack * half_rows, columns), 'lon...  16.3 us
    ppermute x3, waiting for transfers between devices, body(): handed_parts.append(lax.ppermute(returned, 'lat', pair_perm))  14.1 us
    all_to_all x3, starting transfers between devices, body(): lax.all_to_all(pair_lines.reshape(chunk_stack * half_rows, columns), 'lon...  11.9 us
    all_to_all x3, starting transfers between devices, body(): lax.all_to_all(smoothed, 'lon', split_axis=1, concat_axis=0, tiled=True)  11.2 us
    ppermute x3, waiting for transfers between devices, body(): taken = lax.ppermute(given[rows_of_part], 'lat', pair_perm)  8.07 us
    ppermute x1, starting transfers between devices, body(): lax.ppermute(jnp.concatenate([flat_fields[:, -1], lat_courant[:, -1]], ax...  5.48 us
    concatenate x4, local copies, waits for them, and re-layouts, body(): jnp.concatenate([from_below[:stacked, None], flat_fields, from_above[:, N...  4.39 us
  transfers between devices with their start and end apart: 16, of which 9 were waited for; matrix products, arithmetic and copies ran while one was open for 30% of the time, Pallas kernels for 0%

profile of v9, /device:TPU:0, one launch (start us, length us, event | category | flops | bytes accessed | tf_op | source)
XLA Modules:
  0.0 164.5 jit_solution(10477602997953419942)
XLA Ops:
  0.0 1.8 %fusion.354 = (f32[40,1,720]{2,1,0:T(1,128)S(1)}, f32[40,1,720]{2,1,0:T(1,128)S(1)}) fusion(f32[40,16,720]{2,1,0:T(8,128)} %bitcast.169), kind=kLoop, calls=%fused_computation.396 | loop fusion | bytes 460800 | tf_op jit(solution)/shard_map/slice | solution.py:80
  1.8 1.3 collective-permute-start.3
  4.1 5.5 %collective-permute-start.2 = (f32[48,720]{1,0:T(8,128)S(1)}, f32[48,720]{1,0:T(8,128)S(1)}, u32[]{:S(2)}, u32[]{:S(2)}) collective-permute-start(f32[48,720]{1,0:T(8,128)S(1)} %pad_maximum_fusion.7), channel_id=1, source_target_pairs={{0,8},{8,16},{16,24},{1,9},{9,17},{17,25},{2,10},{10,18},{18,26},{... | collective-permute-start | bytes 414728 | tf_op jit(solution)/shard_map/ppermute | solution.py:79
  9.6 1.2 fusion.353
  11.1 3.0 %collective-permute-start.1 = (f32[40,16]{0,1:T(8,128)S(1)}, f32[40,16]{0,1:T(8,128)S(1)}, u32[]{:S(2)}, u32[]{:S(2)}) collective-permute-start(f32[40,16]{0,1:T(8,128)S(1)} %bitcast.187), channel_id=1, source_target_pairs={{1,0},{2,1},{3,2},{4,3},{5,4},{6,5},{7,6},{0,7},{9,8},{10,9},{11,1... | collective-permute-start | bytes 7688 | tf_op jit(solution)/shard_map/ppermute | solution.py:78
  14.7 1.4 constant_dynamic-update-slice_fusion
  22.9 2.0 %multiply_subtract_fusion = f32[5,8,16,721]{3,2,1,0:T(8,128)} fusion(f32[5,8,16,1]{3,2,1,0:T(8,128)S(1)} %copy.121, f32[5,8,16,720]{3,2,1,0:T(8,128)S(1)} %copy-done, f32[5,8,16,1]{3,2,1,0:T(8,128)S(1)} %copy.118, f32[8,16,721]{2,1,0:T(8,128)S(1)} %get-tuple-element.14, f32[8,16,721]{2,1,0:T(8,128)S(1)} %get-tuple-element.13), kind=kLoop, calls=%fused_computation.14 | loop fusion | flops 3230080 | bytes 4432384 | tf_op jit(solution)/shard_map/sub | solution.py:60
  25.9 3.2 %dynamic-update-slice.1 = f32[5,8,17,720]{3,2,1,0:T(8,128)} dynamic-update-slice(f32[5,8,17,720]{3,2,1,0:T(8,128)} %constant_dynamic-update-slice_fusion, f32[5,8,1,720]{3,2,1,0:T(1,128)S(1)} %copy.125, s32[]{} %constant.154, s32[]{} %constant.154, s32[]{} %constant.155, s32[]{} %constant.154) | dynamic-update-slice | bytes 230404 | tf_op jit(solution)/shard_map/concatenate | solution.py:88
  29.4 2.9 %subtract_select_fusion = f32[5,8,17,720]{3,2,1,0:T(8,128)S(1)} fusion(f32[5,8,17,720]{3,2,1,0:T(8,128)} %dynamic-update-slice.1, f32[5,8,16,720]{3,2,1,0:T(8,128)S(1)} %copy-done, f32[5,8,1,720]{3,2,1,0:T(1,128)S(1)} %copy.124, f32[8,17,720]{2,1,0:T(8,128)S(1)} %get-tuple-element.16, f32[8,17,720]{2,1,0:T(8,128)S(1)} %get-tuple-element.15, ...), kind=kLoop, calls=%fused_computation.4 | loop fusion | flops 3427200 | bytes 6658577 | tf_op jit(solution)/shard_map/jit(_where)/select_n | solution.py:95
  32.9 1.3 slice_select_fusion.1
  34.5 2.2 %collective-permute-start.4 = (f32[8,8,720]{2,1,0:T(8,128)S(1)}, f32[8,8,720]{2,1,0:T(8,128)}, u32[]{:S(2)}, u32[]{:S(2)}) collective-permute-start(f32[8,8,720]{2,1,0:T(8,128)S(1)} %slice.133), channel_id=1, source_target_pairs={{0,16},{8,24},{16,0},{24,8},{1,17},{9,25},{17,1},{25,9},{2,18},{10... | collective-permute-start | bytes 552968 | tf_op jit(solution)/shard_map/ppermute | solution.py:129
  40.0 2.0 %collective-permute-start.5 = (f32[20,8,720]{2,1,0:T(8,128)}, f32[20,8,720]{2,1,0:T(8,128)}, u32[]{:S(2)}, u32[]{:S(2)}) collective-permute-start(f32[20,8,720]{2,1,0:T(8,128)} %slice.135), channel_id=1, source_target_pairs={{0,16},{8,24},{16,0},{24,8},{1,17},{9,25},{17,1},{25,9},{2,18},{10... | collective-permute-start | bytes 1382408 | tf_op jit(solution)/shard_map/ppermute | solution.py:129
  42.7 1.8 %slice_select_fusion.4 = f32[8,8,720]{2,1,0:T(8,128)} fusion(f32[8,8,720]{2,1,0:T(8,128)} %collective-permute-done.4, f32[40,8,720]{2,1,0:T(8,128)} %get-tuple-element.7, pred[8]{0:T(512)(128)(4,1)S(1)} %copy-done.12), kind=kLoop, calls=%fused_computation.97 | loop fusion | flops 46080 | bytes 552968 | tf_op jit(solution)/shard_map/jit(_where)/select_n | solution.py:130
  44.5 4.2 %all-to-all-start = ((f32[8,8,720]{2,1,0:T(8,128)}), f32[8,8,720]{2,1,0:T(8,128)}, u32[]{:S(2)}, u32[]{:S(2)}) async-start(f32[8,8,720]{2,1,0:T(8,128)} %slice_select_fusion.4), calls=%async_computation | async-start | bytes 393216 | tf_op jit(solution)/shard_map/all_to_all | solution.py:131
  49.0 1.1 slice_select_fusion.3
  50.9 7.1 %collective-permute-done.5 = f32[20,8,720]{2,1,0:T(8,128)} collective-permute-done((f32[20,8,720]{2,1,0:T(8,128)}, f32[20,8,720]{2,1,0:T(8,128)}, u32[]{:S(2)}, u32[]{:S(2)}) %collective-permute-start.5) | collective-permute-done | bytes 460832 | tf_op jit(solution)/shard_map/ppermute | solution.py:129
  58.0 1.1 slice_select_fusion.2
  60.0 3.9 %all-to-all-start.4 = ((f32[8,12,720]{2,1,0:T(8,128)}), f32[8,12,720]{2,1,0:T(8,128)S(1)}, u32[]{:S(2)}, u32[]{:S(2)}) async-start(f32[8,12,720]{2,1,0:T(8,128)} %all_to_all.81), calls=%async_computation.4 | async-start | bytes 786432 | tf_op jit(solution)/shard_map/all_to_all | solution.py:131
  68.3 1.2 convolution_add_fusion.4
  69.4 7.1 %all-to-all-done.4 = f32[8,12,720]{2,1,0:T(8,128)S(1)} async-done(((f32[8,12,720]{2,1,0:T(8,128)}), f32[8,12,720]{2,1,0:T(8,128)S(1)}, u32[]{:S(2)}, u32[]{:S(2)}) %all-to-all-start.4) | async-done | bytes 276512 | tf_op jit(solution)/shard_map/all_to_all | solution.py:131
  76.5 3.7 %all-to-all-start.2 = ((f32[8,20,720]{2,1,0:T(8,128)}), f32[8,20,720]{2,1,0:T(8,128)S(1)}, u32[]{:S(2)}, u32[]{:S(2)}) async-start(f32[8,20,720]{2,1,0:T(8,128)} %all_to_all.75), calls=%async_computation.2 | async-start | bytes 1179648 | tf_op jit(solution)/shard_map/all_to_all | solution.py:131
  87.5 9.2 %all-to-all-done.2 = f32[8,20,720]{2,1,0:T(8,128)S(1)} async-done(((f32[8,20,720]{2,1,0:T(8,128)}), f32[8,20,720]{2,1,0:T(8,128)S(1)}, u32[]{:S(2)}, u32[]{:S(2)}) %all-to-all-start.2) | async-done | bytes 460832 | tf_op jit(solution)/shard_map/all_to_all | solution.py:131
  96.7 4.3 %all-to-all-start.5 = ((f32[12,8,720]{2,0,1:T(8,128)}), f32[12,8,720]{2,0,1:T(8,128)}, u32[]{:S(2)}, u32[]{:S(2)}) async-start(f32[12,8,720]{2,0,1:T(8,128)} %copy.131), calls=%async_computation.5 | async-start | bytes 786432 | tf_op jit(solution)/shard_map/all_to_all | solution.py:139
  109.8 3.6 %all-to-all-done.5 = f32[12,8,720]{2,0,1:T(8,128)} async-done(((f32[12,8,720]{2,0,1:T(8,128)}), f32[12,8,720]{2,0,1:T(8,128)}, u32[]{:S(2)}, u32[]{:S(2)}) %all-to-all-start.5) | async-done | bytes 276512 | tf_op jit(solution)/shard_map/all_to_all | solution.py:139
  113.4 3.5 %all-to-all-start.3 = ((f32[20,8,720]{2,0,1:T(8,128)}), f32[20,8,720]{2,0,1:T(8,128)S(1)}, u32[]{:S(2)}, u32[]{:S(2)}) async-start(f32[20,8,720]{2,0,1:T(8,128)} %copy.129), calls=%async_computation.3 | async-start | bytes 1179648 | tf_op jit(solution)/shard_map/all_to_all | solution.py:139
  119.5 14.1 %all-to-all-done.3 = f32[20,8,720]{2,0,1:T(8,128)S(1)} async-done(((f32[20,8,720]{2,0,1:T(8,128)}), f32[20,8,720]{2,0,1:T(8,128)S(1)}, u32[]{:S(2)}, u32[]{:S(2)}) %all-to-all-start.3) | async-done | bytes 460832 | tf_op jit(solution)/shard_map/all_to_all | solution.py:139
  133.6 3.4 %all-to-all-start.1 = ((f32[8,8,720]{2,0,1:T(8,128)}), f32[8,8,720]{2,0,1:T(8,128)S(1)}, u32[]{:S(2)}, u32[]{:S(2)}) async-start(f32[8,8,720]{2,0,1:T(8,128)} %copy.127), calls=%async_computation.1 | async-start | bytes 393216 | tf_op jit(solution)/shard_map/all_to_all | solution.py:139
  137.1 2.1 %collective-permute-start.8 = (f32[20,8,720]{2,1,0:T(8,128)S(1)}, f32[20,8,720]{2,1,0:T(8,128)}, u32[]{:S(2)}, u32[]{:S(2)}) collective-permute-start(f32[20,8,720]{2,1,0:T(8,128)S(1)} %reshape.400), channel_id=1, source_target_pairs={{0,16},{8,24},{16,0},{24,8},{1,17},{9,25},{17,1},{25,9},{2,18},{10... | collective-permute-start | bytes 1382408 | tf_op jit(solution)/shard_map/ppermute | solution.py:143
  140.3 5.0 %all-to-all-done.1 = f32[8,8,720]{2,0,1:T(8,128)S(1)} async-done(((f32[8,8,720]{2,0,1:T(8,128)}), f32[8,8,720]{2,0,1:T(8,128)S(1)}, u32[]{:S(2)}, u32[]{:S(2)}) %all-to-all-start.1) | async-done | bytes 184352 | tf_op jit(solution)/shard_map/all_to_all | solution.py:139
  145.3 2.0 %collective-permute-start.7 = (f32[8,8,720]{2,1,0:T(8,128)S(1)}, f32[8,8,720]{2,1,0:T(8,128)S(1)}, u32[]{:S(2)}, u32[]{:S(2)}) collective-permute-start(f32[8,8,720]{2,1,0:T(8,128)S(1)} %bitcast.177), channel_id=1, source_target_pairs={{0,16},{8,24},{16,0},{24,8},{1,17},{9,25},{17,1},{25,9},{2,18},{10... | collective-permute-start | bytes 552968 | tf_op jit(solution)/shard_map/ppermute | solution.py:143
  147.3 14.1 %collective-permute-done.7 = f32[8,8,720]{2,1,0:T(8,128)S(1)} collective-permute-done((f32[8,8,720]{2,1,0:T(8,128)S(1)}, f32[8,8,720]{2,1,0:T(8,128)S(1)}, u32[]{:S(2)}, u32[]{:S(2)}) %collective-permute-start.7) | collective-permute-done | bytes 184352 | tf_op jit(solution)/shard_map/ppermute | solution.py:143
  162.6 1.9 %fusion.3 = f32[5,8,16,720]{3,2,1,0:T(8,128)} fusion(f32[5,8,16,720]{3,2,1,0:T(8,128)S(1)} %copy-done, f32[5,8,16,720]{3,2,1,0:T(8,128)S(1)} %copy-done.2, f32[5,8,8,720]{3,2,1,0:T(8,128)S(1)} %bitcast.173, f32[5,8,8,720]{3,2,1,0:T(8,128)S(1)} %bitcast.172, pred[16]{0:T(512)(128)(4,1)S(1)} %compare_reduce_fusion, pred[]{:T(512)S(6)} %lt.201), kind=kLoop, calls=%fused_computation.13 | loop fusion | flops 2304000 | bytes 7372817 | tf_op jit(solution)/shard_map/add | solution.py:152
  (144 shorter events, 41.5 us)
Async XLA Ops:
  0.0 14.7 %copy-start = (f32[5,8,16,720]{3,2,1,0:T(8,128)S(1)}, f32[5,8,16,720]{3,2,1,0:T(8,128)}, u32[]{:S(2)}) copy-start(f32[5,8,16,720]{3,2,1,0:T(8,128)} %param.5) | copy-start | bytes 5529604
  0.0 14.1 %copy-start.8 = (f32[8,16,720]{2,1,0:T(8,128)S(1)}, f32[8,16,720]{2,1,0:T(8,128)}, u32[]{:S(2)}) copy-start(f32[8,16,720]{2,1,0:T(8,128)} %param.6) | copy-start | bytes 1105924
  1.8 23.0 %collective-permute-start.3 = (f32[40,720]{1,0:T(8,128)S(1)}, f32[40,720]{1,0:T(8,128)}, u32[]{:S(2)}, u32[]{:S(2)}) collective-permute-start(f32[40,720]{1,0:T(8,128)S(1)} %bitcast.180), channel_id=1, source_target_pairs={{8,0},{16,8},{24,16},{9,1},{17,9},{25,17},{10,2},{18,10},{26,18},{... | collective-permute-start | bytes 345608 | tf_op jit(solution)/shard_map/ppermute | solution.py:82
  4.1 24.9 %collective-permute-start.2 = (f32[48,720]{1,0:T(8,128)S(1)}, f32[48,720]{1,0:T(8,128)S(1)}, u32[]{:S(2)}, u32[]{:S(2)}) collective-permute-start(f32[48,720]{1,0:T(8,128)S(1)} %pad_maximum_fusion.7), channel_id=1, source_target_pairs={{0,8},{8,16},{16,24},{1,9},{9,17},{17,25},{2,10},{10,18},{18,26},{... | collective-permute-start | bytes 414728 | tf_op jit(solution)/shard_map/ppermute | solution.py:79
  11.1 9.3 %collective-permute-start.1 = (f32[40,16]{0,1:T(8,128)S(1)}, f32[40,16]{0,1:T(8,128)S(1)}, u32[]{:S(2)}, u32[]{:S(2)}) collective-permute-start(f32[40,16]{0,1:T(8,128)S(1)} %bitcast.187), channel_id=1, source_target_pairs={{1,0},{2,1},{3,2},{4,3},{5,4},{6,5},{7,6},{0,7},{9,8},{10,9},{11,1... | collective-permute-start | bytes 7688 | tf_op jit(solution)/shard_map/ppermute | solution.py:78
  14.6 2.8 %copy-start.14 = (s32[32]{0:T(128)S(1)}, s32[32]{0:T(128)}, u32[]{:S(2)}) copy-start(s32[32]{0:T(128)} %param.8) | copy-start | bytes 388
  14.6 3.7 %copy-start.15 = (s32[32]{0:T(128)S(1)}, s32[32]{0:T(128)}, u32[]{:S(2)}) copy-start(s32[32]{0:T(128)} %param.9) | copy-start | bytes 388
  14.6 6.1 %collective-permute-start = (f32[48,16]{0,1:T(8,128)S(1)}, f32[48,16]{0,1:T(8,128)S(1)}, u32[]{:S(2)}, u32[]{:S(2)}) collective-permute-start(f32[48,16]{0,1:T(8,128)S(1)} %pad_maximum_fusion.8), channel_id=1, source_target_pairs={{0,1},{1,2},{2,3},{3,4},{4,5},{5,6},{6,7},{7,0},{8,9},{9,10},{10,1... | collective-permute-start | bytes 9224 | tf_op jit(solution)/shard_map/ppermute | solution.py:75
  22.8 6.4 %copy-start.9 = (f32[8,16,720]{2,1,0:T(8,128)S(1)}, f32[8,16,720]{2,1,0:T(8,128)}, u32[]{:S(2)}) copy-start(f32[8,16,720]{2,1,0:T(8,128)} %param.7) | copy-start | bytes 1105924
  24.8 4.6 %copy-start.13 = (pred[17]{0:T(512)(128)(4,1)S(1)}, pred[17]{0:T(512)(128)(4,1)}, u32[]{:S(2)}) copy-start(pred[17]{0:T(512)(128)(4,1)} %add_compare_fusion) | copy-start | bytes 55
  29.4 2.9 %copy-start.3 = (f32[5,8,16,721]{3,2,1,0:T(8,128)S(1)}, f32[5,8,16,721]{3,2,1,0:T(8,128)}, u32[]{:S(2)}) copy-start(f32[5,8,16,721]{3,2,1,0:T(8,128)} %multiply_subtract_fusion) | copy-start | bytes 5537284
  32.9 1.6 copy-start.1
  34.5 8.2 %copy-start.12 = (pred[8]{0:T(512)(128)(4,1)S(1)}, pred[8]{0:T(512)(128)(4,1)}, u32[]{:S(2)}) copy-start(pred[8]{0:T(512)(128)(4,1)} %slice_select_fusion.5) | copy-start | bytes 28
  34.5 8.1 %collective-permute-start.4 = (f32[8,8,720]{2,1,0:T(8,128)S(1)}, f32[8,8,720]{2,1,0:T(8,128)}, u32[]{:S(2)}, u32[]{:S(2)}) collective-permute-start(f32[8,8,720]{2,1,0:T(8,128)S(1)} %slice.133), channel_id=1, source_target_pairs={{0,16},{8,24},{16,0},{24,8},{1,17},{9,25},{17,1},{25,9},{2,18},{10... | collective-permute-start | bytes 552968 | tf_op jit(solution)/shard_map/ppermute | solution.py:129
  36.8 12.2 %collective-permute-start.6 = (f32[12,8,720]{2,1,0:T(8,128)S(1)}, f32[12,8,720]{2,1,0:T(8,128)}, u32[]{:S(2)}, u32[]{:S(2)}) collective-permute-start(f32[12,8,720]{2,1,0:T(8,128)S(1)} %slice.137), channel_id=1, source_target_pairs={{0,16},{8,24},{16,0},{24,8},{1,17},{9,25},{17,1},{25,9},{2,18},{10... | collective-permute-start | bytes 829448 | tf_op jit(solution)/shard_map/ppermute | solution.py:129
  40.0 18.0 %copy-start.4 = (f32[40,8,720]{2,1,0:T(8,128)S(1)}, f32[40,8,720]{2,1,0:T(8,128)}, u32[]{:S(2)}) copy-start(f32[40,8,720]{2,1,0:T(8,128)} %get-tuple-element.7) | copy-start | bytes 2764804
  40.0 18.0 %collective-permute-start.5 = (f32[20,8,720]{2,1,0:T(8,128)}, f32[20,8,720]{2,1,0:T(8,128)}, u32[]{:S(2)}, u32[]{:S(2)}) collective-permute-start(f32[20,8,720]{2,1,0:T(8,128)} %slice.135), channel_id=1, source_target_pairs={{0,16},{8,24},{16,0},{24,8},{1,17},{9,25},{17,1},{25,9},{2,18},{10... | collective-permute-start | bytes 1382408 | tf_op jit(solution)/shard_map/ppermute | solution.py:129
  44.5 15.5 %all-to-all-start = ((f32[8,8,720]{2,1,0:T(8,128)}), f32[8,8,720]{2,1,0:T(8,128)}, u32[]{:S(2)}, u32[]{:S(2)}) async-start(f32[8,8,720]{2,1,0:T(8,128)} %slice_select_fusion.4), calls=%async_computation | async-start | bytes 393216 | tf_op jit(solution)/shard_map/all_to_all | solution.py:131
  60.0 6.7 %copy-start.10 = (f32[45,128]{1,0:T(8,128)S(1)}, f32[45,128]{1,0:T(8,128)}, u32[]{:S(2)}) copy-start(f32[45,128]{1,0:T(8,128)} %broadcast_maximum_fusion) | copy-start | bytes 69124
  60.0 6.8 %copy-start.11 = (f32[45,128]{1,0:T(8,128)S(1)}, f32[45,128]{1,0:T(8,128)}, u32[]{:S(2)}) copy-start(f32[45,128]{1,0:T(8,128)} %fusion.140) | copy-start | bytes 69124
  60.0 16.5 %all-to-all-start.4 = ((f32[8,12,720]{2,1,0:T(8,128)}), f32[8,12,720]{2,1,0:T(8,128)S(1)}, u32[]{:S(2)}, u32[]{:S(2)}) async-start(f32[8,12,720]{2,1,0:T(8,128)} %all_to_all.81), calls=%async_computation.4 | async-start | bytes 786432 | tf_op jit(solution)/shard_map/all_to_all | solution.py:131
  68.2 12.0 %copy-start.6 = (f32[8,45,128]{2,1,0:T(8,128)}, f32[8,45,128]{2,1,0:T(8,128)S(1)}, u32[]{:S(2)}) copy-start(f32[8,45,128]{2,1,0:T(8,128)S(1)} %fusion.15) | copy-start | bytes 552964
  76.5 20.2 %all-to-all-start.2 = ((f32[8,20,720]{2,1,0:T(8,128)}), f32[8,20,720]{2,1,0:T(8,128)S(1)}, u32[]{:S(2)}, u32[]{:S(2)}) async-start(f32[8,20,720]{2,1,0:T(8,128)} %all_to_all.75), calls=%async_computation.2 | async-start | bytes 1179648 | tf_op jit(solution)/shard_map/all_to_all | solution.py:131
  96.7 16.7 %all-to-all-start.5 = ((f32[12,8,720]{2,0,1:T(8,128)}), f32[12,8,720]{2,0,1:T(8,128)}, u32[]{:S(2)}, u32[]{:S(2)}) async-start(f32[12,8,720]{2,0,1:T(8,128)} %copy.131), calls=%async_computation.5 | async-start | bytes 786432 | tf_op jit(solution)/shard_map/all_to_all | solution.py:139
  108.4 9.5 %copy-start.5 = (f32[8,45,128]{2,1,0:T(8,128)S(1)}, f32[8,45,128]{2,1,0:T(8,128)}, u32[]{:S(2)}) copy-start(f32[8,45,128]{2,1,0:T(8,128)} %convolution_add_fusion.4) | copy-start | bytes 552964
  108.8 8.1 %copy-start.7 = (f32[8,45,128]{2,1,0:T(8,128)S(1)}, f32[8,45,128]{2,1,0:T(8,128)}, u32[]{:S(2)}) copy-start(f32[8,45,128]{2,1,0:T(8,128)} %copy-done.6) | copy-start | bytes 552964
  113.4 20.2 %all-to-all-start.3 = ((f32[20,8,720]{2,0,1:T(8,128)}), f32[20,8,720]{2,0,1:T(8,128)S(1)}, u32[]{:S(2)}, u32[]{:S(2)}) async-start(f32[20,8,720]{2,0,1:T(8,128)} %copy.129), calls=%async_computation.3 | async-start | bytes 1179648 | tf_op jit(solution)/shard_map/all_to_all | solution.py:139
  133.6 11.7 %all-to-all-start.1 = ((f32[8,8,720]{2,0,1:T(8,128)}), f32[8,8,720]{2,0,1:T(8,128)S(1)}, u32[]{:S(2)}, u32[]{:S(2)}) async-start(f32[8,8,720]{2,0,1:T(8,128)} %copy.127), calls=%async_computation.1 | async-start | bytes 393216 | tf_op jit(solution)/shard_map/all_to_all | solution.py:139
  137.1 24.4 %collective-permute-start.8 = (f32[20,8,720]{2,1,0:T(8,128)S(1)}, f32[20,8,720]{2,1,0:T(8,128)}, u32[]{:S(2)}, u32[]{:S(2)}) collective-permute-start(f32[20,8,720]{2,1,0:T(8,128)S(1)} %reshape.400), channel_id=1, source_target_pairs={{0,16},{8,24},{16,0},{24,8},{1,17},{9,25},{17,1},{25,9},{2,18},{10... | collective-permute-start | bytes 1382408 | tf_op jit(solution)/shard_map/ppermute | solution.py:143
  140.2 21.3 %collective-permute-start.9 = (f32[12,8,720]{2,1,0:T(8,128)S(1)}, f32[12,8,720]{2,1,0:T(8,128)S(1)}, u32[]{:S(2)}, u32[]{:S(2)}) collective-permute-start(f32[12,8,720]{2,1,0:T(8,128)S(1)} %reshape.402), channel_id=1, source_target_pairs={{0,16},{8,24},{16,0},{24,8},{1,17},{9,25},{17,1},{25,9},{2,18},{10... | collective-permute-start | bytes 829448 | tf_op jit(solution)/shard_map/ppermute | solution.py:143
  145.3 17.3 %copy-start.2 = (f32[5,8,16,720]{3,2,1,0:T(8,128)S(1)}, f32[5,8,16,720]{3,2,1,0:T(8,128)}, u32[]{:S(2)}) copy-start(f32[5,8,16,720]{3,2,1,0:T(8,128)} %copy-done.1) | copy-start | bytes 5529604
  145.3 16.2 %collective-permute-start.7 = (f32[8,8,720]{2,1,0:T(8,128)S(1)}, f32[8,8,720]{2,1,0:T(8,128)S(1)}, u32[]{:S(2)}, u32[]{:S(2)}) collective-permute-start(f32[8,8,720]{2,1,0:T(8,128)S(1)} %bitcast.177), channel_id=1, source_target_pairs={{0,16},{8,24},{16,0},{24,8},{1,17},{9,25},{17,1},{25,9},{2,18},{10... | collective-permute-start | bytes 552968 | tf_op jit(solution)/shard_map/ppermute | solution.py:143

commit v10 on v7

--- a/solution.py
+++ b/solution.py
@@ -118,7 +118,7 @@
     row_cut = jnp.where(is_filtered, own_cut, partner_cut).astype(jnp.float32)
     kept_filtered = jnp.where(is_low, is_filtered[:half_rows], is_filtered[half_rows:])
     kept_cut = jnp.where(is_low, row_cut[:half_rows], row_cut[half_rows:])
-    first_fields = field_count * 2 // 5
+    first_fields = field_count * 3 // 5
     field_spans = ((0, first_fields), (first_fields, field_count))
     outputs = []
     for first, last in field_spans:

time: 143 us -> 144 us (level)
  transfers between devices with their start and end apart: 12 -> 12, of which waited for: 6 -> 6; matrix products, arithmetic and copies ran while one was open for 35% -> 36% of each run, Pallas kernels for 0% -> 0%
where the time goes in v10:
time: 144 us; the launch traced here: 142 us
  waiting for transfers between devices  45.5 us (32%)
  starting transfers between devices  32.7 us (23%)
  local copies, waits for them, and re-layouts  30.7 us (21%)
  other arithmetic  16.8 us (12%)
  matrix products  16.1 us (11%)
    all_to_all x2, waiting for transfers between devices, body(): lax.all_to_all(smoothed, 'lon', split_axis=1, concat_axis=0, tiled=True)  15.4 us
    ppermute x2, waiting for transfers between devices, body(): handed_back = lax.ppermute(returned, 'lat', pair_perm)  12 us
    all_to_all x2, waiting for transfers between devices, body(): lax.all_to_all(pair_lines.reshape(chunk_stack * half_rows, columns), 'lon...  9.49 us
    ppermute x2, waiting for transfers between devices, body(): taken = lax.ppermute(given, 'lat', pair_perm)  8.62 us
    all_to_all x2, starting transfers between devices, body(): lax.all_to_all(smoothed, 'lon', split_axis=1, concat_axis=0, tiled=True)  8.48 us
    all_to_all x2, starting transfers between devices, body(): lax.all_to_all(pair_lines.reshape(chunk_stack * half_rows, columns), 'lon...  8.37 us
    all_to_all x4, local copies, waits for them, and re-layouts, body(): lax.all_to_all(smoothed, 'lon', split_axis=1, concat_axis=0, tiled=True)  6.65 us
    ppermute x1, starting transfers between devices, body(): lax.ppermute(jnp.concatenate([flat_fields[:, -1], lat_courant[:, -1]], ax...  6.25 us
  transfers between devices with their start and end apart: 12, of which 6 were waited for; matrix products, arithmetic and copies ran while one was open for 36% of the time, Pallas kernels for 0%

profile of v10, /device:TPU:0, one launch (start us, length us, event | category | flops | bytes accessed | tf_op | source)
XLA Modules:
  0.0 142.4 jit_solution(2025239318179377861)
XLA Ops:
  0.0 1.7 %fusion.251 = (f32[40,1,720]{2,1,0:T(1,128)S(1)}, f32[40,1,720]{2,1,0:T(1,128)S(1)}) fusion(f32[40,16,720]{2,1,0:T(8,128)} %bitcast.147), kind=kLoop, calls=%fused_computation.304 | loop fusion | bytes 460800 | tf_op jit(solution)/shard_map/slice | solution.py:80
  2.3 1.4 collective-permute-start.3
  5.4 6.3 %collective-permute-start.2 = (f32[48,720]{1,0:T(8,128)}, f32[48,720]{1,0:T(8,128)}, u32[]{:S(2)}, u32[]{:S(2)}) collective-permute-start(f32[48,720]{1,0:T(8,128)} %pad_maximum_fusion.11), channel_id=1, source_target_pairs={{0,8},{8,16},{16,24},{1,9},{9,17},{17,25},{2,10},{10,18},{18,26},{... | collective-permute-start | bytes 414728 | tf_op jit(solution)/shard_map/ppermute | solution.py:79
  13.1 3.0 %collective-permute-start.1 = (f32[40,16]{0,1:T(8,128)S(1)}, f32[40,16]{0,1:T(8,128)S(1)}, u32[]{:S(2)}, u32[]{:S(2)}) collective-permute-start(f32[40,16]{0,1:T(8,128)S(1)} %bitcast.164), channel_id=1, source_target_pairs={{1,0},{2,1},{3,2},{4,3},{5,4},{6,5},{7,6},{0,7},{9,8},{10,9},{11,1... | collective-permute-start | bytes 7688 | tf_op jit(solution)/shard_map/ppermute | solution.py:78
  20.2 1.3 slice.128
  30.2 1.6 %collective-permute-start.6 = (f32[16,8,720]{2,1,0:T(8,128)S(1)}, f32[16,8,720]{2,1,0:T(8,128)S(1)}, u32[]{:S(2)}, u32[]{:S(2)}) collective-permute-start(f32[16,8,720]{2,1,0:T(8,128)S(1)} %slice_select_fusion.1), channel_id=1, source_target_pairs={{0,16},{8,24},{16,0},{24,8},{1,17},{9,25},{17,1},{25,9},{2,18},{10... | collective-permute-start | bytes 1105928 | tf_op jit(solution)/shard_map/ppermute | solution.py:134
  35.1 7.2 %collective-permute-done.6 = f32[16,8,720]{2,1,0:T(8,128)S(1)} collective-permute-done((f32[16,8,720]{2,1,0:T(8,128)S(1)}, f32[16,8,720]{2,1,0:T(8,128)S(1)}, u32[]{:S(2)}, u32[]{:S(2)}) %collective-permute-start.6) | collective-permute-done | bytes 368672 | tf_op jit(solution)/shard_map/ppermute | solution.py:134
  43.2 4.0 %all-to-all-start.2 = ((f32[8,16,720]{2,1,0:T(8,128)}), f32[8,16,720]{2,1,0:T(8,128)S(1)}, u32[]{:S(2)}, u32[]{:S(2)}) async-start(f32[8,16,720]{2,1,0:T(8,128)} %bitcast.151), calls=%async_computation.2 | async-start | bytes 786432 | tf_op jit(solution)/shard_map/all_to_all | solution.py:136
  47.8 1.2 gather_fusion.1
  50.5 1.3 fusion.104
  51.8 1.4 %collective-permute-done.4 = f32[24,8,720]{2,1,0:T(8,128)} collective-permute-done((f32[24,8,720]{2,1,0:T(8,128)}, f32[24,8,720]{2,1,0:T(8,128)}, u32[]{:S(2)}, u32[]{:S(2)}) %collective-permute-start.4) | collective-permute-done | bytes 552992 | tf_op jit(solution)/shard_map/ppermute | solution.py:134
  53.2 2.0 %select_select_fusion = f32[24,8,720]{2,1,0:T(8,128)} fusion(f32[24,8,720]{2,1,0:T(8,128)} %collective-permute-done.4, f32[24,16,720]{2,1,0:T(8,128)S(1)} %bitcast.144, pred[8]{0:T(512)(128)(4,1)} %copy-done.14, pred[]{:T(512)S(6)} %lt.139), kind=kLoop, calls=%fused_computation.67 | loop fusion | flops 276480 | bytes 2211849 | tf_op jit(solution)/shard_map/jit(_where)/select_n | solution.py:135
  55.2 4.5 %all-to-all-done.2 = f32[8,16,720]{2,1,0:T(8,128)S(1)} async-done(((f32[8,16,720]{2,1,0:T(8,128)}), f32[8,16,720]{2,1,0:T(8,128)S(1)}, u32[]{:S(2)}, u32[]{:S(2)}) %all-to-all-start.2) | async-done | bytes 368672 | tf_op jit(solution)/shard_map/all_to_all | solution.py:136
  59.7 4.4 %all-to-all-start = ((f32[8,24,720]{2,1,0:T(8,128)}), f32[8,24,720]{2,1,0:T(8,128)}, u32[]{:S(2)}, u32[]{:S(2)}) async-start(f32[8,24,720]{2,1,0:T(8,128)} %bitcast.149), calls=%async_computation | async-start | bytes 1179648 | tf_op jit(solution)/shard_map/all_to_all | solution.py:136
  65.1 1.2 reshape.352
  73.5 1.3 all_to_all.57
  75.7 5.0 %all-to-all-done = f32[8,24,720]{2,1,0:T(8,128)} async-done(((f32[8,24,720]{2,1,0:T(8,128)}), f32[8,24,720]{2,1,0:T(8,128)}, u32[]{:S(2)}, u32[]{:S(2)}) %all-to-all-start) | async-done | bytes 552992 | tf_op jit(solution)/shard_map/all_to_all | solution.py:136
  80.7 3.7 %all-to-all-start.3 = ((f32[16,8,720]{2,0,1:T(8,128)}), f32[16,8,720]{2,0,1:T(8,128)S(1)}, u32[]{:S(2)}, u32[]{:S(2)}) async-start(f32[16,8,720]{2,0,1:T(8,128)} %copy.147), calls=%async_computation.3 | async-start | bytes 786432 | tf_op jit(solution)/shard_map/all_to_all | solution.py:144
  84.4 2.1 %copy.138 = f32[24,8,720]{2,1,0:T(8,128)} copy(f32[24,8,720]{2,0,1:T(8,128)} %bitcast.15) | data formatting | bytes 1105920 | tf_op jit(solution)/shard_map/all_to_all | solution.py:136
  86.5 2.2 %reshape.349 = f32[24,45,128]{2,1,0:T(8,128)} reshape(f32[24,8,720]{2,1,0:T(8,128)} %copy.138) | data formatting | bytes 1105920 | tf_op jit(solution)/shard_map/reshape | solution.py:29
  88.7 1.6 %fusion.113 = f32[45,24,128]{2,0,1:T(8,128)S(1)} fusion(f32[24,45,128]{2,1,0:T(8,128)} %reshape.349), kind=kOutput, calls=%fused_computation.157 | convolution fusion | flops 37343024 | bytes 1105920 | tf_op jit(solution)/shard_map/lan,aj->ljn/dot_general | solution.py:30
  96.7 1.3 fusion.1
  98.1 2.4 %all_to_all.51 = f32[24,8,720]{2,1,0:T(8,128)} reshape(f32[24,45,128]{2,1,0:T(8,128)} %fusion.1) | data formatting | bytes 1105920 | tf_op jit(solution)/shard_map/all_to_all | solution.py:144
  100.5 2.1 %copy.139 = f32[24,8,720]{2,0,1:T(8,128)} copy(f32[24,8,720]{2,1,0:T(8,128)} %all_to_all.51) | data formatting | bytes 1105920 | tf_op jit(solution)/shard_map/all_to_all | solution.py:144
  102.6 4.8 %all-to-all-start.1 = ((f32[24,8,720]{2,0,1:T(8,128)}), f32[24,8,720]{2,0,1:T(8,128)}, u32[]{:S(2)}, u32[]{:S(2)}) async-start(f32[24,8,720]{2,0,1:T(8,128)} %copy.139), calls=%async_computation.1 | async-start | bytes 1179648 | tf_op jit(solution)/shard_map/all_to_all | solution.py:144
  107.4 1.5 %collective-permute-start.7 = (f32[16,8,720]{2,1,0:T(8,128)S(1)}, f32[16,8,720]{2,1,0:T(8,128)}, u32[]{:S(2)}, u32[]{:S(2)}) collective-permute-start(f32[16,8,720]{2,1,0:T(8,128)S(1)} %bitcast.152), channel_id=1, source_target_pairs={{0,16},{8,24},{16,0},{24,8},{1,17},{9,25},{17,1},{25,9},{2,18},{10... | collective-permute-start | bytes 1105928 | tf_op jit(solution)/shard_map/ppermute | solution.py:147
  108.9 15.4 %all-to-all-done.1 = f32[24,8,720]{2,0,1:T(8,128)} async-done(((f32[24,8,720]{2,0,1:T(8,128)}), f32[24,8,720]{2,0,1:T(8,128)}, u32[]{:S(2)}, u32[]{:S(2)}) %all-to-all-start.1) | async-done | bytes 552992 | tf_op jit(solution)/shard_map/all_to_all | solution.py:144
  124.2 1.5 %collective-permute-start.5 = (f32[24,8,720]{2,1,0:T(8,128)}, f32[24,8,720]{2,1,0:T(8,128)S(1)}, u32[]{:S(2)}, u32[]{:S(2)}) collective-permute-start(f32[24,8,720]{2,1,0:T(8,128)} %bitcast.24), channel_id=1, source_target_pairs={{0,16},{8,24},{16,0},{24,8},{1,17},{9,25},{17,1},{25,9},{2,18},{10... | collective-permute-start | bytes 1658888 | tf_op jit(solution)/shard_map/ppermute | solution.py:147
  125.8 1.6 %fusion.15 = f32[16,16,720]{2,1,0:T(8,128)S(1)} fusion(f32[16,8,720]{2,1,0:T(8,128)} %collective-permute-done.7, f32[16,8,720]{2,1,0:T(8,128)S(1)} %bitcast.153, f32[2,8,16,720]{3,2,1,0:T(8,128)S(1)} %slice.152, pred[16]{0:T(512)(128)(4,1)S(1)} %compare_reduce_fusion, pred[]{:T(512)S(6)} %lt.139, f32[2,8,16,720]{3,2,1,0:T(8,128)} %copy-done), kind=kLoop, calls=%fused_computation.47 | loop fusion | flops 921600 | bytes 2949137 | tf_op jit(solution)/shard_map/add | solution.py:154
  127.3 12.0 %collective-permute-done.5 = f32[24,8,720]{2,1,0:T(8,128)S(1)} collective-permute-done((f32[24,8,720]{2,1,0:T(8,128)}, f32[24,8,720]{2,1,0:T(8,128)S(1)}, u32[]{:S(2)}, u32[]{:S(2)}) %collective-permute-start.5) | collective-permute-done | bytes 552992 | tf_op jit(solution)/shard_map/ppermute | solution.py:147
  139.3 1.6 %fusion.11 = f32[24,16,720]{2,1,0:T(8,128)S(1)} fusion(f32[24,8,720]{2,1,0:T(8,128)S(1)} %collective-permute-done.5, f32[24,8,720]{2,1,0:T(8,128)} %bitcast.24, f32[3,8,16,720]{3,2,1,0:T(8,128)S(1)} %slice.128, pred[16]{0:T(512)(128)(4,1)S(1)} %compare_reduce_fusion, pred[]{:T(512)S(6)} %lt.139, f32[3,8,16,720]{3,2,1,0:T(8,128)S(1)} %fusion.8), kind=kLoop, calls=%fused_computation.34 | loop fusion | flops 1382400 | bytes 4423697 | tf_op jit(solution)/shard_map/add | solution.py:154
  141.0 1.4 pad_maximum_fusion
  (133 shorter events, 37.6 us)
Async XLA Ops:
  2.3 13.8 %copy-start.6 = (f32[8,16,720]{2,1,0:T(8,128)S(1)}, f32[8,16,720]{2,1,0:T(8,128)}, u32[]{:S(2)}) copy-start(f32[8,16,720]{2,1,0:T(8,128)} %param.6) | copy-start | bytes 1105924
  2.3 23.5 %collective-permute-start.3 = (f32[40,720]{1,0:T(8,128)}, f32[40,720]{1,0:T(8,128)}, u32[]{:S(2)}, u32[]{:S(2)}) collective-permute-start(f32[40,720]{1,0:T(8,128)} %bitcast.138), channel_id=1, source_target_pairs={{8,0},{16,8},{24,16},{9,1},{17,9},{25,17},{10,2},{18,10},{26,18},{... | collective-permute-start | bytes 345608 | tf_op jit(solution)/shard_map/ppermute | solution.py:82
  5.4 12.5 %copy-start.17 = (s32[32]{0:T(128)S(1)}, s32[32]{0:T(128)}, u32[]{:S(2)}) copy-start(s32[32]{0:T(128)} %param.8) | copy-start | bytes 388
  5.4 12.7 %copy-start.18 = (s32[32]{0:T(128)S(1)}, s32[32]{0:T(128)}, u32[]{:S(2)}) copy-start(s32[32]{0:T(128)} %param.9) | copy-start | bytes 388
  5.4 22.3 %collective-permute-start.2 = (f32[48,720]{1,0:T(8,128)}, f32[48,720]{1,0:T(8,128)}, u32[]{:S(2)}, u32[]{:S(2)}) collective-permute-start(f32[48,720]{1,0:T(8,128)} %pad_maximum_fusion.11), channel_id=1, source_target_pairs={{0,8},{8,16},{16,24},{1,9},{9,17},{17,25},{2,10},{10,18},{18,26},{... | collective-permute-start | bytes 414728 | tf_op jit(solution)/shard_map/ppermute | solution.py:79
  13.1 8.5 %collective-permute-start.1 = (f32[40,16]{0,1:T(8,128)S(1)}, f32[40,16]{0,1:T(8,128)S(1)}, u32[]{:S(2)}, u32[]{:S(2)}) collective-permute-start(f32[40,16]{0,1:T(8,128)S(1)} %bitcast.164), channel_id=1, source_target_pairs={{1,0},{2,1},{3,2},{4,3},{5,4},{6,5},{7,6},{0,7},{9,8},{10,9},{11,1... | collective-permute-start | bytes 7688 | tf_op jit(solution)/shard_map/ppermute | solution.py:78
  16.7 6.2 %collective-permute-start = (f32[48,16]{0,1:T(8,128)S(1)}, f32[48,16]{0,1:T(8,128)S(1)}, u32[]{:S(2)}, u32[]{:S(2)}) collective-permute-start(f32[48,16]{0,1:T(8,128)S(1)} %pad_maximum_fusion.12), channel_id=1, source_target_pairs={{0,1},{1,2},{2,3},{3,4},{4,5},{5,6},{6,7},{7,0},{8,9},{9,10},{10,1... | collective-permute-start | bytes 9224 | tf_op jit(solution)/shard_map/ppermute | solution.py:75
  16.7 1.6 %copy-start.15 = (s32[128]{0:T(128)}, s32[128]{0:T(128)S(1)}, u32[]{:S(2)}) copy-start(s32[128]{0:T(128)S(1)} %iota_multiply_fusion) | copy-start | bytes 1540
  18.1 24.2 %copy-start.14 = (pred[8]{0:T(512)(128)(4,1)}, pred[8]{0:T(512)(128)(4,1)S(1)}, u32[]{:S(2)}) copy-start(pred[8]{0:T(512)(128)(4,1)S(1)} %slice_select_fusion.2) | copy-start | bytes 28
  24.5 0.9 copy-start.7
  24.5 1.0 copy-start.8
  25.5 3.8 %copy-start.9 = (f32[8,16,720]{2,1,0:T(8,128)S(1)}, f32[8,16,720]{2,1,0:T(8,128)}, u32[]{:S(2)}) copy-start(f32[8,16,720]{2,1,0:T(8,128)} %param.7) | copy-start | bytes 1105924
  25.8 3.6 %copy-start.16 = (pred[17]{0:T(512)(128)(4,1)S(1)}, pred[17]{0:T(512)(128)(4,1)}, u32[]{:S(2)}) copy-start(pred[17]{0:T(512)(128)(4,1)} %add_compare_fusion) | copy-start | bytes 55
  30.1 12.2 %copy-start = (f32[2,8,16,720]{3,2,1,0:T(8,128)}, f32[2,8,16,720]{3,2,1,0:T(8,128)S(1)}, u32[]{:S(2)}) copy-start(f32[2,8,16,720]{3,2,1,0:T(8,128)S(1)} %fusion.12) | copy-start | bytes 2211844
  30.2 12.1 %collective-permute-start.6 = (f32[16,8,720]{2,1,0:T(8,128)S(1)}, f32[16,8,720]{2,1,0:T(8,128)S(1)}, u32[]{:S(2)}, u32[]{:S(2)}) collective-permute-start(f32[16,8,720]{2,1,0:T(8,128)S(1)} %slice_select_fusion.1), channel_id=1, source_target_pairs={{0,16},{8,24},{16,0},{24,8},{1,17},{9,25},{17,1},{25,9},{2,18},{10... | collective-permute-start | bytes 1105928 | tf_op jit(solution)/shard_map/ppermute | solution.py:134
  34.6 18.6 %collective-permute-start.4 = (f32[24,8,720]{2,1,0:T(8,128)}, f32[24,8,720]{2,1,0:T(8,128)}, u32[]{:S(2)}, u32[]{:S(2)}) collective-permute-start(f32[24,8,720]{2,1,0:T(8,128)} %slice_select_fusion), channel_id=1, source_target_pairs={{0,16},{8,24},{16,0},{24,8},{1,17},{9,25},{17,1},{25,9},{2,18},{10... | collective-permute-start | bytes 1658888 | tf_op jit(solution)/shard_map/ppermute | solution.py:134
  43.2 16.6 %all-to-all-start.2 = ((f32[8,16,720]{2,1,0:T(8,128)}), f32[8,16,720]{2,1,0:T(8,128)S(1)}, u32[]{:S(2)}, u32[]{:S(2)}) async-start(f32[8,16,720]{2,1,0:T(8,128)} %bitcast.151), calls=%async_computation.2 | async-start | bytes 786432 | tf_op jit(solution)/shard_map/all_to_all | solution.py:136
  59.7 21.0 %all-to-all-start = ((f32[8,24,720]{2,1,0:T(8,128)}), f32[8,24,720]{2,1,0:T(8,128)}, u32[]{:S(2)}, u32[]{:S(2)}) async-start(f32[8,24,720]{2,1,0:T(8,128)} %bitcast.149), calls=%async_computation | async-start | bytes 1179648 | tf_op jit(solution)/shard_map/all_to_all | solution.py:136
  66.3 0.9 copy-start.2
  66.3 0.9 copy-start.4
  67.2 1.2 copy-start.10
  67.2 1.2 copy-start.12
  67.2 1.2 copy-start.19
  80.7 21.9 %all-to-all-start.3 = ((f32[16,8,720]{2,0,1:T(8,128)}), f32[16,8,720]{2,0,1:T(8,128)S(1)}, u32[]{:S(2)}, u32[]{:S(2)}) async-start(f32[16,8,720]{2,0,1:T(8,128)} %copy.147), calls=%async_computation.3 | async-start | bytes 786432 | tf_op jit(solution)/shard_map/all_to_all | solution.py:144
  88.7 1.6 %copy-start.1 = (f32[24,45,128]{2,1,0:T(8,128)S(1)}, f32[24,45,128]{2,1,0:T(8,128)}, u32[]{:S(2)}) copy-start(f32[24,45,128]{2,1,0:T(8,128)} %reshape.349) | copy-start | bytes 1658884
  88.7 2.2 %copy-start.3 = (f32[45,128]{1,0:T(8,128)S(1)}, f32[45,128]{1,0:T(8,128)}, u32[]{:S(2)}) copy-start(f32[45,128]{1,0:T(8,128)} %get-tuple-element.15) | copy-start | bytes 69124
  88.7 2.2 %copy-start.5 = (f32[45,128]{1,0:T(8,128)S(1)}, f32[45,128]{1,0:T(8,128)}, u32[]{:S(2)}) copy-start(f32[45,128]{1,0:T(8,128)} %get-tuple-element.16) | copy-start | bytes 69124
  91.5 0.7 copy-start.11
  91.6 0.7 copy-start.13
  102.6 21.7 %all-to-all-start.1 = ((f32[24,8,720]{2,0,1:T(8,128)}), f32[24,8,720]{2,0,1:T(8,128)}, u32[]{:S(2)}, u32[]{:S(2)}) async-start(f32[24,8,720]{2,0,1:T(8,128)} %copy.139), calls=%async_computation.1 | async-start | bytes 1179648 | tf_op jit(solution)/shard_map/all_to_all | solution.py:144
  107.4 18.4 %collective-permute-start.7 = (f32[16,8,720]{2,1,0:T(8,128)S(1)}, f32[16,8,720]{2,1,0:T(8,128)}, u32[]{:S(2)}, u32[]{:S(2)}) collective-permute-start(f32[16,8,720]{2,1,0:T(8,128)S(1)} %bitcast.152), channel_id=1, source_target_pairs={{0,16},{8,24},{16,0},{24,8},{1,17},{9,25},{17,1},{25,9},{2,18},{10... | collective-permute-start | bytes 1105928 | tf_op jit(solution)/shard_map/ppermute | solution.py:147
  124.2 15.1 %collective-permute-start.5 = (f32[24,8,720]{2,1,0:T(8,128)}, f32[24,8,720]{2,1,0:T(8,128)S(1)}, u32[]{:S(2)}, u32[]{:S(2)}) collective-permute-start(f32[24,8,720]{2,1,0:T(8,128)} %bitcast.24), channel_id=1, source_target_pairs={{0,16},{8,24},{16,0},{24,8},{1,17},{9,25},{17,1},{25,9},{2,18},{10... | collective-permute-start | bytes 1658888 | tf_op jit(solution)/shard_map/ppermute | solution.py:147

commit v11 on v4

--- a/solution.py
+++ b/solution.py
@@ -124,21 +124,29 @@
         rows_of_part = slice(chunk_start, chunk_start + chunk_stack)
         chunk_start += chunk_stack
         line_count = chunk_stack * half_rows // lon_devices
-        line_index = lax.axis_index("lon") * line_count + jnp.arange(line_count, dtype=jnp.int32)
+        lon_index = lax.axis_index("lon")
+        line_index = lon_index * line_count + jnp.arange(line_count, dtype=jnp.int32)
         line_cut = kept_cut[line_index % half_rows]
         taken = lax.ppermute(given[rows_of_part], "lat", pair_perm)
         pair_lines = jnp.where(kept_filtered[None, :, None], kept[rows_of_part], taken)
-        full_lines = lax.all_to_all(
-            pair_lines.reshape(chunk_stack * half_rows, columns),
-            "lon",
-            split_axis=0,
-            concat_axis=1,
-            tiled=True,
+        blocks = pair_lines.reshape(lon_devices, line_count, columns)
+        shift_order = (lon_index - jnp.arange(lon_devices, dtype=jnp.int32)) % lon_devices
+        outgoing = jnp.take(blocks, shift_order, axis=0)
+        pieces = [outgoing[0]]
+        for shift in range(1, lon_devices):
+            toward = [(i, (i - shift) % lon_devices) for i in range(lon_devices)]
+            pieces.append(lax.ppermute(outgoing[shift], "lon", toward))
+        rotated_lines = jnp.concatenate(pieces, axis=1)
+        smoothed = filter_lines(rotated_lines, line_cut)
+        coming = [smoothed[:, :columns]]
+        for shift in range(1, lon_devices):
+            toward = [(i, (i + shift) % lon_devices) for i in range(lon_devices)]
+            coming.append(
+                lax.ppermute(smoothed[:, shift * columns : (shift + 1) * columns], "lon", toward)
+            )
+        returned = jnp.take(jnp.stack(coming), shift_order, axis=0).reshape(
+            chunk_stack, half_rows, columns
         )
-        smoothed = filter_lines(full_lines, line_cut)
-        returned = lax.all_to_all(
-            smoothed, "lon", split_axis=1, concat_axis=0, tiled=True
-        ).reshape(chunk_stack, half_rows, columns)
         returned_parts.append(returned)
         handed_parts.append(lax.ppermute(returned, "lat", pair_perm))
     returned = jnp.concatenate(returned_parts, axis=0)

time: 141 us -> 151 us (1.071); the launches traced: 141 us -> 149 us
  starting transfers between devices: 30.3 us -> 43.3 us
  waiting for transfers between devices: 62 us -> 49.6 us
  local copies, waits for them, and re-layouts: 21.4 us -> 26.6 us
  other arithmetic: 11.6 us -> 15.2 us
    all_to_all x4 -> x0, waiting for transfers between devices: 37.8 us -> none  [the longest x2 22.8 us: body(): lax.all_to_all(smoothed, 'lon', split_axis=1, concat_axis=0, tiled=True)]
    ppermute x0 -> x28, starting transfers between devices: none -> 27.2 us  [the longest x14 14.2 us: body(): pieces.append(lax.ppermute(outgoing[shift], 'lon', toward))]
    ppermute x0 -> x28, waiting for transfers between devices: none -> 19.6 us  [the longest x14 10.1 us: body(): lax.ppermute(smoothed[:, shift * columns:(shift + 1) * columns], 'lon', t...]
    all_to_all x4 -> x0, starting transfers between devices: 14.2 us -> none  [the longest x2 7.17 us: body(): lax.all_to_all(pair_lines.reshape(chunk_stack * half_rows, columns), 'lon...]
    ppermute x2, waiting for transfers between devices: 9.78 us -> 21.7 us  [body(): handed_parts.append(lax.ppermute(returned, 'lat', pair_perm))]
    ppermute x2, waiting for transfers between devices: 12.1 us -> 7.86 us  [body(): taken = lax.ppermute(given[rows_of_part], 'lat', pair_perm)]
    all_to_all x6 -> x0, local copies, waits for them, and re-layouts: 3.86 us -> none  [the longest x4 2.69 us: body(): lax.all_to_all(smoothed, 'lon', split_axis=1, concat_axis=0, tiled=True)]
    gather x0 -> x4, local copies, waits for them, and re-layouts: none -> 3.84 us  [the longest x2 1.93 us: body(): jnp.take(jnp.stack(coming), shift_order, axis=0)]
  transfers between devices with their start and end apart: 12 -> 36, of which waited for: 8 -> 15; matrix products, arithmetic and copies ran while one was open for 20% -> 20% of each run, Pallas kernels for 0% -> 0%
where the time goes in v11:
time: 151 us; the launch traced here: 149 us
  waiting for transfers between devices  49.6 us (33%)
  starting transfers between devices  43.3 us (29%)
  local copies, waits for them, and re-layouts  26.6 us (18%)
  other arithmetic  15.2 us (10%)
  matrix products  13.4 us (9%)
    ppermute x2, waiting for transfers between devices, body(): handed_parts.append(lax.ppermute(returned, 'lat', pair_perm))  21.7 us
    ppermute x14, starting transfers between devices, body(): pieces.append(lax.ppermute(outgoing[shift], 'lon', toward))  14.2 us
    ppermute x14, starting transfers between devices, body(): lax.ppermute(smoothed[:, shift * columns:(shift + 1) * columns], 'lon', t...  13 us
    ppermute x14, waiting for transfers between devices, body(): lax.ppermute(smoothed[:, shift * columns:(shift + 1) * columns], 'lon', t...  10.1 us
    ppermute x14, waiting for transfers between devices, body(): pieces.append(lax.ppermute(outgoing[shift], 'lon', toward))  9.48 us
    ppermute x2, waiting for transfers between devices, body(): taken = lax.ppermute(given[rows_of_part], 'lat', pair_perm)  7.86 us
    ppermute x1, starting transfers between devices, body(): lax.ppermute(jnp.concatenate([flat_fields[:, -1], lat_courant[:, -1]], ax...  5.48 us
    unnamed x78, local copies, waits for them, and re-layouts  4.84 us
  transfers between devices with their start and end apart: 36, of which 15 were waited for; matrix products, arithmetic and copies ran while one was open for 20% of the time, Pallas kernels for 0%

profile of v11, /device:TPU:0, one launch (start us, length us, event | category | flops | bytes accessed | tf_op | source)
XLA Modules:
  0.0 149.1 jit_solution(13593981977002033051)
XLA Ops:
  0.0 1.8 %fusion.248 = (f32[40,1,720]{2,1,0:T(1,128)S(1)}, f32[40,1,720]{2,1,0:T(1,128)S(1)}) fusion(f32[40,16,720]{2,1,0:T(8,128)} %bitcast.197), kind=kLoop, calls=%fused_computation.338 | loop fusion | bytes 460800 | tf_op jit(solution)/shard_map/slice | solution.py:80
  1.8 1.3 collective-permute-start.3
  4.1 5.5 %collective-permute-start.2 = (f32[48,720]{1,0:T(8,128)S(1)}, f32[48,720]{1,0:T(8,128)S(1)}, u32[]{:S(2)}, u32[]{:S(2)}) collective-permute-start(f32[48,720]{1,0:T(8,128)S(1)} %pad_maximum_fusion.7), channel_id=1, source_target_pairs={{0,8},{8,16},{16,24},{1,9},{9,17},{17,25},{2,10},{10,18},{18,26},{... | collective-permute-start | bytes 414728 | tf_op jit(solution)/shard_map/ppermute | solution.py:79
  9.6 1.2 fusion.247
  11.1 3.0 %collective-permute-start.1 = (f32[40,16]{0,1:T(8,128)S(1)}, f32[40,16]{0,1:T(8,128)S(1)}, u32[]{:S(2)}, u32[]{:S(2)}) collective-permute-start(f32[40,16]{0,1:T(8,128)S(1)} %bitcast.222), channel_id=1, source_target_pairs={{1,0},{2,1},{3,2},{4,3},{5,4},{6,5},{7,6},{0,7},{9,8},{10,9},{11,1... | collective-permute-start | bytes 7688 | tf_op jit(solution)/shard_map/ppermute | solution.py:78
  14.7 1.5 %constant_dynamic-update-slice_fusion = f32[5,8,17,720]{3,2,1,0:T(8,128)} fusion(f32[5,8,16,720]{3,2,1,0:T(8,128)S(1)} %copy-done), kind=kLoop, calls=%fused_computation.166 | loop fusion | bytes 3809280
  20.4 2.0 %multiply_subtract_fusion = f32[5,8,16,721]{3,2,1,0:T(8,128)} fusion(f32[5,8,16,1]{3,2,1,0:T(8,128)S(1)} %copy.86, f32[5,8,16,720]{3,2,1,0:T(8,128)S(1)} %copy-done, f32[5,8,16,1]{3,2,1,0:T(8,128)S(1)} %copy.83, f32[8,16,721]{2,1,0:T(8,128)S(1)} %get-tuple-element.31, f32[8,16,721]{2,1,0:T(8,128)S(1)} %get-tuple-element.30), kind=kLoop, calls=%fused_computation.17 | loop fusion | flops 3230080 | bytes 4432384 | tf_op jit(solution)/shard_map/sub | solution.py:60
  23.4 3.2 %dynamic-update-slice.17 = f32[5,8,17,720]{3,2,1,0:T(8,128)} dynamic-update-slice(f32[5,8,17,720]{3,2,1,0:T(8,128)} %constant_dynamic-update-slice_fusion, f32[5,8,1,720]{3,2,1,0:T(1,128)S(1)} %copy.90, s32[]{} %constant.162, s32[]{} %constant.162, s32[]{} %constant.170, s32[]{} %constant.162) | dynamic-update-slice | bytes 230404 | tf_op jit(solution)/shard_map/concatenate | solution.py:88
  26.9 2.9 %subtract_select_fusion = f32[5,8,17,720]{3,2,1,0:T(8,128)S(1)} fusion(f32[5,8,17,720]{3,2,1,0:T(8,128)} %dynamic-update-slice.17, f32[5,8,16,720]{3,2,1,0:T(8,128)S(1)} %copy-done, f32[5,8,1,720]{3,2,1,0:T(1,128)S(1)} %copy.89, f32[8,17,720]{2,1,0:T(8,128)S(1)} %get-tuple-element.33, f32[8,17,720]{2,1,0:T(8,128)S(1)} %get-tuple-element.32, ...), kind=kLoop, calls=%fused_computation.7 | loop fusion | flops 3427200 | bytes 6658577 | tf_op jit(solution)/shard_map/jit(_where)/select_n | solution.py:95
  30.5 1.3 slice_select_fusion.1
  32.1 2.2 %collective-permute-start.4 = (f32[16,8,720]{2,1,0:T(8,128)S(1)}, f32[16,8,720]{2,1,0:T(8,128)}, u32[]{:S(2)}, u32[]{:S(2)}) collective-permute-start(f32[16,8,720]{2,1,0:T(8,128)S(1)} %slice.259), channel_id=1, source_target_pairs={{0,16},{8,24},{16,0},{24,8},{1,17},{9,25},{17,1},{25,9},{2,18},{10... | collective-permute-start | bytes 1105928 | tf_op jit(solution)/shard_map/ppermute | solution.py:130
  34.5 7.9 %collective-permute-done.4 = f32[16,8,720]{2,1,0:T(8,128)} collective-permute-done((f32[16,8,720]{2,1,0:T(8,128)S(1)}, f32[16,8,720]{2,1,0:T(8,128)}, u32[]{:S(2)}, u32[]{:S(2)}) %collective-permute-start.4) | collective-permute-done | bytes 368672 | tf_op jit(solution)/shard_map/ppermute | solution.py:130
  43.6 1.3 gather_fusion.2
  46.7 2.5 %collective-permute-start.5 = (f32[16,720]{1,0:T(8,128)S(1)}, f32[16,720]{1,0:T(8,128)S(1)}, u32[]{:S(2)}, u32[]{:S(2)}) collective-permute-start(f32[16,720]{1,0:T(8,128)S(1)} %get-tuple-element.40), channel_id=1, source_target_pairs={{0,7},{1,0},{2,1},{3,2},{4,3},{5,4},{6,5},{7,6},{8,15},{9,8},{10,9... | collective-permute-start | bytes 138248 | tf_op jit(solution)/shard_map/ppermute | solution.py:138
  49.7 2.2 %collective-permute-start.8 = (f32[16,720]{1,0:T(8,128)}, f32[16,720]{1,0:T(8,128)}, u32[]{:S(2)}, u32[]{:S(2)}) collective-permute-start(f32[16,720]{1,0:T(8,128)} %get-tuple-element.37), channel_id=1, source_target_pairs={{0,4},{1,5},{2,6},{3,7},{4,0},{5,1},{6,2},{7,3},{8,12},{9,13},{10,... | collective-permute-start | bytes 138248 | tf_op jit(solution)/shard_map/ppermute | solution.py:138
  54.2 1.3 gather_fusion.1
  57.1 1.9 %collective-permute-start.19 = (f32[24,8,720]{2,1,0:T(8,128)}, f32[24,8,720]{2,1,0:T(8,128)S(1)}, u32[]{:S(2)}, u32[]{:S(2)}) collective-permute-start(f32[24,8,720]{2,1,0:T(8,128)} %slice.277), channel_id=1, source_target_pairs={{0,16},{8,24},{16,0},{24,8},{1,17},{9,25},{17,1},{25,9},{2,18},{10... | collective-permute-start | bytes 1658888 | tf_op jit(solution)/shard_map/ppermute | solution.py:130
  68.4 2.0 %collective-permute-start.13 = (f32[16,720]{1,0:T(8,128)S(1)}, f32[16,720]{1,0:T(8,128)S(1)}, u32[]{:S(2)}, u32[]{:S(2)}) collective-permute-start(f32[16,720]{1,0:T(8,128)S(1)} %get-tuple-element.47), channel_id=1, source_target_pairs={{0,2},{1,3},{2,4},{3,5},{4,6},{5,7},{6,0},{7,1},{8,10},{9,11},{10,... | collective-permute-start | bytes 138248 | tf_op jit(solution)/shard_map/ppermute | solution.py:145
  70.4 2.1 %collective-permute-start.15 = (f32[16,720]{1,0:T(8,128)S(1)}, f32[16,720]{1,0:T(8,128)S(1)}, u32[]{:S(2)}, u32[]{:S(2)}) collective-permute-start(f32[16,720]{1,0:T(8,128)S(1)} %get-tuple-element.45), channel_id=1, source_target_pairs={{0,4},{1,5},{2,6},{3,7},{4,0},{5,1},{6,2},{7,3},{8,12},{9,13},{10,... | collective-permute-start | bytes 138248 | tf_op jit(solution)/shard_map/ppermute | solution.py:145
  75.5 2.9 %collective-permute-done.14 = f32[16,720]{1,0:T(8,128)S(1)} collective-permute-done((f32[16,720]{1,0:T(8,128)S(1)}, f32[16,720]{1,0:T(8,128)S(1)}, u32[]{:S(2)}, u32[]{:S(2)}) %collective-permute-start.14) | collective-permute-done | bytes 46112 | tf_op jit(solution)/shard_map/ppermute | solution.py:145
  81.0 3.4 %collective-permute-start.20 = (f32[24,720]{1,0:T(8,128)S(1)}, f32[24,720]{1,0:T(8,128)S(1)}, u32[]{:S(2)}, u32[]{:S(2)}) collective-permute-start(f32[24,720]{1,0:T(8,128)S(1)} %get-tuple-element.21), channel_id=1, source_target_pairs={{0,7},{1,0},{2,1},{3,2},{4,3},{5,4},{6,5},{7,6},{8,15},{9,8},{10,9... | collective-permute-start | bytes 207368 | tf_op jit(solution)/shard_map/ppermute | solution.py:138
  84.9 2.4 %collective-permute-start.23 = (f32[24,720]{1,0:T(8,128)S(1)}, f32[24,720]{1,0:T(8,128)S(1)}, u32[]{:S(2)}, u32[]{:S(2)}) collective-permute-start(f32[24,720]{1,0:T(8,128)S(1)} %get-tuple-element.18), channel_id=1, source_target_pairs={{0,4},{1,5},{2,6},{3,7},{4,0},{5,1},{6,2},{7,3},{8,12},{9,13},{10,... | collective-permute-start | bytes 207368 | tf_op jit(solution)/shard_map/ppermute | solution.py:138
  90.7 1.3 gather_fusion.3
  92.1 6.1 %collective-permute-done.23 = f32[24,720]{1,0:T(8,128)S(1)} collective-permute-done((f32[24,720]{1,0:T(8,128)S(1)}, f32[24,720]{1,0:T(8,128)S(1)}, u32[]{:S(2)}, u32[]{:S(2)}) %collective-permute-start.23) | collective-permute-done | bytes 69152 | tf_op jit(solution)/shard_map/ppermute | solution.py:138
  109.6 2.2 %collective-permute-start.29 = (f32[24,720]{1,0:T(8,128)S(1)}, f32[24,720]{1,0:T(8,128)S(1)}, u32[]{:S(2)}, u32[]{:S(2)}) collective-permute-start(f32[24,720]{1,0:T(8,128)S(1)} %get-tuple-element.27), channel_id=1, source_target_pairs={{0,3},{1,4},{2,5},{3,6},{4,7},{5,0},{6,1},{7,2},{8,11},{9,12},{10,... | collective-permute-start | bytes 207368 | tf_op jit(solution)/shard_map/ppermute | solution.py:145
  111.9 1.7 %collective-permute-start.30 = (f32[24,720]{1,0:T(8,128)S(1)}, f32[24,720]{1,0:T(8,128)S(1)}, u32[]{:S(2)}, u32[]{:S(2)}) collective-permute-start(f32[24,720]{1,0:T(8,128)S(1)} %get-tuple-element.26), channel_id=1, source_target_pairs={{0,4},{1,5},{2,6},{3,7},{4,0},{5,1},{6,2},{7,3},{8,12},{9,13},{10,... | collective-permute-start | bytes 207368 | tf_op jit(solution)/shard_map/ppermute | solution.py:145
  115.2 1.7 %collective-permute-start.32 = (f32[24,720]{1,0:T(8,128)S(1)}, f32[24,720]{1,0:T(8,128)S(1)}, u32[]{:S(2)}, u32[]{:S(2)}) collective-permute-start(f32[24,720]{1,0:T(8,128)S(1)} %get-tuple-element.24), channel_id=1, source_target_pairs={{0,6},{1,7},{2,0},{3,1},{4,2},{5,3},{6,4},{7,5},{8,14},{9,15},{10,... | collective-permute-start | bytes 207368 | tf_op jit(solution)/shard_map/ppermute | solution.py:145
  116.9 1.4 collective-permute-start.33
  118.3 3.7 %collective-permute-done.29 = f32[24,720]{1,0:T(8,128)S(1)} collective-permute-done((f32[24,720]{1,0:T(8,128)S(1)}, f32[24,720]{1,0:T(8,128)S(1)}, u32[]{:S(2)}, u32[]{:S(2)}) %collective-permute-start.29) | collective-permute-done | bytes 69152 | tf_op jit(solution)/shard_map/ppermute | solution.py:145
  123.1 1.8 %collective-permute-start.35 = (f32[24,8,720]{2,1,0:T(8,128)S(1)}, f32[24,8,720]{2,1,0:T(8,128)S(1)}, u32[]{:S(2)}, u32[]{:S(2)}) collective-permute-start(f32[24,8,720]{2,1,0:T(8,128)S(1)} %bitcast.204), channel_id=1, source_target_pairs={{0,16},{8,24},{16,0},{24,8},{1,17},{9,25},{17,1},{25,9},{2,18},{10... | collective-permute-start | bytes 1658888 | tf_op jit(solution)/shard_map/ppermute | solution.py:151
  125.4 21.7 %collective-permute-done.34 = f32[16,8,720]{2,1,0:T(8,128)S(1)} collective-permute-done((f32[16,8,720]{2,1,0:T(8,128)S(1)}, f32[16,8,720]{2,1,0:T(8,128)S(1)}, u32[]{:S(2)}, u32[]{:S(2)}) %collective-permute-start.34) | collective-permute-done | bytes 368672 | tf_op jit(solution)/shard_map/ppermute | solution.py:151
  147.2 1.9 %fusion.3 = f32[5,8,16,720]{3,2,1,0:T(8,128)} fusion(f32[5,8,16,720]{3,2,1,0:T(8,128)S(1)} %copy-done, f32[5,8,16,720]{3,2,1,0:T(8,128)S(1)} %copy-done.2, f32[5,8,8,720]{3,2,1,0:T(8,128)S(1)} %bitcast.201, f32[5,8,8,720]{3,2,1,0:T(8,128)S(1)} %bitcast.200, pred[16]{0:T(512)(128)(4,1)S(1)} %copy-done.19, pred[]{:T(512)S(6)} %lt.153), kind=kLoop, calls=%fused_computation.16 | loop fusion | flops 2304000 | bytes 7372817 | tf_op jit(solution)/shard_map/add | solution.py:160
  (214 shorter events, 48.8 us)
Async XLA Ops:
  1.8 20.5 %collective-permute-start.3 = (f32[40,720]{1,0:T(8,128)S(1)}, f32[40,720]{1,0:T(8,128)}, u32[]{:S(2)}, u32[]{:S(2)}) collective-permute-start(f32[40,720]{1,0:T(8,128)S(1)} %bitcast.215), channel_id=1, source_target_pairs={{8,0},{16,8},{24,16},{9,1},{17,9},{25,17},{10,2},{18,10},{26,18},{... | collective-permute-start | bytes 345608 | tf_op jit(solution)/shard_map/ppermute | solution.py:82
  4.1 22.5 %collective-permute-start.2 = (f32[48,720]{1,0:T(8,128)S(1)}, f32[48,720]{1,0:T(8,128)S(1)}, u32[]{:S(2)}, u32[]{:S(2)}) collective-permute-start(f32[48,720]{1,0:T(8,128)S(1)} %pad_maximum_fusion.7), channel_id=1, source_target_pairs={{0,8},{8,16},{16,24},{1,9},{9,17},{17,25},{2,10},{10,18},{18,26},{... | collective-permute-start | bytes 414728 | tf_op jit(solution)/shard_map/ppermute | solution.py:79
  11.1 7.5 %collective-permute-start.1 = (f32[40,16]{0,1:T(8,128)S(1)}, f32[40,16]{0,1:T(8,128)S(1)}, u32[]{:S(2)}, u32[]{:S(2)}) collective-permute-start(f32[40,16]{0,1:T(8,128)S(1)} %bitcast.222), channel_id=1, source_target_pairs={{1,0},{2,1},{3,2},{4,3},{5,4},{6,5},{7,6},{0,7},{9,8},{10,9},{11,1... | collective-permute-start | bytes 7688 | tf_op jit(solution)/shard_map/ppermute | solution.py:78
  32.1 10.3 %collective-permute-start.4 = (f32[16,8,720]{2,1,0:T(8,128)S(1)}, f32[16,8,720]{2,1,0:T(8,128)}, u32[]{:S(2)}, u32[]{:S(2)}) collective-permute-start(f32[16,8,720]{2,1,0:T(8,128)S(1)} %slice.259), channel_id=1, source_target_pairs={{0,16},{8,24},{16,0},{24,8},{1,17},{9,25},{17,1},{25,9},{2,18},{10... | collective-permute-start | bytes 1105928 | tf_op jit(solution)/shard_map/ppermute | solution.py:130
  46.7 5.3 %collective-permute-start.5 = (f32[16,720]{1,0:T(8,128)S(1)}, f32[16,720]{1,0:T(8,128)S(1)}, u32[]{:S(2)}, u32[]{:S(2)}) collective-permute-start(f32[16,720]{1,0:T(8,128)S(1)} %get-tuple-element.40), channel_id=1, source_target_pairs={{0,7},{1,0},{2,1},{3,2},{4,3},{5,4},{6,5},{7,6},{8,15},{9,8},{10,9... | collective-permute-start | bytes 138248 | tf_op jit(solution)/shard_map/ppermute | solution.py:138
  49.7 7.5 %collective-permute-start.7 = (f32[16,720]{1,0:T(8,128)S(1)}, f32[16,720]{1,0:T(8,128)}, u32[]{:S(2)}, u32[]{:S(2)}) collective-permute-start(f32[16,720]{1,0:T(8,128)S(1)} %get-tuple-element.38), channel_id=1, source_target_pairs={{0,5},{1,6},{2,7},{3,0},{4,1},{5,2},{6,3},{7,4},{8,13},{9,14},{10,... | collective-permute-start | bytes 138248 | tf_op jit(solution)/shard_map/ppermute | solution.py:138
  49.7 9.3 %collective-permute-start.8 = (f32[16,720]{1,0:T(8,128)}, f32[16,720]{1,0:T(8,128)}, u32[]{:S(2)}, u32[]{:S(2)}) collective-permute-start(f32[16,720]{1,0:T(8,128)} %get-tuple-element.37), channel_id=1, source_target_pairs={{0,4},{1,5},{2,6},{3,7},{4,0},{5,1},{6,2},{7,3},{8,12},{9,13},{10,... | collective-permute-start | bytes 138248 | tf_op jit(solution)/shard_map/ppermute | solution.py:138
  51.9 8.0 %collective-permute-start.9 = (f32[16,720]{1,0:T(8,128)}, f32[16,720]{1,0:T(8,128)}, u32[]{:S(2)}, u32[]{:S(2)}) collective-permute-start(f32[16,720]{1,0:T(8,128)} %get-tuple-element.36), channel_id=1, source_target_pairs={{0,3},{1,4},{2,5},{3,6},{4,7},{5,0},{6,1},{7,2},{8,11},{9,12},{10,... | collective-permute-start | bytes 138248 | tf_op jit(solution)/shard_map/ppermute | solution.py:138
  51.9 8.0 %collective-permute-start.10 = (f32[16,720]{1,0:T(8,128)}, f32[16,720]{1,0:T(8,128)}, u32[]{:S(2)}, u32[]{:S(2)}) collective-permute-start(f32[16,720]{1,0:T(8,128)} %get-tuple-element.35), channel_id=1, source_target_pairs={{0,2},{1,3},{2,4},{3,5},{4,6},{5,7},{6,0},{7,1},{8,10},{9,11},{10,... | collective-permute-start | bytes 138248 | tf_op jit(solution)/shard_map/ppermute | solution.py:138
  54.2 5.7 %collective-permute-start.11 = (f32[16,720]{1,0:T(8,128)S(1)}, f32[16,720]{1,0:T(8,128)}, u32[]{:S(2)}, u32[]{:S(2)}) collective-permute-start(f32[16,720]{1,0:T(8,128)S(1)} %get-tuple-element.34), channel_id=1, source_target_pairs={{0,1},{1,2},{2,3},{3,4},{4,5},{5,6},{6,7},{7,0},{8,9},{9,10},{10,1... | collective-permute-start | bytes 138248 | tf_op jit(solution)/shard_map/ppermute | solution.py:138
  57.1 22.2 %collective-permute-start.19 = (f32[24,8,720]{2,1,0:T(8,128)}, f32[24,8,720]{2,1,0:T(8,128)S(1)}, u32[]{:S(2)}, u32[]{:S(2)}) collective-permute-start(f32[24,8,720]{2,1,0:T(8,128)} %slice.277), channel_id=1, source_target_pairs={{0,16},{8,24},{16,0},{24,8},{1,17},{9,25},{17,1},{25,9},{2,18},{10... | collective-permute-start | bytes 1658888 | tf_op jit(solution)/shard_map/ppermute | solution.py:130
  68.3 5.3 %collective-permute-start.12 = (f32[16,720]{1,0:T(8,128)S(1)}, f32[16,720]{1,0:T(8,128)S(1)}, u32[]{:S(2)}, u32[]{:S(2)}) collective-permute-start(f32[16,720]{1,0:T(8,128)S(1)} %get-tuple-element.48), channel_id=1, source_target_pairs={{0,1},{1,2},{2,3},{3,4},{4,5},{5,6},{6,7},{7,0},{8,9},{9,10},{10,1... | collective-permute-start | bytes 138248 | tf_op jit(solution)/shard_map/ppermute | solution.py:145
  68.4 6.5 %collective-permute-start.13 = (f32[16,720]{1,0:T(8,128)S(1)}, f32[16,720]{1,0:T(8,128)S(1)}, u32[]{:S(2)}, u32[]{:S(2)}) collective-permute-start(f32[16,720]{1,0:T(8,128)S(1)} %get-tuple-element.47), channel_id=1, source_target_pairs={{0,2},{1,3},{2,4},{3,5},{4,6},{5,7},{6,0},{7,1},{8,10},{9,11},{10,... | collective-permute-start | bytes 138248 | tf_op jit(solution)/shard_map/ppermute | solution.py:145
  70.3 8.1 %collective-permute-start.14 = (f32[16,720]{1,0:T(8,128)S(1)}, f32[16,720]{1,0:T(8,128)S(1)}, u32[]{:S(2)}, u32[]{:S(2)}) collective-permute-start(f32[16,720]{1,0:T(8,128)S(1)} %get-tuple-element.46), channel_id=1, source_target_pairs={{0,3},{1,4},{2,5},{3,6},{4,7},{5,0},{6,1},{7,2},{8,11},{9,12},{10,... | collective-permute-start | bytes 138248 | tf_op jit(solution)/shard_map/ppermute | solution.py:145
  70.4 8.1 %collective-permute-start.15 = (f32[16,720]{1,0:T(8,128)S(1)}, f32[16,720]{1,0:T(8,128)S(1)}, u32[]{:S(2)}, u32[]{:S(2)}) collective-permute-start(f32[16,720]{1,0:T(8,128)S(1)} %get-tuple-element.45), channel_id=1, source_target_pairs={{0,4},{1,5},{2,6},{3,7},{4,0},{5,1},{6,2},{7,3},{8,12},{9,13},{10,... | collective-permute-start | bytes 138248 | tf_op jit(solution)/shard_map/ppermute | solution.py:145
  74.8 9.7 %collective-permute-start.17 = (f32[16,720]{1,0:T(8,128)}, f32[16,720]{1,0:T(8,128)S(1)}, u32[]{:S(2)}, u32[]{:S(2)}) collective-permute-start(f32[16,720]{1,0:T(8,128)} %get-tuple-element.43), channel_id=1, source_target_pairs={{0,6},{1,7},{2,0},{3,1},{4,2},{5,3},{6,4},{7,5},{8,14},{9,15},{10,... | collective-permute-start | bytes 138248 | tf_op jit(solution)/shard_map/ppermute | solution.py:145
  78.4 8.9 %collective-permute-start.18 = (f32[16,720]{1,0:T(8,128)S(1)}, f32[16,720]{1,0:T(8,128)S(1)}, u32[]{:S(2)}, u32[]{:S(2)}) collective-permute-start(f32[16,720]{1,0:T(8,128)S(1)} %get-tuple-element.42), channel_id=1, source_target_pairs={{0,7},{1,0},{2,1},{3,2},{4,3},{5,4},{6,5},{7,6},{8,15},{9,8},{10,9... | collective-permute-start | bytes 138248 | tf_op jit(solution)/shard_map/ppermute | solution.py:145
  81.0 6.9 %collective-permute-start.20 = (f32[24,720]{1,0:T(8,128)S(1)}, f32[24,720]{1,0:T(8,128)S(1)}, u32[]{:S(2)}, u32[]{:S(2)}) collective-permute-start(f32[24,720]{1,0:T(8,128)S(1)} %get-tuple-element.21), channel_id=1, source_target_pairs={{0,7},{1,0},{2,1},{3,2},{4,3},{5,4},{6,5},{7,6},{8,15},{9,8},{10,9... | collective-permute-start | bytes 207368 | tf_op jit(solution)/shard_map/ppermute | solution.py:138
  84.5 7.6 %collective-permute-start.22 = (f32[24,720]{1,0:T(8,128)S(1)}, f32[24,720]{1,0:T(8,128)S(1)}, u32[]{:S(2)}, u32[]{:S(2)}) collective-permute-start(f32[24,720]{1,0:T(8,128)S(1)} %get-tuple-element.19), channel_id=1, source_target_pairs={{0,5},{1,6},{2,7},{3,0},{4,1},{5,2},{6,3},{7,4},{8,13},{9,14},{10,... | collective-permute-start | bytes 207368 | tf_op jit(solution)/shard_map/ppermute | solution.py:138
  84.9 13.3 %collective-permute-start.23 = (f32[24,720]{1,0:T(8,128)S(1)}, f32[24,720]{1,0:T(8,128)S(1)}, u32[]{:S(2)}, u32[]{:S(2)}) collective-permute-start(f32[24,720]{1,0:T(8,128)S(1)} %get-tuple-element.18), channel_id=1, source_target_pairs={{0,4},{1,5},{2,6},{3,7},{4,0},{5,1},{6,2},{7,3},{8,12},{9,13},{10,... | collective-permute-start | bytes 207368 | tf_op jit(solution)/shard_map/ppermute | solution.py:138
  87.9 11.2 %collective-permute-start.24 = (f32[24,720]{1,0:T(8,128)S(1)}, f32[24,720]{1,0:T(8,128)S(1)}, u32[]{:S(2)}, u32[]{:S(2)}) collective-permute-start(f32[24,720]{1,0:T(8,128)S(1)} %get-tuple-element.17), channel_id=1, source_target_pairs={{0,3},{1,4},{2,5},{3,6},{4,7},{5,0},{6,1},{7,2},{8,11},{9,12},{10,... | collective-permute-start | bytes 207368 | tf_op jit(solution)/shard_map/ppermute | solution.py:138
  87.9 11.1 %collective-permute-start.25 = (f32[24,720]{1,0:T(8,128)S(1)}, f32[24,720]{1,0:T(8,128)S(1)}, u32[]{:S(2)}, u32[]{:S(2)}) collective-permute-start(f32[24,720]{1,0:T(8,128)S(1)} %get-tuple-element.16), channel_id=1, source_target_pairs={{0,2},{1,3},{2,4},{3,5},{4,6},{5,7},{6,0},{7,1},{8,10},{9,11},{10,... | collective-permute-start | bytes 207368 | tf_op jit(solution)/shard_map/ppermute | solution.py:138
  89.3 9.7 %collective-permute-start.26 = (f32[24,720]{1,0:T(8,128)S(1)}, f32[24,720]{1,0:T(8,128)S(1)}, u32[]{:S(2)}, u32[]{:S(2)}) collective-permute-start(f32[24,720]{1,0:T(8,128)S(1)} %get-tuple-element.15), channel_id=1, source_target_pairs={{0,1},{1,2},{2,3},{3,4},{4,5},{5,6},{6,7},{7,0},{8,9},{9,10},{10,1... | collective-permute-start | bytes 207368 | tf_op jit(solution)/shard_map/ppermute | solution.py:138
  109.3 5.9 %collective-permute-start.27 = (f32[24,720]{1,0:T(8,128)S(1)}, f32[24,720]{1,0:T(8,128)S(1)}, u32[]{:S(2)}, u32[]{:S(2)}) collective-permute-start(f32[24,720]{1,0:T(8,128)S(1)} %get-tuple-element.29), channel_id=1, source_target_pairs={{0,1},{1,2},{2,3},{3,4},{4,5},{5,6},{6,7},{7,0},{8,9},{9,10},{10,1... | collective-permute-start | bytes 207368 | tf_op jit(solution)/shard_map/ppermute | solution.py:145
  109.4 7.5 %collective-permute-start.28 = (f32[24,720]{1,0:T(8,128)S(1)}, f32[24,720]{1,0:T(8,128)S(1)}, u32[]{:S(2)}, u32[]{:S(2)}) collective-permute-start(f32[24,720]{1,0:T(8,128)S(1)} %get-tuple-element.28), channel_id=1, source_target_pairs={{0,2},{1,3},{2,4},{3,5},{4,6},{5,7},{6,0},{7,1},{8,10},{9,11},{10,... | collective-permute-start | bytes 207368 | tf_op jit(solution)/shard_map/ppermute | solution.py:145
  109.6 12.4 %collective-permute-start.29 = (f32[24,720]{1,0:T(8,128)S(1)}, f32[24,720]{1,0:T(8,128)S(1)}, u32[]{:S(2)}, u32[]{:S(2)}) collective-permute-start(f32[24,720]{1,0:T(8,128)S(1)} %get-tuple-element.27), channel_id=1, source_target_pairs={{0,3},{1,4},{2,5},{3,6},{4,7},{5,0},{6,1},{7,2},{8,11},{9,12},{10,... | collective-permute-start | bytes 207368 | tf_op jit(solution)/shard_map/ppermute | solution.py:145
  111.9 10.4 %collective-permute-start.30 = (f32[24,720]{1,0:T(8,128)S(1)}, f32[24,720]{1,0:T(8,128)S(1)}, u32[]{:S(2)}, u32[]{:S(2)}) collective-permute-start(f32[24,720]{1,0:T(8,128)S(1)} %get-tuple-element.26), channel_id=1, source_target_pairs={{0,4},{1,5},{2,6},{3,7},{4,0},{5,1},{6,2},{7,3},{8,12},{9,13},{10,... | collective-permute-start | bytes 207368 | tf_op jit(solution)/shard_map/ppermute | solution.py:145
  113.6 8.7 %collective-permute-start.31 = (f32[24,720]{1,0:T(8,128)S(1)}, f32[24,720]{1,0:T(8,128)S(1)}, u32[]{:S(2)}, u32[]{:S(2)}) collective-permute-start(f32[24,720]{1,0:T(8,128)S(1)} %get-tuple-element.25), channel_id=1, source_target_pairs={{0,5},{1,6},{2,7},{3,0},{4,1},{5,2},{6,3},{7,4},{8,13},{9,14},{10,... | collective-permute-start | bytes 207368 | tf_op jit(solution)/shard_map/ppermute | solution.py:145
  115.2 7.1 %collective-permute-start.32 = (f32[24,720]{1,0:T(8,128)S(1)}, f32[24,720]{1,0:T(8,128)S(1)}, u32[]{:S(2)}, u32[]{:S(2)}) collective-permute-start(f32[24,720]{1,0:T(8,128)S(1)} %get-tuple-element.24), channel_id=1, source_target_pairs={{0,6},{1,7},{2,0},{3,1},{4,2},{5,3},{6,4},{7,5},{8,14},{9,15},{10,... | collective-permute-start | bytes 207368 | tf_op jit(solution)/shard_map/ppermute | solution.py:145
  116.9 5.4 %collective-permute-start.33 = (f32[24,720]{1,0:T(8,128)S(1)}, f32[24,720]{1,0:T(8,128)S(1)}, u32[]{:S(2)}, u32[]{:S(2)}) collective-permute-start(f32[24,720]{1,0:T(8,128)S(1)} %get-tuple-element.23), channel_id=1, source_target_pairs={{0,7},{1,0},{2,1},{3,2},{4,3},{5,4},{6,5},{7,6},{8,15},{9,8},{10,9... | collective-permute-start | bytes 207368 | tf_op jit(solution)/shard_map/ppermute | solution.py:145
  123.1 24.0 %collective-permute-start.35 = (f32[24,8,720]{2,1,0:T(8,128)S(1)}, f32[24,8,720]{2,1,0:T(8,128)S(1)}, u32[]{:S(2)}, u32[]{:S(2)}) collective-permute-start(f32[24,8,720]{2,1,0:T(8,128)S(1)} %bitcast.204), channel_id=1, source_target_pairs={{0,16},{8,24},{16,0},{24,8},{1,17},{9,25},{17,1},{25,9},{2,18},{10... | collective-permute-start | bytes 1658888 | tf_op jit(solution)/shard_map/ppermute | solution.py:151
  125.0 22.1 %collective-permute-start.34 = (f32[16,8,720]{2,1,0:T(8,128)S(1)}, f32[16,8,720]{2,1,0:T(8,128)S(1)}, u32[]{:S(2)}, u32[]{:S(2)}) collective-permute-start(f32[16,8,720]{2,1,0:T(8,128)S(1)} %bitcast.212), channel_id=1, source_target_pairs={{0,16},{8,24},{16,0},{24,8},{1,17},{9,25},{17,1},{25,9},{2,18},{10... | collective-permute-start | bytes 1105928 | tf_op jit(solution)/shard_map/ppermute | solution.py:151
  (33 other events, 249.4 us)

commit v12 on v4

--- a/solution.py
+++ b/solution.py
@@ -85,17 +85,19 @@
     ).reshape(field_count, level_count, rows_dev, columns + 2)
     wide_courant = jnp.concatenate([from_west[stacked:, :, None], lon_courant], axis=2)
     column_flux = face_flux(wide_courant, wide_fields[..., :-1], wide_fields[..., 1:])
-    tall_fields = jnp.concatenate(
-        [from_below[:stacked, None], flat_fields, from_above[:, None]], axis=1
-    ).reshape(field_count, level_count, rows_dev + 2, columns)
-    tall_courant = jnp.concatenate([from_below[stacked:, None], lat_courant], axis=1)
-    row_flux = face_flux(tall_courant, tall_fields[:, :, :-1], tall_fields[:, :, 1:])
     tile_index = lax.axis_index("lat")
-    lower_row = tile_index * rows_dev - 1 + jnp.arange(rows_dev + 1, dtype=jnp.int32)
-    row_flux = jnp.where((lower_row == rows_dev * lat_devices - 1)[:, None], 0.0, row_flux)
-    increment = -(column_flux[..., 1:] - column_flux[..., :-1]) - (
-        row_flux[:, :, 1:] - row_flux[:, :, :-1]
+    above_fields = from_above.reshape(field_count, level_count, 1, columns)
+    upper = jnp.concatenate([fields[:, :, 1:], above_fields], axis=2)
+    north_flux = face_flux(lat_courant, fields, upper)
+    own_row = tile_index * rows_dev + jnp.arange(rows_dev, dtype=jnp.int32)
+    north_flux = jnp.where((own_row == rows_dev * lat_devices - 1)[:, None], 0.0, north_flux)
+    south_edge = face_flux(
+        from_below[stacked:],
+        from_below[:stacked].reshape(field_count, level_count, columns),
+        fields[:, :, 0],
     )
+    south_flux = jnp.concatenate([south_edge[:, :, None], north_flux[:, :, :-1]], axis=2)
+    increment = -(column_flux[..., 1:] - column_flux[..., :-1]) - (north_flux - south_flux)
     flat_increment = increment.reshape(stacked, rows_dev, columns)
     half_rows = rows_dev // 2
     pair_shift = lat_devices // 2

time: 141 us -> 146 us (1.035)
  other arithmetic: 11.6 us -> 16.4 us
  waiting for transfers between devices: 62 us -> 59.7 us
    concatenate x6 -> x0, local copies, waits for them, and re-layouts: 4.43 us -> none  [the longest x4 4.4 us: body(): jnp.concatenate([from_below[:stacked, None], flat_fields, from_above[:, N...]
    ppermute x1, waiting for transfers between devices: 2.3 us -> 0.01 us  [body(): lax.ppermute(jnp.concatenate([flat_fields[..., -1], lon_courant[..., -1]]...]
    slice x0 -> x2, local copies, waits for them, and re-layouts: none -> 2.19 us  [the longest x1 1.48 us: body(): upper = jnp.concatenate([fields[:, :, 1:], above_fields], axis=2)]
    concatenate x2, local copies, waits for them, and re-layouts: 0.62 us -> 2.8 us  [body(): jnp.concatenate([from_west[:stacked, :, None], flat_fields, from_east[:,...]
    select_n x1, other arithmetic: 2.85 us -> 0.69 us  [body(): jnp.where((own_row == rows_dev * lat_devices - 1)[:, None], 0.0, north_flux)]
    mul x2 -> x3, other arithmetic: 0.28 us -> 1.98 us  [face_flux(): 0.5 * courant * (near_value + far_value)]
    slice x1, local copies, waits for them, and re-layouts: 1.82 us -> 0.17 us  [body(): flat_fields[:, -1]]
    unnamed x46 -> x49, local copies, waits for them, and re-layouts: 3.51 us -> 2.61 us
  transfers between devices with their start and end apart: 12 -> 12, of which waited for: 8 -> 7; matrix products, arithmetic and copies ran while one was open for 20% -> 23% of each run, Pallas kernels for 0% -> 0%
where the time goes in v12:
time: 146 us; the launch traced here: 145 us
  waiting for transfers between devices  59.7 us (41%)
  starting transfers between devices  31.6 us (22%)
  local copies, waits for them, and re-layouts  22.2 us (15%)
  other arithmetic  16.4 us (11%)
  matrix products  14.7 us (10%)
    all_to_all x2, waiting for transfers between devices, body(): lax.all_to_all(smoothed, 'lon', split_axis=1, concat_axis=0, tiled=True)  22.8 us
    all_to_all x2, waiting for transfers between devices, body(): lax.all_to_all(pair_lines.reshape(chunk_stack * half_rows, columns), 'lon...  14.3 us
    ppermute x2, waiting for transfers between devices, body(): taken = lax.ppermute(given[rows_of_part], 'lat', pair_perm)  12.8 us
    ppermute x2, waiting for transfers between devices, body(): handed_parts.append(lax.ppermute(returned, 'lat', pair_perm))  9.78 us
    all_to_all x2, starting transfers between devices, body(): lax.all_to_all(pair_lines.reshape(chunk_stack * half_rows, columns), 'lon...  7.17 us
    all_to_all x2, starting transfers between devices, body(): lax.all_to_all(smoothed, 'lon', split_axis=1, concat_axis=0, tiled=True)  6.99 us
    ppermute x1, starting transfers between devices, body(): lax.ppermute(jnp.concatenate([flat_fields[:, -1], lat_courant[:, -1]], ax...  4.54 us
    ppermute x2, starting transfers between devices, body(): handed_parts.append(lax.ppermute(returned, 'lat', pair_perm))  4.08 us
  transfers between devices with their start and end apart: 12, of which 7 were waited for; matrix products, arithmetic and copies ran while one was open for 23% of the time, Pallas kernels for 0%

profile of v12, /device:TPU:0, one launch (start us, length us, event | category | flops | bytes accessed | tf_op | source)
XLA Modules:
  0.0 145.3 jit_solution(3792138464786406546)
XLA Ops:
  0.0 1.4 fusion.246
  1.6 1.0 slice.82
  3.5 4.1 %collective-permute-start.1 = (f32[40,16]{0,1:T(8,128)S(1)}, f32[40,16]{0,1:T(8,128)S(1)}, u32[]{:S(2)}, u32[]{:S(2)}) collective-permute-start(f32[40,16]{0,1:T(8,128)S(1)} %bitcast.150), channel_id=1, source_target_pairs={{1,0},{2,1},{3,2},{4,3},{5,4},{6,5},{7,6},{0,7},{9,8},{10,9},{11,1... | collective-permute-start | bytes 7688 | tf_op jit(solution)/shard_map/ppermute | solution.py:78
  9.4 4.5 %collective-permute-start.3 = (f32[48,720]{1,0:T(8,128)}, f32[48,720]{1,0:T(8,128)}, u32[]{:S(2)}, u32[]{:S(2)}) collective-permute-start(f32[48,720]{1,0:T(8,128)} %pad_maximum_fusion.6), channel_id=1, source_target_pairs={{0,8},{8,16},{16,24},{1,9},{9,17},{17,25},{2,10},{10,18},{18,26},{... | collective-permute-start | bytes 414728 | tf_op jit(solution)/shard_map/ppermute | solution.py:79
  14.6 1.3 collective-permute-start.2
  20.7 1.5 %slice.88 = f32[5,8,15,720]{3,2,1,0:T(8,128)} slice(f32[5,8,16,720]{3,2,1,0:T(8,128)S(1)} %copy-done), slice={[0:5], [0:8], [1:16], [0:720]} | slice | bytes 3456000 | tf_op jit(solution)/shard_map/slice | solution.py:90
  22.2 1.0 copy.108
  24.2 1.2 fusion.45
  26.0 1.8 %copy.105 = f32[5,8,16,1]{3,2,1,0:T(8,128)} copy(f32[5,8,16,1]{2,1,0,3:T(8,128)} %bitcast.146) | data formatting | bytes 5120 | tf_op jit(solution)/shard_map/concatenate | solution.py:83
  27.8 1.9 %multiply_subtract_fusion = f32[5,8,16,721]{3,2,1,0:T(8,128)S(1)} fusion(f32[5,8,16,1]{3,2,1,0:T(8,128)} %copy.108, f32[5,8,16,720]{3,2,1,0:T(8,128)S(1)} %copy-done, f32[5,8,16,1]{3,2,1,0:T(8,128)} %copy.105, f32[8,16,721]{2,1,0:T(8,128)S(1)} %get-tuple-element.14, f32[8,16,721]{2,1,0:T(8,128)S(1)} %get-tuple-element.13), kind=kLoop, calls=%fused_computation.13 | loop fusion | flops 3230080 | bytes 4432384 | tf_op jit(solution)/shard_map/sub | solution.py:60
  29.7 1.0 copy.109
  34.4 1.1 copy-done.1
  35.5 3.0 %collective-permute-start.4 = (f32[16,8,720]{2,1,0:T(8,128)S(1)}, f32[16,8,720]{2,1,0:T(8,128)S(1)}, u32[]{:S(2)}, u32[]{:S(2)}) collective-permute-start(f32[16,8,720]{2,1,0:T(8,128)S(1)} %slice.122), channel_id=1, source_target_pairs={{0,16},{8,24},{16,0},{24,8},{1,17},{9,25},{17,1},{25,9},{2,18},{10... | collective-permute-start | bytes 1105928 | tf_op jit(solution)/shard_map/ppermute | solution.py:131
  39.4 9.1 %collective-permute-done.4 = f32[16,8,720]{2,1,0:T(8,128)S(1)} collective-permute-done((f32[16,8,720]{2,1,0:T(8,128)S(1)}, f32[16,8,720]{2,1,0:T(8,128)S(1)}, u32[]{:S(2)}, u32[]{:S(2)}) %collective-permute-start.4) | collective-permute-done | bytes 368672 | tf_op jit(solution)/shard_map/ppermute | solution.py:131
  49.4 3.5 %all-to-all-start = ((f32[8,16,720]{2,1,0:T(8,128)}), f32[8,16,720]{2,1,0:T(8,128)S(1)}, u32[]{:S(2)}, u32[]{:S(2)}) async-start(f32[8,16,720]{2,1,0:T(8,128)} %bitcast.140), calls=%async_computation | async-start | bytes 786432 | tf_op jit(solution)/shard_map/all_to_all | solution.py:133
  54.4 3.7 %collective-permute-done.5 = f32[24,8,720]{2,1,0:T(8,128)} collective-permute-done((f32[24,8,720]{2,1,0:T(8,128)}, f32[24,8,720]{2,1,0:T(8,128)}, u32[]{:S(2)}, u32[]{:S(2)}) %collective-permute-start.5) | collective-permute-done | bytes 552992 | tf_op jit(solution)/shard_map/ppermute | solution.py:131
  58.1 2.0 %slice_select_fusion.2 = f32[24,8,720]{2,1,0:T(8,128)} fusion(f32[24,8,720]{2,1,0:T(8,128)} %collective-permute-done.5, f32[40,8,720]{2,1,0:T(8,128)S(1)} %get-tuple-element.7, pred[8]{0:T(512)(128)(4,1)S(1)} %copy-done.19), kind=kLoop, calls=%fused_computation.40 | loop fusion | flops 138240 | bytes 1658888 | tf_op jit(solution)/shard_map/jit(_where)/select_n | solution.py:132
  60.1 5.2 %all-to-all-done = f32[8,16,720]{2,1,0:T(8,128)S(1)} async-done(((f32[8,16,720]{2,1,0:T(8,128)}), f32[8,16,720]{2,1,0:T(8,128)S(1)}, u32[]{:S(2)}, u32[]{:S(2)}) %all-to-all-start) | async-done | bytes 368672 | tf_op jit(solution)/shard_map/all_to_all | solution.py:133
  65.3 3.7 %all-to-all-start.2 = ((f32[8,24,720]{2,1,0:T(8,128)}), f32[8,24,720]{2,1,0:T(8,128)S(1)}, u32[]{:S(2)}, u32[]{:S(2)}) async-start(f32[8,24,720]{2,1,0:T(8,128)} %bitcast.23), calls=%async_computation.2 | async-start | bytes 1179648 | tf_op jit(solution)/shard_map/all_to_all | solution.py:133
  69.0 1.0 copy.113
  70.0 1.2 reshape.299
  76.3 9.2 %all-to-all-done.2 = f32[8,24,720]{2,1,0:T(8,128)S(1)} async-done(((f32[8,24,720]{2,1,0:T(8,128)}), f32[8,24,720]{2,1,0:T(8,128)S(1)}, u32[]{:S(2)}, u32[]{:S(2)}) %all-to-all-start.2) | async-done | bytes 552992 | tf_op jit(solution)/shard_map/all_to_all | solution.py:133
  94.2 1.0 copy.116
  95.3 3.5 %all-to-all-start.3 = ((f32[24,8,720]{2,0,1:T(8,128)}), f32[24,8,720]{2,0,1:T(8,128)S(1)}, u32[]{:S(2)}, u32[]{:S(2)}) async-start(f32[24,8,720]{2,0,1:T(8,128)} %copy.116), calls=%async_computation.3 | async-start | bytes 1179648 | tf_op jit(solution)/shard_map/all_to_all | solution.py:141
  98.8 1.6 %fusion.68 = f32[16,45,128]{2,1,0:T(8,128)S(1)} fusion(f32[16,45,128]{2,1,0:T(8,128)} %copy-done.12), kind=kOutput, calls=%fused_computation.112 | convolution fusion | flops 71008256 | bytes 737280 | tf_op jit(solution)/shard_map/ljk,kn->ljn/dot_general | solution.py:50
  103.1 12.4 %all-to-all-done.3 = f32[24,8,720]{2,0,1:T(8,128)S(1)} async-done(((f32[24,8,720]{2,0,1:T(8,128)}), f32[24,8,720]{2,0,1:T(8,128)S(1)}, u32[]{:S(2)}, u32[]{:S(2)}) %all-to-all-start.3) | async-done | bytes 552992 | tf_op jit(solution)/shard_map/all_to_all | solution.py:141
  115.5 3.5 %all-to-all-start.1 = ((f32[16,8,720]{2,0,1:T(8,128)}), f32[16,8,720]{2,0,1:T(8,128)S(1)}, u32[]{:S(2)}, u32[]{:S(2)}) async-start(f32[16,8,720]{2,0,1:T(8,128)} %copy.114), calls=%async_computation.1 | async-start | bytes 786432 | tf_op jit(solution)/shard_map/all_to_all | solution.py:141
  119.0 2.1 %collective-permute-start.7 = (f32[24,8,720]{2,1,0:T(8,128)S(1)}, f32[24,8,720]{2,1,0:T(8,128)S(1)}, u32[]{:S(2)}, u32[]{:S(2)}) collective-permute-start(f32[24,8,720]{2,1,0:T(8,128)S(1)} %bitcast.137), channel_id=1, source_target_pairs={{0,16},{8,24},{16,0},{24,8},{1,17},{9,25},{17,1},{25,9},{2,18},{10... | collective-permute-start | bytes 1658888 | tf_op jit(solution)/shard_map/ppermute | solution.py:145
  121.0 10.4 %all-to-all-done.1 = f32[16,8,720]{2,0,1:T(8,128)S(1)} async-done(((f32[16,8,720]{2,0,1:T(8,128)}), f32[16,8,720]{2,0,1:T(8,128)S(1)}, u32[]{:S(2)}, u32[]{:S(2)}) %all-to-all-start.1) | async-done | bytes 368672 | tf_op jit(solution)/shard_map/all_to_all | solution.py:141
  131.4 2.0 %collective-permute-start.6 = (f32[16,8,720]{2,1,0:T(8,128)S(1)}, f32[16,8,720]{2,1,0:T(8,128)S(1)}, u32[]{:S(2)}, u32[]{:S(2)}) collective-permute-start(f32[16,8,720]{2,1,0:T(8,128)S(1)} %bitcast.141), channel_id=1, source_target_pairs={{0,16},{8,24},{16,0},{24,8},{1,17},{9,25},{17,1},{25,9},{2,18},{10... | collective-permute-start | bytes 1105928 | tf_op jit(solution)/shard_map/ppermute | solution.py:145
  133.5 9.8 %collective-permute-done.6 = f32[16,8,720]{2,1,0:T(8,128)S(1)} collective-permute-done((f32[16,8,720]{2,1,0:T(8,128)S(1)}, f32[16,8,720]{2,1,0:T(8,128)S(1)}, u32[]{:S(2)}, u32[]{:S(2)}) %collective-permute-start.6) | collective-permute-done | bytes 368672 | tf_op jit(solution)/shard_map/ppermute | solution.py:145
  143.4 1.9 %fusion.3 = f32[5,8,16,720]{3,2,1,0:T(8,128)} fusion(f32[5,8,16,720]{3,2,1,0:T(8,128)S(1)} %copy-done, f32[5,8,16,720]{3,2,1,0:T(8,128)S(1)} %copy-done.2, f32[5,8,8,720]{3,2,1,0:T(8,128)S(1)} %bitcast.135, f32[5,8,8,720]{3,2,1,0:T(8,128)S(1)} %bitcast.134, pred[16]{0:T(512)(128)(4,1)S(1)} %compare_reduce_fusion, pred[]{:T(512)S(6)} %lt.139), kind=kLoop, calls=%fused_computation.11 | loop fusion | flops 2304000 | bytes 7372817 | tf_op jit(solution)/shard_map/add | solution.py:154
  (125 shorter events, 33.2 us)
Async XLA Ops:
  0.0 7.5 %copy-start = (f32[5,8,16,720]{3,2,1,0:T(8,128)S(1)}, f32[5,8,16,720]{3,2,1,0:T(8,128)}, u32[]{:S(2)}) copy-start(f32[5,8,16,720]{3,2,1,0:T(8,128)} %param.5) | copy-start | bytes 5529604
  1.6 14.3 %copy-start.14 = (f32[8,16,720]{2,1,0:T(8,128)S(1)}, f32[8,16,720]{2,1,0:T(8,128)}, u32[]{:S(2)}) copy-start(f32[8,16,720]{2,1,0:T(8,128)} %param.7) | copy-start | bytes 1105924
  2.8 20.5 %collective-permute-start = (f32[48,16]{0,1:T(8,128)S(1)}, f32[48,16]{0,1:T(8,128)S(1)}, u32[]{:S(2)}, u32[]{:S(2)}) collective-permute-start(f32[48,16]{0,1:T(8,128)S(1)} %pad_maximum_fusion.7), channel_id=1, source_target_pairs={{0,1},{1,2},{2,3},{3,4},{4,5},{5,6},{6,7},{7,0},{8,9},{9,10},{10,1... | collective-permute-start | bytes 9224 | tf_op jit(solution)/shard_map/ppermute | solution.py:75
  3.5 18.7 %collective-permute-start.1 = (f32[40,16]{0,1:T(8,128)S(1)}, f32[40,16]{0,1:T(8,128)S(1)}, u32[]{:S(2)}, u32[]{:S(2)}) collective-permute-start(f32[40,16]{0,1:T(8,128)S(1)} %bitcast.150), channel_id=1, source_target_pairs={{1,0},{2,1},{3,2},{4,3},{5,4},{6,5},{7,6},{0,7},{9,8},{10,9},{11,1... | collective-permute-start | bytes 7688 | tf_op jit(solution)/shard_map/ppermute | solution.py:78
  9.4 22.1 %collective-permute-start.3 = (f32[48,720]{1,0:T(8,128)}, f32[48,720]{1,0:T(8,128)}, u32[]{:S(2)}, u32[]{:S(2)}) collective-permute-start(f32[48,720]{1,0:T(8,128)} %pad_maximum_fusion.6), channel_id=1, source_target_pairs={{0,8},{8,16},{16,24},{1,9},{9,17},{17,25},{2,10},{10,18},{18,26},{... | collective-permute-start | bytes 414728 | tf_op jit(solution)/shard_map/ppermute | solution.py:79
  14.6 15.1 %collective-permute-start.2 = (f32[40,720]{1,0:T(8,128)}, f32[40,720]{1,0:T(8,128)}, u32[]{:S(2)}, u32[]{:S(2)}) collective-permute-start(f32[40,720]{1,0:T(8,128)} %bitcast.126), channel_id=1, source_target_pairs={{8,0},{16,8},{24,16},{9,1},{17,9},{25,17},{10,2},{18,10},{26,18},{... | collective-permute-start | bytes 345608 | tf_op jit(solution)/shard_map/ppermute | solution.py:82
  27.8 3.0 %copy-start.3 = (f32[5,8,15,720]{3,2,1,0:T(8,128)S(1)}, f32[5,8,15,720]{3,2,1,0:T(8,128)}, u32[]{:S(2)}) copy-start(f32[5,8,15,720]{3,2,1,0:T(8,128)} %slice.88) | copy-start | bytes 5184004
  27.8 3.0 %copy-start.21 = (pred[16]{0:T(512)(128)(4,1)S(1)}, pred[16]{0:T(512)(128)(4,1)}, u32[]{:S(2)}) copy-start(pred[16]{0:T(512)(128)(4,1)} %broadcast_compare_fusion) | copy-start | bytes 52
  30.8 1.5 %copy-start.13 = (f32[5,8,1,720]{3,2,1,0:T(1,128)S(1)}, f32[5,8,1,720]{3,2,1,0:T(1,128)}, u32[]{:S(2)}) copy-start(f32[5,8,1,720]{3,2,1,0:T(1,128)} %slice.94) | copy-start | bytes 345604
  34.2 1.3 copy-start.1
  34.2 4.3 %copy-start.22 = (s32[16]{0:T(128)S(1)}, s32[16]{0:T(128)}, u32[]{:S(2)}) copy-start(s32[16]{0:T(128)} %fusion.155) | copy-start | bytes 196
  34.2 4.3 %copy-start.20 = (s32[128]{0:T(128)S(1)}, s32[128]{0:T(128)}, u32[]{:S(2)}) copy-start(s32[128]{0:T(128)} %iota_multiply_fusion) | copy-start | bytes 1540
  35.5 13.1 %copy-start.19 = (pred[8]{0:T(512)(128)(4,1)S(1)}, pred[8]{0:T(512)(128)(4,1)}, u32[]{:S(2)}) copy-start(pred[8]{0:T(512)(128)(4,1)} %slice_select_fusion.4) | copy-start | bytes 28
  35.5 13.0 %collective-permute-start.4 = (f32[16,8,720]{2,1,0:T(8,128)S(1)}, f32[16,8,720]{2,1,0:T(8,128)S(1)}, u32[]{:S(2)}, u32[]{:S(2)}) collective-permute-start(f32[16,8,720]{2,1,0:T(8,128)S(1)} %slice.122), channel_id=1, source_target_pairs={{0,16},{8,24},{16,0},{24,8},{1,17},{9,25},{17,1},{25,9},{2,18},{10... | collective-permute-start | bytes 1105928 | tf_op jit(solution)/shard_map/ppermute | solution.py:131
  38.5 35.9 %copy-start.15 = (f32[45,128]{1,0:T(8,128)}, f32[45,128]{1,0:T(8,128)S(1)}, u32[]{:S(2)}) copy-start(f32[45,128]{1,0:T(8,128)S(1)} %broadcast_maximum_fusion) | copy-start | bytes 69124
  39.4 18.7 %collective-permute-start.5 = (f32[24,8,720]{2,1,0:T(8,128)}, f32[24,8,720]{2,1,0:T(8,128)}, u32[]{:S(2)}, u32[]{:S(2)}) collective-permute-start(f32[24,8,720]{2,1,0:T(8,128)} %slice.124), channel_id=1, source_target_pairs={{0,16},{8,24},{16,0},{24,8},{1,17},{9,25},{17,1},{25,9},{2,18},{10... | collective-permute-start | bytes 1658888 | tf_op jit(solution)/shard_map/ppermute | solution.py:131
  49.4 15.9 %all-to-all-start = ((f32[8,16,720]{2,1,0:T(8,128)}), f32[8,16,720]{2,1,0:T(8,128)S(1)}, u32[]{:S(2)}, u32[]{:S(2)}) async-start(f32[8,16,720]{2,1,0:T(8,128)} %bitcast.140), calls=%async_computation | async-start | bytes 786432 | tf_op jit(solution)/shard_map/all_to_all | solution.py:133
  54.3 20.1 %copy-start.4 = (f32[45,128]{1,0:T(8,128)}, f32[45,128]{1,0:T(8,128)S(1)}, u32[]{:S(2)}) copy-start(f32[45,128]{1,0:T(8,128)S(1)} %get-tuple-element.19) | copy-start | bytes 69124
  54.3 20.1 %copy-start.7 = (f32[45,128]{1,0:T(8,128)}, f32[45,128]{1,0:T(8,128)S(1)}, u32[]{:S(2)}) copy-start(f32[45,128]{1,0:T(8,128)S(1)} %get-tuple-element.20) | copy-start | bytes 69124
  54.4 20.0 %copy-start.17 = (f32[45,128]{1,0:T(8,128)}, f32[45,128]{1,0:T(8,128)S(1)}, u32[]{:S(2)}) copy-start(f32[45,128]{1,0:T(8,128)S(1)} %fusion.99) | copy-start | bytes 69124
  65.3 20.2 %all-to-all-start.2 = ((f32[8,24,720]{2,1,0:T(8,128)}), f32[8,24,720]{2,1,0:T(8,128)S(1)}, u32[]{:S(2)}, u32[]{:S(2)}) async-start(f32[8,24,720]{2,1,0:T(8,128)} %bitcast.23), calls=%async_computation.2 | async-start | bytes 1179648 | tf_op jit(solution)/shard_map/all_to_all | solution.py:133
  73.2 1.8 %copy-start.10 = (f32[16,45,128]{2,1,0:T(8,128)}, f32[16,45,128]{2,1,0:T(8,128)S(1)}, u32[]{:S(2)}) copy-start(f32[16,45,128]{2,1,0:T(8,128)S(1)} %fusion.8) | copy-start | bytes 1105924
  87.2 1.3 copy-start.16
  87.2 1.3 copy-start.18
  94.2 6.2 %copy-start.11 = (f32[16,45,128]{2,1,0:T(8,128)S(1)}, f32[16,45,128]{2,1,0:T(8,128)}, u32[]{:S(2)}) copy-start(f32[16,45,128]{2,1,0:T(8,128)} %copy-done.10) | copy-start | bytes 1105924
  94.2 6.7 %copy-start.6 = (f32[45,128]{1,0:T(8,128)S(1)}, f32[45,128]{1,0:T(8,128)}, u32[]{:S(2)}) copy-start(f32[45,128]{1,0:T(8,128)} %copy-done.4) | copy-start | bytes 69124
  94.2 6.7 %copy-start.9 = (f32[45,128]{1,0:T(8,128)S(1)}, f32[45,128]{1,0:T(8,128)}, u32[]{:S(2)}) copy-start(f32[45,128]{1,0:T(8,128)} %copy-done.7) | copy-start | bytes 69124
  95.3 20.2 %all-to-all-start.3 = ((f32[24,8,720]{2,0,1:T(8,128)}), f32[24,8,720]{2,0,1:T(8,128)S(1)}, u32[]{:S(2)}, u32[]{:S(2)}) async-start(f32[24,8,720]{2,0,1:T(8,128)} %copy.116), calls=%async_computation.3 | async-start | bytes 1179648 | tf_op jit(solution)/shard_map/all_to_all | solution.py:141
  115.5 15.9 %all-to-all-start.1 = ((f32[16,8,720]{2,0,1:T(8,128)}), f32[16,8,720]{2,0,1:T(8,128)S(1)}, u32[]{:S(2)}, u32[]{:S(2)}) async-start(f32[16,8,720]{2,0,1:T(8,128)} %copy.114), calls=%async_computation.1 | async-start | bytes 786432 | tf_op jit(solution)/shard_map/all_to_all | solution.py:141
  119.0 24.3 %collective-permute-start.7 = (f32[24,8,720]{2,1,0:T(8,128)S(1)}, f32[24,8,720]{2,1,0:T(8,128)S(1)}, u32[]{:S(2)}, u32[]{:S(2)}) collective-permute-start(f32[24,8,720]{2,1,0:T(8,128)S(1)} %bitcast.137), channel_id=1, source_target_pairs={{0,16},{8,24},{16,0},{24,8},{1,17},{9,25},{17,1},{25,9},{2,18},{10... | collective-permute-start | bytes 1658888 | tf_op jit(solution)/shard_map/ppermute | solution.py:145
  131.4 11.9 %copy-start.2 = (f32[5,8,16,720]{3,2,1,0:T(8,128)S(1)}, f32[5,8,16,720]{3,2,1,0:T(8,128)}, u32[]{:S(2)}) copy-start(f32[5,8,16,720]{3,2,1,0:T(8,128)} %copy-done.1) | copy-start | bytes 5529604
  131.4 11.9 %collective-permute-start.6 = (f32[16,8,720]{2,1,0:T(8,128)S(1)}, f32[16,8,720]{2,1,0:T(8,128)S(1)}, u32[]{:S(2)}, u32[]{:S(2)}) collective-permute-start(f32[16,8,720]{2,1,0:T(8,128)S(1)} %bitcast.141), channel_id=1, source_target_pairs={{0,16},{8,24},{16,0},{24,8},{1,17},{9,25},{17,1},{25,9},{2,18},{10... | collective-permute-start | bytes 1105928 | tf_op jit(solution)/shard_map/ppermute | solution.py:145
  (3 other events, 2.9 us)

commit v13 on v4

--- a/solution.py
+++ b/solution.py
@@ -73,22 +73,22 @@
     northward = [(i, i + 1) for i in range(lat_devices - 1)]
     southward = [(i + 1, i) for i in range(lat_devices - 1)]
     from_west = lax.ppermute(
-        jnp.concatenate([flat_fields[..., -1], lon_courant[..., -1]], axis=0), "lon", eastward
+        jnp.concatenate([fields[..., -1], lon_courant[None, ..., -1]], axis=0), "lon", eastward
     )
-    from_east = lax.ppermute(flat_fields[..., 0], "lon", westward)
+    from_east = lax.ppermute(fields[..., 0], "lon", westward)
     from_below = lax.ppermute(
-        jnp.concatenate([flat_fields[:, -1], lat_courant[:, -1]], axis=0), "lat", northward
+        jnp.concatenate([fields[:, :, -1], lat_courant[None, :, -1]], axis=0), "lat", northward
     )
-    from_above = lax.ppermute(flat_fields[:, 0], "lat", southward)
+    from_above = lax.ppermute(fields[:, :, 0], "lat", southward)
     wide_fields = jnp.concatenate(
-        [from_west[:stacked, :, None], flat_fields, from_east[:, :, None]], axis=2
-    ).reshape(field_count, level_count, rows_dev, columns + 2)
-    wide_courant = jnp.concatenate([from_west[stacked:, :, None], lon_courant], axis=2)
+        [from_west[:field_count, ..., None], fields, from_east[..., None]], axis=3
+    )
+    wide_courant = jnp.concatenate([from_west[field_count, ..., None], lon_courant], axis=2)
     column_flux = face_flux(wide_courant, wide_fields[..., :-1], wide_fields[..., 1:])
     tall_fields = jnp.concatenate(
-        [from_below[:stacked, None], flat_fields, from_above[:, None]], axis=1
-    ).reshape(field_count, level_count, rows_dev + 2, columns)
-    tall_courant = jnp.concatenate([from_below[stacked:, None], lat_courant], axis=1)
+        [from_below[:field_count, :, None], fields, from_above[:, :, None]], axis=2
+    )
+    tall_courant = jnp.concatenate([from_below[field_count, :, None], lat_courant], axis=1)
     row_flux = face_flux(tall_courant, tall_fields[:, :, :-1], tall_fields[:, :, 1:])
     tile_index = lax.axis_index("lat")
     lower_row = tile_index * rows_dev - 1 + jnp.arange(rows_dev + 1, dtype=jnp.int32)

time: 141 us -> 142 us (level)
    concatenate x10 -> x5, local copies, waits for them, and re-layouts: 5.31 us -> 3.4 us  [the longest x1 3.24 us: body(): jnp.concatenate([from_below[:field_count, :, None], fields, from_above[:,...]
    broadcast_in_dim x0 -> x6, local copies, waits for them, and re-layouts: none -> 1.79 us  [the longest x1 1.03 us: body(): from_above[:, :, None]]
    unnamed x46 -> x49, local copies, waits for them, and re-layouts: 3.51 us -> 4.21 us
    slice x7 -> x4, local copies, waits for them, and re-layouts: 4.55 us -> 4.08 us  [the longest x1 1.82 us: body(): fields[:, :, -1]]
where the time goes in v13:
time: 142 us; the launch traced here: 141 us
  waiting for transfers between devices  62.3 us (44%)
  starting transfers between devices  30.4 us (21%)
  local copies, waits for them, and re-layouts  21.2 us (15%)
  matrix products  14.7 us (10%)
  other arithmetic  11.5 us (8%)
    all_to_all x2, waiting for transfers between devices, body(): lax.all_to_all(smoothed, 'lon', split_axis=1, concat_axis=0, tiled=True)  22.8 us
    all_to_all x2, waiting for transfers between devices, body(): lax.all_to_all(pair_lines.reshape(chunk_stack * half_rows, columns), 'lon...  15.3 us
    ppermute x2, waiting for transfers between devices, body(): taken = lax.ppermute(given[rows_of_part], 'lat', pair_perm)  11.9 us
    ppermute x2, waiting for transfers between devices, body(): handed_parts.append(lax.ppermute(returned, 'lat', pair_perm))  9.78 us
    all_to_all x2, starting transfers between devices, body(): lax.all_to_all(pair_lines.reshape(chunk_stack * half_rows, columns), 'lon...  7.17 us
    all_to_all x2, starting transfers between devices, body(): lax.all_to_all(smoothed, 'lon', split_axis=1, concat_axis=0, tiled=True)  6.99 us
    ppermute x1, starting transfers between devices, body(): lax.ppermute(jnp.concatenate([fields[:, :, -1], lat_courant[None, :, -1]]...  5.48 us
    unnamed x49, local copies, waits for them, and re-layouts  4.21 us
  transfers between devices with their start and end apart: 12, of which 8 were waited for; matrix products, arithmetic and copies ran while one was open for 20% of the time, Pallas kernels for 0%

profile of v13, /device:TPU:0, one launch (start us, length us, event | category | flops | bytes accessed | tf_op | source)
XLA Modules:
  0.0 140.8 jit_solution(5544687707888314479)
XLA Ops:
  0.0 1.8 %fusion.247 = (f32[5,8,1,720]{3,2,1,0:T(1,128)S(1)}, f32[5,8,1,720]{3,2,1,0:T(1,128)S(1)}) fusion(f32[5,8,16,720]{3,2,1,0:T(8,128)} %param.5), kind=kLoop, calls=%fused_computation.290 | loop fusion | bytes 460800 | tf_op jit(solution)/shard_map/slice | solution.py:80
  1.8 1.3 collective-permute-start.3
  4.1 5.5 %collective-permute-start.2 = (f32[6,8,720]{2,1,0:T(8,128)S(1)}, f32[6,8,720]{2,1,0:T(8,128)S(1)}, u32[]{:S(2)}, u32[]{:S(2)}) collective-permute-start(f32[6,8,720]{2,1,0:T(8,128)S(1)} %pad_maximum_fusion.7), channel_id=1, source_target_pairs={{0,8},{8,16},{16,24},{1,9},{9,17},{17,25},{2,10},{10,18},{18,26},{... | collective-permute-start | bytes 414728 | tf_op jit(solution)/shard_map/ppermute | solution.py:79
  9.6 1.2 fusion.246
  11.2 3.1 %collective-permute-start.1 = (f32[5,8,16]{2,1,0:T(8,128)S(1)}, f32[5,8,16]{2,1,0:T(8,128)S(1)}, u32[]{:S(2)}, u32[]{:S(2)}) collective-permute-start(f32[5,8,16]{2,1,0:T(8,128)S(1)} %bitcast.141), channel_id=1, source_target_pairs={{1,0},{2,1},{3,2},{4,3},{5,4},{6,5},{7,6},{0,7},{9,8},{10,9},{11,1... | collective-permute-start | bytes 7688 | tf_op jit(solution)/shard_map/ppermute | solution.py:78
  14.8 1.6 %constant_dynamic-update-slice_fusion = f32[5,8,17,720]{3,2,1,0:T(8,128)} fusion(f32[5,8,16,720]{3,2,1,0:T(8,128)S(1)} %copy-done), kind=kLoop, calls=%fused_computation.187 | loop fusion | bytes 3809280
  17.3 2.6 %collective-permute-done = f32[6,8,16]{2,1,0:T(8,128)S(1)} collective-permute-done((f32[6,8,16]{2,1,0:T(8,128)S(1)}, f32[6,8,16]{2,1,0:T(8,128)S(1)}, u32[]{:S(2)}, u32[]{:S(2)}) %collective-permute-start) | collective-permute-done | bytes 3104 | tf_op jit(solution)/shard_map/ppermute | solution.py:75
  20.5 2.0 %multiply_subtract_fusion = f32[5,8,16,721]{3,2,1,0:T(8,128)} fusion(f32[5,8,16,1]{3,2,1,0:T(8,128)S(1)} %copy.52, f32[5,8,16,720]{3,2,1,0:T(8,128)S(1)} %copy-done, f32[5,8,16,1]{3,2,1,0:T(8,128)S(1)} %copy.50, f32[8,16,721]{2,1,0:T(8,128)S(1)} %get-tuple-element.14, f32[8,16,721]{2,1,0:T(8,128)S(1)} %get-tuple-element.13), kind=kLoop, calls=%fused_computation.13 | loop fusion | flops 3230080 | bytes 4432384 | tf_op jit(solution)/shard_map/sub | solution.py:60
  22.4 1.0 copy.58
  23.5 3.2 %dynamic-update-slice.1 = f32[5,8,17,720]{3,2,1,0:T(8,128)} dynamic-update-slice(f32[5,8,17,720]{3,2,1,0:T(8,128)} %constant_dynamic-update-slice_fusion, f32[5,8,1,720]{3,2,1,0:T(1,128)S(1)} %copy.58, s32[]{} %constant.131, s32[]{} %constant.131, s32[]{} %constant.132, s32[]{} %constant.131) | dynamic-update-slice | bytes 230404 | tf_op jit(solution)/shard_map/concatenate | solution.py:88
  27.0 2.9 %subtract_select_fusion = f32[5,8,17,720]{3,2,1,0:T(8,128)S(1)} fusion(f32[5,8,17,720]{3,2,1,0:T(8,128)} %dynamic-update-slice.1, f32[5,8,16,720]{3,2,1,0:T(8,128)S(1)} %copy-done, f32[5,8,1,720]{3,2,1,0:T(1,128)S(1)} %copy.56, f32[8,17,720]{2,1,0:T(8,128)S(1)} %get-tuple-element.16, f32[8,17,720]{2,1,0:T(8,128)S(1)} %get-tuple-element.15, ...), kind=kLoop, calls=%fused_computation.3 | loop fusion | flops 3427200 | bytes 6658577 | tf_op jit(solution)/shard_map/jit(_where)/select_n | solution.py:95
  30.7 1.1 copy-done.1
  31.9 2.2 %collective-permute-start.4 = (f32[16,8,720]{2,1,0:T(8,128)S(1)}, f32[16,8,720]{2,1,0:T(8,128)S(1)}, u32[]{:S(2)}, u32[]{:S(2)}) collective-permute-start(f32[16,8,720]{2,1,0:T(8,128)S(1)} %slice.119), channel_id=1, source_target_pairs={{0,16},{8,24},{16,0},{24,8},{1,17},{9,25},{17,1},{25,9},{2,18},{10... | collective-permute-start | bytes 1105928 | tf_op jit(solution)/shard_map/ppermute | solution.py:129
  35.0 9.1 %collective-permute-done.4 = f32[16,8,720]{2,1,0:T(8,128)S(1)} collective-permute-done((f32[16,8,720]{2,1,0:T(8,128)S(1)}, f32[16,8,720]{2,1,0:T(8,128)S(1)}, u32[]{:S(2)}, u32[]{:S(2)}) %collective-permute-start.4) | collective-permute-done | bytes 368672 | tf_op jit(solution)/shard_map/ppermute | solution.py:129
  45.0 3.5 %all-to-all-start = ((f32[8,16,720]{2,1,0:T(8,128)}), f32[8,16,720]{2,1,0:T(8,128)S(1)}, u32[]{:S(2)}, u32[]{:S(2)}) async-start(f32[8,16,720]{2,1,0:T(8,128)} %bitcast.134), calls=%async_computation | async-start | bytes 786432 | tf_op jit(solution)/shard_map/all_to_all | solution.py:131
  50.0 2.8 %collective-permute-done.5 = f32[24,8,720]{2,1,0:T(8,128)} collective-permute-done((f32[24,8,720]{2,1,0:T(8,128)}, f32[24,8,720]{2,1,0:T(8,128)}, u32[]{:S(2)}, u32[]{:S(2)}) %collective-permute-start.5) | collective-permute-done | bytes 552992 | tf_op jit(solution)/shard_map/ppermute | solution.py:129
  52.8 2.0 %slice_select_fusion.2 = f32[24,8,720]{2,1,0:T(8,128)} fusion(f32[24,8,720]{2,1,0:T(8,128)} %collective-permute-done.5, f32[40,8,720]{2,1,0:T(8,128)S(1)} %get-tuple-element.7, pred[8]{0:T(512)(128)(4,1)S(1)} %slice_select_fusion.4), kind=kLoop, calls=%fused_computation.40 | loop fusion | flops 138240 | bytes 1658888 | tf_op jit(solution)/shard_map/jit(_where)/select_n | solution.py:130
  54.8 6.1 %all-to-all-done = f32[8,16,720]{2,1,0:T(8,128)S(1)} async-done(((f32[8,16,720]{2,1,0:T(8,128)}), f32[8,16,720]{2,1,0:T(8,128)S(1)}, u32[]{:S(2)}, u32[]{:S(2)}) %all-to-all-start) | async-done | bytes 368672 | tf_op jit(solution)/shard_map/all_to_all | solution.py:131
  60.9 3.7 %all-to-all-start.2 = ((f32[8,24,720]{2,1,0:T(8,128)}), f32[8,24,720]{2,1,0:T(8,128)S(1)}, u32[]{:S(2)}, u32[]{:S(2)}) async-start(f32[8,24,720]{2,1,0:T(8,128)} %bitcast.25), calls=%async_computation.2 | async-start | bytes 1179648 | tf_op jit(solution)/shard_map/all_to_all | solution.py:131
  64.6 1.0 copy.59
  65.6 1.2 reshape.315
  71.9 9.2 %all-to-all-done.2 = f32[8,24,720]{2,1,0:T(8,128)S(1)} async-done(((f32[8,24,720]{2,1,0:T(8,128)}), f32[8,24,720]{2,1,0:T(8,128)S(1)}, u32[]{:S(2)}, u32[]{:S(2)}) %all-to-all-start.2) | async-done | bytes 552992 | tf_op jit(solution)/shard_map/all_to_all | solution.py:131
  89.8 1.0 copy.62
  90.8 3.5 %all-to-all-start.3 = ((f32[24,8,720]{2,0,1:T(8,128)}), f32[24,8,720]{2,0,1:T(8,128)S(1)}, u32[]{:S(2)}, u32[]{:S(2)}) async-start(f32[24,8,720]{2,0,1:T(8,128)} %copy.62), calls=%async_computation.3 | async-start | bytes 1179648 | tf_op jit(solution)/shard_map/all_to_all | solution.py:139
  94.3 1.6 %fusion.72 = f32[16,45,128]{2,1,0:T(8,128)S(1)} fusion(f32[16,45,128]{2,1,0:T(8,128)} %copy-done.12), kind=kOutput, calls=%fused_computation.115 | convolution fusion | flops 71008256 | bytes 737280 | tf_op jit(solution)/shard_map/ljk,kn->ljn/dot_general | solution.py:49
  98.7 12.4 %all-to-all-done.3 = f32[24,8,720]{2,0,1:T(8,128)S(1)} async-done(((f32[24,8,720]{2,0,1:T(8,128)}), f32[24,8,720]{2,0,1:T(8,128)S(1)}, u32[]{:S(2)}, u32[]{:S(2)}) %all-to-all-start.3) | async-done | bytes 552992 | tf_op jit(solution)/shard_map/all_to_all | solution.py:139
  111.0 3.5 %all-to-all-start.1 = ((f32[16,8,720]{2,0,1:T(8,128)}), f32[16,8,720]{2,0,1:T(8,128)S(1)}, u32[]{:S(2)}, u32[]{:S(2)}) async-start(f32[16,8,720]{2,0,1:T(8,128)} %copy.60), calls=%async_computation.1 | async-start | bytes 786432 | tf_op jit(solution)/shard_map/all_to_all | solution.py:139
  114.5 2.1 %collective-permute-start.7 = (f32[24,8,720]{2,1,0:T(8,128)S(1)}, f32[24,8,720]{2,1,0:T(8,128)S(1)}, u32[]{:S(2)}, u32[]{:S(2)}) collective-permute-start(f32[24,8,720]{2,1,0:T(8,128)S(1)} %bitcast.131), channel_id=1, source_target_pairs={{0,16},{8,24},{16,0},{24,8},{1,17},{9,25},{17,1},{25,9},{2,18},{10... | collective-permute-start | bytes 1658888 | tf_op jit(solution)/shard_map/ppermute | solution.py:143
  116.6 10.4 %all-to-all-done.1 = f32[16,8,720]{2,0,1:T(8,128)S(1)} async-done(((f32[16,8,720]{2,0,1:T(8,128)}), f32[16,8,720]{2,0,1:T(8,128)S(1)}, u32[]{:S(2)}, u32[]{:S(2)}) %all-to-all-start.1) | async-done | bytes 368672 | tf_op jit(solution)/shard_map/all_to_all | solution.py:139
  127.0 2.0 %collective-permute-start.6 = (f32[16,8,720]{2,1,0:T(8,128)S(1)}, f32[16,8,720]{2,1,0:T(8,128)S(1)}, u32[]{:S(2)}, u32[]{:S(2)}) collective-permute-start(f32[16,8,720]{2,1,0:T(8,128)S(1)} %bitcast.135), channel_id=1, source_target_pairs={{0,16},{8,24},{16,0},{24,8},{1,17},{9,25},{17,1},{25,9},{2,18},{10... | collective-permute-start | bytes 1105928 | tf_op jit(solution)/shard_map/ppermute | solution.py:143
  129.0 9.8 %collective-permute-done.6 = f32[16,8,720]{2,1,0:T(8,128)S(1)} collective-permute-done((f32[16,8,720]{2,1,0:T(8,128)S(1)}, f32[16,8,720]{2,1,0:T(8,128)S(1)}, u32[]{:S(2)}, u32[]{:S(2)}) %collective-permute-start.6) | collective-permute-done | bytes 368672 | tf_op jit(solution)/shard_map/ppermute | solution.py:143
  138.9 1.9 %fusion.3 = f32[5,8,16,720]{3,2,1,0:T(8,128)} fusion(f32[5,8,16,720]{3,2,1,0:T(8,128)S(1)} %copy-done, f32[5,8,16,720]{3,2,1,0:T(8,128)S(1)} %copy-done.2, f32[5,8,8,720]{3,2,1,0:T(8,128)S(1)} %bitcast.129, f32[5,8,8,720]{3,2,1,0:T(8,128)S(1)} %bitcast.128, pred[16]{0:T(512)(128)(4,1)S(1)} %compare_reduce_fusion, pred[]{:T(512)S(6)} %lt.139), kind=kLoop, calls=%fused_computation.12 | loop fusion | flops 2304000 | bytes 7372817 | tf_op jit(solution)/shard_map/add | solution.py:152
  (120 shorter events, 24.0 us)
Async XLA Ops:
  0.0 14.8 %copy-start = (f32[5,8,16,720]{3,2,1,0:T(8,128)S(1)}, f32[5,8,16,720]{3,2,1,0:T(8,128)}, u32[]{:S(2)}) copy-start(f32[5,8,16,720]{3,2,1,0:T(8,128)} %param.5) | copy-start | bytes 5529604
  0.0 14.2 %copy-start.13 = (f32[8,16,720]{2,1,0:T(8,128)S(1)}, f32[8,16,720]{2,1,0:T(8,128)}, u32[]{:S(2)}) copy-start(f32[8,16,720]{2,1,0:T(8,128)} %param.6) | copy-start | bytes 1105924
  1.8 20.6 %collective-permute-start.3 = (f32[5,8,720]{2,1,0:T(8,128)S(1)}, f32[5,8,720]{2,1,0:T(8,128)}, u32[]{:S(2)}, u32[]{:S(2)}) collective-permute-start(f32[5,8,720]{2,1,0:T(8,128)S(1)} %bitcast.138), channel_id=1, source_target_pairs={{8,0},{16,8},{24,16},{9,1},{17,9},{25,17},{10,2},{18,10},{26,18},{... | collective-permute-start | bytes 345608 | tf_op jit(solution)/shard_map/ppermute | solution.py:82
  4.1 22.6 %collective-permute-start.2 = (f32[6,8,720]{2,1,0:T(8,128)S(1)}, f32[6,8,720]{2,1,0:T(8,128)S(1)}, u32[]{:S(2)}, u32[]{:S(2)}) collective-permute-start(f32[6,8,720]{2,1,0:T(8,128)S(1)} %pad_maximum_fusion.7), channel_id=1, source_target_pairs={{0,8},{8,16},{16,24},{1,9},{9,17},{17,25},{2,10},{10,18},{18,26},{... | collective-permute-start | bytes 414728 | tf_op jit(solution)/shard_map/ppermute | solution.py:79
  11.2 5.8 %collective-permute-start.1 = (f32[5,8,16]{2,1,0:T(8,128)S(1)}, f32[5,8,16]{2,1,0:T(8,128)S(1)}, u32[]{:S(2)}, u32[]{:S(2)}) collective-permute-start(f32[5,8,16]{2,1,0:T(8,128)S(1)} %bitcast.141), channel_id=1, source_target_pairs={{1,0},{2,1},{3,2},{4,3},{5,4},{6,5},{7,6},{0,7},{9,8},{10,9},{11,1... | collective-permute-start | bytes 7688 | tf_op jit(solution)/shard_map/ppermute | solution.py:78
  14.7 1.7 %copy-start.19 = (s32[32]{0:T(128)S(1)}, s32[32]{0:T(128)}, u32[]{:S(2)}) copy-start(s32[32]{0:T(128)} %param.8) | copy-start | bytes 388
  14.7 1.9 %copy-start.20 = (s32[32]{0:T(128)S(1)}, s32[32]{0:T(128)}, u32[]{:S(2)}) copy-start(s32[32]{0:T(128)} %param.9) | copy-start | bytes 388
  14.7 5.1 %collective-permute-start = (f32[6,8,16]{2,1,0:T(8,128)S(1)}, f32[6,8,16]{2,1,0:T(8,128)S(1)}, u32[]{:S(2)}, u32[]{:S(2)}) collective-permute-start(f32[6,8,16]{2,1,0:T(8,128)S(1)} %pad_maximum_fusion.8), channel_id=1, source_target_pairs={{0,1},{1,2},{2,3},{3,4},{4,5},{5,6},{6,7},{7,0},{8,9},{9,10},{10,1... | collective-permute-start | bytes 9224 | tf_op jit(solution)/shard_map/ppermute | solution.py:75
  20.5 6.4 %copy-start.14 = (f32[8,16,720]{2,1,0:T(8,128)S(1)}, f32[8,16,720]{2,1,0:T(8,128)}, u32[]{:S(2)}) copy-start(f32[8,16,720]{2,1,0:T(8,128)} %param.7) | copy-start | bytes 1105924
  27.0 2.9 %copy-start.3 = (f32[5,8,16,721]{3,2,1,0:T(8,128)S(1)}, f32[5,8,16,721]{3,2,1,0:T(8,128)}, u32[]{:S(2)}) copy-start(f32[5,8,16,721]{3,2,1,0:T(8,128)} %multiply_subtract_fusion) | copy-start | bytes 5537284
  30.6 1.3 copy-start.1
  31.9 12.3 %collective-permute-start.4 = (f32[16,8,720]{2,1,0:T(8,128)S(1)}, f32[16,8,720]{2,1,0:T(8,128)S(1)}, u32[]{:S(2)}, u32[]{:S(2)}) collective-permute-start(f32[16,8,720]{2,1,0:T(8,128)S(1)} %slice.119), channel_id=1, source_target_pairs={{0,16},{8,24},{16,0},{24,8},{1,17},{9,25},{17,1},{25,9},{2,18},{10... | collective-permute-start | bytes 1105928 | tf_op jit(solution)/shard_map/ppermute | solution.py:129
  34.1 35.9 %copy-start.15 = (f32[45,128]{1,0:T(8,128)}, f32[45,128]{1,0:T(8,128)S(1)}, u32[]{:S(2)}) copy-start(f32[45,128]{1,0:T(8,128)S(1)} %broadcast_maximum_fusion) | copy-start | bytes 69124
  35.0 17.7 %collective-permute-start.5 = (f32[24,8,720]{2,1,0:T(8,128)}, f32[24,8,720]{2,1,0:T(8,128)}, u32[]{:S(2)}, u32[]{:S(2)}) collective-permute-start(f32[24,8,720]{2,1,0:T(8,128)} %slice.121), channel_id=1, source_target_pairs={{0,16},{8,24},{16,0},{24,8},{1,17},{9,25},{17,1},{25,9},{2,18},{10... | collective-permute-start | bytes 1658888 | tf_op jit(solution)/shard_map/ppermute | solution.py:129
  45.0 15.9 %all-to-all-start = ((f32[8,16,720]{2,1,0:T(8,128)}), f32[8,16,720]{2,1,0:T(8,128)S(1)}, u32[]{:S(2)}, u32[]{:S(2)}) async-start(f32[8,16,720]{2,1,0:T(8,128)} %bitcast.134), calls=%async_computation | async-start | bytes 786432 | tf_op jit(solution)/shard_map/all_to_all | solution.py:131
  49.9 20.1 %copy-start.4 = (f32[45,128]{1,0:T(8,128)}, f32[45,128]{1,0:T(8,128)S(1)}, u32[]{:S(2)}) copy-start(f32[45,128]{1,0:T(8,128)S(1)} %get-tuple-element.17) | copy-start | bytes 69124
  49.9 20.1 %copy-start.7 = (f32[45,128]{1,0:T(8,128)}, f32[45,128]{1,0:T(8,128)S(1)}, u32[]{:S(2)}) copy-start(f32[45,128]{1,0:T(8,128)S(1)} %get-tuple-element.18) | copy-start | bytes 69124
  50.0 20.0 %copy-start.17 = (f32[45,128]{1,0:T(8,128)}, f32[45,128]{1,0:T(8,128)S(1)}, u32[]{:S(2)}) copy-start(f32[45,128]{1,0:T(8,128)S(1)} %fusion.100) | copy-start | bytes 69124
  60.9 20.2 %all-to-all-start.2 = ((f32[8,24,720]{2,1,0:T(8,128)}), f32[8,24,720]{2,1,0:T(8,128)S(1)}, u32[]{:S(2)}, u32[]{:S(2)}) async-start(f32[8,24,720]{2,1,0:T(8,128)} %bitcast.25), calls=%async_computation.2 | async-start | bytes 1179648 | tf_op jit(solution)/shard_map/all_to_all | solution.py:131
  68.8 1.8 %copy-start.10 = (f32[16,45,128]{2,1,0:T(8,128)}, f32[16,45,128]{2,1,0:T(8,128)S(1)}, u32[]{:S(2)}) copy-start(f32[16,45,128]{2,1,0:T(8,128)S(1)} %fusion.9) | copy-start | bytes 1105924
  81.7 1.0 copy-start.5
  81.7 1.0 copy-start.8
  82.7 1.3 copy-start.16
  82.7 1.3 copy-start.18
  89.8 6.1 %copy-start.11 = (f32[16,45,128]{2,1,0:T(8,128)S(1)}, f32[16,45,128]{2,1,0:T(8,128)}, u32[]{:S(2)}) copy-start(f32[16,45,128]{2,1,0:T(8,128)} %copy-done.10) | copy-start | bytes 1105924
  89.8 6.7 %copy-start.6 = (f32[45,128]{1,0:T(8,128)S(1)}, f32[45,128]{1,0:T(8,128)}, u32[]{:S(2)}) copy-start(f32[45,128]{1,0:T(8,128)} %copy-done.4) | copy-start | bytes 69124
  89.8 6.7 %copy-start.9 = (f32[45,128]{1,0:T(8,128)S(1)}, f32[45,128]{1,0:T(8,128)}, u32[]{:S(2)}) copy-start(f32[45,128]{1,0:T(8,128)} %copy-done.7) | copy-start | bytes 69124
  90.8 20.2 %all-to-all-start.3 = ((f32[24,8,720]{2,0,1:T(8,128)}), f32[24,8,720]{2,0,1:T(8,128)S(1)}, u32[]{:S(2)}, u32[]{:S(2)}) async-start(f32[24,8,720]{2,0,1:T(8,128)} %copy.62), calls=%async_computation.3 | async-start | bytes 1179648 | tf_op jit(solution)/shard_map/all_to_all | solution.py:139
  111.0 15.9 %all-to-all-start.1 = ((f32[16,8,720]{2,0,1:T(8,128)}), f32[16,8,720]{2,0,1:T(8,128)S(1)}, u32[]{:S(2)}, u32[]{:S(2)}) async-start(f32[16,8,720]{2,0,1:T(8,128)} %copy.60), calls=%async_computation.1 | async-start | bytes 786432 | tf_op jit(solution)/shard_map/all_to_all | solution.py:139
  114.5 24.3 %collective-permute-start.7 = (f32[24,8,720]{2,1,0:T(8,128)S(1)}, f32[24,8,720]{2,1,0:T(8,128)S(1)}, u32[]{:S(2)}, u32[]{:S(2)}) collective-permute-start(f32[24,8,720]{2,1,0:T(8,128)S(1)} %bitcast.131), channel_id=1, source_target_pairs={{0,16},{8,24},{16,0},{24,8},{1,17},{9,25},{17,1},{25,9},{2,18},{10... | collective-permute-start | bytes 1658888 | tf_op jit(solution)/shard_map/ppermute | solution.py:143
  127.0 11.9 %copy-start.2 = (f32[5,8,16,720]{3,2,1,0:T(8,128)S(1)}, f32[5,8,16,720]{3,2,1,0:T(8,128)}, u32[]{:S(2)}) copy-start(f32[5,8,16,720]{3,2,1,0:T(8,128)} %copy-done.1) | copy-start | bytes 5529604
  127.0 11.9 %collective-permute-start.6 = (f32[16,8,720]{2,1,0:T(8,128)S(1)}, f32[16,8,720]{2,1,0:T(8,128)S(1)}, u32[]{:S(2)}, u32[]{:S(2)}) collective-permute-start(f32[16,8,720]{2,1,0:T(8,128)S(1)} %bitcast.135), channel_id=1, source_target_pairs={{0,16},{8,24},{16,0},{24,8},{1,17},{9,25},{17,1},{25,9},{2,18},{10... | collective-permute-start | bytes 1105928 | tf_op jit(solution)/shard_map/ppermute | solution.py:143
  (1 other events, 0.7 us)

commit v14 on v9

--- a/solution.py
+++ b/solution.py
@@ -117,7 +117,7 @@
     given = jnp.where(is_low, high_half, low_half)
     kept_filtered = jnp.where(is_low, is_filtered[:half_rows], is_filtered[half_rows:])
     kept_cut = jnp.where(is_low, row_cut[:half_rows], row_cut[half_rows:])
-    chunk_sizes = (stacked // 5, stacked // 2, stacked - stacked // 5 - stacked // 2)
+    chunk_sizes = (stacked * 4 // 5, stacked - stacked * 4 // 5)
     returned_parts, handed_parts = [], []
     chunk_start = 0
     for chunk_stack in chunk_sizes:

time: 166 us -> 156 us (0.940)
  starting transfers between devices: 41.4 us -> 25.1 us
  blocking collectives: 0 us -> 10.7 us
  waiting for transfers between devices: 61.2 us -> 67.8 us
  local copies, waits for them, and re-layouts: 24.4 us -> 19.2 us
  other arithmetic: 18.4 us -> 14.8 us
    ppermute x3 -> x2, waiting for transfers between devices: 8.07 us -> 20.9 us  [body(): taken = lax.ppermute(given[rows_of_part], 'lat', pair_perm)]
    all_to_all x0 -> x1, blocking collectives: none -> 10.7 us  [body(): lax.all_to_all(smoothed, 'lon', split_axis=1, concat_axis=0, tiled=True)]
    all_to_all x3 -> x1, starting transfers between devices: 11.2 us -> 3.55 us  [body(): lax.all_to_all(smoothed, 'lon', split_axis=1, concat_axis=0, tiled=True)]
    all_to_all x3 -> x1, waiting for transfers between devices: 22.7 us -> 16.4 us  [body(): lax.all_to_all(smoothed, 'lon', split_axis=1, concat_axis=0, tiled=True)]
    ppermute x3 -> x2, waiting for transfers between devices: 14.1 us -> 9.21 us  [body(): handed_parts.append(lax.ppermute(returned, 'lat', pair_perm))]
    all_to_all x3 -> x2, waiting for transfers between devices: 16.3 us -> 21 us  [body(): lax.all_to_all(pair_lines.reshape(chunk_stack * half_rows, columns), 'lon...]
    all_to_all x3 -> x2, starting transfers between devices: 11.9 us -> 7.52 us  [body(): lax.all_to_all(pair_lines.reshape(chunk_stack * half_rows, columns), 'lon...]
    all_to_all x5 -> x2, local copies, waits for them, and re-layouts: 2.97 us -> 0.53 us  [body(): lax.all_to_all(pair_lines.reshape(chunk_stack * half_rows, columns), 'lon...]
  transfers between devices with their start and end apart: 16 -> 11, of which waited for: 9 -> 6; matrix products, arithmetic and copies ran while one was open for 30% -> 19% of each run, Pallas kernels for 0% -> 0%
where the time goes in v14:
time: 156 us
  waiting for transfers between devices  67.8 us (43%)
  starting transfers between devices  25.1 us (16%)
  local copies, waits for them, and re-layouts  19.2 us (12%)
  matrix products  17.3 us (11%)
  other arithmetic  14.8 us (9%)
  blocking collectives  10.7 us (7%)
    all_to_all x2, waiting for transfers between devices, body(): lax.all_to_all(pair_lines.reshape(chunk_stack * half_rows, columns), 'lon...  21 us
    ppermute x2, waiting for transfers between devices, body(): taken = lax.ppermute(given[rows_of_part], 'lat', pair_perm)  20.9 us
    all_to_all x1, waiting for transfers between devices, body(): lax.all_to_all(smoothed, 'lon', split_axis=1, concat_axis=0, tiled=True)  16.4 us
    all_to_all x1, blocking collectives, body(): lax.all_to_all(smoothed, 'lon', split_axis=1, concat_axis=0, tiled=True)  10.7 us
    ppermute x2, waiting for transfers between devices, body(): handed_parts.append(lax.ppermute(returned, 'lat', pair_perm))  9.21 us
    all_to_all x2, starting transfers between devices, body(): lax.all_to_all(pair_lines.reshape(chunk_stack * half_rows, columns), 'lon...  7.52 us
    ppermute x1, starting transfers between devices, body(): lax.ppermute(jnp.concatenate([flat_fields[:, -1], lat_courant[:, -1]], ax...  5.48 us
    concatenate x4, local copies, waits for them, and re-layouts, body(): jnp.concatenate([from_below[:stacked, None], flat_fields, from_above[:, N...  4.44 us
  transfers between devices with their start and end apart: 11, of which 6 were waited for; matrix products, arithmetic and copies ran while one was open for 19% of the time, Pallas kernels for 0%

profile of v14, /device:TPU:0, one launch (start us, length us, event | category | flops | bytes accessed | tf_op | source)
XLA Modules:
  0.0 155.8 jit_solution(10370125155812450400)
XLA Ops:
  0.0 1.8 %fusion.247 = (f32[40,1,720]{2,1,0:T(1,128)S(1)}, f32[40,1,720]{2,1,0:T(1,128)S(1)}) fusion(f32[40,16,720]{2,1,0:T(8,128)} %bitcast.126), kind=kLoop, calls=%fused_computation.289 | loop fusion | bytes 460800 | tf_op jit(solution)/shard_map/slice | solution.py:80
  1.8 1.3 collective-permute-start.3
  4.1 5.5 %collective-permute-start.2 = (f32[48,720]{1,0:T(8,128)S(1)}, f32[48,720]{1,0:T(8,128)S(1)}, u32[]{:S(2)}, u32[]{:S(2)}) collective-permute-start(f32[48,720]{1,0:T(8,128)S(1)} %pad_maximum_fusion.7), channel_id=1, source_target_pairs={{0,8},{8,16},{16,24},{1,9},{9,17},{17,25},{2,10},{10,18},{18,26},{... | collective-permute-start | bytes 414728 | tf_op jit(solution)/shard_map/ppermute | solution.py:79
  9.6 1.2 fusion.246
  11.1 3.0 %collective-permute-start.1 = (f32[40,16]{0,1:T(8,128)S(1)}, f32[40,16]{0,1:T(8,128)S(1)}, u32[]{:S(2)}, u32[]{:S(2)}) collective-permute-start(f32[40,16]{0,1:T(8,128)S(1)} %bitcast.146), channel_id=1, source_target_pairs={{1,0},{2,1},{3,2},{4,3},{5,4},{6,5},{7,6},{0,7},{9,8},{10,9},{11,1... | collective-permute-start | bytes 7688 | tf_op jit(solution)/shard_map/ppermute | solution.py:78
  14.7 1.5 constant_dynamic-update-slice_fusion
  20.4 1.9 %multiply_subtract_fusion = f32[5,8,16,721]{3,2,1,0:T(8,128)} fusion(f32[5,8,16,1]{3,2,1,0:T(8,128)S(1)} %copy.110, f32[5,8,16,720]{3,2,1,0:T(8,128)S(1)} %copy-done, f32[5,8,16,1]{3,2,1,0:T(8,128)S(1)} %copy.107, f32[8,16,721]{2,1,0:T(8,128)S(1)} %get-tuple-element.14, f32[8,16,721]{2,1,0:T(8,128)S(1)} %get-tuple-element.13), kind=kLoop, calls=%fused_computation.13 | loop fusion | flops 3230080 | bytes 4432384 | tf_op jit(solution)/shard_map/sub | solution.py:60
  22.3 1.0 copy.114
  23.3 3.3 %dynamic-update-slice.1 = f32[5,8,17,720]{3,2,1,0:T(8,128)} dynamic-update-slice(f32[5,8,17,720]{3,2,1,0:T(8,128)} %constant_dynamic-update-slice_fusion, f32[5,8,1,720]{3,2,1,0:T(1,128)S(1)} %copy.114, s32[]{} %constant.131, s32[]{} %constant.131, s32[]{} %constant.132, s32[]{} %constant.131) | dynamic-update-slice | bytes 230404 | tf_op jit(solution)/shard_map/concatenate | solution.py:88
  27.0 2.9 %subtract_select_fusion = f32[5,8,17,720]{3,2,1,0:T(8,128)S(1)} fusion(f32[5,8,17,720]{3,2,1,0:T(8,128)} %dynamic-update-slice.1, f32[5,8,16,720]{3,2,1,0:T(8,128)S(1)} %copy-done, f32[5,8,1,720]{3,2,1,0:T(1,128)S(1)} %copy.113, f32[8,17,720]{2,1,0:T(8,128)S(1)} %get-tuple-element.16, f32[8,17,720]{2,1,0:T(8,128)S(1)} %get-tuple-element.15, ...), kind=kLoop, calls=%fused_computation.3 | loop fusion | flops 3427200 | bytes 6658577 | tf_op jit(solution)/shard_map/jit(_where)/select_n | solution.py:95
  30.6 1.1 copy-done.1
  32.7 2.2 %collective-permute-start.4 = (f32[32,8,720]{2,1,0:T(8,128)}, f32[32,8,720]{2,1,0:T(8,128)}, u32[]{:S(2)}, u32[]{:S(2)}) collective-permute-start(f32[32,8,720]{2,1,0:T(8,128)} %slice.123), channel_id=1, source_target_pairs={{0,16},{8,24},{16,0},{24,8},{1,17},{9,25},{17,1},{25,9},{2,18},{10... | collective-permute-start | bytes 2211848 | tf_op jit(solution)/shard_map/ppermute | solution.py:129
  35.1 20.9 %collective-permute-done.5 = f32[8,8,720]{2,1,0:T(8,128)S(1)} collective-permute-done((f32[8,8,720]{2,1,0:T(8,128)S(1)}, f32[8,8,720]{2,1,0:T(8,128)S(1)}, u32[]{:S(2)}, u32[]{:S(2)}) %collective-permute-start.5) | collective-permute-done | bytes 184352 | tf_op jit(solution)/shard_map/ppermute | solution.py:129
  56.7 3.8 %all-to-all-start.2 = ((f32[8,8,720]{2,1,0:T(8,128)}), f32[8,8,720]{2,1,0:T(8,128)S(1)}, u32[]{:S(2)}, u32[]{:S(2)}) async-start(f32[8,8,720]{2,1,0:T(8,128)} %slice_select_fusion.3), calls=%async_computation.2 | async-start | bytes 393216 | tf_op jit(solution)/shard_map/all_to_all | solution.py:131
  61.1 1.3 gather_fusion
  62.4 2.2 %slice_select_fusion.2 = f32[32,8,720]{2,1,0:T(8,128)} fusion(f32[32,8,720]{2,1,0:T(8,128)} %collective-permute-done.4, f32[40,8,720]{2,1,0:T(8,128)S(1)} %get-tuple-element.7, pred[8]{0:T(512)(128)(4,1)S(1)} %copy-done.26), kind=kLoop, calls=%fused_computation.40 | loop fusion | flops 184320 | bytes 2211848 | tf_op jit(solution)/shard_map/jit(_where)/select_n | solution.py:130
  64.6 4.2 %all-to-all-done.2 = f32[8,8,720]{2,1,0:T(8,128)S(1)} async-done(((f32[8,8,720]{2,1,0:T(8,128)}), f32[8,8,720]{2,1,0:T(8,128)S(1)}, u32[]{:S(2)}, u32[]{:S(2)}) %all-to-all-start.2) | async-done | bytes 184352 | tf_op jit(solution)/shard_map/all_to_all | solution.py:131
  68.8 3.7 %all-to-all-start = ((f32[8,32,720]{2,1,0:T(8,128)}), f32[8,32,720]{2,1,0:T(8,128)S(1)}, u32[]{:S(2)}, u32[]{:S(2)}) async-start(f32[8,32,720]{2,1,0:T(8,128)} %bitcast.131), calls=%async_computation | async-start | bytes 1572864 | tf_op jit(solution)/shard_map/all_to_all | solution.py:131
  74.1 1.1 fusion.39
  75.3 1.2 fusion.10
  76.5 16.8 %all-to-all-done = f32[8,32,720]{2,1,0:T(8,128)S(1)} async-done(((f32[8,32,720]{2,1,0:T(8,128)}), f32[8,32,720]{2,1,0:T(8,128)S(1)}, u32[]{:S(2)}, u32[]{:S(2)}) %all-to-all-start) | async-done | bytes 737312 | tf_op jit(solution)/shard_map/all_to_all | solution.py:131
  103.3 1.4 copy.116
  104.7 3.5 %all-to-all-start.1 = ((f32[32,8,720]{2,0,1:T(8,128)}), f32[32,8,720]{2,0,1:T(8,128)S(1)}, u32[]{:S(2)}, u32[]{:S(2)}) async-start(f32[32,8,720]{2,0,1:T(8,128)} %copy.116), calls=%async_computation.1 | async-start | bytes 1572864 | tf_op jit(solution)/shard_map/all_to_all | solution.py:139
  108.8 1.4 fusion.11
  111.7 1.0 fusion.44
  112.7 16.4 %all-to-all-done.1 = f32[32,8,720]{2,0,1:T(8,128)S(1)} async-done(((f32[32,8,720]{2,0,1:T(8,128)}), f32[32,8,720]{2,0,1:T(8,128)S(1)}, u32[]{:S(2)}, u32[]{:S(2)}) %all-to-all-start.1) | async-done | bytes 737312 | tf_op jit(solution)/shard_map/all_to_all | solution.py:139
  129.1 2.0 %collective-permute-start.6 = (f32[32,8,720]{2,1,0:T(8,128)S(1)}, f32[32,8,720]{2,1,0:T(8,128)}, u32[]{:S(2)}, u32[]{:S(2)}) collective-permute-start(f32[32,8,720]{2,1,0:T(8,128)S(1)} %bitcast.133), channel_id=1, source_target_pairs={{0,16},{8,24},{16,0},{24,8},{1,17},{9,25},{17,1},{25,9},{2,18},{10... | collective-permute-start | bytes 2211848 | tf_op jit(solution)/shard_map/ppermute | solution.py:143
  131.1 1.3 fusion.9
  132.7 10.7 %all_to_all.61 = f32[8,8,720]{2,0,1:T(8,128)S(1)} all-to-all(f32[8,8,720]{2,0,1:T(8,128)S(1)} %copy.118), channel_id=1, replica_groups=mesh['lat'=4,'lon'=8] {'lon'}, dimensions={1} | all-to-all | bytes 368640 | tf_op jit(solution)/shard_map/all_to_all | solution.py:139
  143.5 9.2 %collective-permute-done.7 = f32[8,8,720]{2,1,0:T(8,128)S(1)} collective-permute-done((f32[8,8,720]{2,1,0:T(8,128)S(1)}, f32[8,8,720]{2,1,0:T(8,128)S(1)}, u32[]{:S(2)}, u32[]{:S(2)}) %collective-permute-start.7) | collective-permute-done | bytes 184352 | tf_op jit(solution)/shard_map/ppermute | solution.py:143
  152.7 1.2 pad_maximum_fusion.4
  153.9 1.9 %fusion.3 = f32[5,8,16,720]{3,2,1,0:T(8,128)} fusion(f32[5,8,16,720]{3,2,1,0:T(8,128)S(1)} %copy-done, f32[5,8,16,720]{3,2,1,0:T(8,128)S(1)} %copy-done.2, f32[5,8,8,720]{3,2,1,0:T(8,128)S(1)} %bitcast.130, f32[5,8,8,720]{3,2,1,0:T(8,128)S(1)} %bitcast.129, pred[16]{0:T(512)(128)(4,1)S(1)} %copy-done.24, pred[]{:T(512)S(6)} %lt.140), kind=kLoop, calls=%fused_computation.12 | loop fusion | flops 2304000 | bytes 7372817 | tf_op jit(solution)/shard_map/add | solution.py:152
  (146 shorter events, 23.0 us)
Async XLA Ops:
  0.0 14.7 %copy-start = (f32[5,8,16,720]{3,2,1,0:T(8,128)S(1)}, f32[5,8,16,720]{3,2,1,0:T(8,128)}, u32[]{:S(2)}) copy-start(f32[5,8,16,720]{3,2,1,0:T(8,128)} %param.5) | copy-start | bytes 5529604
  0.0 14.1 %copy-start.15 = (f32[8,16,720]{2,1,0:T(8,128)S(1)}, f32[8,16,720]{2,1,0:T(8,128)}, u32[]{:S(2)}) copy-start(f32[8,16,720]{2,1,0:T(8,128)} %param.6) | copy-start | bytes 1105924
  1.8 20.5 %collective-permute-start.3 = (f32[40,720]{1,0:T(8,128)S(1)}, f32[40,720]{1,0:T(8,128)}, u32[]{:S(2)}, u32[]{:S(2)}) collective-permute-start(f32[40,720]{1,0:T(8,128)S(1)} %bitcast.139), channel_id=1, source_target_pairs={{8,0},{16,8},{24,16},{9,1},{17,9},{25,17},{10,2},{18,10},{26,18},{... | collective-permute-start | bytes 345608 | tf_op jit(solution)/shard_map/ppermute | solution.py:82
  4.1 22.5 %collective-permute-start.2 = (f32[48,720]{1,0:T(8,128)S(1)}, f32[48,720]{1,0:T(8,128)S(1)}, u32[]{:S(2)}, u32[]{:S(2)}) collective-permute-start(f32[48,720]{1,0:T(8,128)S(1)} %pad_maximum_fusion.7), channel_id=1, source_target_pairs={{0,8},{8,16},{16,24},{1,9},{9,17},{17,25},{2,10},{10,18},{18,26},{... | collective-permute-start | bytes 414728 | tf_op jit(solution)/shard_map/ppermute | solution.py:79
  11.1 7.8 %collective-permute-start.1 = (f32[40,16]{0,1:T(8,128)S(1)}, f32[40,16]{0,1:T(8,128)S(1)}, u32[]{:S(2)}, u32[]{:S(2)}) collective-permute-start(f32[40,16]{0,1:T(8,128)S(1)} %bitcast.146), channel_id=1, source_target_pairs={{1,0},{2,1},{3,2},{4,3},{5,4},{6,5},{7,6},{0,7},{9,8},{10,9},{11,1... | collective-permute-start | bytes 7688 | tf_op jit(solution)/shard_map/ppermute | solution.py:78
  14.6 4.9 %collective-permute-start = (f32[48,16]{0,1:T(8,128)S(1)}, f32[48,16]{0,1:T(8,128)S(1)}, u32[]{:S(2)}, u32[]{:S(2)}) collective-permute-start(f32[48,16]{0,1:T(8,128)S(1)} %pad_maximum_fusion.8), channel_id=1, source_target_pairs={{0,1},{1,2},{2,3},{3,4},{4,5},{5,6},{6,7},{7,0},{8,9},{9,10},{10,1... | collective-permute-start | bytes 9224 | tf_op jit(solution)/shard_map/ppermute | solution.py:75
  16.2 59.0 %copy-start.17 = (f32[45,128]{1,0:T(8,128)}, f32[45,128]{1,0:T(8,128)S(1)}, u32[]{:S(2)}) copy-start(f32[45,128]{1,0:T(8,128)S(1)} %broadcast_maximum_fusion) | copy-start | bytes 69124
  16.3 59.0 %copy-start.20 = (f32[45,128]{1,0:T(8,128)}, f32[45,128]{1,0:T(8,128)S(1)}, u32[]{:S(2)}) copy-start(f32[45,128]{1,0:T(8,128)S(1)} %fusion.100) | copy-start | bytes 69124
  20.4 6.5 %copy-start.16 = (f32[8,16,720]{2,1,0:T(8,128)S(1)}, f32[8,16,720]{2,1,0:T(8,128)}, u32[]{:S(2)}) copy-start(f32[8,16,720]{2,1,0:T(8,128)} %param.7) | copy-start | bytes 1105924
  22.3 4.6 %copy-start.27 = (pred[17]{0:T(512)(128)(4,1)S(1)}, pred[17]{0:T(512)(128)(4,1)}, u32[]{:S(2)}) copy-start(pred[17]{0:T(512)(128)(4,1)} %add_compare_fusion) | copy-start | bytes 55
  30.5 4.4 %copy-start.28 = (s32[8]{0:T(128)S(1)}, s32[8]{0:T(128)}, u32[]{:S(2)}) copy-start(s32[8]{0:T(128)} %fusion.157) | copy-start | bytes 100
  31.7 24.2 %copy-start.26 = (pred[8]{0:T(512)(128)(4,1)S(1)}, pred[8]{0:T(512)(128)(4,1)}, u32[]{:S(2)}) copy-start(pred[8]{0:T(512)(128)(4,1)} %slice_select_fusion.4) | copy-start | bytes 28
  32.7 29.7 %collective-permute-start.4 = (f32[32,8,720]{2,1,0:T(8,128)}, f32[32,8,720]{2,1,0:T(8,128)}, u32[]{:S(2)}, u32[]{:S(2)}) collective-permute-start(f32[32,8,720]{2,1,0:T(8,128)} %slice.123), channel_id=1, source_target_pairs={{0,16},{8,24},{16,0},{24,8},{1,17},{9,25},{17,1},{25,9},{2,18},{10... | collective-permute-start | bytes 2211848 | tf_op jit(solution)/shard_map/ppermute | solution.py:129
  34.9 21.0 %collective-permute-start.5 = (f32[8,8,720]{2,1,0:T(8,128)S(1)}, f32[8,8,720]{2,1,0:T(8,128)S(1)}, u32[]{:S(2)}, u32[]{:S(2)}) collective-permute-start(f32[8,8,720]{2,1,0:T(8,128)S(1)} %slice.125), channel_id=1, source_target_pairs={{0,16},{8,24},{16,0},{24,8},{1,17},{9,25},{17,1},{25,9},{2,18},{10... | collective-permute-start | bytes 552968 | tf_op jit(solution)/shard_map/ppermute | solution.py:129
  56.7 12.1 %all-to-all-start.2 = ((f32[8,8,720]{2,1,0:T(8,128)}), f32[8,8,720]{2,1,0:T(8,128)S(1)}, u32[]{:S(2)}, u32[]{:S(2)}) async-start(f32[8,8,720]{2,1,0:T(8,128)} %slice_select_fusion.3), calls=%async_computation.2 | async-start | bytes 393216 | tf_op jit(solution)/shard_map/all_to_all | solution.py:131
  61.1 14.1 %copy-start.31 = (f32[8]{0:T(128)}, f32[8]{0:T(128)S(1)}, u32[]{:S(2)}) copy-start(f32[8]{0:T(128)S(1)} %gather_fusion.1) | copy-start | bytes 100
  68.8 24.5 %all-to-all-start = ((f32[8,32,720]{2,1,0:T(8,128)}), f32[8,32,720]{2,1,0:T(8,128)S(1)}, u32[]{:S(2)}, u32[]{:S(2)}) async-start(f32[8,32,720]{2,1,0:T(8,128)} %bitcast.131), calls=%async_computation | async-start | bytes 1572864 | tf_op jit(solution)/shard_map/all_to_all | solution.py:131
  72.7 3.8 %copy-start.4 = (f32[45,128]{1,0:T(8,128)}, f32[45,128]{1,0:T(8,128)S(1)}, u32[]{:S(2)}) copy-start(f32[45,128]{1,0:T(8,128)S(1)} %get-tuple-element.17) | copy-start | bytes 69124
  72.7 3.8 %copy-start.7 = (f32[45,128]{1,0:T(8,128)}, f32[45,128]{1,0:T(8,128)S(1)}, u32[]{:S(2)}) copy-start(f32[45,128]{1,0:T(8,128)S(1)} %get-tuple-element.18) | copy-start | bytes 69124
  103.2 5.0 %copy-start.14 = (f32[8,45,128]{2,1,0:T(8,128)S(1)}, f32[8,45,128]{2,1,0:T(8,128)}, u32[]{:S(2)}) copy-start(f32[8,45,128]{2,1,0:T(8,128)} %fusion.10) | copy-start | bytes 552964
  103.2 5.5 %copy-start.6 = (f32[45,128]{1,0:T(8,128)S(1)}, f32[45,128]{1,0:T(8,128)}, u32[]{:S(2)}) copy-start(f32[45,128]{1,0:T(8,128)} %copy-done.4) | copy-start | bytes 69124
  103.3 5.5 %copy-start.9 = (f32[45,128]{1,0:T(8,128)S(1)}, f32[45,128]{1,0:T(8,128)}, u32[]{:S(2)}) copy-start(f32[45,128]{1,0:T(8,128)} %copy-done.7) | copy-start | bytes 69124
  103.3 5.5 %copy-start.11 = (f32[45,8,128]{2,0,1:T(8,128)S(1)}, f32[45,8,128]{2,0,1:T(8,128)}, u32[]{:S(2)}) copy-start(f32[45,8,128]{2,0,1:T(8,128)} %copy-done.10) | copy-start | bytes 552964
  103.3 5.5 %copy-start.13 = (f32[45,8,128]{2,0,1:T(8,128)S(1)}, f32[45,8,128]{2,0,1:T(8,128)}, u32[]{:S(2)}) copy-start(f32[45,8,128]{2,0,1:T(8,128)} %copy-done.12) | copy-start | bytes 552964
  103.3 5.5 %copy-start.19 = (f32[45,128]{1,0:T(8,128)S(1)}, f32[45,128]{1,0:T(8,128)}, u32[]{:S(2)}) copy-start(f32[45,128]{1,0:T(8,128)} %copy-done.17) | copy-start | bytes 69124
  103.3 5.5 %copy-start.22 = (f32[45,128]{1,0:T(8,128)S(1)}, f32[45,128]{1,0:T(8,128)}, u32[]{:S(2)}) copy-start(f32[45,128]{1,0:T(8,128)} %copy-done.20) | copy-start | bytes 69124
  103.3 5.5 %copy-start.32 = (f32[8]{0:T(128)S(1)}, f32[8]{0:T(128)}, u32[]{:S(2)}) copy-start(f32[8]{0:T(128)} %copy-done.31) | copy-start | bytes 100
  104.7 24.4 %all-to-all-start.1 = ((f32[32,8,720]{2,0,1:T(8,128)}), f32[32,8,720]{2,0,1:T(8,128)S(1)}, u32[]{:S(2)}, u32[]{:S(2)}) async-start(f32[32,8,720]{2,0,1:T(8,128)} %copy.116), calls=%async_computation.1 | async-start | bytes 1572864 | tf_op jit(solution)/shard_map/all_to_all | solution.py:139
  129.1 23.6 %collective-permute-start.6 = (f32[32,8,720]{2,1,0:T(8,128)S(1)}, f32[32,8,720]{2,1,0:T(8,128)}, u32[]{:S(2)}, u32[]{:S(2)}) collective-permute-start(f32[32,8,720]{2,1,0:T(8,128)S(1)} %bitcast.133), channel_id=1, source_target_pairs={{0,16},{8,24},{16,0},{24,8},{1,17},{9,25},{17,1},{25,9},{2,18},{10... | collective-permute-start | bytes 2211848 | tf_op jit(solution)/shard_map/ppermute | solution.py:143
  143.4 10.5 %copy-start.2 = (f32[5,8,16,720]{3,2,1,0:T(8,128)S(1)}, f32[5,8,16,720]{3,2,1,0:T(8,128)}, u32[]{:S(2)}) copy-start(f32[5,8,16,720]{3,2,1,0:T(8,128)} %copy-done.1) | copy-start | bytes 5529604
  143.4 10.5 %copy-start.24 = (pred[16]{0:T(512)(128)(4,1)S(1)}, pred[16]{0:T(512)(128)(4,1)}, u32[]{:S(2)}) copy-start(pred[16]{0:T(512)(128)(4,1)} %copy-done.23) | copy-start | bytes 52
  143.4 9.3 %collective-permute-start.7 = (f32[8,8,720]{2,1,0:T(8,128)S(1)}, f32[8,8,720]{2,1,0:T(8,128)S(1)}, u32[]{:S(2)}, u32[]{:S(2)}) collective-permute-start(f32[8,8,720]{2,1,0:T(8,128)S(1)} %bitcast.136), channel_id=1, source_target_pairs={{0,16},{8,24},{16,0},{24,8},{1,17},{9,25},{17,1},{25,9},{2,18},{10... | collective-permute-start | bytes 552968 | tf_op jit(solution)/shard_map/ppermute | solution.py:143
  (13 other events, 25.8 us)

commit v15 on v8

--- a/solution.py
+++ b/solution.py
@@ -19,7 +19,7 @@
     return (jnp.cos(angle), jnp.sin(angle))
 
 
-def filter_lines(lines, line_cut):
+def filter_lines(lines, line_cut, lines_im=None):
     line_total, circle = lines.shape
     outer = circle // radix_len
     mixer = partial(jnp.einsum, precision=lax.Precision.HIGH)
@@ -29,6 +29,10 @@
     values = lines.reshape(line_total, outer, radix_len)
     first_re = mixer("lan,aj->ljn", values, outer_cos)
     first_im = -mixer("lan,aj->ljn", values, outer_sin)
+    if lines_im is not None:
+        values_im = lines_im.reshape(line_total, outer, radix_len)
+        first_re = first_re + mixer("lan,aj->ljn", values_im, outer_sin)
+        first_im = first_im + mixer("lan,aj->ljn", values_im, outer_cos)
     turned_re = first_re * twist_cos + first_im * twist_sin
     turned_im = first_im * twist_cos - first_re * twist_sin
     spec_re = mixer("ljn,nk->ljk", turned_re, inner_cos) + mixer(
@@ -53,7 +57,15 @@
     result = mixer("ljn,ja->lan", untwist_re, outer_cos) - mixer(
         "ljn,ja->lan", untwist_im, outer_sin
     )
-    return (result / circle).reshape(line_total, circle)
+    if lines_im is None:
+        return (result / circle).reshape(line_total, circle)
+    result_im = mixer("ljn,ja->lan", untwist_im, outer_cos) + mixer(
+        "ljn,ja->lan", untwist_re, outer_sin
+    )
+    return (
+        (result / circle).reshape(line_total, circle),
+        (result_im / circle).reshape(line_total, circle),
+    )
 
 
 def face_flux(courant, near_value, far_value):
@@ -135,7 +147,24 @@
             concat_axis=1,
             tiled=True,
         )
-        smoothed = filter_lines(full_lines, line_cut)
+        if line_count % (2 * half_rows) == 0:
+            groups = line_count // (2 * half_rows)
+            paired = full_lines.reshape(groups, 2, half_rows, full_lines.shape[1])
+            pair_cut = line_cut.reshape(groups, 2, half_rows)[:, 0].reshape(-1)
+            smooth_re, smooth_im = filter_lines(
+                paired[:, 0].reshape(groups * half_rows, -1),
+                pair_cut,
+                paired[:, 1].reshape(groups * half_rows, -1),
+            )
+            smoothed = jnp.stack(
+                [
+                    smooth_re.reshape(groups, half_rows, -1),
+                    smooth_im.reshape(groups, half_rows, -1),
+                ],
+                axis=1,
+            ).reshape(full_lines.shape)
+        else:
+            smoothed = filter_lines(full_lines, line_cut)
         returned = lax.all_to_all(
             smoothed, "lon", split_axis=1, concat_axis=0, tiled=True
         ).reshape(chunk_stack, half_rows, columns)

time: 141 us -> 148 us (1.050)
  other arithmetic: 11.6 us -> 15.8 us
  waiting for transfers between devices: 62 us -> 63.6 us
    unnamed x46 -> x22, local copies, waits for them, and re-layouts: 3.51 us -> 1.95 us
where the time goes in v15:
time: 148 us; the launch traced here: 147 us
  waiting for transfers between devices  63.6 us (43%)
  starting transfers between devices  30.3 us (20%)
  local copies, waits for them, and re-layouts  21.7 us (15%)
  other arithmetic  15.8 us (11%)
  matrix products  15 us (10%)
    all_to_all x2, waiting for transfers between devices, body(): lax.all_to_all(smoothed, 'lon', split_axis=1, concat_axis=0, tiled=True)  23.5 us
    all_to_all x2, waiting for transfers between devices, body(): lax.all_to_all(pair_lines.reshape(chunk_stack * half_rows, columns), 'lon...  16.3 us
    ppermute x2, waiting for transfers between devices, body(): taken = lax.ppermute(given[rows_of_part], 'lat', pair_perm)  12.4 us
    ppermute x2, waiting for transfers between devices, body(): handed_parts.append(lax.ppermute(returned, 'lat', pair_perm))  9.78 us
    all_to_all x2, starting transfers between devices, body(): lax.all_to_all(pair_lines.reshape(chunk_stack * half_rows, columns), 'lon...  7.17 us
    all_to_all x2, starting transfers between devices, body(): lax.all_to_all(smoothed, 'lon', split_axis=1, concat_axis=0, tiled=True)  6.99 us
    ppermute x1, starting transfers between devices, body(): lax.ppermute(jnp.concatenate([flat_fields[:, -1], lat_courant[:, -1]], ax...  5.48 us
    concatenate x4, local copies, waits for them, and re-layouts, body(): jnp.concatenate([from_below[:stacked, None], flat_fields, from_above[:, N...  4.39 us
  transfers between devices with their start and end apart: 12, of which 8 were waited for; matrix products, arithmetic and copies ran while one was open for 20% of the time, Pallas kernels for 0%

profile of v15, /device:TPU:0, one launch (start us, length us, event | category | flops | bytes accessed | tf_op | source)
XLA Modules:
  0.0 147.0 jit_solution(1776047219753000070)
XLA Ops:
  0.0 1.8 %fusion.276 = (f32[40,1,720]{2,1,0:T(1,128)S(1)}, f32[40,1,720]{2,1,0:T(1,128)S(1)}) fusion(f32[40,16,720]{2,1,0:T(8,128)} %bitcast.145), kind=kLoop, calls=%fused_computation.319 | loop fusion | bytes 460800 | tf_op jit(solution)/shard_map/slice | solution.py:92
  1.8 1.3 collective-permute-start.3
  4.1 5.5 %collective-permute-start.2 = (f32[48,720]{1,0:T(8,128)S(1)}, f32[48,720]{1,0:T(8,128)S(1)}, u32[]{:S(2)}, u32[]{:S(2)}) collective-permute-start(f32[48,720]{1,0:T(8,128)S(1)} %pad_maximum_fusion.8), channel_id=1, source_target_pairs={{0,8},{8,16},{16,24},{1,9},{9,17},{17,25},{2,10},{10,18},{18,26},{... | collective-permute-start | bytes 414728 | tf_op jit(solution)/shard_map/ppermute | solution.py:91
  9.6 1.2 fusion.275
  11.1 3.0 %collective-permute-start.1 = (f32[40,16]{0,1:T(8,128)S(1)}, f32[40,16]{0,1:T(8,128)S(1)}, u32[]{:S(2)}, u32[]{:S(2)}) collective-permute-start(f32[40,16]{0,1:T(8,128)S(1)} %bitcast.166), channel_id=1, source_target_pairs={{1,0},{2,1},{3,2},{4,3},{5,4},{6,5},{7,6},{0,7},{9,8},{10,9},{11,1... | collective-permute-start | bytes 7688 | tf_op jit(solution)/shard_map/ppermute | solution.py:90
  14.7 1.5 %constant_dynamic-update-slice_fusion = f32[5,8,17,720]{3,2,1,0:T(8,128)} fusion(f32[5,8,16,720]{3,2,1,0:T(8,128)S(1)} %copy-done), kind=kLoop, calls=%fused_computation.203 | loop fusion | bytes 3809280
  17.9 1.6 %collective-permute-done = f32[48,16]{0,1:T(8,128)S(1)} collective-permute-done((f32[48,16]{0,1:T(8,128)S(1)}, f32[48,16]{0,1:T(8,128)S(1)}, u32[]{:S(2)}, u32[]{:S(2)}) %collective-permute-start) | collective-permute-done | bytes 3104 | tf_op jit(solution)/shard_map/ppermute | solution.py:87
  20.4 2.0 %multiply_subtract_fusion = f32[5,8,16,721]{3,2,1,0:T(8,128)} fusion(f32[5,8,16,1]{3,2,1,0:T(8,128)S(1)} %copy.128, f32[5,8,16,720]{3,2,1,0:T(8,128)S(1)} %copy-done, f32[5,8,16,1]{3,2,1,0:T(8,128)S(1)} %copy.125, f32[8,16,721]{2,1,0:T(8,128)S(1)} %get-tuple-element.14, f32[8,16,721]{2,1,0:T(8,128)S(1)} %get-tuple-element.13), kind=kLoop, calls=%fused_computation.13 | loop fusion | flops 3230080 | bytes 4432384 | tf_op jit(solution)/shard_map/sub | solution.py:72
  23.4 3.2 %dynamic-update-slice.1 = f32[5,8,17,720]{3,2,1,0:T(8,128)} dynamic-update-slice(f32[5,8,17,720]{3,2,1,0:T(8,128)} %constant_dynamic-update-slice_fusion, f32[5,8,1,720]{3,2,1,0:T(1,128)S(1)} %copy.132, s32[]{} %constant.133, s32[]{} %constant.133, s32[]{} %constant.134, s32[]{} %constant.133) | dynamic-update-slice | bytes 230404 | tf_op jit(solution)/shard_map/concatenate | solution.py:100
  26.9 2.9 %subtract_select_fusion = f32[5,8,17,720]{3,2,1,0:T(8,128)S(1)} fusion(f32[5,8,17,720]{3,2,1,0:T(8,128)} %dynamic-update-slice.1, f32[5,8,16,720]{3,2,1,0:T(8,128)S(1)} %copy-done, f32[5,8,1,720]{3,2,1,0:T(1,128)S(1)} %copy.131, f32[8,17,720]{2,1,0:T(8,128)S(1)} %get-tuple-element.16, f32[8,17,720]{2,1,0:T(8,128)S(1)} %get-tuple-element.15, ...), kind=kLoop, calls=%fused_computation.3 | loop fusion | flops 3427200 | bytes 6658577 | tf_op jit(solution)/shard_map/jit(_where)/select_n | solution.py:107
  30.4 1.2 slice_select_fusion.1
  32.1 2.2 %collective-permute-start.5 = (f32[16,8,720]{2,1,0:T(8,128)S(1)}, f32[16,8,720]{2,1,0:T(8,128)}, u32[]{:S(2)}, u32[]{:S(2)}) collective-permute-start(f32[16,8,720]{2,1,0:T(8,128)S(1)} %slice.137), channel_id=1, source_target_pairs={{0,16},{8,24},{16,0},{24,8},{1,17},{9,25},{17,1},{25,9},{2,18},{10... | collective-permute-start | bytes 1105928 | tf_op jit(solution)/shard_map/ppermute | solution.py:141
  35.2 9.2 %collective-permute-done.5 = f32[16,8,720]{2,1,0:T(8,128)} collective-permute-done((f32[16,8,720]{2,1,0:T(8,128)S(1)}, f32[16,8,720]{2,1,0:T(8,128)}, u32[]{:S(2)}, u32[]{:S(2)}) %collective-permute-start.5) | collective-permute-done | bytes 368672 | tf_op jit(solution)/shard_map/ppermute | solution.py:141
  44.4 2.0 %slice_select_fusion.3 = f32[16,8,720]{2,1,0:T(8,128)} fusion(f32[16,8,720]{2,1,0:T(8,128)} %collective-permute-done.5, f32[40,8,720]{2,1,0:T(8,128)} %get-tuple-element.7, pred[8]{0:T(512)(128)(4,1)S(1)} %slice_select_fusion.4), kind=kLoop, calls=%fused_computation.64 | loop fusion | flops 92160 | bytes 1105928 | tf_op jit(solution)/shard_map/jit(_where)/select_n | solution.py:142
  46.4 3.5 %all-to-all-start.2 = ((f32[8,16,720]{2,1,0:T(8,128)}), f32[8,16,720]{2,1,0:T(8,128)S(1)}, u32[]{:S(2)}, u32[]{:S(2)}) async-start(f32[8,16,720]{2,1,0:T(8,128)} %bitcast.155), calls=%async_computation.2 | async-start | bytes 786432 | tf_op jit(solution)/shard_map/all_to_all | solution.py:143
  50.7 3.2 %collective-permute-done.4 = f32[24,8,720]{2,1,0:T(8,128)} collective-permute-done((f32[24,8,720]{2,1,0:T(8,128)}, f32[24,8,720]{2,1,0:T(8,128)}, u32[]{:S(2)}, u32[]{:S(2)}) %collective-permute-start.4) | collective-permute-done | bytes 552992 | tf_op jit(solution)/shard_map/ppermute | solution.py:141
  53.9 2.0 %slice_select_fusion.2 = f32[24,8,720]{2,1,0:T(8,128)} fusion(f32[24,8,720]{2,1,0:T(8,128)} %collective-permute-done.4, f32[40,8,720]{2,1,0:T(8,128)S(1)} %copy-done.4, pred[8]{0:T(512)(128)(4,1)S(1)} %slice_select_fusion.4), kind=kLoop, calls=%fused_computation.45 | loop fusion | flops 138240 | bytes 1658888 | tf_op jit(solution)/shard_map/jit(_where)/select_n | solution.py:142
  55.9 6.4 %all-to-all-done.2 = f32[8,16,720]{2,1,0:T(8,128)S(1)} async-done(((f32[8,16,720]{2,1,0:T(8,128)}), f32[8,16,720]{2,1,0:T(8,128)S(1)}, u32[]{:S(2)}, u32[]{:S(2)}) %all-to-all-start.2) | async-done | bytes 368672 | tf_op jit(solution)/shard_map/all_to_all | solution.py:143
  62.3 3.7 %all-to-all-start = ((f32[8,24,720]{2,1,0:T(8,128)}), f32[8,24,720]{2,1,0:T(8,128)S(1)}, u32[]{:S(2)}, u32[]{:S(2)}) async-start(f32[8,24,720]{2,1,0:T(8,128)} %bitcast.151), calls=%async_computation | async-start | bytes 1179648 | tf_op jit(solution)/shard_map/all_to_all | solution.py:143
  72.6 9.9 %all-to-all-done = f32[8,24,720]{2,1,0:T(8,128)S(1)} async-done(((f32[8,24,720]{2,1,0:T(8,128)}), f32[8,24,720]{2,1,0:T(8,128)S(1)}, u32[]{:S(2)}, u32[]{:S(2)}) %all-to-all-start) | async-done | bytes 552992 | tf_op jit(solution)/shard_map/all_to_all | solution.py:143
  83.6 1.4 reshape.335
  92.0 1.4 fusion.5
  93.3 1.6 %all_to_all.51 = f32[24,8,720]{2,1,0:T(8,128)S(1)} reshape(f32[24,45,128]{2,1,0:T(8,128)} %fusion.5) | data formatting | bytes 1105920 | tf_op jit(solution)/shard_map/all_to_all | solution.py:168
  95.9 3.5 %all-to-all-start.1 = ((f32[24,8,720]{2,0,1:T(8,128)}), f32[24,8,720]{2,0,1:T(8,128)S(1)}, u32[]{:S(2)}, u32[]{:S(2)}) async-start(f32[24,8,720]{2,0,1:T(8,128)} %copy.134), calls=%async_computation.1 | async-start | bytes 1179648 | tf_op jit(solution)/shard_map/all_to_all | solution.py:168
  103.1 13.1 %all-to-all-done.1 = f32[24,8,720]{2,0,1:T(8,128)S(1)} async-done(((f32[24,8,720]{2,0,1:T(8,128)}), f32[24,8,720]{2,0,1:T(8,128)S(1)}, u32[]{:S(2)}, u32[]{:S(2)}) %all-to-all-start.1) | async-done | bytes 552992 | tf_op jit(solution)/shard_map/all_to_all | solution.py:168
  116.2 3.5 %all-to-all-start.3 = ((f32[16,8,720]{2,0,1:T(8,128)}), f32[16,8,720]{2,0,1:T(8,128)S(1)}, u32[]{:S(2)}, u32[]{:S(2)}) async-start(f32[16,8,720]{2,0,1:T(8,128)} %copy.140), calls=%async_computation.3 | async-start | bytes 786432 | tf_op jit(solution)/shard_map/all_to_all | solution.py:168
  119.6 2.1 %collective-permute-start.6 = (f32[24,8,720]{2,1,0:T(8,128)S(1)}, f32[24,8,720]{2,1,0:T(8,128)}, u32[]{:S(2)}, u32[]{:S(2)}) collective-permute-start(f32[24,8,720]{2,1,0:T(8,128)S(1)} %bitcast.152), channel_id=1, source_target_pairs={{0,16},{8,24},{16,0},{24,8},{1,17},{9,25},{17,1},{25,9},{2,18},{10... | collective-permute-start | bytes 1658888 | tf_op jit(solution)/shard_map/ppermute | solution.py:172
  121.7 10.4 %all-to-all-done.3 = f32[16,8,720]{2,0,1:T(8,128)S(1)} async-done(((f32[16,8,720]{2,0,1:T(8,128)}), f32[16,8,720]{2,0,1:T(8,128)S(1)}, u32[]{:S(2)}, u32[]{:S(2)}) %all-to-all-start.3) | async-done | bytes 368672 | tf_op jit(solution)/shard_map/all_to_all | solution.py:168
  132.1 2.0 %collective-permute-start.7 = (f32[16,8,720]{2,1,0:T(8,128)S(1)}, f32[16,8,720]{2,1,0:T(8,128)S(1)}, u32[]{:S(2)}, u32[]{:S(2)}) collective-permute-start(f32[16,8,720]{2,1,0:T(8,128)S(1)} %bitcast.156), channel_id=1, source_target_pairs={{0,16},{8,24},{16,0},{24,8},{1,17},{9,25},{17,1},{25,9},{2,18},{10... | collective-permute-start | bytes 1105928 | tf_op jit(solution)/shard_map/ppermute | solution.py:172
  134.2 9.8 %collective-permute-done.7 = f32[16,8,720]{2,1,0:T(8,128)S(1)} collective-permute-done((f32[16,8,720]{2,1,0:T(8,128)S(1)}, f32[16,8,720]{2,1,0:T(8,128)S(1)}, u32[]{:S(2)}, u32[]{:S(2)}) %collective-permute-start.7) | collective-permute-done | bytes 368672 | tf_op jit(solution)/shard_map/ppermute | solution.py:172
  144.0 1.1 pad_maximum_fusion.4
  145.1 1.9 %fusion.3 = f32[5,8,16,720]{3,2,1,0:T(8,128)} fusion(f32[5,8,16,720]{3,2,1,0:T(8,128)S(1)} %copy-done, f32[5,8,16,720]{3,2,1,0:T(8,128)S(1)} %copy-done.2, f32[5,8,8,720]{3,2,1,0:T(8,128)S(1)} %bitcast.149, f32[5,8,8,720]{3,2,1,0:T(8,128)S(1)} %bitcast.148, pred[16]{0:T(512)(128)(4,1)S(1)} %compare_reduce_fusion, pred[]{:T(512)S(6)} %lt.147), kind=kLoop, calls=%fused_computation.12 | loop fusion | flops 2304000 | bytes 7372817 | tf_op jit(solution)/shard_map/add | solution.py:181
  (107 shorter events, 27.4 us)
Async XLA Ops:
  0.0 14.7 %copy-start = (f32[5,8,16,720]{3,2,1,0:T(8,128)S(1)}, f32[5,8,16,720]{3,2,1,0:T(8,128)}, u32[]{:S(2)}) copy-start(f32[5,8,16,720]{3,2,1,0:T(8,128)} %param.5) | copy-start | bytes 5529604
  0.0 14.1 %copy-start.5 = (f32[8,16,720]{2,1,0:T(8,128)S(1)}, f32[8,16,720]{2,1,0:T(8,128)}, u32[]{:S(2)}) copy-start(f32[8,16,720]{2,1,0:T(8,128)} %param.6) | copy-start | bytes 1105924
  1.8 20.5 %collective-permute-start.3 = (f32[40,720]{1,0:T(8,128)S(1)}, f32[40,720]{1,0:T(8,128)}, u32[]{:S(2)}, u32[]{:S(2)}) collective-permute-start(f32[40,720]{1,0:T(8,128)S(1)} %bitcast.159), channel_id=1, source_target_pairs={{8,0},{16,8},{24,16},{9,1},{17,9},{25,17},{10,2},{18,10},{26,18},{... | collective-permute-start | bytes 345608 | tf_op jit(solution)/shard_map/ppermute | solution.py:94
  4.1 22.4 %collective-permute-start.2 = (f32[48,720]{1,0:T(8,128)S(1)}, f32[48,720]{1,0:T(8,128)S(1)}, u32[]{:S(2)}, u32[]{:S(2)}) collective-permute-start(f32[48,720]{1,0:T(8,128)S(1)} %pad_maximum_fusion.8), channel_id=1, source_target_pairs={{0,8},{8,16},{16,24},{1,9},{9,17},{17,25},{2,10},{10,18},{18,26},{... | collective-permute-start | bytes 414728 | tf_op jit(solution)/shard_map/ppermute | solution.py:91
  11.1 6.5 %collective-permute-start.1 = (f32[40,16]{0,1:T(8,128)S(1)}, f32[40,16]{0,1:T(8,128)S(1)}, u32[]{:S(2)}, u32[]{:S(2)}) collective-permute-start(f32[40,16]{0,1:T(8,128)S(1)} %bitcast.166), channel_id=1, source_target_pairs={{1,0},{2,1},{3,2},{4,3},{5,4},{6,5},{7,6},{0,7},{9,8},{10,9},{11,1... | collective-permute-start | bytes 7688 | tf_op jit(solution)/shard_map/ppermute | solution.py:90
  14.6 1.6 %copy-start.7 = (s32[32]{0:T(128)S(1)}, s32[32]{0:T(128)}, u32[]{:S(2)}) copy-start(s32[32]{0:T(128)} %param.8) | copy-start | bytes 388
  14.6 1.8 %copy-start.8 = (s32[32]{0:T(128)S(1)}, s32[32]{0:T(128)}, u32[]{:S(2)}) copy-start(s32[32]{0:T(128)} %param.9) | copy-start | bytes 388
  14.6 4.9 %collective-permute-start = (f32[48,16]{0,1:T(8,128)S(1)}, f32[48,16]{0,1:T(8,128)S(1)}, u32[]{:S(2)}, u32[]{:S(2)}) collective-permute-start(f32[48,16]{0,1:T(8,128)S(1)} %pad_maximum_fusion.9), channel_id=1, source_target_pairs={{0,1},{1,2},{2,3},{3,4},{4,5},{5,6},{6,7},{7,0},{8,9},{9,10},{10,1... | collective-permute-start | bytes 9224 | tf_op jit(solution)/shard_map/ppermute | solution.py:87
  20.4 6.4 %copy-start.6 = (f32[8,16,720]{2,1,0:T(8,128)S(1)}, f32[8,16,720]{2,1,0:T(8,128)}, u32[]{:S(2)}) copy-start(f32[8,16,720]{2,1,0:T(8,128)} %param.7) | copy-start | bytes 1105924
  26.9 2.9 %copy-start.3 = (f32[5,8,16,721]{3,2,1,0:T(8,128)S(1)}, f32[5,8,16,721]{3,2,1,0:T(8,128)}, u32[]{:S(2)}) copy-start(f32[5,8,16,721]{3,2,1,0:T(8,128)} %multiply_subtract_fusion) | copy-start | bytes 5537284
  30.4 1.6 %copy-start.1 = (f32[5,8,16,720]{3,2,1,0:T(8,128)}, f32[5,8,16,720]{3,2,1,0:T(8,128)S(1)}, u32[]{:S(2)}) copy-start(f32[5,8,16,720]{3,2,1,0:T(8,128)S(1)} %fusion) | copy-start | bytes 5529604
  32.1 12.4 %collective-permute-start.5 = (f32[16,8,720]{2,1,0:T(8,128)S(1)}, f32[16,8,720]{2,1,0:T(8,128)}, u32[]{:S(2)}, u32[]{:S(2)}) collective-permute-start(f32[16,8,720]{2,1,0:T(8,128)S(1)} %slice.137), channel_id=1, source_target_pairs={{0,16},{8,24},{16,0},{24,8},{1,17},{9,25},{17,1},{25,9},{2,18},{10... | collective-permute-start | bytes 1105928 | tf_op jit(solution)/shard_map/ppermute | solution.py:141
  35.2 18.7 %copy-start.4 = (f32[40,8,720]{2,1,0:T(8,128)S(1)}, f32[40,8,720]{2,1,0:T(8,128)}, u32[]{:S(2)}) copy-start(f32[40,8,720]{2,1,0:T(8,128)} %get-tuple-element.7) | copy-start | bytes 2764804
  35.2 18.7 %collective-permute-start.4 = (f32[24,8,720]{2,1,0:T(8,128)}, f32[24,8,720]{2,1,0:T(8,128)}, u32[]{:S(2)}, u32[]{:S(2)}) collective-permute-start(f32[24,8,720]{2,1,0:T(8,128)} %slice.135), channel_id=1, source_target_pairs={{0,16},{8,24},{16,0},{24,8},{1,17},{9,25},{17,1},{25,9},{2,18},{10... | collective-permute-start | bytes 1658888 | tf_op jit(solution)/shard_map/ppermute | solution.py:141
  46.4 15.9 %all-to-all-start.2 = ((f32[8,16,720]{2,1,0:T(8,128)}), f32[8,16,720]{2,1,0:T(8,128)S(1)}, u32[]{:S(2)}, u32[]{:S(2)}) async-start(f32[8,16,720]{2,1,0:T(8,128)} %bitcast.155), calls=%async_computation.2 | async-start | bytes 786432 | tf_op jit(solution)/shard_map/all_to_all | solution.py:143
  62.3 20.2 %all-to-all-start = ((f32[8,24,720]{2,1,0:T(8,128)}), f32[8,24,720]{2,1,0:T(8,128)S(1)}, u32[]{:S(2)}, u32[]{:S(2)}) async-start(f32[8,24,720]{2,1,0:T(8,128)} %bitcast.151), calls=%async_computation | async-start | bytes 1179648 | tf_op jit(solution)/shard_map/all_to_all | solution.py:143
  95.9 20.2 %all-to-all-start.1 = ((f32[24,8,720]{2,0,1:T(8,128)}), f32[24,8,720]{2,0,1:T(8,128)S(1)}, u32[]{:S(2)}, u32[]{:S(2)}) async-start(f32[24,8,720]{2,0,1:T(8,128)} %copy.134), calls=%async_computation.1 | async-start | bytes 1179648 | tf_op jit(solution)/shard_map/all_to_all | solution.py:168
  116.2 15.9 %all-to-all-start.3 = ((f32[16,8,720]{2,0,1:T(8,128)}), f32[16,8,720]{2,0,1:T(8,128)S(1)}, u32[]{:S(2)}, u32[]{:S(2)}) async-start(f32[16,8,720]{2,0,1:T(8,128)} %copy.140), calls=%async_computation.3 | async-start | bytes 786432 | tf_op jit(solution)/shard_map/all_to_all | solution.py:168
  119.6 24.3 %collective-permute-start.6 = (f32[24,8,720]{2,1,0:T(8,128)S(1)}, f32[24,8,720]{2,1,0:T(8,128)}, u32[]{:S(2)}, u32[]{:S(2)}) collective-permute-start(f32[24,8,720]{2,1,0:T(8,128)S(1)} %bitcast.152), channel_id=1, source_target_pairs={{0,16},{8,24},{16,0},{24,8},{1,17},{9,25},{17,1},{25,9},{2,18},{10... | collective-permute-start | bytes 1658888 | tf_op jit(solution)/shard_map/ppermute | solution.py:172
  132.1 13.0 %copy-start.2 = (f32[5,8,16,720]{3,2,1,0:T(8,128)S(1)}, f32[5,8,16,720]{3,2,1,0:T(8,128)}, u32[]{:S(2)}) copy-start(f32[5,8,16,720]{3,2,1,0:T(8,128)} %copy-done.1) | copy-start | bytes 5529604
  132.1 11.9 %collective-permute-start.7 = (f32[16,8,720]{2,1,0:T(8,128)S(1)}, f32[16,8,720]{2,1,0:T(8,128)S(1)}, u32[]{:S(2)}, u32[]{:S(2)}) collective-permute-start(f32[16,8,720]{2,1,0:T(8,128)S(1)} %bitcast.156), channel_id=1, source_target_pairs={{0,16},{8,24},{16,0},{24,8},{1,17},{9,25},{17,1},{25,9},{2,18},{10... | collective-permute-start | bytes 1105928 | tf_op jit(solution)/shard_map/ppermute | solution.py:172

commit v16 on v4

--- a/solution.py
+++ b/solution.py
@@ -99,7 +99,16 @@
     flat_increment = increment.reshape(stacked, rows_dev, columns)
     half_rows = rows_dev // 2
     pair_shift = lat_devices // 2
-    pair_perm = [(i, (i + pair_shift) % lat_devices) for i in range(lat_devices)]
+    filter_count = filter_rows.shape[0]
+    fewest_north, most_north = filter_count // 4, 3 * filter_count // 4
+    low_gives = [a for a in range(pair_shift) if rows_dev * a + half_rows < most_north]
+    high_gives = [a for a in range(pair_shift) if fewest_north <= rows_dev * a + half_rows - 1]
+    forward_perm = [(a, a + pair_shift) for a in low_gives] + [
+        (a + pair_shift, a) for a in high_gives
+    ]
+    backward_perm = [(a + pair_shift, a) for a in low_gives] + [
+        (a, a + pair_shift) for a in high_gives
+    ]
     is_low = tile_index < pair_shift
     partner_index = (tile_index + pair_shift) % lat_devices
 
@@ -126,7 +135,7 @@
         line_count = chunk_stack * half_rows // lon_devices
         line_index = lax.axis_index("lon") * line_count + jnp.arange(line_count, dtype=jnp.int32)
         line_cut = kept_cut[line_index % half_rows]
-        taken = lax.ppermute(given[rows_of_part], "lat", pair_perm)
+        taken = lax.ppermute(given[rows_of_part], "lat", forward_perm)
         pair_lines = jnp.where(kept_filtered[None, :, None], kept[rows_of_part], taken)
         full_lines = lax.all_to_all(
             pair_lines.reshape(chunk_stack * half_rows, columns),
@@ -140,7 +149,7 @@
             smoothed, "lon", split_axis=1, concat_axis=0, tiled=True
         ).reshape(chunk_stack, half_rows, columns)
         returned_parts.append(returned)
-        handed_parts.append(lax.ppermute(returned, "lat", pair_perm))
+        handed_parts.append(lax.ppermute(returned, "lat", backward_perm))
     returned = jnp.concatenate(returned_parts, axis=0)
     handed_back = jnp.concatenate(handed_parts, axis=0)
     smooth_rows = jnp.where(

time: 141 us -> 145 us (1.028)
  starting transfers between devices: 30.3 us -> 32.9 us
    ppermute x4, starting transfers between devices: 6.29 us -> 8.89 us  [the longest x2 6.19 us: body(): taken = lax.ppermute(given[rows_of_part], 'lat', forward_perm)]
where the time goes in v16:
time: 145 us; the launch traced here: 144 us
  waiting for transfers between devices  62.5 us (43%)
  starting transfers between devices  32.9 us (23%)
  local copies, waits for them, and re-layouts  21.4 us (15%)
  matrix products  14.7 us (10%)
  other arithmetic  11.6 us (8%)
    all_to_all x2, waiting for transfers between devices, body(): lax.all_to_all(smoothed, 'lon', split_axis=1, concat_axis=0, tiled=True)  23.5 us
    all_to_all x2, waiting for transfers between devices, body(): lax.all_to_all(pair_lines.reshape(chunk_stack * half_rows, columns), 'lon...  15.3 us
    ppermute x2, waiting for transfers between devices, body(): handed_parts.append(lax.ppermute(returned, 'lat', backward_perm))  12.1 us
    ppermute x2, waiting for transfers between devices, body(): taken = lax.ppermute(given[rows_of_part], 'lat', forward_perm)  9.25 us
    all_to_all x2, starting transfers between devices, body(): lax.all_to_all(pair_lines.reshape(chunk_stack * half_rows, columns), 'lon...  7.17 us
    all_to_all x2, starting transfers between devices, body(): lax.all_to_all(smoothed, 'lon', split_axis=1, concat_axis=0, tiled=True)  6.99 us
    ppermute x2, starting transfers between devices, body(): taken = lax.ppermute(given[rows_of_part], 'lat', forward_perm)  6.19 us
    ppermute x1, starting transfers between devices, body(): lax.ppermute(jnp.concatenate([flat_fields[:, -1], lat_courant[:, -1]], ax...  5.48 us
  transfers between devices with their start and end apart: 12, of which 8 were waited for; matrix products, arithmetic and copies ran while one was open for 20% of the time, Pallas kernels for 0%

profile of v16, /device:TPU:0, one launch (start us, length us, event | category | flops | bytes accessed | tf_op | source)
XLA Modules:
  0.0 143.8 jit_solution(3899943641622698402)
XLA Ops:
  0.0 1.8 %fusion.247 = (f32[40,1,720]{2,1,0:T(1,128)S(1)}, f32[40,1,720]{2,1,0:T(1,128)S(1)}) fusion(f32[40,16,720]{2,1,0:T(8,128)} %bitcast.129), kind=kLoop, calls=%fused_computation.289 | loop fusion | bytes 460800 | tf_op jit(solution)/shard_map/slice | solution.py:80
  1.8 1.3 collective-permute-start.3
  4.1 5.5 %collective-permute-start.2 = (f32[48,720]{1,0:T(8,128)S(1)}, f32[48,720]{1,0:T(8,128)S(1)}, u32[]{:S(2)}, u32[]{:S(2)}) collective-permute-start(f32[48,720]{1,0:T(8,128)S(1)} %pad_maximum_fusion.7), channel_id=1, source_target_pairs={{0,8},{8,16},{16,24},{1,9},{9,17},{17,25},{2,10},{10,18},{18,26},{... | collective-permute-start | bytes 414728 | tf_op jit(solution)/shard_map/ppermute | solution.py:79
  9.6 1.2 fusion.246
  11.1 3.0 %collective-permute-start.1 = (f32[40,16]{0,1:T(8,128)S(1)}, f32[40,16]{0,1:T(8,128)S(1)}, u32[]{:S(2)}, u32[]{:S(2)}) collective-permute-start(f32[40,16]{0,1:T(8,128)S(1)} %bitcast.149), channel_id=1, source_target_pairs={{1,0},{2,1},{3,2},{4,3},{5,4},{6,5},{7,6},{0,7},{9,8},{10,9},{11,1... | collective-permute-start | bytes 7688 | tf_op jit(solution)/shard_map/ppermute | solution.py:78
  14.7 1.6 %constant_dynamic-update-slice_fusion = f32[5,8,17,720]{3,2,1,0:T(8,128)} fusion(f32[5,8,16,720]{3,2,1,0:T(8,128)S(1)} %copy-done), kind=kLoop, calls=%fused_computation.186 | loop fusion | bytes 3809280
  17.2 2.3 %collective-permute-done = f32[48,16]{0,1:T(8,128)S(1)} collective-permute-done((f32[48,16]{0,1:T(8,128)S(1)}, f32[48,16]{0,1:T(8,128)S(1)}, u32[]{:S(2)}, u32[]{:S(2)}) %collective-permute-start) | collective-permute-done | bytes 3104 | tf_op jit(solution)/shard_map/ppermute | solution.py:75
  20.4 2.0 %multiply_subtract_fusion = f32[5,8,16,721]{3,2,1,0:T(8,128)} fusion(f32[5,8,16,1]{3,2,1,0:T(8,128)S(1)} %copy.106, f32[5,8,16,720]{3,2,1,0:T(8,128)S(1)} %copy-done, f32[5,8,16,1]{3,2,1,0:T(8,128)S(1)} %copy.103, f32[8,16,721]{2,1,0:T(8,128)S(1)} %get-tuple-element.14, f32[8,16,721]{2,1,0:T(8,128)S(1)} %get-tuple-element.13), kind=kLoop, calls=%fused_computation.13 | loop fusion | flops 3230080 | bytes 4432384 | tf_op jit(solution)/shard_map/sub | solution.py:60
  22.3 1.0 copy.110
  23.4 3.2 %dynamic-update-slice.1 = f32[5,8,17,720]{3,2,1,0:T(8,128)} dynamic-update-slice(f32[5,8,17,720]{3,2,1,0:T(8,128)} %constant_dynamic-update-slice_fusion, f32[5,8,1,720]{3,2,1,0:T(1,128)S(1)} %copy.110, s32[]{} %constant.131, s32[]{} %constant.131, s32[]{} %constant.132, s32[]{} %constant.131) | dynamic-update-slice | bytes 230404 | tf_op jit(solution)/shard_map/concatenate | solution.py:88
  26.9 2.9 %subtract_select_fusion = f32[5,8,17,720]{3,2,1,0:T(8,128)S(1)} fusion(f32[5,8,17,720]{3,2,1,0:T(8,128)} %dynamic-update-slice.1, f32[5,8,16,720]{3,2,1,0:T(8,128)S(1)} %copy-done, f32[5,8,1,720]{3,2,1,0:T(1,128)S(1)} %copy.109, f32[8,17,720]{2,1,0:T(8,128)S(1)} %get-tuple-element.16, f32[8,17,720]{2,1,0:T(8,128)S(1)} %get-tuple-element.15, ...), kind=kLoop, calls=%fused_computation.3 | loop fusion | flops 3427200 | bytes 6658577 | tf_op jit(solution)/shard_map/jit(_where)/select_n | solution.py:95
  30.6 1.1 copy-done.1
  31.7 4.1 %collective-permute-start.4 = (f32[16,8,720]{2,1,0:T(8,128)S(1)}, f32[16,8,720]{2,1,0:T(8,128)S(1)}, u32[]{:S(2)}, u32[]{:S(2)}) collective-permute-start(f32[16,8,720]{2,1,0:T(8,128)S(1)} %slice.123), channel_id=1, source_target_pairs={{0,16},{24,8},{1,17},{25,9},{2,18},{26,10},{3,19},{27,11},{4,20},{... | collective-permute-start | bytes 1105928 | tf_op jit(solution)/shard_map/ppermute | solution.py:138
  36.8 2.1 %collective-permute-start.5 = (f32[24,8,720]{2,1,0:T(8,128)}, f32[24,8,720]{2,1,0:T(8,128)}, u32[]{:S(2)}, u32[]{:S(2)}) collective-permute-start(f32[24,8,720]{2,1,0:T(8,128)} %slice.125), channel_id=1, source_target_pairs={{0,16},{24,8},{1,17},{25,9},{2,18},{26,10},{3,19},{27,11},{4,20},{... | collective-permute-start | bytes 1658888 | tf_op jit(solution)/shard_map/ppermute | solution.py:138
  38.9 6.5 %collective-permute-done.4 = f32[16,8,720]{2,1,0:T(8,128)S(1)} collective-permute-done((f32[16,8,720]{2,1,0:T(8,128)S(1)}, f32[16,8,720]{2,1,0:T(8,128)S(1)}, u32[]{:S(2)}, u32[]{:S(2)}) %collective-permute-start.4) | collective-permute-done | bytes 368672 | tf_op jit(solution)/shard_map/ppermute | solution.py:138
  46.2 3.5 %all-to-all-start = ((f32[8,16,720]{2,1,0:T(8,128)}), f32[8,16,720]{2,1,0:T(8,128)S(1)}, u32[]{:S(2)}, u32[]{:S(2)}) async-start(f32[8,16,720]{2,1,0:T(8,128)} %bitcast.138), calls=%async_computation | async-start | bytes 786432 | tf_op jit(solution)/shard_map/all_to_all | solution.py:140
  51.2 2.8 %collective-permute-done.5 = f32[24,8,720]{2,1,0:T(8,128)} collective-permute-done((f32[24,8,720]{2,1,0:T(8,128)}, f32[24,8,720]{2,1,0:T(8,128)}, u32[]{:S(2)}, u32[]{:S(2)}) %collective-permute-start.5) | collective-permute-done | bytes 552992 | tf_op jit(solution)/shard_map/ppermute | solution.py:138
  54.0 2.0 %slice_select_fusion.2 = f32[24,8,720]{2,1,0:T(8,128)} fusion(f32[24,8,720]{2,1,0:T(8,128)} %collective-permute-done.5, f32[40,8,720]{2,1,0:T(8,128)S(1)} %get-tuple-element.7, pred[8]{0:T(512)(128)(4,1)S(1)} %slice_select_fusion.4), kind=kLoop, calls=%fused_computation.40 | loop fusion | flops 138240 | bytes 1658888 | tf_op jit(solution)/shard_map/jit(_where)/select_n | solution.py:139
  56.0 6.1 %all-to-all-done = f32[8,16,720]{2,1,0:T(8,128)S(1)} async-done(((f32[8,16,720]{2,1,0:T(8,128)}), f32[8,16,720]{2,1,0:T(8,128)S(1)}, u32[]{:S(2)}, u32[]{:S(2)}) %all-to-all-start) | async-done | bytes 368672 | tf_op jit(solution)/shard_map/all_to_all | solution.py:140
  62.1 3.7 %all-to-all-start.2 = ((f32[8,24,720]{2,1,0:T(8,128)}), f32[8,24,720]{2,1,0:T(8,128)S(1)}, u32[]{:S(2)}, u32[]{:S(2)}) async-start(f32[8,24,720]{2,1,0:T(8,128)} %bitcast.24), calls=%async_computation.2 | async-start | bytes 1179648 | tf_op jit(solution)/shard_map/all_to_all | solution.py:140
  66.8 1.2 reshape.332
  73.2 9.2 %all-to-all-done.2 = f32[8,24,720]{2,1,0:T(8,128)S(1)} async-done(((f32[8,24,720]{2,1,0:T(8,128)}), f32[8,24,720]{2,1,0:T(8,128)S(1)}, u32[]{:S(2)}, u32[]{:S(2)}) %all-to-all-start.2) | async-done | bytes 552992 | tf_op jit(solution)/shard_map/all_to_all | solution.py:140
  91.0 1.0 copy.114
  92.0 3.5 %all-to-all-start.3 = ((f32[24,8,720]{2,0,1:T(8,128)}), f32[24,8,720]{2,0,1:T(8,128)S(1)}, u32[]{:S(2)}, u32[]{:S(2)}) async-start(f32[24,8,720]{2,0,1:T(8,128)} %copy.114), calls=%async_computation.3 | async-start | bytes 1179648 | tf_op jit(solution)/shard_map/all_to_all | solution.py:148
  95.6 1.6 %fusion.72 = f32[16,45,128]{2,1,0:T(8,128)S(1)} fusion(f32[16,45,128]{2,1,0:T(8,128)} %copy-done.12), kind=kOutput, calls=%fused_computation.115 | convolution fusion | flops 71008256 | bytes 737280 | tf_op jit(solution)/shard_map/ljk,kn->ljn/dot_general | solution.py:49
  99.9 12.4 %all-to-all-done.3 = f32[24,8,720]{2,0,1:T(8,128)S(1)} async-done(((f32[24,8,720]{2,0,1:T(8,128)}), f32[24,8,720]{2,0,1:T(8,128)S(1)}, u32[]{:S(2)}, u32[]{:S(2)}) %all-to-all-start.3) | async-done | bytes 552992 | tf_op jit(solution)/shard_map/all_to_all | solution.py:148
  112.3 3.5 %all-to-all-start.1 = ((f32[16,8,720]{2,0,1:T(8,128)}), f32[16,8,720]{2,0,1:T(8,128)S(1)}, u32[]{:S(2)}, u32[]{:S(2)}) async-start(f32[16,8,720]{2,0,1:T(8,128)} %copy.112), calls=%async_computation.1 | async-start | bytes 786432 | tf_op jit(solution)/shard_map/all_to_all | solution.py:148
  115.7 1.3 collective-permute-start.7
  117.0 11.2 %all-to-all-done.1 = f32[16,8,720]{2,0,1:T(8,128)S(1)} async-done(((f32[16,8,720]{2,0,1:T(8,128)}), f32[16,8,720]{2,0,1:T(8,128)S(1)}, u32[]{:S(2)}, u32[]{:S(2)}) %all-to-all-start.1) | async-done | bytes 368672 | tf_op jit(solution)/shard_map/all_to_all | solution.py:148
  128.2 1.4 collective-permute-start.6
  129.7 12.1 %collective-permute-done.6 = f32[16,8,720]{2,1,0:T(8,128)S(1)} collective-permute-done((f32[16,8,720]{2,1,0:T(8,128)S(1)}, f32[16,8,720]{2,1,0:T(8,128)S(1)}, u32[]{:S(2)}, u32[]{:S(2)}) %collective-permute-start.6) | collective-permute-done | bytes 368672 | tf_op jit(solution)/shard_map/ppermute | solution.py:152
  141.9 1.9 %fusion.3 = f32[5,8,16,720]{3,2,1,0:T(8,128)} fusion(f32[5,8,16,720]{3,2,1,0:T(8,128)S(1)} %copy-done, f32[5,8,16,720]{3,2,1,0:T(8,128)S(1)} %copy-done.2, f32[5,8,8,720]{3,2,1,0:T(8,128)S(1)} %bitcast.133, f32[5,8,8,720]{3,2,1,0:T(8,128)S(1)} %bitcast.132, pred[16]{0:T(512)(128)(4,1)S(1)} %compare_reduce_fusion, pred[]{:T(512)S(6)} %lt.139), kind=kLoop, calls=%fused_computation.12 | loop fusion | flops 2304000 | bytes 7372817 | tf_op jit(solution)/shard_map/add | solution.py:161
  (121 shorter events, 25.1 us)
Async XLA Ops:
  0.0 14.7 %copy-start = (f32[5,8,16,720]{3,2,1,0:T(8,128)S(1)}, f32[5,8,16,720]{3,2,1,0:T(8,128)}, u32[]{:S(2)}) copy-start(f32[5,8,16,720]{3,2,1,0:T(8,128)} %param.5) | copy-start | bytes 5529604
  0.0 14.1 %copy-start.13 = (f32[8,16,720]{2,1,0:T(8,128)S(1)}, f32[8,16,720]{2,1,0:T(8,128)}, u32[]{:S(2)}) copy-start(f32[8,16,720]{2,1,0:T(8,128)} %param.6) | copy-start | bytes 1105924
  1.8 20.5 %collective-permute-start.3 = (f32[40,720]{1,0:T(8,128)S(1)}, f32[40,720]{1,0:T(8,128)}, u32[]{:S(2)}, u32[]{:S(2)}) collective-permute-start(f32[40,720]{1,0:T(8,128)S(1)} %bitcast.142), channel_id=1, source_target_pairs={{8,0},{16,8},{24,16},{9,1},{17,9},{25,17},{10,2},{18,10},{26,18},{... | collective-permute-start | bytes 345608 | tf_op jit(solution)/shard_map/ppermute | solution.py:82
  4.1 22.5 %collective-permute-start.2 = (f32[48,720]{1,0:T(8,128)S(1)}, f32[48,720]{1,0:T(8,128)S(1)}, u32[]{:S(2)}, u32[]{:S(2)}) collective-permute-start(f32[48,720]{1,0:T(8,128)S(1)} %pad_maximum_fusion.7), channel_id=1, source_target_pairs={{0,8},{8,16},{16,24},{1,9},{9,17},{17,25},{2,10},{10,18},{18,26},{... | collective-permute-start | bytes 414728 | tf_op jit(solution)/shard_map/ppermute | solution.py:79
  11.1 5.8 %collective-permute-start.1 = (f32[40,16]{0,1:T(8,128)S(1)}, f32[40,16]{0,1:T(8,128)S(1)}, u32[]{:S(2)}, u32[]{:S(2)}) collective-permute-start(f32[40,16]{0,1:T(8,128)S(1)} %bitcast.149), channel_id=1, source_target_pairs={{1,0},{2,1},{3,2},{4,3},{5,4},{6,5},{7,6},{0,7},{9,8},{10,9},{11,1... | collective-permute-start | bytes 7688 | tf_op jit(solution)/shard_map/ppermute | solution.py:78
  14.6 1.6 %copy-start.19 = (s32[32]{0:T(128)S(1)}, s32[32]{0:T(128)}, u32[]{:S(2)}) copy-start(s32[32]{0:T(128)} %param.8) | copy-start | bytes 388
  14.6 1.9 %copy-start.20 = (s32[32]{0:T(128)S(1)}, s32[32]{0:T(128)}, u32[]{:S(2)}) copy-start(s32[32]{0:T(128)} %param.9) | copy-start | bytes 388
  14.6 4.9 %collective-permute-start = (f32[48,16]{0,1:T(8,128)S(1)}, f32[48,16]{0,1:T(8,128)S(1)}, u32[]{:S(2)}, u32[]{:S(2)}) collective-permute-start(f32[48,16]{0,1:T(8,128)S(1)} %pad_maximum_fusion.8), channel_id=1, source_target_pairs={{0,1},{1,2},{2,3},{3,4},{4,5},{5,6},{6,7},{7,0},{8,9},{9,10},{10,1... | collective-permute-start | bytes 9224 | tf_op jit(solution)/shard_map/ppermute | solution.py:75
  20.4 6.4 %copy-start.14 = (f32[8,16,720]{2,1,0:T(8,128)S(1)}, f32[8,16,720]{2,1,0:T(8,128)}, u32[]{:S(2)}) copy-start(f32[8,16,720]{2,1,0:T(8,128)} %param.7) | copy-start | bytes 1105924
  26.9 2.9 %copy-start.3 = (f32[5,8,16,721]{3,2,1,0:T(8,128)S(1)}, f32[5,8,16,721]{3,2,1,0:T(8,128)}, u32[]{:S(2)}) copy-start(f32[5,8,16,721]{3,2,1,0:T(8,128)} %multiply_subtract_fusion) | copy-start | bytes 5537284
  30.4 1.3 copy-start.1
  31.7 13.6 %collective-permute-start.4 = (f32[16,8,720]{2,1,0:T(8,128)S(1)}, f32[16,8,720]{2,1,0:T(8,128)S(1)}, u32[]{:S(2)}, u32[]{:S(2)}) collective-permute-start(f32[16,8,720]{2,1,0:T(8,128)S(1)} %slice.123), channel_id=1, source_target_pairs={{0,16},{24,8},{1,17},{25,9},{2,18},{26,10},{3,19},{27,11},{4,20},{... | collective-permute-start | bytes 1105928 | tf_op jit(solution)/shard_map/ppermute | solution.py:138
  35.9 35.3 %copy-start.15 = (f32[45,128]{1,0:T(8,128)}, f32[45,128]{1,0:T(8,128)S(1)}, u32[]{:S(2)}) copy-start(f32[45,128]{1,0:T(8,128)S(1)} %broadcast_maximum_fusion) | copy-start | bytes 69124
  36.8 17.2 %collective-permute-start.5 = (f32[24,8,720]{2,1,0:T(8,128)}, f32[24,8,720]{2,1,0:T(8,128)}, u32[]{:S(2)}, u32[]{:S(2)}) collective-permute-start(f32[24,8,720]{2,1,0:T(8,128)} %slice.125), channel_id=1, source_target_pairs={{0,16},{24,8},{1,17},{25,9},{2,18},{26,10},{3,19},{27,11},{4,20},{... | collective-permute-start | bytes 1658888 | tf_op jit(solution)/shard_map/ppermute | solution.py:138
  46.2 15.9 %all-to-all-start = ((f32[8,16,720]{2,1,0:T(8,128)}), f32[8,16,720]{2,1,0:T(8,128)S(1)}, u32[]{:S(2)}, u32[]{:S(2)}) async-start(f32[8,16,720]{2,1,0:T(8,128)} %bitcast.138), calls=%async_computation | async-start | bytes 786432 | tf_op jit(solution)/shard_map/all_to_all | solution.py:140
  51.2 20.1 %copy-start.4 = (f32[45,128]{1,0:T(8,128)}, f32[45,128]{1,0:T(8,128)S(1)}, u32[]{:S(2)}) copy-start(f32[45,128]{1,0:T(8,128)S(1)} %get-tuple-element.17) | copy-start | bytes 69124
  51.2 20.1 %copy-start.7 = (f32[45,128]{1,0:T(8,128)}, f32[45,128]{1,0:T(8,128)S(1)}, u32[]{:S(2)}) copy-start(f32[45,128]{1,0:T(8,128)S(1)} %get-tuple-element.18) | copy-start | bytes 69124
  51.2 20.0 %copy-start.17 = (f32[45,128]{1,0:T(8,128)}, f32[45,128]{1,0:T(8,128)S(1)}, u32[]{:S(2)}) copy-start(f32[45,128]{1,0:T(8,128)S(1)} %fusion.100) | copy-start | bytes 69124
  62.1 20.2 %all-to-all-start.2 = ((f32[8,24,720]{2,1,0:T(8,128)}), f32[8,24,720]{2,1,0:T(8,128)S(1)}, u32[]{:S(2)}, u32[]{:S(2)}) async-start(f32[8,24,720]{2,1,0:T(8,128)} %bitcast.24), calls=%async_computation.2 | async-start | bytes 1179648 | tf_op jit(solution)/shard_map/all_to_all | solution.py:140
  70.1 1.8 %copy-start.10 = (f32[16,45,128]{2,1,0:T(8,128)}, f32[16,45,128]{2,1,0:T(8,128)S(1)}, u32[]{:S(2)}) copy-start(f32[16,45,128]{2,1,0:T(8,128)S(1)} %fusion.9) | copy-start | bytes 1105924
  82.9 1.0 copy-start.5
  83.0 1.0 copy-start.8
  84.0 1.3 copy-start.16
  84.0 1.3 copy-start.18
  91.0 6.1 %copy-start.11 = (f32[16,45,128]{2,1,0:T(8,128)S(1)}, f32[16,45,128]{2,1,0:T(8,128)}, u32[]{:S(2)}) copy-start(f32[16,45,128]{2,1,0:T(8,128)} %copy-done.10) | copy-start | bytes 1105924
  91.0 6.7 %copy-start.6 = (f32[45,128]{1,0:T(8,128)S(1)}, f32[45,128]{1,0:T(8,128)}, u32[]{:S(2)}) copy-start(f32[45,128]{1,0:T(8,128)} %copy-done.4) | copy-start | bytes 69124
  91.0 6.7 %copy-start.9 = (f32[45,128]{1,0:T(8,128)S(1)}, f32[45,128]{1,0:T(8,128)}, u32[]{:S(2)}) copy-start(f32[45,128]{1,0:T(8,128)} %copy-done.7) | copy-start | bytes 69124
  92.0 20.2 %all-to-all-start.3 = ((f32[24,8,720]{2,0,1:T(8,128)}), f32[24,8,720]{2,0,1:T(8,128)S(1)}, u32[]{:S(2)}, u32[]{:S(2)}) async-start(f32[24,8,720]{2,0,1:T(8,128)} %copy.114), calls=%async_computation.3 | async-start | bytes 1179648 | tf_op jit(solution)/shard_map/all_to_all | solution.py:148
  112.3 15.9 %all-to-all-start.1 = ((f32[16,8,720]{2,0,1:T(8,128)}), f32[16,8,720]{2,0,1:T(8,128)S(1)}, u32[]{:S(2)}, u32[]{:S(2)}) async-start(f32[16,8,720]{2,0,1:T(8,128)} %copy.112), calls=%async_computation.1 | async-start | bytes 786432 | tf_op jit(solution)/shard_map/all_to_all | solution.py:148
  115.7 26.1 %collective-permute-start.7 = (f32[24,8,720]{2,1,0:T(8,128)S(1)}, f32[24,8,720]{2,1,0:T(8,128)S(1)}, u32[]{:S(2)}, u32[]{:S(2)}) collective-permute-start(f32[24,8,720]{2,1,0:T(8,128)S(1)} %bitcast.135), channel_id=1, source_target_pairs={{16,0},{8,24},{17,1},{9,25},{18,2},{10,26},{19,3},{11,27},{20,4},{... | collective-permute-start | bytes 1658888 | tf_op jit(solution)/shard_map/ppermute | solution.py:152
  128.2 13.7 %copy-start.2 = (f32[5,8,16,720]{3,2,1,0:T(8,128)S(1)}, f32[5,8,16,720]{3,2,1,0:T(8,128)}, u32[]{:S(2)}) copy-start(f32[5,8,16,720]{3,2,1,0:T(8,128)} %copy-done.1) | copy-start | bytes 5529604
  128.2 13.6 %collective-permute-start.6 = (f32[16,8,720]{2,1,0:T(8,128)S(1)}, f32[16,8,720]{2,1,0:T(8,128)S(1)}, u32[]{:S(2)}, u32[]{:S(2)}) collective-permute-start(f32[16,8,720]{2,1,0:T(8,128)S(1)} %bitcast.139), channel_id=1, source_target_pairs={{16,0},{8,24},{17,1},{9,25},{18,2},{10,26},{19,3},{11,27},{20,4},{... | collective-permute-start | bytes 1105928 | tf_op jit(solution)/shard_map/ppermute | solution.py:152
  (1 other events, 0.7 us)

commit v17 on v4

--- a/solution.py
+++ b/solution.py
@@ -113,8 +113,9 @@
     row_cut = jnp.where(is_filtered, own_cut, partner_cut).astype(jnp.float32)
     low_half = flat_increment[:, :half_rows]
     high_half = flat_increment[:, half_rows:]
-    kept = jnp.where(is_low, low_half, high_half)
-    given = jnp.where(is_low, high_half, low_half)
+    kept_start = jnp.where(is_low, 0, half_rows)
+    kept = lax.dynamic_slice_in_dim(flat_increment, kept_start, half_rows, axis=1)
+    given = lax.dynamic_slice_in_dim(flat_increment, half_rows - kept_start, half_rows, axis=1)
     kept_filtered = jnp.where(is_low, is_filtered[:half_rows], is_filtered[half_rows:])
     kept_cut = jnp.where(is_low, row_cut[:half_rows], row_cut[half_rows:])
     chunk_sizes = (stacked * 2 // 5, stacked - stacked * 2 // 5)

time: 141 us -> 143 us (1.014)
    ppermute x2, waiting for transfers between devices: 12.1 us -> 9.9 us  [body(): taken = lax.ppermute(given[rows_of_part], 'lat', pair_perm)]
  transfers between devices with their start and end apart: 12 -> 12, of which waited for: 8 -> 8; matrix products, arithmetic and copies ran while one was open for 20% -> 21% of each run, Pallas kernels for 0% -> 0%
where the time goes in v17:
time: 143 us; the launch traced here: 142 us
  waiting for transfers between devices  61 us (43%)
  starting transfers between devices  30.3 us (21%)
  local copies, waits for them, and re-layouts  22.5 us (16%)
  matrix products  14.7 us (10%)
  other arithmetic  12.4 us (9%)
    all_to_all x2, waiting for transfers between devices, body(): lax.all_to_all(smoothed, 'lon', split_axis=1, concat_axis=0, tiled=True)  22.7 us
    all_to_all x2, waiting for transfers between devices, body(): lax.all_to_all(pair_lines.reshape(chunk_stack * half_rows, columns), 'lon...  16.3 us
    ppermute x2, waiting for transfers between devices, body(): taken = lax.ppermute(given[rows_of_part], 'lat', pair_perm)  9.9 us
    ppermute x2, waiting for transfers between devices, body(): handed_parts.append(lax.ppermute(returned, 'lat', pair_perm))  9.78 us
    all_to_all x2, starting transfers between devices, body(): lax.all_to_all(pair_lines.reshape(chunk_stack * half_rows, columns), 'lon...  7.17 us
    all_to_all x2, starting transfers between devices, body(): lax.all_to_all(smoothed, 'lon', split_axis=1, concat_axis=0, tiled=True)  6.99 us
    ppermute x1, starting transfers between devices, body(): lax.ppermute(jnp.concatenate([flat_fields[:, -1], lat_courant[:, -1]], ax...  5.48 us
    concatenate x4, local copies, waits for them, and re-layouts, body(): jnp.concatenate([from_below[:stacked, None], flat_fields, from_above[:, N...  4.4 us
  transfers between devices with their start and end apart: 12, of which 8 were waited for; matrix products, arithmetic and copies ran while one was open for 21% of the time, Pallas kernels for 0%

profile of v17, /device:TPU:0, one launch (start us, length us, event | category | flops | bytes accessed | tf_op | source)
XLA Modules:
  0.0 141.7 jit_solution(7278474971123124518)
XLA Ops:
  0.0 1.8 %fusion.247 = (f32[40,1,720]{2,1,0:T(1,128)S(1)}, f32[40,1,720]{2,1,0:T(1,128)S(1)}) fusion(f32[40,16,720]{2,1,0:T(8,128)} %bitcast.129), kind=kLoop, calls=%fused_computation.289 | loop fusion | bytes 460800 | tf_op jit(solution)/shard_map/slice | solution.py:80
  1.8 1.3 collective-permute-start.3
  4.1 5.5 %collective-permute-start.2 = (f32[48,720]{1,0:T(8,128)S(1)}, f32[48,720]{1,0:T(8,128)S(1)}, u32[]{:S(2)}, u32[]{:S(2)}) collective-permute-start(f32[48,720]{1,0:T(8,128)S(1)} %pad_maximum_fusion.7), channel_id=1, source_target_pairs={{0,8},{8,16},{16,24},{1,9},{9,17},{17,25},{2,10},{10,18},{18,26},{... | collective-permute-start | bytes 414728 | tf_op jit(solution)/shard_map/ppermute | solution.py:79
  9.6 1.2 fusion.246
  11.1 3.0 %collective-permute-start.1 = (f32[40,16]{0,1:T(8,128)S(1)}, f32[40,16]{0,1:T(8,128)S(1)}, u32[]{:S(2)}, u32[]{:S(2)}) collective-permute-start(f32[40,16]{0,1:T(8,128)S(1)} %bitcast.151), channel_id=1, source_target_pairs={{1,0},{2,1},{3,2},{4,3},{5,4},{6,5},{7,6},{0,7},{9,8},{10,9},{11,1... | collective-permute-start | bytes 7688 | tf_op jit(solution)/shard_map/ppermute | solution.py:78
  14.7 1.5 %constant_dynamic-update-slice_fusion = f32[5,8,17,720]{3,2,1,0:T(8,128)} fusion(f32[5,8,16,720]{3,2,1,0:T(8,128)S(1)} %copy-done), kind=kLoop, calls=%fused_computation.184 | loop fusion | bytes 3809280
  17.2 2.4 %collective-permute-done = f32[48,16]{0,1:T(8,128)S(1)} collective-permute-done((f32[48,16]{0,1:T(8,128)S(1)}, f32[48,16]{0,1:T(8,128)S(1)}, u32[]{:S(2)}, u32[]{:S(2)}) %collective-permute-start) | collective-permute-done | bytes 3104 | tf_op jit(solution)/shard_map/ppermute | solution.py:75
  20.4 2.0 %multiply_subtract_fusion = f32[5,8,16,721]{3,2,1,0:T(8,128)} fusion(f32[5,8,16,1]{3,2,1,0:T(8,128)S(1)} %copy.106, f32[5,8,16,720]{3,2,1,0:T(8,128)S(1)} %copy-done, f32[5,8,16,1]{3,2,1,0:T(8,128)S(1)} %copy.103, f32[8,16,721]{2,1,0:T(8,128)S(1)} %get-tuple-element.12, f32[8,16,721]{2,1,0:T(8,128)S(1)} %get-tuple-element.11), kind=kLoop, calls=%fused_computation.13 | loop fusion | flops 3230080 | bytes 4432384 | tf_op jit(solution)/shard_map/sub | solution.py:60
  22.3 1.0 copy.110
  23.4 3.2 %dynamic-update-slice.1 = f32[5,8,17,720]{3,2,1,0:T(8,128)} dynamic-update-slice(f32[5,8,17,720]{3,2,1,0:T(8,128)} %constant_dynamic-update-slice_fusion, f32[5,8,1,720]{3,2,1,0:T(1,128)S(1)} %copy.110, s32[]{} %constant.133, s32[]{} %constant.133, s32[]{} %constant.134, s32[]{} %constant.133) | dynamic-update-slice | bytes 230404 | tf_op jit(solution)/shard_map/concatenate | solution.py:88
  26.9 2.9 %subtract_select_fusion = f32[5,8,17,720]{3,2,1,0:T(8,128)S(1)} fusion(f32[5,8,17,720]{3,2,1,0:T(8,128)} %dynamic-update-slice.1, f32[5,8,16,720]{3,2,1,0:T(8,128)S(1)} %copy-done, f32[5,8,1,720]{3,2,1,0:T(1,128)S(1)} %copy.109, f32[8,17,720]{2,1,0:T(8,128)S(1)} %get-tuple-element.14, f32[8,17,720]{2,1,0:T(8,128)S(1)} %get-tuple-element.13, ...), kind=kLoop, calls=%fused_computation.3 | loop fusion | flops 3427200 | bytes 6658577 | tf_op jit(solution)/shard_map/jit(_where)/select_n | solution.py:95
  30.5 1.3 copy-done.1
  31.7 2.2 %collective-permute-start.4 = (f32[16,8,720]{2,1,0:T(8,128)S(1)}, f32[16,8,720]{2,1,0:T(8,128)S(1)}, u32[]{:S(2)}, u32[]{:S(2)}) collective-permute-start(f32[16,8,720]{2,1,0:T(8,128)S(1)} %constant_dynamic-slice_fusion), channel_id=1, source_target_pairs={{0,16},{8,24},{16,0},{24,8},{1,17},{9,25},{17,1},{25,9},{2,18},{10... | collective-permute-start | bytes 1105928 | tf_op jit(solution)/shard_map/ppermute | solution.py:130
  34.0 1.9 %constant_dynamic-slice_fusion.1 = f32[24,8,720]{2,1,0:T(8,128)} fusion(f32[40,16,720]{2,1,0:T(8,128)} %bitcast.132, s32[]{:T(128)S(6)} %add.328, s32[]{:T(128)S(6)} %select_n.231), kind=kLoop, calls=%fused_computation.212 | loop fusion | bytes 1105928 | tf_op jit(solution)/shard_map/slice | solution.py:130
  35.9 8.1 %collective-permute-done.4 = f32[16,8,720]{2,1,0:T(8,128)S(1)} collective-permute-done((f32[16,8,720]{2,1,0:T(8,128)S(1)}, f32[16,8,720]{2,1,0:T(8,128)S(1)}, u32[]{:S(2)}, u32[]{:S(2)}) %collective-permute-start.4) | collective-permute-done | bytes 368672 | tf_op jit(solution)/shard_map/ppermute | solution.py:130
  44.0 1.9 %dynamic-slice_select_fusion.1 = f32[16,8,720]{2,1,0:T(8,128)} fusion(f32[16,8,720]{2,1,0:T(8,128)S(1)} %collective-permute-done.4, f32[40,16,720]{2,1,0:T(8,128)} %bitcast.133, s32[]{:T(128)S(6)} %select_n.230, pred[8]{0:T(512)(128)(4,1)S(1)} %slice_select_fusion), kind=kLoop, calls=%fused_computation.59 | loop fusion | flops 92160 | bytes 1105932 | tf_op jit(solution)/shard_map/jit(_where)/select_n | solution.py:131
  45.9 3.5 %all-to-all-start = ((f32[8,16,720]{2,1,0:T(8,128)}), f32[8,16,720]{2,1,0:T(8,128)S(1)}, u32[]{:S(2)}, u32[]{:S(2)}) async-start(f32[8,16,720]{2,1,0:T(8,128)} %bitcast.13), calls=%async_computation | async-start | bytes 786432 | tf_op jit(solution)/shard_map/all_to_all | solution.py:132
  50.9 1.9 %collective-permute-done.5 = f32[24,8,720]{2,1,0:T(8,128)S(1)} collective-permute-done((f32[24,8,720]{2,1,0:T(8,128)}, f32[24,8,720]{2,1,0:T(8,128)S(1)}, u32[]{:S(2)}, u32[]{:S(2)}) %collective-permute-start.5) | collective-permute-done | bytes 552992 | tf_op jit(solution)/shard_map/ppermute | solution.py:130
  52.7 2.0 %dynamic-slice_select_fusion = f32[24,8,720]{2,1,0:T(8,128)} fusion(f32[24,8,720]{2,1,0:T(8,128)S(1)} %collective-permute-done.5, f32[40,16,720]{2,1,0:T(8,128)} %bitcast.134, s32[]{:T(128)S(6)} %add.328, s32[]{:T(128)S(6)} %select_n.230, pred[8]{0:T(512)(128)(4,1)S(1)} %slice_select_fusion), kind=kLoop, calls=%fused_computation.38 | loop fusion | flops 138240 | bytes 1658896 | tf_op jit(solution)/shard_map/jit(_where)/select_n | solution.py:131
  54.7 7.1 %all-to-all-done = f32[8,16,720]{2,1,0:T(8,128)S(1)} async-done(((f32[8,16,720]{2,1,0:T(8,128)}), f32[8,16,720]{2,1,0:T(8,128)S(1)}, u32[]{:S(2)}, u32[]{:S(2)}) %all-to-all-start) | async-done | bytes 368672 | tf_op jit(solution)/shard_map/all_to_all | solution.py:132
  61.8 3.7 %all-to-all-start.2 = ((f32[8,24,720]{2,1,0:T(8,128)}), f32[8,24,720]{2,1,0:T(8,128)S(1)}, u32[]{:S(2)}, u32[]{:S(2)}) async-start(f32[8,24,720]{2,1,0:T(8,128)} %bitcast.24), calls=%async_computation.2 | async-start | bytes 1179648 | tf_op jit(solution)/shard_map/all_to_all | solution.py:132
  66.5 1.2 reshape.332
  72.8 9.2 %all-to-all-done.2 = f32[8,24,720]{2,1,0:T(8,128)S(1)} async-done(((f32[8,24,720]{2,1,0:T(8,128)}), f32[8,24,720]{2,1,0:T(8,128)S(1)}, u32[]{:S(2)}, u32[]{:S(2)}) %all-to-all-start.2) | async-done | bytes 552992 | tf_op jit(solution)/shard_map/all_to_all | solution.py:132
  91.7 3.5 %all-to-all-start.3 = ((f32[24,8,720]{2,0,1:T(8,128)}), f32[24,8,720]{2,0,1:T(8,128)S(1)}, u32[]{:S(2)}, u32[]{:S(2)}) async-start(f32[24,8,720]{2,0,1:T(8,128)} %copy.114), calls=%async_computation.3 | async-start | bytes 1179648 | tf_op jit(solution)/shard_map/all_to_all | solution.py:140
  95.2 1.6 %fusion.72 = f32[16,45,128]{2,1,0:T(8,128)S(1)} fusion(f32[16,45,128]{2,1,0:T(8,128)} %copy-done.12), kind=kOutput, calls=%fused_computation.113 | convolution fusion | flops 71008256 | bytes 737280 | tf_op jit(solution)/shard_map/ljk,kn->ljn/dot_general | solution.py:49
  99.6 12.4 %all-to-all-done.3 = f32[24,8,720]{2,0,1:T(8,128)S(1)} async-done(((f32[24,8,720]{2,0,1:T(8,128)}), f32[24,8,720]{2,0,1:T(8,128)S(1)}, u32[]{:S(2)}, u32[]{:S(2)}) %all-to-all-start.3) | async-done | bytes 552992 | tf_op jit(solution)/shard_map/all_to_all | solution.py:140
  111.9 3.5 %all-to-all-start.1 = ((f32[16,8,720]{2,0,1:T(8,128)}), f32[16,8,720]{2,0,1:T(8,128)S(1)}, u32[]{:S(2)}, u32[]{:S(2)}) async-start(f32[16,8,720]{2,0,1:T(8,128)} %copy.112), calls=%async_computation.1 | async-start | bytes 786432 | tf_op jit(solution)/shard_map/all_to_all | solution.py:140
  115.4 2.1 %collective-permute-start.7 = (f32[24,8,720]{2,1,0:T(8,128)S(1)}, f32[24,8,720]{2,1,0:T(8,128)S(1)}, u32[]{:S(2)}, u32[]{:S(2)}) collective-permute-start(f32[24,8,720]{2,1,0:T(8,128)S(1)} %bitcast.138), channel_id=1, source_target_pairs={{0,16},{8,24},{16,0},{24,8},{1,17},{9,25},{17,1},{25,9},{2,18},{10... | collective-permute-start | bytes 1658888 | tf_op jit(solution)/shard_map/ppermute | solution.py:144
  117.5 10.4 %all-to-all-done.1 = f32[16,8,720]{2,0,1:T(8,128)S(1)} async-done(((f32[16,8,720]{2,0,1:T(8,128)}), f32[16,8,720]{2,0,1:T(8,128)S(1)}, u32[]{:S(2)}, u32[]{:S(2)}) %all-to-all-start.1) | async-done | bytes 368672 | tf_op jit(solution)/shard_map/all_to_all | solution.py:140
  127.9 2.0 %collective-permute-start.6 = (f32[16,8,720]{2,1,0:T(8,128)S(1)}, f32[16,8,720]{2,1,0:T(8,128)S(1)}, u32[]{:S(2)}, u32[]{:S(2)}) collective-permute-start(f32[16,8,720]{2,1,0:T(8,128)S(1)} %bitcast.141), channel_id=1, source_target_pairs={{0,16},{8,24},{16,0},{24,8},{1,17},{9,25},{17,1},{25,9},{2,18},{10... | collective-permute-start | bytes 1105928 | tf_op jit(solution)/shard_map/ppermute | solution.py:144
  130.0 9.8 %collective-permute-done.6 = f32[16,8,720]{2,1,0:T(8,128)S(1)} collective-permute-done((f32[16,8,720]{2,1,0:T(8,128)S(1)}, f32[16,8,720]{2,1,0:T(8,128)S(1)}, u32[]{:S(2)}, u32[]{:S(2)}) %collective-permute-start.6) | collective-permute-done | bytes 368672 | tf_op jit(solution)/shard_map/ppermute | solution.py:144
  139.8 1.9 %fusion.3 = f32[5,8,16,720]{3,2,1,0:T(8,128)} fusion(f32[5,8,16,720]{3,2,1,0:T(8,128)S(1)} %copy-done, f32[5,8,16,720]{3,2,1,0:T(8,128)S(1)} %copy-done.2, f32[5,8,8,720]{3,2,1,0:T(8,128)S(1)} %bitcast.136, f32[5,8,8,720]{3,2,1,0:T(8,128)S(1)} %bitcast.135, pred[16]{0:T(512)(128)(4,1)S(1)} %compare_reduce_fusion, pred[]{:T(512)S(6)} %lt.143), kind=kLoop, calls=%fused_computation.12 | loop fusion | flops 2304000 | bytes 7372817 | tf_op jit(solution)/shard_map/add | solution.py:153
  (120 shorter events, 24.3 us)
Async XLA Ops:
  0.0 14.7 %copy-start = (f32[5,8,16,720]{3,2,1,0:T(8,128)S(1)}, f32[5,8,16,720]{3,2,1,0:T(8,128)}, u32[]{:S(2)}) copy-start(f32[5,8,16,720]{3,2,1,0:T(8,128)} %param.5) | copy-start | bytes 5529604
  0.0 14.1 %copy-start.13 = (f32[8,16,720]{2,1,0:T(8,128)S(1)}, f32[8,16,720]{2,1,0:T(8,128)}, u32[]{:S(2)}) copy-start(f32[8,16,720]{2,1,0:T(8,128)} %param.6) | copy-start | bytes 1105924
  1.8 20.5 %collective-permute-start.3 = (f32[40,720]{1,0:T(8,128)S(1)}, f32[40,720]{1,0:T(8,128)}, u32[]{:S(2)}, u32[]{:S(2)}) collective-permute-start(f32[40,720]{1,0:T(8,128)S(1)} %bitcast.144), channel_id=1, source_target_pairs={{8,0},{16,8},{24,16},{9,1},{17,9},{25,17},{10,2},{18,10},{26,18},{... | collective-permute-start | bytes 345608 | tf_op jit(solution)/shard_map/ppermute | solution.py:82
  4.1 22.5 %collective-permute-start.2 = (f32[48,720]{1,0:T(8,128)S(1)}, f32[48,720]{1,0:T(8,128)S(1)}, u32[]{:S(2)}, u32[]{:S(2)}) collective-permute-start(f32[48,720]{1,0:T(8,128)S(1)} %pad_maximum_fusion.7), channel_id=1, source_target_pairs={{0,8},{8,16},{16,24},{1,9},{9,17},{17,25},{2,10},{10,18},{18,26},{... | collective-permute-start | bytes 414728 | tf_op jit(solution)/shard_map/ppermute | solution.py:79
  11.1 5.7 %collective-permute-start.1 = (f32[40,16]{0,1:T(8,128)S(1)}, f32[40,16]{0,1:T(8,128)S(1)}, u32[]{:S(2)}, u32[]{:S(2)}) collective-permute-start(f32[40,16]{0,1:T(8,128)S(1)} %bitcast.151), channel_id=1, source_target_pairs={{1,0},{2,1},{3,2},{4,3},{5,4},{6,5},{7,6},{0,7},{9,8},{10,9},{11,1... | collective-permute-start | bytes 7688 | tf_op jit(solution)/shard_map/ppermute | solution.py:78
  14.6 1.5 %copy-start.19 = (s32[32]{0:T(128)S(1)}, s32[32]{0:T(128)}, u32[]{:S(2)}) copy-start(s32[32]{0:T(128)} %param.8) | copy-start | bytes 388
  14.6 1.8 %copy-start.20 = (s32[32]{0:T(128)S(1)}, s32[32]{0:T(128)}, u32[]{:S(2)}) copy-start(s32[32]{0:T(128)} %param.9) | copy-start | bytes 388
  14.6 4.9 %collective-permute-start = (f32[48,16]{0,1:T(8,128)S(1)}, f32[48,16]{0,1:T(8,128)S(1)}, u32[]{:S(2)}, u32[]{:S(2)}) collective-permute-start(f32[48,16]{0,1:T(8,128)S(1)} %pad_maximum_fusion.8), channel_id=1, source_target_pairs={{0,1},{1,2},{2,3},{3,4},{4,5},{5,6},{6,7},{7,0},{8,9},{9,10},{10,1... | collective-permute-start | bytes 9224 | tf_op jit(solution)/shard_map/ppermute | solution.py:75
  20.4 6.4 %copy-start.14 = (f32[8,16,720]{2,1,0:T(8,128)S(1)}, f32[8,16,720]{2,1,0:T(8,128)}, u32[]{:S(2)}) copy-start(f32[8,16,720]{2,1,0:T(8,128)} %param.7) | copy-start | bytes 1105924
  26.9 2.9 %copy-start.3 = (f32[5,8,16,721]{3,2,1,0:T(8,128)S(1)}, f32[5,8,16,721]{3,2,1,0:T(8,128)}, u32[]{:S(2)}) copy-start(f32[5,8,16,721]{3,2,1,0:T(8,128)} %multiply_subtract_fusion) | copy-start | bytes 5537284
  30.4 1.3 copy-start.1
  31.7 12.2 %collective-permute-start.4 = (f32[16,8,720]{2,1,0:T(8,128)S(1)}, f32[16,8,720]{2,1,0:T(8,128)S(1)}, u32[]{:S(2)}, u32[]{:S(2)}) collective-permute-start(f32[16,8,720]{2,1,0:T(8,128)S(1)} %constant_dynamic-slice_fusion), channel_id=1, source_target_pairs={{0,16},{8,24},{16,0},{24,8},{1,17},{9,25},{17,1},{25,9},{2,18},{10... | collective-permute-start | bytes 1105928 | tf_op jit(solution)/shard_map/ppermute | solution.py:130
  34.0 36.9 %copy-start.15 = (f32[45,128]{1,0:T(8,128)}, f32[45,128]{1,0:T(8,128)S(1)}, u32[]{:S(2)}) copy-start(f32[45,128]{1,0:T(8,128)S(1)} %broadcast_maximum_fusion) | copy-start | bytes 69124
  35.9 16.8 %collective-permute-start.5 = (f32[24,8,720]{2,1,0:T(8,128)}, f32[24,8,720]{2,1,0:T(8,128)S(1)}, u32[]{:S(2)}, u32[]{:S(2)}) collective-permute-start(f32[24,8,720]{2,1,0:T(8,128)} %constant_dynamic-slice_fusion.1), channel_id=1, source_target_pairs={{0,16},{8,24},{16,0},{24,8},{1,17},{9,25},{17,1},{25,9},{2,18},{10... | collective-permute-start | bytes 1658888 | tf_op jit(solution)/shard_map/ppermute | solution.py:130
  45.9 15.9 %all-to-all-start = ((f32[8,16,720]{2,1,0:T(8,128)}), f32[8,16,720]{2,1,0:T(8,128)S(1)}, u32[]{:S(2)}, u32[]{:S(2)}) async-start(f32[8,16,720]{2,1,0:T(8,128)} %bitcast.13), calls=%async_computation | async-start | bytes 786432 | tf_op jit(solution)/shard_map/all_to_all | solution.py:132
  50.8 20.1 %copy-start.4 = (f32[45,128]{1,0:T(8,128)}, f32[45,128]{1,0:T(8,128)S(1)}, u32[]{:S(2)}) copy-start(f32[45,128]{1,0:T(8,128)S(1)} %get-tuple-element.15) | copy-start | bytes 69124
  50.8 20.1 %copy-start.7 = (f32[45,128]{1,0:T(8,128)}, f32[45,128]{1,0:T(8,128)S(1)}, u32[]{:S(2)}) copy-start(f32[45,128]{1,0:T(8,128)S(1)} %get-tuple-element.16) | copy-start | bytes 69124
  50.9 20.1 %copy-start.17 = (f32[45,128]{1,0:T(8,128)}, f32[45,128]{1,0:T(8,128)S(1)}, u32[]{:S(2)}) copy-start(f32[45,128]{1,0:T(8,128)S(1)} %fusion.100) | copy-start | bytes 69124
  61.8 20.2 %all-to-all-start.2 = ((f32[8,24,720]{2,1,0:T(8,128)}), f32[8,24,720]{2,1,0:T(8,128)S(1)}, u32[]{:S(2)}, u32[]{:S(2)}) async-start(f32[8,24,720]{2,1,0:T(8,128)} %bitcast.24), calls=%async_computation.2 | async-start | bytes 1179648 | tf_op jit(solution)/shard_map/all_to_all | solution.py:132
  69.8 1.8 %copy-start.10 = (f32[16,45,128]{2,1,0:T(8,128)}, f32[16,45,128]{2,1,0:T(8,128)S(1)}, u32[]{:S(2)}) copy-start(f32[16,45,128]{2,1,0:T(8,128)S(1)} %fusion.9) | copy-start | bytes 1105924
  82.6 1.0 copy-start.5
  82.6 1.0 copy-start.8
  83.6 1.3 copy-start.16
  83.6 1.3 copy-start.18
  90.7 6.1 %copy-start.11 = (f32[16,45,128]{2,1,0:T(8,128)S(1)}, f32[16,45,128]{2,1,0:T(8,128)}, u32[]{:S(2)}) copy-start(f32[16,45,128]{2,1,0:T(8,128)} %copy-done.10) | copy-start | bytes 1105924
  90.7 6.7 %copy-start.6 = (f32[45,128]{1,0:T(8,128)S(1)}, f32[45,128]{1,0:T(8,128)}, u32[]{:S(2)}) copy-start(f32[45,128]{1,0:T(8,128)} %copy-done.4) | copy-start | bytes 69124
  90.7 6.7 %copy-start.9 = (f32[45,128]{1,0:T(8,128)S(1)}, f32[45,128]{1,0:T(8,128)}, u32[]{:S(2)}) copy-start(f32[45,128]{1,0:T(8,128)} %copy-done.7) | copy-start | bytes 69124
  91.7 20.2 %all-to-all-start.3 = ((f32[24,8,720]{2,0,1:T(8,128)}), f32[24,8,720]{2,0,1:T(8,128)S(1)}, u32[]{:S(2)}, u32[]{:S(2)}) async-start(f32[24,8,720]{2,0,1:T(8,128)} %copy.114), calls=%async_computation.3 | async-start | bytes 1179648 | tf_op jit(solution)/shard_map/all_to_all | solution.py:140
  111.9 15.9 %all-to-all-start.1 = ((f32[16,8,720]{2,0,1:T(8,128)}), f32[16,8,720]{2,0,1:T(8,128)S(1)}, u32[]{:S(2)}, u32[]{:S(2)}) async-start(f32[16,8,720]{2,0,1:T(8,128)} %copy.112), calls=%async_computation.1 | async-start | bytes 786432 | tf_op jit(solution)/shard_map/all_to_all | solution.py:140
  115.4 24.4 %collective-permute-start.7 = (f32[24,8,720]{2,1,0:T(8,128)S(1)}, f32[24,8,720]{2,1,0:T(8,128)S(1)}, u32[]{:S(2)}, u32[]{:S(2)}) collective-permute-start(f32[24,8,720]{2,1,0:T(8,128)S(1)} %bitcast.138), channel_id=1, source_target_pairs={{0,16},{8,24},{16,0},{24,8},{1,17},{9,25},{17,1},{25,9},{2,18},{10... | collective-permute-start | bytes 1658888 | tf_op jit(solution)/shard_map/ppermute | solution.py:144
  127.9 12.0 %copy-start.2 = (f32[5,8,16,720]{3,2,1,0:T(8,128)S(1)}, f32[5,8,16,720]{3,2,1,0:T(8,128)}, u32[]{:S(2)}) copy-start(f32[5,8,16,720]{3,2,1,0:T(8,128)} %copy-done.1) | copy-start | bytes 5529604
  127.9 11.9 %collective-permute-start.6 = (f32[16,8,720]{2,1,0:T(8,128)S(1)}, f32[16,8,720]{2,1,0:T(8,128)S(1)}, u32[]{:S(2)}, u32[]{:S(2)}) collective-permute-start(f32[16,8,720]{2,1,0:T(8,128)S(1)} %bitcast.141), channel_id=1, source_target_pairs={{0,16},{8,24},{16,0},{24,8},{1,17},{9,25},{17,1},{25,9},{2,18},{10... | collective-permute-start | bytes 1105928 | tf_op jit(solution)/shard_map/ppermute | solution.py:144
  (1 other events, 0.7 us)

commit v18 on v14

--- a/solution.py
+++ b/solution.py
@@ -117,7 +117,7 @@
     given = jnp.where(is_low, high_half, low_half)
     kept_filtered = jnp.where(is_low, is_filtered[:half_rows], is_filtered[half_rows:])
     kept_cut = jnp.where(is_low, row_cut[:half_rows], row_cut[half_rows:])
-    chunk_sizes = (stacked * 4 // 5, stacked - stacked * 4 // 5)
+    chunk_sizes = (stacked * 3 // 10, stacked - stacked * 3 // 10)
     returned_parts, handed_parts = [], []
     chunk_start = 0
     for chunk_stack in chunk_sizes:

time: 156 us -> 160 us (1.026)
  local copies, waits for them, and re-layouts: 19.2 us -> 31.3 us
  blocking collectives: 10.7 us -> 0 us
  starting transfers between devices: 25.1 us -> 32.5 us
  waiting for transfers between devices: 67.8 us -> 61.2 us
    all_to_all x1 -> x0, blocking collectives: 10.7 us -> none  [body(): lax.all_to_all(smoothed, 'lon', split_axis=1, concat_axis=0, tiled=True)]
    ppermute x2, waiting for transfers between devices: 20.9 us -> 11.2 us  [body(): taken = lax.ppermute(given[rows_of_part], 'lat', pair_perm)]
    all_to_all x1 -> x2, waiting for transfers between devices: 16.4 us -> 25.9 us  [body(): lax.all_to_all(smoothed, 'lon', split_axis=1, concat_axis=0, tiled=True)]
    all_to_all x2, waiting for transfers between devices: 21 us -> 15.5 us  [body(): lax.all_to_all(pair_lines.reshape(chunk_stack * half_rows, columns), 'lon...]
    all_to_all x1 -> x2, starting transfers between devices: 3.55 us -> 7.77 us  [body(): lax.all_to_all(smoothed, 'lon', split_axis=1, concat_axis=0, tiled=True)]
    all_to_all x2 -> x4, local copies, waits for them, and re-layouts: 0.53 us -> 4.15 us  [body(): lax.all_to_all(pair_lines.reshape(chunk_stack * half_rows, columns), 'lon...]
    unnamed x72 -> x30, local copies, waits for them, and re-layouts: 2.8 us -> 4.97 us
    ppermute x2, starting transfers between devices: 2.03 us -> 4.11 us  [body(): handed_parts.append(lax.ppermute(returned, 'lat', pair_perm))]
  transfers between devices with their start and end apart: 11 -> 12, of which waited for: 6 -> 7; matrix products, arithmetic and copies ran while one was open for 19% -> 21% of each run, Pallas kernels for 0% -> 0%
where the time goes in v18:
time: 160 us; the launch traced here: 158 us
  waiting for transfers between devices  61.2 us (38%)
  starting transfers between devices  32.5 us (20%)
  local copies, waits for them, and re-layouts  31.3 us (20%)
  matrix products  16.7 us (10%)
  other arithmetic  16.1 us (10%)
    all_to_all x2, waiting for transfers between devices, body(): lax.all_to_all(smoothed, 'lon', split_axis=1, concat_axis=0, tiled=True)  25.9 us
    all_to_all x2, waiting for transfers between devices, body(): lax.all_to_all(pair_lines.reshape(chunk_stack * half_rows, columns), 'lon...  15.5 us
    ppermute x2, waiting for transfers between devices, body(): taken = lax.ppermute(given[rows_of_part], 'lat', pair_perm)  11.2 us
    ppermute x2, waiting for transfers between devices, body(): handed_parts.append(lax.ppermute(returned, 'lat', pair_perm))  8.71 us
    all_to_all x2, starting transfers between devices, body(): lax.all_to_all(smoothed, 'lon', split_axis=1, concat_axis=0, tiled=True)  7.77 us
    all_to_all x2, starting transfers between devices, body(): lax.all_to_all(pair_lines.reshape(chunk_stack * half_rows, columns), 'lon...  7.33 us
    ppermute x1, starting transfers between devices, body(): lax.ppermute(jnp.concatenate([flat_fields[:, -1], lat_courant[:, -1]], ax...  5.49 us
    concatenate x4, local copies, waits for them, and re-layouts, body(): jnp.concatenate([from_below[:stacked, None], flat_fields, from_above[:, N...  5.31 us
  transfers between devices with their start and end apart: 12, of which 7 were waited for; matrix products, arithmetic and copies ran while one was open for 21% of the time, Pallas kernels for 0%

profile of v18, /device:TPU:0, one launch (start us, length us, event | category | flops | bytes accessed | tf_op | source)
XLA Modules:
  0.0 158.4 jit_solution(6690409014177968263)
XLA Ops:
  0.0 1.8 %fusion.247 = (f32[40,1,720]{2,1,0:T(1,128)S(1)}, f32[40,1,720]{2,1,0:T(1,128)S(1)}) fusion(f32[40,16,720]{2,1,0:T(8,128)} %bitcast.123), kind=kLoop, calls=%fused_computation.289 | loop fusion | bytes 460800 | tf_op jit(solution)/shard_map/slice | solution.py:80
  3.5 5.5 %collective-permute-start.2 = (f32[48,720]{1,0:T(8,128)}, f32[48,720]{1,0:T(8,128)}, u32[]{:S(2)}, u32[]{:S(2)}) collective-permute-start(f32[48,720]{1,0:T(8,128)} %pad_maximum_fusion.7), channel_id=1, source_target_pairs={{0,8},{8,16},{16,24},{1,9},{9,17},{17,25},{2,10},{10,18},{18,26},{... | collective-permute-start | bytes 414728 | tf_op jit(solution)/shard_map/ppermute | solution.py:79
  9.7 1.3 collective-permute-start.3
  10.9 1.2 fusion.246
  12.9 3.6 %collective-permute-start.1 = (f32[40,16]{0,1:T(8,128)S(1)}, f32[40,16]{0,1:T(8,128)S(1)}, u32[]{:S(2)}, u32[]{:S(2)}) collective-permute-start(f32[40,16]{0,1:T(8,128)S(1)} %bitcast.138), channel_id=1, source_target_pairs={{1,0},{2,1},{3,2},{4,3},{5,4},{6,5},{7,6},{0,7},{9,8},{10,9},{11,1... | collective-permute-start | bytes 7688 | tf_op jit(solution)/shard_map/ppermute | solution.py:78
  16.5 1.4 constant_dynamic-update-slice_fusion
  21.9 2.0 %multiply_subtract_fusion = f32[5,8,16,721]{3,2,1,0:T(8,128)} fusion(f32[5,8,16,1]{3,2,1,0:T(8,128)S(1)} %copy.106, f32[5,8,16,720]{3,2,1,0:T(8,128)S(1)} %copy-done, f32[5,8,16,1]{3,2,1,0:T(8,128)S(1)} %copy.103, f32[8,16,721]{2,1,0:T(8,128)S(1)} %get-tuple-element.14, f32[8,16,721]{2,1,0:T(8,128)S(1)} %get-tuple-element.13), kind=kLoop, calls=%fused_computation.13 | loop fusion | flops 3230080 | bytes 4432384 | tf_op jit(solution)/shard_map/sub | solution.py:60
  24.9 3.2 %dynamic-update-slice.1 = f32[5,8,17,720]{3,2,1,0:T(8,128)} dynamic-update-slice(f32[5,8,17,720]{3,2,1,0:T(8,128)} %constant_dynamic-update-slice_fusion, f32[5,8,1,720]{3,2,1,0:T(1,128)S(1)} %copy.110, s32[]{} %constant.133, s32[]{} %constant.133, s32[]{} %constant.134, s32[]{} %constant.133) | dynamic-update-slice | bytes 230404 | tf_op jit(solution)/shard_map/concatenate | solution.py:88
  31.1 2.9 %subtract_select_fusion = f32[5,8,17,720]{3,2,1,0:T(8,128)S(1)} fusion(f32[5,8,17,720]{3,2,1,0:T(8,128)} %dynamic-update-slice.1, f32[5,8,16,720]{3,2,1,0:T(8,128)S(1)} %copy-done, f32[5,8,1,720]{3,2,1,0:T(1,128)S(1)} %copy.109, f32[8,17,720]{2,1,0:T(8,128)S(1)} %get-tuple-element.16, f32[8,17,720]{2,1,0:T(8,128)S(1)} %get-tuple-element.15, ...), kind=kLoop, calls=%fused_computation.3 | loop fusion | flops 3427200 | bytes 6658577 | tf_op jit(solution)/shard_map/jit(_where)/select_n | solution.py:95
  37.7 2.9 %collective-permute-start.4 = (f32[12,8,720]{2,1,0:T(8,128)}, f32[12,8,720]{2,1,0:T(8,128)S(1)}, u32[]{:S(2)}, u32[]{:S(2)}) collective-permute-start(f32[12,8,720]{2,1,0:T(8,128)} %slice.123), channel_id=1, source_target_pairs={{0,16},{8,24},{16,0},{24,8},{1,17},{9,25},{17,1},{25,9},{2,18},{10... | collective-permute-start | bytes 829448 | tf_op jit(solution)/shard_map/ppermute | solution.py:129
  41.9 2.0 %slice.125 = f32[28,8,720]{2,1,0:T(8,128)} slice(f32[40,8,720]{2,1,0:T(8,128)} %copy-done.4), slice={[12:40], [0:8], [0:720]} | slice | bytes 1290240 | tf_op jit(solution)/shard_map/slice | solution.py:129
  44.0 4.3 %collective-permute-done.4 = f32[12,8,720]{2,1,0:T(8,128)S(1)} collective-permute-done((f32[12,8,720]{2,1,0:T(8,128)}, f32[12,8,720]{2,1,0:T(8,128)S(1)}, u32[]{:S(2)}, u32[]{:S(2)}) %collective-permute-start.4) | collective-permute-done | bytes 276512 | tf_op jit(solution)/shard_map/ppermute | solution.py:129
  50.9 3.5 %all-to-all-start = ((f32[8,12,720]{2,1,0:T(8,128)}), f32[8,12,720]{2,1,0:T(8,128)S(1)}, u32[]{:S(2)}, u32[]{:S(2)}) async-start(f32[8,12,720]{2,1,0:T(8,128)} %all_to_all.48), calls=%async_computation | async-start | bytes 786432 | tf_op jit(solution)/shard_map/all_to_all | solution.py:131
  54.4 6.9 %collective-permute-done.5 = f32[28,8,720]{2,1,0:T(8,128)} collective-permute-done((f32[28,8,720]{2,1,0:T(8,128)}, f32[28,8,720]{2,1,0:T(8,128)}, u32[]{:S(2)}, u32[]{:S(2)}) %collective-permute-start.5) | collective-permute-done | bytes 645152 | tf_op jit(solution)/shard_map/ppermute | solution.py:129
  61.3 2.1 %slice_select_fusion.2 = f32[28,8,720]{2,1,0:T(8,128)} fusion(f32[28,8,720]{2,1,0:T(8,128)} %collective-permute-done.5, f32[40,8,720]{2,1,0:T(8,128)S(1)} %get-tuple-element.7, pred[8]{0:T(512)(128)(4,1)S(1)} %slice_select_fusion.4), kind=kLoop, calls=%fused_computation.40 | loop fusion | flops 161280 | bytes 1935368 | tf_op jit(solution)/shard_map/jit(_where)/select_n | solution.py:130
  63.4 2.1 %all_to_all.54 = f32[8,28,720]{2,1,0:T(8,128)} reshape(f32[28,8,720]{2,1,0:T(8,128)} %slice_select_fusion.2) | data formatting | bytes 1290240 | tf_op jit(solution)/shard_map/all_to_all | solution.py:131
  65.5 1.4 all-to-all-done
  66.9 3.9 %all-to-all-start.2 = ((f32[8,28,720]{2,1,0:T(8,128)}), f32[8,28,720]{2,1,0:T(8,128)S(1)}, u32[]{:S(2)}, u32[]{:S(2)}) async-start(f32[8,28,720]{2,1,0:T(8,128)} %all_to_all.54), calls=%async_computation.2 | async-start | bytes 1572864 | tf_op jit(solution)/shard_map/all_to_all | solution.py:131
  74.6 1.2 fusion.72
  76.4 1.2 fusion.10
  77.7 14.1 %all-to-all-done.2 = f32[8,28,720]{2,1,0:T(8,128)S(1)} async-done(((f32[8,28,720]{2,1,0:T(8,128)}), f32[8,28,720]{2,1,0:T(8,128)S(1)}, u32[]{:S(2)}, u32[]{:S(2)}) %all-to-all-start.2) | async-done | bytes 645152 | tf_op jit(solution)/shard_map/all_to_all | solution.py:131
  102.2 3.7 %all-to-all-start.3 = ((f32[28,8,720]{2,0,1:T(8,128)}), f32[28,8,720]{2,0,1:T(8,128)S(1)}, u32[]{:S(2)}, u32[]{:S(2)}) async-start(f32[28,8,720]{2,0,1:T(8,128)} %copy.114), calls=%async_computation.3 | async-start | bytes 1572864 | tf_op jit(solution)/shard_map/all_to_all | solution.py:139
  105.9 1.5 fusion.69
  107.4 1.5 convolution_subtract_fusion.4
  111.3 15.5 %all-to-all-done.3 = f32[28,8,720]{2,0,1:T(8,128)S(1)} async-done(((f32[28,8,720]{2,0,1:T(8,128)}), f32[28,8,720]{2,0,1:T(8,128)S(1)}, u32[]{:S(2)}, u32[]{:S(2)}) %all-to-all-start.3) | async-done | bytes 645152 | tf_op jit(solution)/shard_map/all_to_all | solution.py:139
  126.8 4.1 %all-to-all-start.1 = ((f32[12,8,720]{2,0,1:T(8,128)}), f32[12,8,720]{2,0,1:T(8,128)}, u32[]{:S(2)}, u32[]{:S(2)}) async-start(f32[12,8,720]{2,0,1:T(8,128)} %copy.112), calls=%async_computation.1 | async-start | bytes 786432 | tf_op jit(solution)/shard_map/all_to_all | solution.py:139
  131.0 2.1 %collective-permute-start.7 = (f32[28,8,720]{2,1,0:T(8,128)S(1)}, f32[28,8,720]{2,1,0:T(8,128)}, u32[]{:S(2)}, u32[]{:S(2)}) collective-permute-start(f32[28,8,720]{2,1,0:T(8,128)S(1)} %reshape.335), channel_id=1, source_target_pairs={{0,16},{8,24},{16,0},{24,8},{1,17},{9,25},{17,1},{25,9},{2,18},{10... | collective-permute-start | bytes 1935368 | tf_op jit(solution)/shard_map/ppermute | solution.py:143
  133.1 10.4 %all-to-all-done.1 = f32[12,8,720]{2,0,1:T(8,128)} async-done(((f32[12,8,720]{2,0,1:T(8,128)}), f32[12,8,720]{2,0,1:T(8,128)}, u32[]{:S(2)}, u32[]{:S(2)}) %all-to-all-start.1) | async-done | bytes 276512 | tf_op jit(solution)/shard_map/all_to_all | solution.py:139
  144.5 2.0 %collective-permute-start.6 = (f32[12,8,720]{2,1,0:T(8,128)S(1)}, f32[12,8,720]{2,1,0:T(8,128)S(1)}, u32[]{:S(2)}, u32[]{:S(2)}) collective-permute-start(f32[12,8,720]{2,1,0:T(8,128)S(1)} %reshape.333), channel_id=1, source_target_pairs={{0,16},{8,24},{16,0},{24,8},{1,17},{9,25},{17,1},{25,9},{2,18},{10... | collective-permute-start | bytes 829448 | tf_op jit(solution)/shard_map/ppermute | solution.py:143
  146.6 8.7 %collective-permute-done.6 = f32[12,8,720]{2,1,0:T(8,128)S(1)} collective-permute-done((f32[12,8,720]{2,1,0:T(8,128)S(1)}, f32[12,8,720]{2,1,0:T(8,128)S(1)}, u32[]{:S(2)}, u32[]{:S(2)}) %collective-permute-start.6) | collective-permute-done | bytes 276512 | tf_op jit(solution)/shard_map/ppermute | solution.py:143
  155.3 1.2 pad_maximum_fusion.4
  156.5 1.9 %fusion.3 = f32[5,8,16,720]{3,2,1,0:T(8,128)} fusion(f32[5,8,16,720]{3,2,1,0:T(8,128)S(1)} %copy-done, f32[5,8,16,720]{3,2,1,0:T(8,128)S(1)} %copy-done.2, f32[5,8,8,720]{3,2,1,0:T(8,128)S(1)} %bitcast.127, f32[5,8,8,720]{3,2,1,0:T(8,128)S(1)} %bitcast.126, pred[16]{0:T(512)(128)(4,1)S(1)} %compare_reduce_fusion, pred[]{:T(512)S(6)} %lt.139), kind=kLoop, calls=%fused_computation.12 | loop fusion | flops 2304000 | bytes 7372817 | tf_op jit(solution)/shard_map/add | solution.py:152
  (109 shorter events, 36.9 us)
Async XLA Ops:
  0.0 16.5 %copy-start = (f32[5,8,16,720]{3,2,1,0:T(8,128)S(1)}, f32[5,8,16,720]{3,2,1,0:T(8,128)}, u32[]{:S(2)}) copy-start(f32[5,8,16,720]{3,2,1,0:T(8,128)} %param.5) | copy-start | bytes 5529604
  0.0 12.4 %copy-start.8 = (f32[8,16,720]{2,1,0:T(8,128)S(1)}, f32[8,16,720]{2,1,0:T(8,128)}, u32[]{:S(2)}) copy-start(f32[8,16,720]{2,1,0:T(8,128)} %param.6) | copy-start | bytes 1105924
  3.5 24.7 %collective-permute-start.2 = (f32[48,720]{1,0:T(8,128)}, f32[48,720]{1,0:T(8,128)}, u32[]{:S(2)}, u32[]{:S(2)}) collective-permute-start(f32[48,720]{1,0:T(8,128)} %pad_maximum_fusion.7), channel_id=1, source_target_pairs={{0,8},{8,16},{16,24},{1,9},{9,17},{17,25},{2,10},{10,18},{18,26},{... | collective-permute-start | bytes 414728 | tf_op jit(solution)/shard_map/ppermute | solution.py:79
  9.7 14.3 %collective-permute-start.3 = (f32[40,720]{1,0:T(8,128)}, f32[40,720]{1,0:T(8,128)}, u32[]{:S(2)}, u32[]{:S(2)}) collective-permute-start(f32[40,720]{1,0:T(8,128)} %bitcast.119), channel_id=1, source_target_pairs={{8,0},{16,8},{24,16},{9,1},{17,9},{25,17},{10,2},{18,10},{26,18},{... | collective-permute-start | bytes 345608 | tf_op jit(solution)/shard_map/ppermute | solution.py:82
  12.7 6.9 %collective-permute-start = (f32[48,16]{0,1:T(8,128)S(1)}, f32[48,16]{0,1:T(8,128)S(1)}, u32[]{:S(2)}, u32[]{:S(2)}) collective-permute-start(f32[48,16]{0,1:T(8,128)S(1)} %pad_maximum_fusion.8), channel_id=1, source_target_pairs={{0,1},{1,2},{2,3},{3,4},{4,5},{5,6},{6,7},{7,0},{8,9},{9,10},{10,1... | collective-permute-start | bytes 9224 | tf_op jit(solution)/shard_map/ppermute | solution.py:75
  12.9 6.3 %collective-permute-start.1 = (f32[40,16]{0,1:T(8,128)S(1)}, f32[40,16]{0,1:T(8,128)S(1)}, u32[]{:S(2)}, u32[]{:S(2)}) collective-permute-start(f32[40,16]{0,1:T(8,128)S(1)} %bitcast.138), channel_id=1, source_target_pairs={{1,0},{2,1},{3,2},{4,3},{5,4},{6,5},{7,6},{0,7},{9,8},{10,9},{11,1... | collective-permute-start | bytes 7688 | tf_op jit(solution)/shard_map/ppermute | solution.py:78
  16.5 2.3 %copy-start.11 = (s32[32]{0:T(128)S(1)}, s32[32]{0:T(128)}, u32[]{:S(2)}) copy-start(s32[32]{0:T(128)} %param.8) | copy-start | bytes 388
  16.5 2.5 %copy-start.12 = (s32[32]{0:T(128)S(1)}, s32[32]{0:T(128)}, u32[]{:S(2)}) copy-start(s32[32]{0:T(128)} %param.9) | copy-start | bytes 388
  31.1 2.9 %copy-start.3 = (f32[5,8,16,721]{3,2,1,0:T(8,128)S(1)}, f32[5,8,16,721]{3,2,1,0:T(8,128)}, u32[]{:S(2)}) copy-start(f32[5,8,16,721]{3,2,1,0:T(8,128)} %multiply_subtract_fusion) | copy-start | bytes 5537284
  34.6 1.3 copy-start.1
  35.9 1.0 copy-start.4
  37.7 10.7 %collective-permute-start.4 = (f32[12,8,720]{2,1,0:T(8,128)}, f32[12,8,720]{2,1,0:T(8,128)S(1)}, u32[]{:S(2)}, u32[]{:S(2)}) collective-permute-start(f32[12,8,720]{2,1,0:T(8,128)} %slice.123), channel_id=1, source_target_pairs={{0,16},{8,24},{16,0},{24,8},{1,17},{9,25},{17,1},{25,9},{2,18},{10... | collective-permute-start | bytes 829448 | tf_op jit(solution)/shard_map/ppermute | solution.py:129
  44.0 17.3 %collective-permute-start.5 = (f32[28,8,720]{2,1,0:T(8,128)}, f32[28,8,720]{2,1,0:T(8,128)}, u32[]{:S(2)}, u32[]{:S(2)}) collective-permute-start(f32[28,8,720]{2,1,0:T(8,128)} %slice.125), channel_id=1, source_target_pairs={{0,16},{8,24},{16,0},{24,8},{1,17},{9,25},{17,1},{25,9},{2,18},{10... | collective-permute-start | bytes 1935368 | tf_op jit(solution)/shard_map/ppermute | solution.py:129
  48.4 0.7 copy-start.9
  50.9 15.9 %all-to-all-start = ((f32[8,12,720]{2,1,0:T(8,128)}), f32[8,12,720]{2,1,0:T(8,128)S(1)}, u32[]{:S(2)}, u32[]{:S(2)}) async-start(f32[8,12,720]{2,1,0:T(8,128)} %all_to_all.48), calls=%async_computation | async-start | bytes 786432 | tf_op jit(solution)/shard_map/all_to_all | solution.py:131
  66.9 24.9 %all-to-all-start.2 = ((f32[8,28,720]{2,1,0:T(8,128)}), f32[8,28,720]{2,1,0:T(8,128)S(1)}, u32[]{:S(2)}, u32[]{:S(2)}) async-start(f32[8,28,720]{2,1,0:T(8,128)} %all_to_all.54), calls=%async_computation.2 | async-start | bytes 1572864 | tf_op jit(solution)/shard_map/all_to_all | solution.py:131
  70.7 3.4 %copy-start.10 = (f32[45,128]{1,0:T(8,128)S(1)}, f32[45,128]{1,0:T(8,128)}, u32[]{:S(2)}) copy-start(f32[45,128]{1,0:T(8,128)} %broadcast_maximum_fusion) | copy-start | bytes 69124
  74.6 1.8 %copy-start.5 = (f32[12,45,128]{2,1,0:T(8,128)}, f32[12,45,128]{2,1,0:T(8,128)S(1)}, u32[]{:S(2)}) copy-start(f32[12,45,128]{2,1,0:T(8,128)S(1)} %fusion.11) | copy-start | bytes 829444
  102.2 5.2 %copy-start.7 = (f32[12,45,128]{2,1,0:T(8,128)S(1)}, f32[12,45,128]{2,1,0:T(8,128)}, u32[]{:S(2)}) copy-start(f32[12,45,128]{2,1,0:T(8,128)} %fusion.72) | copy-start | bytes 829444
  102.2 6.7 %copy-start.6 = (f32[12,45,128]{2,1,0:T(8,128)S(1)}, f32[12,45,128]{2,1,0:T(8,128)}, u32[]{:S(2)}) copy-start(f32[12,45,128]{2,1,0:T(8,128)} %copy-done.5) | copy-start | bytes 829444
  102.2 24.6 %all-to-all-start.3 = ((f32[28,8,720]{2,0,1:T(8,128)}), f32[28,8,720]{2,0,1:T(8,128)S(1)}, u32[]{:S(2)}, u32[]{:S(2)}) async-start(f32[28,8,720]{2,0,1:T(8,128)} %copy.114), calls=%async_computation.3 | async-start | bytes 1572864 | tf_op jit(solution)/shard_map/all_to_all | solution.py:139
  126.8 16.7 %all-to-all-start.1 = ((f32[12,8,720]{2,0,1:T(8,128)}), f32[12,8,720]{2,0,1:T(8,128)}, u32[]{:S(2)}, u32[]{:S(2)}) async-start(f32[12,8,720]{2,0,1:T(8,128)} %copy.112), calls=%async_computation.1 | async-start | bytes 786432 | tf_op jit(solution)/shard_map/all_to_all | solution.py:139
  131.0 24.3 %collective-permute-start.7 = (f32[28,8,720]{2,1,0:T(8,128)S(1)}, f32[28,8,720]{2,1,0:T(8,128)}, u32[]{:S(2)}, u32[]{:S(2)}) collective-permute-start(f32[28,8,720]{2,1,0:T(8,128)S(1)} %reshape.335), channel_id=1, source_target_pairs={{0,16},{8,24},{16,0},{24,8},{1,17},{9,25},{17,1},{25,9},{2,18},{10... | collective-permute-start | bytes 1935368 | tf_op jit(solution)/shard_map/ppermute | solution.py:143
  144.5 12.0 %copy-start.2 = (f32[5,8,16,720]{3,2,1,0:T(8,128)S(1)}, f32[5,8,16,720]{3,2,1,0:T(8,128)}, u32[]{:S(2)}) copy-start(f32[5,8,16,720]{3,2,1,0:T(8,128)} %copy-done.1) | copy-start | bytes 5529604
  144.5 10.8 %collective-permute-start.6 = (f32[12,8,720]{2,1,0:T(8,128)S(1)}, f32[12,8,720]{2,1,0:T(8,128)S(1)}, u32[]{:S(2)}, u32[]{:S(2)}) collective-permute-start(f32[12,8,720]{2,1,0:T(8,128)S(1)} %reshape.333), channel_id=1, source_target_pairs={{0,16},{8,24},{16,0},{24,8},{1,17},{9,25},{17,1},{25,9},{2,18},{10... | collective-permute-start | bytes 829448 | tf_op jit(solution)/shard_map/ppermute | solution.py:143
